TPU v7x, 32 devices: a whole 2x2x4 slice. The times are simulated.
32 devices in a mesh: src: 2 (over core), rows: 16 (over z, y, x).
Axes of the slice: x: 2, y: 2, z: 4, core: 2. Of those that a mesh axis runs over, the one named last changes fastest.
Arguments:
- slip_units: int32 [512, 2000], P(None, 'src'), may hold values from 0 to 15
- slip_scales: float32 [512, 16], P(None, 'src'), may hold values from 0.02 to 0.2
- green: bfloat16 [2000, 491520], P('src', 'rows'), may hold values from -0.08944272 to 0.08944272
- coast_gauges: int32 [2048, 8], replicated, may hold values from 0 to 2047
- coast_amps: float32 [2048, 8], replicated, may hold values from 0.05 to 0.3
- coast_counts: int32 [2048], replicated, may hold values from 1 to 8
Outputs:
- onshore: float32 [512, 2048], P('src', 'rows')
Inputs may be any that keep to these rules, and one draw needn't show every extreme that they name: coast_gauges names gauges.
All inputs are finite; a program needn't handle non-finite values.
Results may differ from a plain program's by a relative error of at most 0.0039.
Values may be sent and summed in bfloat16 or wider, within the bound.
No kernel may reach another device: no remote copies, remote signals or barrier semaphores. Data moves between devices by JAX's collectives and lax.ppermute only.
A program may use at most 192 MiB of HBM per device.

v0:
```python
import numpy as np
import jax
import jax.numpy as jnp
from jax import lax
from jax.experimental import pallas as pl
from jax.experimental.pallas import tpu as pltpu
from jax.sharding import PartitionSpec as P

NT = 240
UBLK = 125
SEG = 1920


def matmul_kernel(slip_ref, green_ref, other_ref, mine_ref):
    half = other_ref.shape[0]
    product = jnp.dot(slip_ref[...], green_ref[...], preferred_element_type=jnp.float32)
    other_ref[...] = product[:half].astype(jnp.bfloat16)
    mine_ref[...] = product[half:].astype(jnp.bfloat16)


def partials_of(slip_ordered, green, chunk, width, tile):
    scenarios, sources = slip_ordered.shape
    half = scenarios // 2
    steps = width // tile
    return pl.pallas_call(
        matmul_kernel,
        grid=(steps,),
        in_specs=[
            pl.BlockSpec((scenarios, sources), lambda j: (0, 0)),
            pl.BlockSpec((sources, tile), lambda j: (0, chunk * steps + j)),
        ],
        out_specs=[pl.BlockSpec((half, tile), lambda j: (0, j))] * 2,
        out_shape=[jax.ShapeDtypeStruct((half, width), jnp.bfloat16)] * 2,
        cost_estimate=pl.CostEstimate(
            flops=2 * scenarios * sources * width,
            transcendentals=0,
            bytes_accessed=2 * (sources * width + scenarios * width),
        ),
    )(slip_ordered, green)


def peak_kernel(mine_ref, recv_ref, out_ref):
    wave = mine_ref[...].astype(jnp.float32) + recv_ref[...].astype(jnp.float32)
    flipped = jnp.abs(wave).T
    gauges = SEG // NT
    out_ref[...] = jnp.max(flipped.reshape(gauges, NT, flipped.shape[1]), axis=1)


def peaks_of(mine, recv):
    rows, cols = mine.shape
    blocks = cols // SEG
    gauges = SEG // NT
    band = 128 if rows % 128 == 0 else rows
    return pl.pallas_call(
        peak_kernel,
        grid=(blocks, rows // band),
        in_specs=[pl.BlockSpec((band, SEG), lambda j, i: (i, j))] * 2,
        out_specs=pl.BlockSpec((gauges, band), lambda j, i: (j, i)),
        out_shape=jax.ShapeDtypeStruct((blocks * gauges, rows), jnp.float32),
        cost_estimate=pl.CostEstimate(
            flops=3 * rows * cols, transcendentals=0, bytes_accessed=4 * rows * cols
        ),
    )(mine, recv)


def doubling_masks(owners):
    masks = []
    m = 1
    while m < owners:
        masks.append(m)
        m *= 2
    return masks[::-1]


def gather_rows(block, owners):
    me = lax.axis_index("rows")
    held = block
    for m in doubling_masks(owners):
        pairs = [(i, i ^ m) for i in range(owners)]
        got = lax.ppermute(held, "rows", pairs)
        upper = (me & m) != 0
        held = jnp.where(
            upper, jnp.concatenate([got, held], 0), jnp.concatenate([held, got], 0)
        )
    return held


def arrival_order(owners):
    order = [0]
    for m in doubling_masks(owners):
        order = order + [d ^ m for d in order]
    return order


def body(slip_units, slip_scales, green, coast_gauges, coast_amps, coast_counts):
    scenarios = slip_units.shape[0]
    sources_here = slip_units.shape[1]
    block_count = slip_scales.shape[1]
    slip_weights = (
        (
            slip_units.astype(jnp.float32).reshape(scenarios, block_count, UBLK)
            * slip_scales[:, :, None]
        )
        .reshape(scenarios, sources_here)
        .astype(jnp.bfloat16)
    )
    me = lax.axis_index("src")
    groups = lax.axis_size("src")
    portion = scenarios // groups
    slip_mine = lax.dynamic_slice_in_dim(slip_weights, me * portion, portion, 0)
    slip_other = lax.dynamic_slice_in_dim(slip_weights, (1 - me) * portion, portion, 0)
    slip_ordered = jnp.concatenate([slip_other, slip_mine], 0)
    pairs = [(0, 1), (1, 0)]

    owners = lax.axis_size("rows")
    columns = green.shape[1]
    gauges_here = columns // NT
    segments = columns // SEG
    chunks = max(c for c in (1, 2, 4) if segments % c == 0)
    width = columns // chunks
    tile = SEG
    per_chunk = gauges_here // chunks
    order = arrival_order(owners)
    pieces = []
    ids = []
    for c in range(chunks):
        other, mine = partials_of(slip_ordered, green, c, width, tile)
        received = lax.ppermute(other, "src", pairs)
        peaks_c = peaks_of(mine, received)
        pieces.append(gather_rows(peaks_c, owners))
        ids.append(
            (np.asarray(order)[:, None] * gauges_here + c * per_chunk + np.arange(per_chunk)[None, :]).reshape(-1)
        )
    gathered = jnp.concatenate(pieces, axis=0) if chunks > 1 else pieces[0]
    gauge_ids = jnp.asarray(np.concatenate(ids).astype(np.int32))

    tile_total = coast_gauges.shape[0]
    slot_count = coast_gauges.shape[1]
    tiles_here = tile_total // owners
    active_slot = jnp.arange(slot_count, dtype=jnp.int32)[None, :] < coast_counts[:, None]
    weights = jnp.where(active_slot, coast_amps, jnp.zeros_like(coast_amps))
    first_tile = lax.axis_index("rows") * tiles_here
    mine_gauges = lax.dynamic_slice_in_dim(coast_gauges, first_tile, tiles_here, 0)
    mine_weights = lax.dynamic_slice_in_dim(weights, first_tile, tiles_here, 0)
    matches = mine_gauges[:, :, None] == gauge_ids[None, None, :]
    tile_table = jnp.sum(jnp.where(matches, mine_weights[:, :, None], 0.0), axis=1)
    onshore = lax.dot_general(
        gathered,
        tile_table,
        (((0,), (1,)), ((), ())),
        precision=lax.Precision.HIGHEST,
        preferred_element_type=jnp.float32,
    )
    return onshore


def solution(mesh):
    in_specs = (P(None, "src"), P(None, "src"), P("src", "rows"), P(), P(), P())
    out_specs = P("src", "rows")
    return jax.shard_map(body, mesh=mesh, in_specs=in_specs, out_specs=out_specs, check_vma=False)
```

profile of v0, /device:TPU:0, one launch (start us, length us, event | category | flops | bytes accessed | tf_op | source)
XLA Modules:
  0.0 148.7 jit_solution(15428808175195097849)
XLA Ops:
  2.6 1.9 %copy.21 = f32[512,1000]{1,0:T(8,128)S(1)} copy(f32[512,1000]{0,1:T(8,128)} %mul.21) | data formatting | bytes 4096000 | tf_op jit(solution)/shard_map/mul | solution.py:101
  4.5 3.1 %convert_element_type.6 = f32[512,1000]{0,1:T(8,128)} convert(s32[512,1000]{0,1:T(8,128)} %param.7) | non-fusion elementwise | flops 512000 | bytes 4096000 | tf_op jit(solution)/shard_map/convert_element_type | solution.py:101
  7.6 2.9 %copy.20 = f32[512,1000]{1,0:T(8,128)} copy(f32[512,1000]{0,1:T(8,128)} %convert_element_type.6) | data formatting | bytes 4096000 | tf_op jit(solution)/shard_map/convert_element_type | solution.py:101
  10.5 1.9 %multiply_convert_fusion = bf16[512,1000]{1,0:T(8,128)(2,1)S(1)} fusion(f32[512,1000]{1,0:T(8,128)} %copy.20, f32[512,1000]{1,0:T(8,128)S(1)} %copy.21), kind=kLoop, calls=%fused_computation.9 | loop fusion | flops 1024000 | bytes 5120000 | tf_op jit(solution)/shard_map/convert_element_type | solution.py:105
  13.5 13.5 %shard_map.73 = (bf16[256,7680]{1,0:T(8,128)(2,1)}, bf16[256,7680]{1,0:T(8,128)(2,1)}) custom-call(bf16[512,1000]{1,0:T(8,128)(2,1)} %pad_maximum_fusion.slip_ref, bf16[1000,30720]{1,0:T(8,128)(2,1)} %green_ref.7), custom_call_target="tpu_custom_call" | custom-call | flops 7864320000 | bytes 23224320 | tf_op jit(solution)/shard_map/pallas_call | solution.py:25
  27.5 13.5 %shard_map.75 = (bf16[256,7680]{1,0:T(8,128)(2,1)}, bf16[256,7680]{1,0:T(8,128)(2,1)}) custom-call(bf16[512,1000]{1,0:T(8,128)(2,1)} %pad_maximum_fusion.slip_ref, bf16[1000,30720]{1,0:T(8,128)(2,1)} %green_ref.7), custom_call_target="tpu_custom_call" | custom-call | flops 7864320000 | bytes 23224320 | tf_op jit(solution)/shard_map/pallas_call | solution.py:25
  41.1 13.6 %shard_map.77 = (bf16[256,7680]{1,0:T(8,128)(2,1)}, bf16[256,7680]{1,0:T(8,128)(2,1)}) custom-call(bf16[512,1000]{1,0:T(8,128)(2,1)} %pad_maximum_fusion.slip_ref, bf16[1000,30720]{1,0:T(8,128)(2,1)} %green_ref.7), custom_call_target="tpu_custom_call" | custom-call | flops 7864320000 | bytes 23224320 | tf_op jit(solution)/shard_map/pallas_call | solution.py:25
  55.1 13.5 %shard_map.79 = (bf16[256,7680]{1,0:T(8,128)(2,1)}, bf16[256,7680]{1,0:T(8,128)(2,1)}) custom-call(bf16[512,1000]{1,0:T(8,128)(2,1)} %pad_maximum_fusion.slip_ref, bf16[1000,30720]{1,0:T(8,128)(2,1)} %green_ref.7), custom_call_target="tpu_custom_call" | custom-call | flops 7864320000 | bytes 23224320 | tf_op jit(solution)/shard_map/pallas_call | solution.py:25
  70.4 7.6 %shard_map.74 = f32[32,256]{1,0:T(8,128)} custom-call(bf16[256,7680]{1,0:T(8,128)(2,1)} %get-tuple-element.13.mine_ref, bf16[256,7680]{1,0:T(8,128)(2,1)} %collective-permute-done.recv_ref), custom_call_target="tpu_custom_call" | custom-call | flops 5898240 | bytes 7864320 | tf_op jit(solution)/shard_map/pallas_call | solution.py:54
  77.9 4.0 %collective-permute-start.1 = (f32[32,256]{1,0:T(8,128)}, f32[32,256]{1,0:T(8,128)S(1)}, u32[]{:S(2)}, u32[]{:S(2)}) collective-permute-start(f32[32,256]{1,0:T(8,128)} %shard_map.74), channel_id=1, source_target_pairs={{0,8},{1,9},{2,10},{3,11},{4,12},{5,13},{6,14},{7,15},{8,0},{9,1},... | collective-permute-start | bytes 98312 | tf_op jit(solution)/shard_map/ppermute | solution.py:80
  82.0 2.7 %select_reduce_fusion = f32[128,2048]{1,0:T(8,128)S(1)} fusion(f32[128,8]{1,0:T(8,128)S(1)} %copy.23, s32[2048]{0:T(1024)S(1)} %copy-done.4, s32[128,8]{1,0:T(8,128)S(1)} %copy.22), kind=kLoop, calls=%fused_computation | loop fusion | flops 6029312 | bytes 1064960 | tf_op jit(solution)/shard_map/reduce_sum | solution.py:146
  84.6 7.5 %shard_map.76 = f32[32,256]{1,0:T(8,128)} custom-call(bf16[256,7680]{1,0:T(8,128)(2,1)} %get-tuple-element.15.mine_ref, bf16[256,7680]{1,0:T(8,128)(2,1)} %collective-permute-done.5.recv_ref), custom_call_target="tpu_custom_call" | custom-call | flops 5898240 | bytes 7864320 | tf_op jit(solution)/shard_map/pallas_call | solution.py:54
  92.2 7.5 %shard_map.78 = f32[32,256]{1,0:T(8,128)} custom-call(bf16[256,7680]{1,0:T(8,128)(2,1)} %get-tuple-element.17.mine_ref, bf16[256,7680]{1,0:T(8,128)(2,1)} %collective-permute-done.10.recv_ref), custom_call_target="tpu_custom_call" | custom-call | flops 5898240 | bytes 7864320 | tf_op jit(solution)/shard_map/pallas_call | solution.py:54
  99.7 2.9 %collective-permute-start.11 = (f32[32,256]{1,0:T(8,128)}, f32[32,256]{1,0:T(8,128)S(1)}, u32[]{:S(2)}, u32[]{:S(2)}) collective-permute-start(f32[32,256]{1,0:T(8,128)} %shard_map.78), channel_id=1, source_target_pairs={{0,8},{1,9},{2,10},{3,11},{4,12},{5,13},{6,14},{7,15},{8,0},{9,1},... | collective-permute-start | bytes 98312 | tf_op jit(solution)/shard_map/ppermute | solution.py:80
  102.6 7.6 %shard_map.80 = f32[32,256]{1,0:T(8,128)} custom-call(bf16[256,7680]{1,0:T(8,128)(2,1)} %get-tuple-element.19.mine_ref, bf16[256,7680]{1,0:T(8,128)(2,1)} %collective-permute-done.15.recv_ref), custom_call_target="tpu_custom_call" | custom-call | flops 5898240 | bytes 7864320 | tf_op jit(solution)/shard_map/pallas_call | solution.py:54
  110.3 2.0 %collective-permute-start.2 = (f32[64,256]{1,0:T(8,128)S(1)}, f32[64,256]{1,0:T(8,128)S(1)}, u32[]{:S(2)}, u32[]{:S(2)}) collective-permute-start(f32[64,256]{1,0:T(8,128)S(1)} %maximum_select_fusion.12), channel_id=1, source_target_pairs={{0,4},{1,5},{2,6},{3,7},{4,0},{5,1},{6,2},{7,3},{8,12},{9,13},{10,... | collective-permute-start | bytes 196616 | tf_op jit(solution)/shard_map/ppermute | solution.py:80
  112.5 2.0 %collective-permute-start.12 = (f32[64,256]{1,0:T(8,128)S(1)}, f32[64,256]{1,0:T(8,128)S(1)}, u32[]{:S(2)}, u32[]{:S(2)}) collective-permute-start(f32[64,256]{1,0:T(8,128)S(1)} %maximum_select_fusion.14), channel_id=1, source_target_pairs={{0,4},{1,5},{2,6},{3,7},{4,0},{5,1},{6,2},{7,3},{8,12},{9,13},{10,... | collective-permute-start | bytes 196616 | tf_op jit(solution)/shard_map/ppermute | solution.py:80
  116.2 1.7 %collective-permute-start.17 = (f32[64,256]{1,0:T(8,128)S(1)}, f32[64,256]{1,0:T(8,128)S(1)}, u32[]{:S(2)}, u32[]{:S(2)}) collective-permute-start(f32[64,256]{1,0:T(8,128)S(1)} %maximum_select_fusion.15), channel_id=1, source_target_pairs={{0,4},{1,5},{2,6},{3,7},{4,0},{5,1},{6,2},{7,3},{8,12},{9,13},{10,... | collective-permute-start | bytes 196616 | tf_op jit(solution)/shard_map/ppermute | solution.py:80
  122.3 2.1 %collective-permute-done.3 = f32[128,256]{1,0:T(8,128)S(1)} collective-permute-done((f32[128,256]{1,0:T(8,128)S(1)}, f32[128,256]{1,0:T(8,128)S(1)}, u32[]{:S(2)}, u32[]{:S(2)}) %collective-permute-start.3) | collective-permute-done | bytes 131104 | tf_op jit(solution)/shard_map/ppermute | solution.py:80
  130.9 2.9 %collective-permute-done.4 = f32[256,256]{1,0:T(8,128)S(1)} collective-permute-done((f32[256,256]{1,0:T(8,128)S(1)}, f32[256,256]{1,0:T(8,128)S(1)}, u32[]{:S(2)}, u32[]{:S(2)}) %collective-permute-start.4) | collective-permute-done | bytes 262176 | tf_op jit(solution)/shard_map/ppermute | solution.py:80
  133.8 5.1 %collective-permute-done.9 = f32[256,256]{1,0:T(8,128)S(1)} collective-permute-done((f32[256,256]{1,0:T(8,128)S(1)}, f32[256,256]{1,0:T(8,128)S(1)}, u32[]{:S(2)}, u32[]{:S(2)}) %collective-permute-start.9) | collective-permute-done | bytes 262176 | tf_op jit(solution)/shard_map/ppermute | solution.py:80
  139.0 2.8 %collective-permute-done.14 = f32[256,256]{1,0:T(8,128)S(1)} collective-permute-done((f32[256,256]{1,0:T(8,128)S(1)}, f32[256,256]{1,0:T(8,128)S(1)}, u32[]{:S(2)}, u32[]{:S(2)}) %collective-permute-start.14) | collective-permute-done | bytes 262176 | tf_op jit(solution)/shard_map/ppermute | solution.py:80
  141.8 2.8 %collective-permute-done.19 = f32[256,256]{1,0:T(8,128)S(1)} collective-permute-done((f32[256,256]{1,0:T(8,128)S(1)}, f32[256,256]{1,0:T(8,128)S(1)}, u32[]{:S(2)}, u32[]{:S(2)}) %collective-permute-start.19) | collective-permute-done | bytes 262176 | tf_op jit(solution)/shard_map/ppermute | solution.py:80
  144.6 4.1 %fusion = f32[256,128]{1,0:T(8,128)} fusion(f32[128,2048]{1,0:T(8,128)S(1)} %select_reduce_fusion, f32[512,256]{1,0:T(8,128)S(1)} %maximum_select_fusion.3, f32[512,256]{1,0:T(8,128)S(1)} %maximum_select_fusion.2, f32[512,256]{1,0:T(8,128)S(1)} %maximum_select_fusion.1, f32[512,256]{1,0:T(8,128)S(1)} %maximum_select_fusion), kind=kOutput, calls=%fused_computation.1 | convolution fusion | flops 806879232 | bytes 3276800 | tf_op jit(solution)/shard_map/dot_general | solution.py:147
  (65 shorter events, 19.5 us)
Async XLA Ops:
  0.0 70.2 %copy-start = (s32[2048,8]{0,1:T(8,128)S(1)}, s32[2048,8]{0,1:T(8,128)}, u32[]{:S(2)}) copy-start(s32[2048,8]{0,1:T(8,128)} %param.10) | copy-start | bytes 196612
  27.0 43.3 %collective-permute-start = (bf16[256,7680]{1,0:T(8,128)(2,1)}, bf16[256,7680]{1,0:T(8,128)(2,1)}, u32[]{:S(2)}, u32[]{:S(2)}) collective-permute-start(bf16[256,7680]{1,0:T(8,128)(2,1)} %get-tuple-element.14), channel_id=1, source_target_pairs={{0,16},{16,0},{1,17},{17,1},{2,18},{18,2},{3,19},{19,3},{4,20},{20... | collective-permute-start | bytes 11796488 | tf_op jit(solution)/shard_map/ppermute | solution.py:128
  41.0 43.6 %collective-permute-start.5 = (bf16[256,7680]{1,0:T(8,128)(2,1)}, bf16[256,7680]{1,0:T(8,128)(2,1)}, u32[]{:S(2)}, u32[]{:S(2)}) collective-permute-start(bf16[256,7680]{1,0:T(8,128)(2,1)} %get-tuple-element.16), channel_id=1, source_target_pairs={{0,16},{16,0},{1,17},{17,1},{2,18},{18,2},{3,19},{19,3},{4,20},{20... | collective-permute-start | bytes 11796488 | tf_op jit(solution)/shard_map/ppermute | solution.py:128
  54.6 37.5 %collective-permute-start.10 = (bf16[256,7680]{1,0:T(8,128)(2,1)}, bf16[256,7680]{1,0:T(8,128)(2,1)}, u32[]{:S(2)}, u32[]{:S(2)}) collective-permute-start(bf16[256,7680]{1,0:T(8,128)(2,1)} %get-tuple-element.18), channel_id=1, source_target_pairs={{0,16},{16,0},{1,17},{17,1},{2,18},{18,2},{3,19},{19,3},{4,20},{20... | collective-permute-start | bytes 11796488 | tf_op jit(solution)/shard_map/ppermute | solution.py:128
  68.6 34.0 %collective-permute-start.15 = (bf16[256,7680]{1,0:T(8,128)(2,1)}, bf16[256,7680]{1,0:T(8,128)(2,1)}, u32[]{:S(2)}, u32[]{:S(2)}) collective-permute-start(bf16[256,7680]{1,0:T(8,128)(2,1)} %get-tuple-element.20), channel_id=1, source_target_pairs={{0,16},{16,0},{1,17},{17,1},{2,18},{18,2},{3,19},{19,3},{4,20},{20... | collective-permute-start | bytes 11796488 | tf_op jit(solution)/shard_map/ppermute | solution.py:128
  70.3 11.6 %copy-start.4 = (s32[2048]{0:T(1024)S(1)}, s32[2048]{0:T(1024)}, u32[]{:S(2)}) copy-start(s32[2048]{0:T(1024)} %constant.32.clone) | copy-start | bytes 24580
  77.9 32.3 %collective-permute-start.1 = (f32[32,256]{1,0:T(8,128)}, f32[32,256]{1,0:T(8,128)S(1)}, u32[]{:S(2)}, u32[]{:S(2)}) collective-permute-start(f32[32,256]{1,0:T(8,128)} %shard_map.74), channel_id=1, source_target_pairs={{0,8},{1,9},{2,10},{3,11},{4,12},{5,13},{6,14},{7,15},{8,0},{9,1},... | collective-permute-start | bytes 98312 | tf_op jit(solution)/shard_map/ppermute | solution.py:80
  92.2 20.0 %collective-permute-start.6 = (f32[32,256]{1,0:T(8,128)}, f32[32,256]{1,0:T(8,128)S(1)}, u32[]{:S(2)}, u32[]{:S(2)}) collective-permute-start(f32[32,256]{1,0:T(8,128)} %shard_map.76), channel_id=1, source_target_pairs={{0,8},{1,9},{2,10},{3,11},{4,12},{5,13},{6,14},{7,15},{8,0},{9,1},... | collective-permute-start | bytes 98312 | tf_op jit(solution)/shard_map/ppermute | solution.py:80
  99.7 12.7 %collective-permute-start.11 = (f32[32,256]{1,0:T(8,128)}, f32[32,256]{1,0:T(8,128)S(1)}, u32[]{:S(2)}, u32[]{:S(2)}) collective-permute-start(f32[32,256]{1,0:T(8,128)} %shard_map.78), channel_id=1, source_target_pairs={{0,8},{1,9},{2,10},{3,11},{4,12},{5,13},{6,14},{7,15},{8,0},{9,1},... | collective-permute-start | bytes 98312 | tf_op jit(solution)/shard_map/ppermute | solution.py:80
  102.6 9.6 %copy-start.2 = (f32[32,256]{1,0:T(8,128)S(1)}, f32[32,256]{1,0:T(8,128)}, u32[]{:S(2)}) copy-start(f32[32,256]{1,0:T(8,128)} %shard_map.76) | copy-start | bytes 98308
  102.6 9.8 %copy-start.3 = (f32[32,256]{1,0:T(8,128)S(1)}, f32[32,256]{1,0:T(8,128)}, u32[]{:S(2)}) copy-start(f32[32,256]{1,0:T(8,128)} %shard_map.78) | copy-start | bytes 98308
  110.2 5.1 %collective-permute-start.16 = (f32[32,256]{1,0:T(8,128)}, f32[32,256]{1,0:T(8,128)S(1)}, u32[]{:S(2)}, u32[]{:S(2)}) collective-permute-start(f32[32,256]{1,0:T(8,128)} %shard_map.80), channel_id=1, source_target_pairs={{0,8},{1,9},{2,10},{3,11},{4,12},{5,13},{6,14},{7,15},{8,0},{9,1},... | collective-permute-start | bytes 98312 | tf_op jit(solution)/shard_map/ppermute | solution.py:80
  110.3 7.7 %collective-permute-start.2 = (f32[64,256]{1,0:T(8,128)S(1)}, f32[64,256]{1,0:T(8,128)S(1)}, u32[]{:S(2)}, u32[]{:S(2)}) collective-permute-start(f32[64,256]{1,0:T(8,128)S(1)} %maximum_select_fusion.12), channel_id=1, source_target_pairs={{0,4},{1,5},{2,6},{3,7},{4,0},{5,1},{6,2},{7,3},{8,12},{9,13},{10,... | collective-permute-start | bytes 196616 | tf_op jit(solution)/shard_map/ppermute | solution.py:80
  112.2 7.3 %collective-permute-start.7 = (f32[64,256]{1,0:T(8,128)S(1)}, f32[64,256]{1,0:T(8,128)S(1)}, u32[]{:S(2)}, u32[]{:S(2)}) collective-permute-start(f32[64,256]{1,0:T(8,128)S(1)} %maximum_select_fusion.13), channel_id=1, source_target_pairs={{0,4},{1,5},{2,6},{3,7},{4,0},{5,1},{6,2},{7,3},{8,12},{9,13},{10,... | collective-permute-start | bytes 196616 | tf_op jit(solution)/shard_map/ppermute | solution.py:80
  112.5 7.7 %collective-permute-start.12 = (f32[64,256]{1,0:T(8,128)S(1)}, f32[64,256]{1,0:T(8,128)S(1)}, u32[]{:S(2)}, u32[]{:S(2)}) collective-permute-start(f32[64,256]{1,0:T(8,128)S(1)} %maximum_select_fusion.14), channel_id=1, source_target_pairs={{0,4},{1,5},{2,6},{3,7},{4,0},{5,1},{6,2},{7,3},{8,12},{9,13},{10,... | collective-permute-start | bytes 196616 | tf_op jit(solution)/shard_map/ppermute | solution.py:80
  116.2 5.6 %collective-permute-start.17 = (f32[64,256]{1,0:T(8,128)S(1)}, f32[64,256]{1,0:T(8,128)S(1)}, u32[]{:S(2)}, u32[]{:S(2)}) collective-permute-start(f32[64,256]{1,0:T(8,128)S(1)} %maximum_select_fusion.15), channel_id=1, source_target_pairs={{0,4},{1,5},{2,6},{3,7},{4,0},{5,1},{6,2},{7,3},{8,12},{9,13},{10,... | collective-permute-start | bytes 196616 | tf_op jit(solution)/shard_map/ppermute | solution.py:80
  118.0 6.5 %collective-permute-start.3 = (f32[128,256]{1,0:T(8,128)S(1)}, f32[128,256]{1,0:T(8,128)S(1)}, u32[]{:S(2)}, u32[]{:S(2)}) collective-permute-start(f32[128,256]{1,0:T(8,128)S(1)} %maximum_select_fusion.8), channel_id=1, source_target_pairs={{0,2},{1,3},{2,0},{3,1},{4,6},{5,7},{6,4},{7,5},{8,10},{9,11},{10,... | collective-permute-start | bytes 393224 | tf_op jit(solution)/shard_map/ppermute | solution.py:80
  119.6 7.0 %collective-permute-start.8 = (f32[128,256]{1,0:T(8,128)S(1)}, f32[128,256]{1,0:T(8,128)S(1)}, u32[]{:S(2)}, u32[]{:S(2)}) collective-permute-start(f32[128,256]{1,0:T(8,128)S(1)} %maximum_select_fusion.9), channel_id=1, source_target_pairs={{0,2},{1,3},{2,0},{3,1},{4,6},{5,7},{6,4},{7,5},{8,10},{9,11},{10,... | collective-permute-start | bytes 393224 | tf_op jit(solution)/shard_map/ppermute | solution.py:80
  120.2 8.0 %collective-permute-start.13 = (f32[128,256]{1,0:T(8,128)S(1)}, f32[128,256]{1,0:T(8,128)S(1)}, u32[]{:S(2)}, u32[]{:S(2)}) collective-permute-start(f32[128,256]{1,0:T(8,128)S(1)} %maximum_select_fusion.10), channel_id=1, source_target_pairs={{0,2},{1,3},{2,0},{3,1},{4,6},{5,7},{6,4},{7,5},{8,10},{9,11},{10,... | collective-permute-start | bytes 393224 | tf_op jit(solution)/shard_map/ppermute | solution.py:80
  121.8 7.8 %collective-permute-start.18 = (f32[128,256]{1,0:T(8,128)S(1)}, f32[128,256]{1,0:T(8,128)S(1)}, u32[]{:S(2)}, u32[]{:S(2)}) collective-permute-start(f32[128,256]{1,0:T(8,128)S(1)} %maximum_select_fusion.11), channel_id=1, source_target_pairs={{0,2},{1,3},{2,0},{3,1},{4,6},{5,7},{6,4},{7,5},{8,10},{9,11},{10,... | collective-permute-start | bytes 393224 | tf_op jit(solution)/shard_map/ppermute | solution.py:80
  124.5 9.3 %collective-permute-start.4 = (f32[256,256]{1,0:T(8,128)S(1)}, f32[256,256]{1,0:T(8,128)S(1)}, u32[]{:S(2)}, u32[]{:S(2)}) collective-permute-start(f32[256,256]{1,0:T(8,128)S(1)} %maximum_select_fusion.4), channel_id=1, source_target_pairs={{0,1},{1,0},{2,3},{3,2},{4,5},{5,4},{6,7},{7,6},{8,9},{9,8},{10,11... | collective-permute-start | bytes 786440 | tf_op jit(solution)/shard_map/ppermute | solution.py:80
  126.6 12.4 %collective-permute-start.9 = (f32[256,256]{1,0:T(8,128)S(1)}, f32[256,256]{1,0:T(8,128)S(1)}, u32[]{:S(2)}, u32[]{:S(2)}) collective-permute-start(f32[256,256]{1,0:T(8,128)S(1)} %maximum_select_fusion.5), channel_id=1, source_target_pairs={{0,1},{1,0},{2,3},{3,2},{4,5},{5,4},{6,7},{7,6},{8,9},{9,8},{10,11... | collective-permute-start | bytes 786440 | tf_op jit(solution)/shard_map/ppermute | solution.py:80
  128.1 13.6 %collective-permute-start.14 = (f32[256,256]{1,0:T(8,128)S(1)}, f32[256,256]{1,0:T(8,128)S(1)}, u32[]{:S(2)}, u32[]{:S(2)}) collective-permute-start(f32[256,256]{1,0:T(8,128)S(1)} %maximum_select_fusion.6), channel_id=1, source_target_pairs={{0,1},{1,0},{2,3},{3,2},{4,5},{5,4},{6,7},{7,6},{8,9},{9,8},{10,11... | collective-permute-start | bytes 786440 | tf_op jit(solution)/shard_map/ppermute | solution.py:80
  129.6 15.0 %collective-permute-start.19 = (f32[256,256]{1,0:T(8,128)S(1)}, f32[256,256]{1,0:T(8,128)S(1)}, u32[]{:S(2)}, u32[]{:S(2)}) collective-permute-start(f32[256,256]{1,0:T(8,128)S(1)} %maximum_select_fusion.7), channel_id=1, source_target_pairs={{0,1},{1,0},{2,3},{3,2},{4,5},{5,4},{6,7},{7,6},{8,9},{9,8},{10,11... | collective-permute-start | bytes 786440 | tf_op jit(solution)/shard_map/ppermute | solution.py:80
  (1 other events, 7.6 us)
where the time goes:
time: 150 us; the launch traced here: 149 us
  Pallas kernels  84.3 us (56%)
  starting transfers between devices  24 us (16%)
  waiting for transfers between devices  17.1 us (11%)
  other arithmetic  10.6 us (7%)
  local copies, waits for them, and re-layouts  8.45 us (6%)
  matrix products  4.14 us (3%)
    pallas_call x4, Pallas kernels, partials_of(): pl.pallas_call(matmul_kernel, grid=(steps,), in_specs=[pl.BlockSpec((scen...  54.1 us
    pallas_call x4, Pallas kernels, peaks_of(): pl.pallas_call(peak_kernel, grid=(blocks, rows // band), in_specs=[pl.Blo...  30.2 us
    ppermute x16, starting transfers between devices, gather_rows(): got = lax.ppermute(held, 'rows', pairs)  23 us
    ppermute x16, waiting for transfers between devices, gather_rows(): got = lax.ppermute(held, 'rows', pairs)  17.1 us
    mul x3, local copies, waits for them, and re-layouts, body(): slip_units.astype(jnp.float32).reshape(scenarios, block_count, UBLK)  4.49 us
    dot_general x1, matrix products, body(): lax.dot_general(gathered, tile_table, (((0,), (1,)), ((), ())), precision...  4.14 us
    convert_element_type x1, other arithmetic, body(): slip_units.astype(jnp.float32).reshape(scenarios, block_count, UBLK)  3.09 us
  transfers between devices with their start and end apart: 20, of which 7 were waited for; matrix products, arithmetic and copies ran while one was open for 4% of the time, Pallas kernels for 48%

commit v1 on v0

--- a/solution.py
+++ b/solution.py
@@ -12,25 +12,27 @@
 
 
 def matmul_kernel(slip_ref, green_ref, other_ref, mine_ref):
-    half = other_ref.shape[0]
-    product = jnp.dot(slip_ref[...], green_ref[...], preferred_element_type=jnp.float32)
-    other_ref[...] = product[:half].astype(jnp.bfloat16)
-    mine_ref[...] = product[half:].astype(jnp.bfloat16)
+    half = other_ref.shape[1]
+    product = lax.dot_general(
+        green_ref[...], slip_ref[...], (((0,), (0,)), ((), ())), preferred_element_type=jnp.float32
+    )
+    other_ref[...] = product[:, :half].astype(jnp.bfloat16)
+    mine_ref[...] = product[:, half:].astype(jnp.bfloat16)
 
 
 def partials_of(slip_ordered, green, chunk, width, tile):
-    scenarios, sources = slip_ordered.shape
+    sources, scenarios = slip_ordered.shape
     half = scenarios // 2
     steps = width // tile
     return pl.pallas_call(
         matmul_kernel,
         grid=(steps,),
         in_specs=[
-            pl.BlockSpec((scenarios, sources), lambda j: (0, 0)),
+            pl.BlockSpec((sources, scenarios), lambda j: (0, 0)),
             pl.BlockSpec((sources, tile), lambda j: (0, chunk * steps + j)),
         ],
-        out_specs=[pl.BlockSpec((half, tile), lambda j: (0, j))] * 2,
-        out_shape=[jax.ShapeDtypeStruct((half, width), jnp.bfloat16)] * 2,
+        out_specs=[pl.BlockSpec((tile, half), lambda j: (j, 0))] * 2,
+        out_shape=[jax.ShapeDtypeStruct((width, half), jnp.bfloat16)] * 2,
         cost_estimate=pl.CostEstimate(
             flops=2 * scenarios * sources * width,
             transcendentals=0,
@@ -41,21 +43,19 @@
 
 def peak_kernel(mine_ref, recv_ref, out_ref):
     wave = mine_ref[...].astype(jnp.float32) + recv_ref[...].astype(jnp.float32)
-    flipped = jnp.abs(wave).T
     gauges = SEG // NT
-    out_ref[...] = jnp.max(flipped.reshape(gauges, NT, flipped.shape[1]), axis=1)
+    out_ref[...] = jnp.max(jnp.abs(wave).reshape(gauges, NT, wave.shape[1]), axis=1)
 
 
 def peaks_of(mine, recv):
-    rows, cols = mine.shape
+    cols, rows = mine.shape
     blocks = cols // SEG
     gauges = SEG // NT
-    band = 128 if rows % 128 == 0 else rows
     return pl.pallas_call(
         peak_kernel,
-        grid=(blocks, rows // band),
-        in_specs=[pl.BlockSpec((band, SEG), lambda j, i: (i, j))] * 2,
-        out_specs=pl.BlockSpec((gauges, band), lambda j, i: (j, i)),
+        grid=(blocks,),
+        in_specs=[pl.BlockSpec((SEG, rows), lambda j: (j, 0))] * 2,
+        out_specs=pl.BlockSpec((gauges, rows), lambda j: (j, 0)),
         out_shape=jax.ShapeDtypeStruct((blocks * gauges, rows), jnp.float32),
         cost_estimate=pl.CostEstimate(
             flops=3 * rows * cols, transcendentals=0, bytes_accessed=4 * rows * cols
@@ -94,22 +94,15 @@
 
 def body(slip_units, slip_scales, green, coast_gauges, coast_amps, coast_counts):
     scenarios = slip_units.shape[0]
-    sources_here = slip_units.shape[1]
-    block_count = slip_scales.shape[1]
-    slip_weights = (
-        (
-            slip_units.astype(jnp.float32).reshape(scenarios, block_count, UBLK)
-            * slip_scales[:, :, None]
-        )
-        .reshape(scenarios, sources_here)
-        .astype(jnp.bfloat16)
-    )
+    units_t = slip_units.T.astype(jnp.float32)
+    scale_rows = jnp.repeat(slip_scales.T, UBLK, axis=0)
+    slip_t = (units_t * scale_rows).astype(jnp.bfloat16)
     me = lax.axis_index("src")
     groups = lax.axis_size("src")
     portion = scenarios // groups
-    slip_mine = lax.dynamic_slice_in_dim(slip_weights, me * portion, portion, 0)
-    slip_other = lax.dynamic_slice_in_dim(slip_weights, (1 - me) * portion, portion, 0)
-    slip_ordered = jnp.concatenate([slip_other, slip_mine], 0)
+    slip_mine = lax.dynamic_slice_in_dim(slip_t, me * portion, portion, 1)
+    slip_other = lax.dynamic_slice_in_dim(slip_t, (1 - me) * portion, portion, 1)
+    slip_ordered = jnp.concatenate([slip_other, slip_mine], 1)
     pairs = [(0, 1), (1, 0)]
 
     owners = lax.axis_size("rows")

time: 150 us -> 131 us (0.87)
  Pallas kernels: 84.3 us -> 72.9 us
  local copies, waits for them, and re-layouts: 8.45 us -> 3.65 us
  other arithmetic: 10.6 us -> 8.27 us
    pallas_call x8, Pallas kernels: 84.3 us -> 72.9 us  [the longest x4 53.6 us: partials_of(): pl.pallas_call(matmul_kernel, grid=(steps,), in_specs=[pl.BlockSpec((sour...]
    mul x3 -> x0, local copies, waits for them, and re-layouts: 4.49 us -> none  [body(): slip_units.astype(jnp.float32).reshape(scenarios, block_count, UBLK)]
    convert_element_type x1 -> x0, local copies, waits for them, and re-layouts: 2.88 us -> none  [body(): slip_units.astype(jnp.float32).reshape(scenarios, block_count, UBLK)]
    convert_element_type x2 -> x1, other arithmetic: 4.97 us -> 2.72 us  [body(): slip_t = (units_t * scale_rows).astype(jnp.bfloat16)]
    reshape x0 -> x1, local copies, waits for them, and re-layouts: none -> 1.58 us  [body(): scale_rows = jnp.repeat(slip_scales.T, UBLK, axis=0)]
  transfers between devices with their start and end apart: 20 -> 20, of which waited for: 7 -> 7; matrix products, arithmetic and copies ran while one was open for 4% -> 4% of each run, Pallas kernels for 48% -> 46%
where the time goes in v1:
time: 131 us; the launch traced here: 130 us
  Pallas kernels  72.9 us (56%)
  starting transfers between devices  24 us (18%)
  waiting for transfers between devices  17.1 us (13%)
  other arithmetic  8.27 us (6%)
  matrix products  4.14 us (3%)
  local copies, waits for them, and re-layouts  3.65 us (3%)
    pallas_call x4, Pallas kernels, partials_of(): pl.pallas_call(matmul_kernel, grid=(steps,), in_specs=[pl.BlockSpec((sour...  53.6 us
    ppermute x16, starting transfers between devices, gather_rows(): got = lax.ppermute(held, 'rows', pairs)  23 us
    pallas_call x4, Pallas kernels, peaks_of(): pl.pallas_call(peak_kernel, grid=(blocks,), in_specs=[pl.BlockSpec((SEG,...  19.3 us
    ppermute x16, waiting for transfers between devices, gather_rows(): got = lax.ppermute(held, 'rows', pairs)  17 us
    dot_general x1, matrix products, body(): lax.dot_general(gathered, tile_table, (((0,), (1,)), ((), ())), precision...  4.14 us
    convert_element_type x1, other arithmetic, body(): slip_t = (units_t * scale_rows).astype(jnp.bfloat16)  2.72 us
    reduce_sum x1, other arithmetic, body(): jnp.sum(jnp.where(matches, mine_weights[:, :, None], 0.0), axis=1)  2.66 us
  transfers between devices with their start and end apart: 20, of which 7 were waited for; matrix products, arithmetic and copies ran while one was open for 4% of the time, Pallas kernels for 46%

profile of v1, /device:TPU:0, one launch (start us, length us, event | category | flops | bytes accessed | tf_op | source)
XLA Modules:
  0.0 130.2 jit_solution(6277633560163839875)
XLA Ops:
  1.0 1.6 %reshape.7 = f32[1000,512]{1,0:T(8,128)} reshape(f32[8,125,512]{2,1,0:T(8,128)S(1)} %broadcast_in_dim.23) | data formatting | bytes 4096000 | tf_op jit(solution)/shard_map/reshape | solution.py:98
  2.6 2.7 %fusion.8 = bf16[1000,512]{1,0:T(8,128)(2,1)S(1)} fusion(f32[1000,512]{1,0:T(8,128)} %reshape.7, s32[512,1000]{0,1:T(8,128)} %param.7), kind=kLoop, calls=%fused_computation.10 | loop fusion | flops 1536000 | bytes 5120000 | tf_op jit(solution)/shard_map/convert_element_type | solution.py:99
  6.4 13.4 %shard_map.73 = (bf16[7680,256]{1,0:T(8,128)(2,1)}, bf16[7680,256]{1,0:T(8,128)(2,1)}) custom-call(bf16[1000,512]{1,0:T(8,128)(2,1)} %pad_maximum_fusion.slip_ref, bf16[1000,30720]{1,0:T(8,128)(2,1)} %green_ref.7), custom_call_target="tpu_custom_call" | custom-call | flops 7864320000 | bytes 23224320 | tf_op jit(solution)/shard_map/pallas_call | solution.py:27
  20.3 13.5 %shard_map.75 = (bf16[7680,256]{1,0:T(8,128)(2,1)}, bf16[7680,256]{1,0:T(8,128)(2,1)}) custom-call(bf16[1000,512]{1,0:T(8,128)(2,1)} %pad_maximum_fusion.slip_ref, bf16[1000,30720]{1,0:T(8,128)(2,1)} %green_ref.7), custom_call_target="tpu_custom_call" | custom-call | flops 7864320000 | bytes 23224320 | tf_op jit(solution)/shard_map/pallas_call | solution.py:27
  33.8 13.4 %shard_map.77 = (bf16[7680,256]{1,0:T(8,128)(2,1)}, bf16[7680,256]{1,0:T(8,128)(2,1)}) custom-call(bf16[1000,512]{1,0:T(8,128)(2,1)} %pad_maximum_fusion.slip_ref, bf16[1000,30720]{1,0:T(8,128)(2,1)} %green_ref.7), custom_call_target="tpu_custom_call" | custom-call | flops 7864320000 | bytes 23224320 | tf_op jit(solution)/shard_map/pallas_call | solution.py:27
  47.7 13.3 %shard_map.79 = (bf16[7680,256]{1,0:T(8,128)(2,1)}, bf16[7680,256]{1,0:T(8,128)(2,1)}) custom-call(bf16[1000,512]{1,0:T(8,128)(2,1)} %pad_maximum_fusion.slip_ref, bf16[1000,30720]{1,0:T(8,128)(2,1)} %green_ref.7), custom_call_target="tpu_custom_call" | custom-call | flops 7864320000 | bytes 23224320 | tf_op jit(solution)/shard_map/pallas_call | solution.py:27
  62.8 4.8 %shard_map.74 = f32[32,256]{1,0:T(8,128)} custom-call(bf16[7680,256]{1,0:T(8,128)(2,1)} %get-tuple-element.13.mine_ref, bf16[7680,256]{1,0:T(8,128)(2,1)} %collective-permute-done.recv_ref), custom_call_target="tpu_custom_call" | custom-call | flops 5898240 | bytes 7864320 | tf_op jit(solution)/shard_map/pallas_call | solution.py:54
  67.6 4.0 %collective-permute-start.1 = (f32[32,256]{1,0:T(8,128)}, f32[32,256]{1,0:T(8,128)S(1)}, u32[]{:S(2)}, u32[]{:S(2)}) collective-permute-start(f32[32,256]{1,0:T(8,128)} %shard_map.74), channel_id=1, source_target_pairs={{0,8},{1,9},{2,10},{3,11},{4,12},{5,13},{6,14},{7,15},{8,0},{9,1},... | collective-permute-start | bytes 98312 | tf_op jit(solution)/shard_map/ppermute | solution.py:80
  71.6 2.7 %select_reduce_fusion = f32[128,2048]{1,0:T(8,128)S(1)} fusion(f32[128,8]{1,0:T(8,128)S(1)} %copy.13, s32[2048]{0:T(1024)S(1)} %copy-done.4, s32[128,8]{1,0:T(8,128)S(1)} %copy.12), kind=kLoop, calls=%fused_computation | loop fusion | flops 6029312 | bytes 1064960 | tf_op jit(solution)/shard_map/reduce_sum | solution.py:139
  74.3 4.8 %shard_map.76 = f32[32,256]{1,0:T(8,128)} custom-call(bf16[7680,256]{1,0:T(8,128)(2,1)} %get-tuple-element.15.mine_ref, bf16[7680,256]{1,0:T(8,128)(2,1)} %collective-permute-done.5.recv_ref), custom_call_target="tpu_custom_call" | custom-call | flops 5898240 | bytes 7864320 | tf_op jit(solution)/shard_map/pallas_call | solution.py:54
  79.1 4.8 %shard_map.78 = f32[32,256]{1,0:T(8,128)} custom-call(bf16[7680,256]{1,0:T(8,128)(2,1)} %get-tuple-element.17.mine_ref, bf16[7680,256]{1,0:T(8,128)(2,1)} %collective-permute-done.10.recv_ref), custom_call_target="tpu_custom_call" | custom-call | flops 5898240 | bytes 7864320 | tf_op jit(solution)/shard_map/pallas_call | solution.py:54
  84.0 2.9 %collective-permute-start.11 = (f32[32,256]{1,0:T(8,128)}, f32[32,256]{1,0:T(8,128)S(1)}, u32[]{:S(2)}, u32[]{:S(2)}) collective-permute-start(f32[32,256]{1,0:T(8,128)} %shard_map.78), channel_id=1, source_target_pairs={{0,8},{1,9},{2,10},{3,11},{4,12},{5,13},{6,14},{7,15},{8,0},{9,1},... | collective-permute-start | bytes 98312 | tf_op jit(solution)/shard_map/ppermute | solution.py:80
  86.9 4.9 %shard_map.80 = f32[32,256]{1,0:T(8,128)} custom-call(bf16[7680,256]{1,0:T(8,128)(2,1)} %get-tuple-element.19.mine_ref, bf16[7680,256]{1,0:T(8,128)(2,1)} %collective-permute-done.15.recv_ref), custom_call_target="tpu_custom_call" | custom-call | flops 5898240 | bytes 7864320 | tf_op jit(solution)/shard_map/pallas_call | solution.py:54
  91.8 2.0 %collective-permute-start.2 = (f32[64,256]{1,0:T(8,128)S(1)}, f32[64,256]{1,0:T(8,128)S(1)}, u32[]{:S(2)}, u32[]{:S(2)}) collective-permute-start(f32[64,256]{1,0:T(8,128)S(1)} %maximum_select_fusion.12), channel_id=1, source_target_pairs={{0,4},{1,5},{2,6},{3,7},{4,0},{5,1},{6,2},{7,3},{8,12},{9,13},{10,... | collective-permute-start | bytes 196616 | tf_op jit(solution)/shard_map/ppermute | solution.py:80
  94.0 2.0 %collective-permute-start.12 = (f32[64,256]{1,0:T(8,128)S(1)}, f32[64,256]{1,0:T(8,128)S(1)}, u32[]{:S(2)}, u32[]{:S(2)}) collective-permute-start(f32[64,256]{1,0:T(8,128)S(1)} %maximum_select_fusion.14), channel_id=1, source_target_pairs={{0,4},{1,5},{2,6},{3,7},{4,0},{5,1},{6,2},{7,3},{8,12},{9,13},{10,... | collective-permute-start | bytes 196616 | tf_op jit(solution)/shard_map/ppermute | solution.py:80
  97.7 1.8 %collective-permute-start.17 = (f32[64,256]{1,0:T(8,128)S(1)}, f32[64,256]{1,0:T(8,128)S(1)}, u32[]{:S(2)}, u32[]{:S(2)}) collective-permute-start(f32[64,256]{1,0:T(8,128)S(1)} %maximum_select_fusion.15), channel_id=1, source_target_pairs={{0,4},{1,5},{2,6},{3,7},{4,0},{5,1},{6,2},{7,3},{8,12},{9,13},{10,... | collective-permute-start | bytes 196616 | tf_op jit(solution)/shard_map/ppermute | solution.py:80
  99.5 1.6 %collective-permute-start.3 = (f32[128,256]{1,0:T(8,128)S(1)}, f32[128,256]{1,0:T(8,128)S(1)}, u32[]{:S(2)}, u32[]{:S(2)}) collective-permute-start(f32[128,256]{1,0:T(8,128)S(1)} %maximum_select_fusion.8), channel_id=1, source_target_pairs={{0,2},{1,3},{2,0},{3,1},{4,6},{5,7},{6,4},{7,5},{8,10},{9,11},{10,... | collective-permute-start | bytes 393224 | tf_op jit(solution)/shard_map/ppermute | solution.py:80
  101.7 1.6 %collective-permute-start.13 = (f32[128,256]{1,0:T(8,128)S(1)}, f32[128,256]{1,0:T(8,128)S(1)}, u32[]{:S(2)}, u32[]{:S(2)}) collective-permute-start(f32[128,256]{1,0:T(8,128)S(1)} %maximum_select_fusion.10), channel_id=1, source_target_pairs={{0,2},{1,3},{2,0},{3,1},{4,6},{5,7},{6,4},{7,5},{8,10},{9,11},{10,... | collective-permute-start | bytes 393224 | tf_op jit(solution)/shard_map/ppermute | solution.py:80
  103.9 2.1 %collective-permute-done.3 = f32[128,256]{1,0:T(8,128)S(1)} collective-permute-done((f32[128,256]{1,0:T(8,128)S(1)}, f32[128,256]{1,0:T(8,128)S(1)}, u32[]{:S(2)}, u32[]{:S(2)}) %collective-permute-start.3) | collective-permute-done | bytes 131104 | tf_op jit(solution)/shard_map/ppermute | solution.py:80
  112.4 2.9 %collective-permute-done.4 = f32[256,256]{1,0:T(8,128)S(1)} collective-permute-done((f32[256,256]{1,0:T(8,128)S(1)}, f32[256,256]{1,0:T(8,128)S(1)}, u32[]{:S(2)}, u32[]{:S(2)}) %collective-permute-start.4) | collective-permute-done | bytes 262176 | tf_op jit(solution)/shard_map/ppermute | solution.py:80
  115.4 5.1 %collective-permute-done.9 = f32[256,256]{1,0:T(8,128)S(1)} collective-permute-done((f32[256,256]{1,0:T(8,128)S(1)}, f32[256,256]{1,0:T(8,128)S(1)}, u32[]{:S(2)}, u32[]{:S(2)}) %collective-permute-start.9) | collective-permute-done | bytes 262176 | tf_op jit(solution)/shard_map/ppermute | solution.py:80
  120.5 2.8 %collective-permute-done.14 = f32[256,256]{1,0:T(8,128)S(1)} collective-permute-done((f32[256,256]{1,0:T(8,128)S(1)}, f32[256,256]{1,0:T(8,128)S(1)}, u32[]{:S(2)}, u32[]{:S(2)}) %collective-permute-start.14) | collective-permute-done | bytes 262176 | tf_op jit(solution)/shard_map/ppermute | solution.py:80
  123.3 2.8 %collective-permute-done.19 = f32[256,256]{1,0:T(8,128)S(1)} collective-permute-done((f32[256,256]{1,0:T(8,128)S(1)}, f32[256,256]{1,0:T(8,128)S(1)}, u32[]{:S(2)}, u32[]{:S(2)}) %collective-permute-start.19) | collective-permute-done | bytes 262176 | tf_op jit(solution)/shard_map/ppermute | solution.py:80
  126.1 4.1 %fusion = f32[256,128]{1,0:T(8,128)} fusion(f32[128,2048]{1,0:T(8,128)S(1)} %select_reduce_fusion, f32[512,256]{1,0:T(8,128)S(1)} %maximum_select_fusion.3, f32[512,256]{1,0:T(8,128)S(1)} %maximum_select_fusion.2, f32[512,256]{1,0:T(8,128)S(1)} %maximum_select_fusion.1, f32[512,256]{1,0:T(8,128)S(1)} %maximum_select_fusion), kind=kOutput, calls=%fused_computation.1 | convolution fusion | flops 806879232 | bytes 3276800 | tf_op jit(solution)/shard_map/dot_general | solution.py:140
  (62 shorter events, 14.7 us)
Async XLA Ops:
  0.0 62.6 %copy-start = (s32[2048,8]{0,1:T(8,128)S(1)}, s32[2048,8]{0,1:T(8,128)}, u32[]{:S(2)}) copy-start(s32[2048,8]{0,1:T(8,128)} %param.10) | copy-start | bytes 196612
  19.8 42.9 %collective-permute-start = (bf16[7680,256]{1,0:T(8,128)(2,1)}, bf16[7680,256]{1,0:T(8,128)(2,1)}, u32[]{:S(2)}, u32[]{:S(2)}) collective-permute-start(bf16[7680,256]{1,0:T(8,128)(2,1)} %get-tuple-element.14), channel_id=1, source_target_pairs={{0,16},{16,0},{1,17},{17,1},{2,18},{18,2},{3,19},{19,3},{4,20},{20... | collective-permute-start | bytes 11796488 | tf_op jit(solution)/shard_map/ppermute | solution.py:121
  33.7 40.6 %collective-permute-start.5 = (bf16[7680,256]{1,0:T(8,128)(2,1)}, bf16[7680,256]{1,0:T(8,128)(2,1)}, u32[]{:S(2)}, u32[]{:S(2)}) collective-permute-start(bf16[7680,256]{1,0:T(8,128)(2,1)} %get-tuple-element.16), channel_id=1, source_target_pairs={{0,16},{16,0},{1,17},{17,1},{2,18},{18,2},{3,19},{19,3},{4,20},{20... | collective-permute-start | bytes 11796488 | tf_op jit(solution)/shard_map/ppermute | solution.py:121
  47.2 31.9 %collective-permute-start.10 = (bf16[7680,256]{1,0:T(8,128)(2,1)}, bf16[7680,256]{1,0:T(8,128)(2,1)}, u32[]{:S(2)}, u32[]{:S(2)}) collective-permute-start(bf16[7680,256]{1,0:T(8,128)(2,1)} %get-tuple-element.18), channel_id=1, source_target_pairs={{0,16},{16,0},{1,17},{17,1},{2,18},{18,2},{3,19},{19,3},{4,20},{20... | collective-permute-start | bytes 11796488 | tf_op jit(solution)/shard_map/ppermute | solution.py:121
  61.0 25.9 %collective-permute-start.15 = (bf16[7680,256]{1,0:T(8,128)(2,1)}, bf16[7680,256]{1,0:T(8,128)(2,1)}, u32[]{:S(2)}, u32[]{:S(2)}) collective-permute-start(bf16[7680,256]{1,0:T(8,128)(2,1)} %get-tuple-element.20), channel_id=1, source_target_pairs={{0,16},{16,0},{1,17},{17,1},{2,18},{18,2},{3,19},{19,3},{4,20},{20... | collective-permute-start | bytes 11796488 | tf_op jit(solution)/shard_map/ppermute | solution.py:121
  62.7 8.9 %copy-start.4 = (s32[2048]{0:T(1024)S(1)}, s32[2048]{0:T(1024)}, u32[]{:S(2)}) copy-start(s32[2048]{0:T(1024)} %constant.32.clone) | copy-start | bytes 24580
  67.6 24.2 %collective-permute-start.1 = (f32[32,256]{1,0:T(8,128)}, f32[32,256]{1,0:T(8,128)S(1)}, u32[]{:S(2)}, u32[]{:S(2)}) collective-permute-start(f32[32,256]{1,0:T(8,128)} %shard_map.74), channel_id=1, source_target_pairs={{0,8},{1,9},{2,10},{3,11},{4,12},{5,13},{6,14},{7,15},{8,0},{9,1},... | collective-permute-start | bytes 98312 | tf_op jit(solution)/shard_map/ppermute | solution.py:80
  79.1 14.6 %collective-permute-start.6 = (f32[32,256]{1,0:T(8,128)}, f32[32,256]{1,0:T(8,128)S(1)}, u32[]{:S(2)}, u32[]{:S(2)}) collective-permute-start(f32[32,256]{1,0:T(8,128)} %shard_map.76), channel_id=1, source_target_pairs={{0,8},{1,9},{2,10},{3,11},{4,12},{5,13},{6,14},{7,15},{8,0},{9,1},... | collective-permute-start | bytes 98312 | tf_op jit(solution)/shard_map/ppermute | solution.py:80
  84.0 10.0 %collective-permute-start.11 = (f32[32,256]{1,0:T(8,128)}, f32[32,256]{1,0:T(8,128)S(1)}, u32[]{:S(2)}, u32[]{:S(2)}) collective-permute-start(f32[32,256]{1,0:T(8,128)} %shard_map.78), channel_id=1, source_target_pairs={{0,8},{1,9},{2,10},{3,11},{4,12},{5,13},{6,14},{7,15},{8,0},{9,1},... | collective-permute-start | bytes 98312 | tf_op jit(solution)/shard_map/ppermute | solution.py:80
  86.9 6.9 %copy-start.2 = (f32[32,256]{1,0:T(8,128)S(1)}, f32[32,256]{1,0:T(8,128)}, u32[]{:S(2)}) copy-start(f32[32,256]{1,0:T(8,128)} %shard_map.76) | copy-start | bytes 98308
  86.9 7.1 %copy-start.3 = (f32[32,256]{1,0:T(8,128)S(1)}, f32[32,256]{1,0:T(8,128)}, u32[]{:S(2)}) copy-start(f32[32,256]{1,0:T(8,128)} %shard_map.78) | copy-start | bytes 98308
  91.7 5.1 %collective-permute-start.16 = (f32[32,256]{1,0:T(8,128)}, f32[32,256]{1,0:T(8,128)S(1)}, u32[]{:S(2)}, u32[]{:S(2)}) collective-permute-start(f32[32,256]{1,0:T(8,128)} %shard_map.80), channel_id=1, source_target_pairs={{0,8},{1,9},{2,10},{3,11},{4,12},{5,13},{6,14},{7,15},{8,0},{9,1},... | collective-permute-start | bytes 98312 | tf_op jit(solution)/shard_map/ppermute | solution.py:80
  91.8 7.7 %collective-permute-start.2 = (f32[64,256]{1,0:T(8,128)S(1)}, f32[64,256]{1,0:T(8,128)S(1)}, u32[]{:S(2)}, u32[]{:S(2)}) collective-permute-start(f32[64,256]{1,0:T(8,128)S(1)} %maximum_select_fusion.12), channel_id=1, source_target_pairs={{0,4},{1,5},{2,6},{3,7},{4,0},{5,1},{6,2},{7,3},{8,12},{9,13},{10,... | collective-permute-start | bytes 196616 | tf_op jit(solution)/shard_map/ppermute | solution.py:80
  93.8 7.3 %collective-permute-start.7 = (f32[64,256]{1,0:T(8,128)S(1)}, f32[64,256]{1,0:T(8,128)S(1)}, u32[]{:S(2)}, u32[]{:S(2)}) collective-permute-start(f32[64,256]{1,0:T(8,128)S(1)} %maximum_select_fusion.13), channel_id=1, source_target_pairs={{0,4},{1,5},{2,6},{3,7},{4,0},{5,1},{6,2},{7,3},{8,12},{9,13},{10,... | collective-permute-start | bytes 196616 | tf_op jit(solution)/shard_map/ppermute | solution.py:80
  94.0 7.7 %collective-permute-start.12 = (f32[64,256]{1,0:T(8,128)S(1)}, f32[64,256]{1,0:T(8,128)S(1)}, u32[]{:S(2)}, u32[]{:S(2)}) collective-permute-start(f32[64,256]{1,0:T(8,128)S(1)} %maximum_select_fusion.14), channel_id=1, source_target_pairs={{0,4},{1,5},{2,6},{3,7},{4,0},{5,1},{6,2},{7,3},{8,12},{9,13},{10,... | collective-permute-start | bytes 196616 | tf_op jit(solution)/shard_map/ppermute | solution.py:80
  97.7 5.6 %collective-permute-start.17 = (f32[64,256]{1,0:T(8,128)S(1)}, f32[64,256]{1,0:T(8,128)S(1)}, u32[]{:S(2)}, u32[]{:S(2)}) collective-permute-start(f32[64,256]{1,0:T(8,128)S(1)} %maximum_select_fusion.15), channel_id=1, source_target_pairs={{0,4},{1,5},{2,6},{3,7},{4,0},{5,1},{6,2},{7,3},{8,12},{9,13},{10,... | collective-permute-start | bytes 196616 | tf_op jit(solution)/shard_map/ppermute | solution.py:80
  99.5 6.5 %collective-permute-start.3 = (f32[128,256]{1,0:T(8,128)S(1)}, f32[128,256]{1,0:T(8,128)S(1)}, u32[]{:S(2)}, u32[]{:S(2)}) collective-permute-start(f32[128,256]{1,0:T(8,128)S(1)} %maximum_select_fusion.8), channel_id=1, source_target_pairs={{0,2},{1,3},{2,0},{3,1},{4,6},{5,7},{6,4},{7,5},{8,10},{9,11},{10,... | collective-permute-start | bytes 393224 | tf_op jit(solution)/shard_map/ppermute | solution.py:80
  101.1 7.0 %collective-permute-start.8 = (f32[128,256]{1,0:T(8,128)S(1)}, f32[128,256]{1,0:T(8,128)S(1)}, u32[]{:S(2)}, u32[]{:S(2)}) collective-permute-start(f32[128,256]{1,0:T(8,128)S(1)} %maximum_select_fusion.9), channel_id=1, source_target_pairs={{0,2},{1,3},{2,0},{3,1},{4,6},{5,7},{6,4},{7,5},{8,10},{9,11},{10,... | collective-permute-start | bytes 393224 | tf_op jit(solution)/shard_map/ppermute | solution.py:80
  101.7 8.0 %collective-permute-start.13 = (f32[128,256]{1,0:T(8,128)S(1)}, f32[128,256]{1,0:T(8,128)S(1)}, u32[]{:S(2)}, u32[]{:S(2)}) collective-permute-start(f32[128,256]{1,0:T(8,128)S(1)} %maximum_select_fusion.10), channel_id=1, source_target_pairs={{0,2},{1,3},{2,0},{3,1},{4,6},{5,7},{6,4},{7,5},{8,10},{9,11},{10,... | collective-permute-start | bytes 393224 | tf_op jit(solution)/shard_map/ppermute | solution.py:80
  103.3 7.8 %collective-permute-start.18 = (f32[128,256]{1,0:T(8,128)S(1)}, f32[128,256]{1,0:T(8,128)S(1)}, u32[]{:S(2)}, u32[]{:S(2)}) collective-permute-start(f32[128,256]{1,0:T(8,128)S(1)} %maximum_select_fusion.11), channel_id=1, source_target_pairs={{0,2},{1,3},{2,0},{3,1},{4,6},{5,7},{6,4},{7,5},{8,10},{9,11},{10,... | collective-permute-start | bytes 393224 | tf_op jit(solution)/shard_map/ppermute | solution.py:80
  106.0 9.3 %collective-permute-start.4 = (f32[256,256]{1,0:T(8,128)S(1)}, f32[256,256]{1,0:T(8,128)S(1)}, u32[]{:S(2)}, u32[]{:S(2)}) collective-permute-start(f32[256,256]{1,0:T(8,128)S(1)} %maximum_select_fusion.4), channel_id=1, source_target_pairs={{0,1},{1,0},{2,3},{3,2},{4,5},{5,4},{6,7},{7,6},{8,9},{9,8},{10,11... | collective-permute-start | bytes 786440 | tf_op jit(solution)/shard_map/ppermute | solution.py:80
  108.1 12.4 %collective-permute-start.9 = (f32[256,256]{1,0:T(8,128)S(1)}, f32[256,256]{1,0:T(8,128)S(1)}, u32[]{:S(2)}, u32[]{:S(2)}) collective-permute-start(f32[256,256]{1,0:T(8,128)S(1)} %maximum_select_fusion.5), channel_id=1, source_target_pairs={{0,1},{1,0},{2,3},{3,2},{4,5},{5,4},{6,7},{7,6},{8,9},{9,8},{10,11... | collective-permute-start | bytes 786440 | tf_op jit(solution)/shard_map/ppermute | solution.py:80
  109.7 13.6 %collective-permute-start.14 = (f32[256,256]{1,0:T(8,128)S(1)}, f32[256,256]{1,0:T(8,128)S(1)}, u32[]{:S(2)}, u32[]{:S(2)}) collective-permute-start(f32[256,256]{1,0:T(8,128)S(1)} %maximum_select_fusion.6), channel_id=1, source_target_pairs={{0,1},{1,0},{2,3},{3,2},{4,5},{5,4},{6,7},{7,6},{8,9},{9,8},{10,11... | collective-permute-start | bytes 786440 | tf_op jit(solution)/shard_map/ppermute | solution.py:80
  111.1 15.0 %collective-permute-start.19 = (f32[256,256]{1,0:T(8,128)S(1)}, f32[256,256]{1,0:T(8,128)S(1)}, u32[]{:S(2)}, u32[]{:S(2)}) collective-permute-start(f32[256,256]{1,0:T(8,128)S(1)} %maximum_select_fusion.7), channel_id=1, source_target_pairs={{0,1},{1,0},{2,3},{3,2},{4,5},{5,4},{6,7},{7,6},{8,9},{9,8},{10,11... | collective-permute-start | bytes 786440 | tf_op jit(solution)/shard_map/ppermute | solution.py:80
  (1 other events, 4.9 us)

commit v2 on v1

--- a/solution.py
+++ b/solution.py
@@ -45,6 +45,43 @@
     wave = mine_ref[...].astype(jnp.float32) + recv_ref[...].astype(jnp.float32)
     gauges = SEG // NT
     out_ref[...] = jnp.max(jnp.abs(wave).reshape(gauges, NT, wave.shape[1]), axis=1)
+
+
+def fused_kernel(slip_ref, green_ref, mine_prev_ref, recv_prev_ref, other_ref, mine_ref, peaks_ref):
+    matmul_kernel(slip_ref, green_ref, other_ref, mine_ref)
+    peak_kernel(mine_prev_ref, recv_prev_ref, peaks_ref)
+
+
+def fused_of(slip_ordered, green, chunk, width, mine_prev, recv_prev):
+    sources, scenarios = slip_ordered.shape
+    half = scenarios // 2
+    steps = width // SEG
+    gauges = SEG // NT
+    return pl.pallas_call(
+        fused_kernel,
+        grid=(steps,),
+        in_specs=[
+            pl.BlockSpec((sources, scenarios), lambda j: (0, 0)),
+            pl.BlockSpec((sources, SEG), lambda j: (0, chunk * steps + j)),
+            pl.BlockSpec((SEG, half), lambda j: (j, 0)),
+            pl.BlockSpec((SEG, half), lambda j: (j, 0)),
+        ],
+        out_specs=[
+            pl.BlockSpec((SEG, half), lambda j: (j, 0)),
+            pl.BlockSpec((SEG, half), lambda j: (j, 0)),
+            pl.BlockSpec((gauges, half), lambda j: (j, 0)),
+        ],
+        out_shape=[
+            jax.ShapeDtypeStruct((width, half), jnp.bfloat16),
+            jax.ShapeDtypeStruct((width, half), jnp.bfloat16),
+            jax.ShapeDtypeStruct((steps * gauges, half), jnp.float32),
+        ],
+        cost_estimate=pl.CostEstimate(
+            flops=2 * scenarios * sources * width,
+            transcendentals=0,
+            bytes_accessed=2 * (sources * width + 2 * scenarios * width),
+        ),
+    )(slip_ordered, green, mine_prev, recv_prev)
 
 
 def peaks_of(mine, recv):
@@ -114,17 +151,25 @@
     tile = SEG
     per_chunk = gauges_here // chunks
     order = arrival_order(owners)
-    pieces = []
-    ids = []
+    lag = 2 if chunks > 2 else 0
+    mines, receiveds, peaks = [], [], [None] * chunks
     for c in range(chunks):
-        other, mine = partials_of(slip_ordered, green, c, width, tile)
-        received = lax.ppermute(other, "src", pairs)
-        peaks_c = peaks_of(mine, received)
-        pieces.append(gather_rows(peaks_c, owners))
-        ids.append(
-            (np.asarray(order)[:, None] * gauges_here + c * per_chunk + np.arange(per_chunk)[None, :]).reshape(-1)
-        )
-    gathered = jnp.concatenate(pieces, axis=0) if chunks > 1 else pieces[0]
+        if lag and c >= lag:
+            other, mine, peaks[c - lag] = fused_of(
+                slip_ordered, green, c, width, mines[c - lag], receiveds[c - lag]
+            )
+        else:
+            other, mine = partials_of(slip_ordered, green, c, width, tile)
+        mines.append(mine)
+        receiveds.append(lax.ppermute(other, "src", pairs))
+    for c in range(chunks):
+        if peaks[c] is None:
+            peaks[c] = peaks_of(mines[c], receiveds[c])
+    pieces = [gather_rows(p, owners) for p in peaks]
+    ids = [
+        (np.asarray(order)[:, None] * gauges_here + c * per_chunk + np.arange(per_chunk)[None, :]).reshape(-1)
+        for c in range(chunks)
+    ]
     gauge_ids = jnp.asarray(np.concatenate(ids).astype(np.int32))
 
     tile_total = coast_gauges.shape[0]
@@ -137,13 +182,17 @@
     mine_weights = lax.dynamic_slice_in_dim(weights, first_tile, tiles_here, 0)
     matches = mine_gauges[:, :, None] == gauge_ids[None, None, :]
     tile_table = jnp.sum(jnp.where(matches, mine_weights[:, :, None], 0.0), axis=1)
-    onshore = lax.dot_general(
-        gathered,
-        tile_table,
-        (((0,), (1,)), ((), ())),
-        precision=lax.Precision.HIGHEST,
-        preferred_element_type=jnp.float32,
-    )
+    span = owners * per_chunk
+    onshore = None
+    for c in range(chunks):
+        term = lax.dot_general(
+            pieces[c],
+            tile_table[:, c * span:(c + 1) * span],
+            (((0,), (1,)), ((), ())),
+            precision=lax.Precision.HIGHEST,
+            preferred_element_type=jnp.float32,
+        )
+        onshore = term if onshore is None else onshore + term
     return onshore
 
 

time: 131 us -> 127 us (0.969)
  Pallas kernels: 72.9 us -> 67.3 us
    pallas_call x0 -> x2, Pallas kernels: none -> 30.8 us  [fused_of(): pl.pallas_call(fused_kernel, grid=(steps,), in_specs=[pl.BlockSpec((sourc...]
    pallas_call x4 -> x2, Pallas kernels: 53.6 us -> 26.8 us  [partials_of(): pl.pallas_call(matmul_kernel, grid=(steps,), in_specs=[pl.BlockSpec((sour...]
    pallas_call x4 -> x2, Pallas kernels: 19.3 us -> 9.69 us  [peaks_of(): pl.pallas_call(peak_kernel, grid=(blocks,), in_specs=[pl.BlockSpec((SEG,...]
    dot_general x1 -> x4, matrix products: 4.14 us -> 4.66 us  [body(): lax.dot_general(pieces[c], tile_table[:, c * span:(c + 1) * span], (((0,)...]
  transfers between devices with their start and end apart: 20 -> 20, of which waited for: 7 -> 8; matrix products, arithmetic and copies ran while one was open for 4% -> 7% of each run, Pallas kernels for 46% -> 43%
where the time goes in v2:
time: 127 us; the launch traced here: 126 us
  Pallas kernels  67.3 us (53%)
  starting transfers between devices  24.6 us (19%)
  waiting for transfers between devices  17 us (13%)
  other arithmetic  8.93 us (7%)
  matrix products  4.66 us (4%)
  local copies, waits for them, and re-layouts  3.62 us (3%)
    pallas_call x2, Pallas kernels, fused_of(): pl.pallas_call(fused_kernel, grid=(steps,), in_specs=[pl.BlockSpec((sourc...  30.8 us
    pallas_call x2, Pallas kernels, partials_of(): pl.pallas_call(matmul_kernel, grid=(steps,), in_specs=[pl.BlockSpec((sour...  26.8 us
    ppermute x16, starting transfers between devices, gather_rows(): got = lax.ppermute(held, 'rows', pairs)  23.6 us
    ppermute x16, waiting for transfers between devices, gather_rows(): got = lax.ppermute(held, 'rows', pairs)  17 us
    pallas_call x2, Pallas kernels, peaks_of(): pl.pallas_call(peak_kernel, grid=(blocks,), in_specs=[pl.BlockSpec((SEG,...  9.69 us
    dot_general x4, matrix products, body(): lax.dot_general(pieces[c], tile_table[:, c * span:(c + 1) * span], (((0,)...  4.66 us
    convert_element_type x1, other arithmetic, body(): slip_t = (units_t * scale_rows).astype(jnp.bfloat16)  2.72 us
    reduce_sum x1, other arithmetic, body(): jnp.sum(jnp.where(matches, mine_weights[:, :, None], 0.0), axis=1)  2.66 us
  transfers between devices with their start and end apart: 20, of which 8 were waited for; matrix products, arithmetic and copies ran while one was open for 7% of the time, Pallas kernels for 43%

profile of v2, /device:TPU:0, one launch (start us, length us, event | category | flops | bytes accessed | tf_op | source)
XLA Modules:
  0.0 126.2 jit_solution(16179677234866306222)
XLA Ops:
  1.0 1.6 %reshape.7 = f32[1000,512]{1,0:T(8,128)} reshape(f32[8,125,512]{2,1,0:T(8,128)S(1)} %broadcast_in_dim.23) | data formatting | bytes 4096000 | tf_op jit(solution)/shard_map/reshape | solution.py:135
  2.6 2.7 %fusion = bf16[1000,512]{1,0:T(8,128)(2,1)S(1)} fusion(f32[1000,512]{1,0:T(8,128)} %reshape.7, s32[512,1000]{0,1:T(8,128)} %param.7), kind=kLoop, calls=%fused_computation.2 | loop fusion | flops 1536000 | bytes 5120000 | tf_op jit(solution)/shard_map/convert_element_type | solution.py:136
  6.4 13.4 %shard_map.75 = (bf16[7680,256]{1,0:T(8,128)(2,1)}, bf16[7680,256]{1,0:T(8,128)(2,1)}) custom-call(bf16[1000,512]{1,0:T(8,128)(2,1)} %pad_maximum_fusion.slip_ref, bf16[1000,30720]{1,0:T(8,128)(2,1)} %green_ref.7), custom_call_target="tpu_custom_call" | custom-call | flops 7864320000 | bytes 23224320 | tf_op jit(solution)/shard_map/pallas_call | solution.py:27
  20.3 13.4 %shard_map.73 = (bf16[7680,256]{1,0:T(8,128)(2,1)}, bf16[7680,256]{1,0:T(8,128)(2,1)}) custom-call(bf16[1000,512]{1,0:T(8,128)(2,1)} %pad_maximum_fusion.slip_ref, bf16[1000,30720]{1,0:T(8,128)(2,1)} %green_ref.7), custom_call_target="tpu_custom_call" | custom-call | flops 7864320000 | bytes 23224320 | tf_op jit(solution)/shard_map/pallas_call | solution.py:27
  33.7 15.4 %shard_map.76 = (bf16[7680,256]{1,0:T(8,128)(2,1)}, bf16[7680,256]{1,0:T(8,128)(2,1)}, f32[32,256]{1,0:T(8,128)}) custom-call(bf16[1000,512]{1,0:T(8,128)(2,1)} %pad_maximum_fusion.slip_ref, bf16[1000,30720]{1,0:T(8,128)(2,1)} %green_ref.7, bf16[7680,256]{1,0:T(8,128)(2,1)} %get-tuple-element.18.mine_prev_ref, ...), custom_call_target="tpu_custom_call" | custom-call | flops 7864320000 | bytes 31088640 | tf_op jit(solution)/shard_map/pallas_call | solution.py:60
  49.6 15.4 %shard_map.74 = (bf16[7680,256]{1,0:T(8,128)(2,1)}, bf16[7680,256]{1,0:T(8,128)(2,1)}, f32[32,256]{1,0:T(8,128)}) custom-call(bf16[1000,512]{1,0:T(8,128)(2,1)} %pad_maximum_fusion.slip_ref, bf16[1000,30720]{1,0:T(8,128)(2,1)} %green_ref.7, bf16[7680,256]{1,0:T(8,128)(2,1)} %get-tuple-element.15.mine_prev_ref, ...), custom_call_target="tpu_custom_call" | custom-call | flops 7864320000 | bytes 31088640 | tf_op jit(solution)/shard_map/pallas_call | solution.py:60
  66.5 4.0 %collective-permute-start.6 = (f32[32,256]{1,0:T(8,128)S(1)}, f32[32,256]{1,0:T(8,128)S(1)}, u32[]{:S(2)}, u32[]{:S(2)}) collective-permute-start(f32[32,256]{1,0:T(8,128)S(1)} %copy-done.2), channel_id=1, source_target_pairs={{0,8},{1,9},{2,10},{3,11},{4,12},{5,13},{6,14},{7,15},{8,0},{9,1},... | collective-permute-start | bytes 98312 | tf_op jit(solution)/shard_map/ppermute | solution.py:117
  70.8 1.6 %collective-permute-done.6 = f32[32,256]{1,0:T(8,128)S(1)} collective-permute-done((f32[32,256]{1,0:T(8,128)S(1)}, f32[32,256]{1,0:T(8,128)S(1)}, u32[]{:S(2)}, u32[]{:S(2)}) %collective-permute-start.6) | collective-permute-done | bytes 32800 | tf_op jit(solution)/shard_map/ppermute | solution.py:117
  72.4 2.0 %collective-permute-start.7 = (f32[64,256]{1,0:T(8,128)S(1)}, f32[64,256]{1,0:T(8,128)S(1)}, u32[]{:S(2)}, u32[]{:S(2)}) collective-permute-start(f32[64,256]{1,0:T(8,128)S(1)} %maximum_select_fusion.17), channel_id=1, source_target_pairs={{0,4},{1,5},{2,6},{3,7},{4,0},{5,1},{6,2},{7,3},{8,12},{9,13},{10,... | collective-permute-start | bytes 196616 | tf_op jit(solution)/shard_map/ppermute | solution.py:117
  74.4 1.6 %collective-permute-done.1 = f32[32,256]{1,0:T(8,128)S(1)} collective-permute-done((f32[32,256]{1,0:T(8,128)}, f32[32,256]{1,0:T(8,128)S(1)}, u32[]{:S(2)}, u32[]{:S(2)}) %collective-permute-start.1) | collective-permute-done | bytes 32800 | tf_op jit(solution)/shard_map/ppermute | solution.py:117
  78.3 1.6 %collective-permute-start.8 = (f32[128,256]{1,0:T(8,128)S(1)}, f32[128,256]{1,0:T(8,128)S(1)}, u32[]{:S(2)}, u32[]{:S(2)}) collective-permute-start(f32[128,256]{1,0:T(8,128)S(1)} %maximum_select_fusion.13), channel_id=1, source_target_pairs={{0,2},{1,3},{2,0},{3,1},{4,6},{5,7},{6,4},{7,5},{8,10},{9,11},{10,... | collective-permute-start | bytes 393224 | tf_op jit(solution)/shard_map/ppermute | solution.py:117
  79.9 2.7 %select_reduce_fusion = f32[128,2048]{1,0:T(8,128)S(1)} fusion(f32[128,8]{1,0:T(8,128)S(1)} %copy.13, s32[2048]{0:T(1024)S(1)} %copy-done.3, s32[128,8]{1,0:T(8,128)S(1)} %copy.12), kind=kLoop, calls=%fused_computation | loop fusion | flops 6029312 | bytes 1064960 | tf_op jit(solution)/shard_map/reduce_sum | solution.py:184
  83.2 4.8 %shard_map.78 = f32[32,256]{1,0:T(8,128)} custom-call(bf16[7680,256]{1,0:T(8,128)(2,1)} %get-tuple-element.23.mine_ref, bf16[7680,256]{1,0:T(8,128)(2,1)} %collective-permute-done.15.recv_ref), custom_call_target="tpu_custom_call" | custom-call | flops 5898240 | bytes 7864320 | tf_op jit(solution)/shard_map/pallas_call | solution.py:91
  88.0 2.0 %collective-permute-start.16 = (f32[32,256]{1,0:T(8,128)}, f32[32,256]{1,0:T(8,128)S(1)}, u32[]{:S(2)}, u32[]{:S(2)}) collective-permute-start(f32[32,256]{1,0:T(8,128)} %shard_map.78), channel_id=1, source_target_pairs={{0,8},{1,9},{2,10},{3,11},{4,12},{5,13},{6,14},{7,15},{8,0},{9,1},... | collective-permute-start | bytes 98312 | tf_op jit(solution)/shard_map/ppermute | solution.py:117
  90.0 1.6 %collective-permute-start.9 = (f32[256,256]{1,0:T(8,128)S(1)}, f32[256,256]{1,0:T(8,128)S(1)}, u32[]{:S(2)}, u32[]{:S(2)}) collective-permute-start(f32[256,256]{1,0:T(8,128)S(1)} %maximum_select_fusion.9), channel_id=1, source_target_pairs={{0,1},{1,0},{2,3},{3,2},{4,5},{5,4},{6,7},{7,6},{8,9},{9,8},{10,11... | collective-permute-start | bytes 786440 | tf_op jit(solution)/shard_map/ppermute | solution.py:117
  91.5 4.9 %shard_map.77 = f32[32,256]{1,0:T(8,128)} custom-call(bf16[7680,256]{1,0:T(8,128)(2,1)} %get-tuple-element.21.mine_ref, bf16[7680,256]{1,0:T(8,128)(2,1)} %collective-permute-done.10.recv_ref), custom_call_target="tpu_custom_call" | custom-call | flops 5898240 | bytes 7864320 | tf_op jit(solution)/shard_map/pallas_call | solution.py:91
  97.4 1.6 %collective-permute-start.17 = (f32[64,256]{1,0:T(8,128)S(1)}, f32[64,256]{1,0:T(8,128)S(1)}, u32[]{:S(2)}, u32[]{:S(2)}) collective-permute-start(f32[64,256]{1,0:T(8,128)S(1)} %maximum_select_fusion.19), channel_id=1, source_target_pairs={{0,4},{1,5},{2,6},{3,7},{4,0},{5,1},{6,2},{7,3},{8,12},{9,13},{10,... | collective-permute-start | bytes 196616 | tf_op jit(solution)/shard_map/ppermute | solution.py:117
  99.0 2.5 %collective-permute-done.11 = f32[32,256]{1,0:T(8,128)S(1)} collective-permute-done((f32[32,256]{1,0:T(8,128)}, f32[32,256]{1,0:T(8,128)S(1)}, u32[]{:S(2)}, u32[]{:S(2)}) %collective-permute-start.11) | collective-permute-done | bytes 32800 | tf_op jit(solution)/shard_map/ppermute | solution.py:117
  102.4 2.4 %collective-permute-start.12 = (f32[64,256]{1,0:T(8,128)S(1)}, f32[64,256]{1,0:T(8,128)S(1)}, u32[]{:S(2)}, u32[]{:S(2)}) collective-permute-start(f32[64,256]{1,0:T(8,128)S(1)} %maximum_select_fusion.18), channel_id=1, source_target_pairs={{0,4},{1,5},{2,6},{3,7},{4,0},{5,1},{6,2},{7,3},{8,12},{9,13},{10,... | collective-permute-start | bytes 196616 | tf_op jit(solution)/shard_map/ppermute | solution.py:117
  104.8 1.6 %collective-permute-start.18 = (f32[128,256]{1,0:T(8,128)S(1)}, f32[128,256]{1,0:T(8,128)S(1)}, u32[]{:S(2)}, u32[]{:S(2)}) collective-permute-start(f32[128,256]{1,0:T(8,128)S(1)} %maximum_select_fusion.15), channel_id=1, source_target_pairs={{0,2},{1,3},{2,0},{3,1},{4,6},{5,7},{6,4},{7,5},{8,10},{9,11},{10,... | collective-permute-start | bytes 393224 | tf_op jit(solution)/shard_map/ppermute | solution.py:117
  107.1 1.6 %collective-permute-start.13 = (f32[128,256]{1,0:T(8,128)S(1)}, f32[128,256]{1,0:T(8,128)S(1)}, u32[]{:S(2)}, u32[]{:S(2)}) collective-permute-start(f32[128,256]{1,0:T(8,128)S(1)} %maximum_select_fusion.14), channel_id=1, source_target_pairs={{0,2},{1,3},{2,0},{3,1},{4,6},{5,7},{6,4},{7,5},{8,10},{9,11},{10,... | collective-permute-start | bytes 393224 | tf_op jit(solution)/shard_map/ppermute | solution.py:117
  113.7 7.0 %collective-permute-done.19 = f32[256,256]{1,0:T(8,128)S(1)} collective-permute-done((f32[256,256]{1,0:T(8,128)S(1)}, f32[256,256]{1,0:T(8,128)S(1)}, u32[]{:S(2)}, u32[]{:S(2)}) %collective-permute-start.19) | collective-permute-done | bytes 262176 | tf_op jit(solution)/shard_map/ppermute | solution.py:117
  121.7 1.8 %collective-permute-done.14 = f32[256,256]{1,0:T(8,128)S(1)} collective-permute-done((f32[256,256]{1,0:T(8,128)S(1)}, f32[256,256]{1,0:T(8,128)S(1)}, u32[]{:S(2)}, u32[]{:S(2)}) %collective-permute-start.14) | collective-permute-done | bytes 262176 | tf_op jit(solution)/shard_map/ppermute | solution.py:117
  124.6 1.7 %fusion.2 = f32[256,128]{1,0:T(8,128)} fusion(f32[256,128]{1,0:T(8,128)S(1)} %fusion.20, f32[256,128]{1,0:T(8,128)S(1)} %fusion.14, f32[256,128]{1,0:T(8,128)S(1)} %fusion.8, f32[256,256]{1,0:T(8,128)S(1)} %maximum_select_fusion.8, f32[256,256]{1,0:T(8,128)S(1)} %collective-permute-done.4, f32[128,2048]{1,0:T(8,128)S(1)} %select_reduce_fusion, pred[]{:T(512)S(6)} %ne.8), kind=kOutput, calls=%fused_computation.5 | convolution fusion | flops 201818112 | bytes 1310721 | tf_op jit(solution)/shard_map/dot_general | solution.py:188
  (57 shorter events, 17.3 us)
Async XLA Ops:
  0.0 70.5 %copy-start = (s32[2048,8]{0,1:T(8,128)S(1)}, s32[2048,8]{0,1:T(8,128)}, u32[]{:S(2)}) copy-start(s32[2048,8]{0,1:T(8,128)} %param.10) | copy-start | bytes 196612
  19.8 13.9 %collective-permute-start.5 = (bf16[7680,256]{1,0:T(8,128)(2,1)}, bf16[7680,256]{1,0:T(8,128)(2,1)}, u32[]{:S(2)}, u32[]{:S(2)}) collective-permute-start(bf16[7680,256]{1,0:T(8,128)(2,1)} %get-tuple-element.19), channel_id=1, source_target_pairs={{0,16},{16,0},{1,17},{17,1},{2,18},{18,2},{3,19},{19,3},{4,20},{20... | collective-permute-start | bytes 11796488 | tf_op jit(solution)/shard_map/ppermute | solution.py:164
  33.7 15.9 %collective-permute-start = (bf16[7680,256]{1,0:T(8,128)(2,1)}, bf16[7680,256]{1,0:T(8,128)(2,1)}, u32[]{:S(2)}, u32[]{:S(2)}) collective-permute-start(bf16[7680,256]{1,0:T(8,128)(2,1)} %get-tuple-element.16), channel_id=1, source_target_pairs={{0,16},{16,0},{1,17},{17,1},{2,18},{18,2},{3,19},{19,3},{4,20},{20... | collective-permute-start | bytes 11796488 | tf_op jit(solution)/shard_map/ppermute | solution.py:164
  49.1 34.0 %collective-permute-start.15 = (bf16[7680,256]{1,0:T(8,128)(2,1)}, bf16[7680,256]{1,0:T(8,128)(2,1)}, u32[]{:S(2)}, u32[]{:S(2)}) collective-permute-start(bf16[7680,256]{1,0:T(8,128)(2,1)} %get-tuple-element.24), channel_id=1, source_target_pairs={{0,16},{16,0},{1,17},{17,1},{2,18},{18,2},{3,19},{19,3},{4,20},{20... | collective-permute-start | bytes 11796488 | tf_op jit(solution)/shard_map/ppermute | solution.py:164
  49.6 16.9 %copy-start.2 = (f32[32,256]{1,0:T(8,128)S(1)}, f32[32,256]{1,0:T(8,128)}, u32[]{:S(2)}) copy-start(f32[32,256]{1,0:T(8,128)} %get-tuple-element.20) | copy-start | bytes 98308
  49.6 30.3 %copy-start.3 = (s32[2048]{0:T(1024)S(1)}, s32[2048]{0:T(1024)}, u32[]{:S(2)}) copy-start(s32[2048]{0:T(1024)} %constant.32.clone) | copy-start | bytes 24580
  65.0 26.6 %collective-permute-start.10 = (bf16[7680,256]{1,0:T(8,128)(2,1)}, bf16[7680,256]{1,0:T(8,128)(2,1)}, u32[]{:S(2)}, u32[]{:S(2)}) collective-permute-start(bf16[7680,256]{1,0:T(8,128)(2,1)} %get-tuple-element.22), channel_id=1, source_target_pairs={{0,16},{16,0},{1,17},{17,1},{2,18},{18,2},{3,19},{19,3},{4,20},{20... | collective-permute-start | bytes 11796488 | tf_op jit(solution)/shard_map/ppermute | solution.py:164
  66.5 5.9 %collective-permute-start.6 = (f32[32,256]{1,0:T(8,128)S(1)}, f32[32,256]{1,0:T(8,128)S(1)}, u32[]{:S(2)}, u32[]{:S(2)}) collective-permute-start(f32[32,256]{1,0:T(8,128)S(1)} %copy-done.2), channel_id=1, source_target_pairs={{0,8},{1,9},{2,10},{3,11},{4,12},{5,13},{6,14},{7,15},{8,0},{9,1},... | collective-permute-start | bytes 98312 | tf_op jit(solution)/shard_map/ppermute | solution.py:117
  70.7 5.2 %collective-permute-start.1 = (f32[32,256]{1,0:T(8,128)}, f32[32,256]{1,0:T(8,128)S(1)}, u32[]{:S(2)}, u32[]{:S(2)}) collective-permute-start(f32[32,256]{1,0:T(8,128)} %get-tuple-element.17), channel_id=1, source_target_pairs={{0,8},{1,9},{2,10},{3,11},{4,12},{5,13},{6,14},{7,15},{8,0},{9,1},... | collective-permute-start | bytes 98312 | tf_op jit(solution)/shard_map/ppermute | solution.py:117
  72.4 5.8 %collective-permute-start.7 = (f32[64,256]{1,0:T(8,128)S(1)}, f32[64,256]{1,0:T(8,128)S(1)}, u32[]{:S(2)}, u32[]{:S(2)}) collective-permute-start(f32[64,256]{1,0:T(8,128)S(1)} %maximum_select_fusion.17), channel_id=1, source_target_pairs={{0,4},{1,5},{2,6},{3,7},{4,0},{5,1},{6,2},{7,3},{8,12},{9,13},{10,... | collective-permute-start | bytes 196616 | tf_op jit(solution)/shard_map/ppermute | solution.py:117
  76.8 5.7 %collective-permute-start.2 = (f32[64,256]{1,0:T(8,128)S(1)}, f32[64,256]{1,0:T(8,128)S(1)}, u32[]{:S(2)}, u32[]{:S(2)}) collective-permute-start(f32[64,256]{1,0:T(8,128)S(1)} %maximum_select_fusion.16), channel_id=1, source_target_pairs={{0,4},{1,5},{2,6},{3,7},{4,0},{5,1},{6,2},{7,3},{8,12},{9,13},{10,... | collective-permute-start | bytes 196616 | tf_op jit(solution)/shard_map/ppermute | solution.py:117
  78.3 11.7 %collective-permute-start.8 = (f32[128,256]{1,0:T(8,128)S(1)}, f32[128,256]{1,0:T(8,128)S(1)}, u32[]{:S(2)}, u32[]{:S(2)}) collective-permute-start(f32[128,256]{1,0:T(8,128)S(1)} %maximum_select_fusion.13), channel_id=1, source_target_pairs={{0,2},{1,3},{2,0},{3,1},{4,6},{5,7},{6,4},{7,5},{8,10},{9,11},{10,... | collective-permute-start | bytes 393224 | tf_op jit(solution)/shard_map/ppermute | solution.py:117
  82.6 26.1 %collective-permute-start.3 = (f32[128,256]{1,0:T(8,128)S(1)}, f32[128,256]{1,0:T(8,128)S(1)}, u32[]{:S(2)}, u32[]{:S(2)}) collective-permute-start(f32[128,256]{1,0:T(8,128)S(1)} %maximum_select_fusion.12), channel_id=1, source_target_pairs={{0,2},{1,3},{2,0},{3,1},{4,6},{5,7},{6,4},{7,5},{8,10},{9,11},{10,... | collective-permute-start | bytes 393224 | tf_op jit(solution)/shard_map/ppermute | solution.py:117
  88.0 9.4 %collective-permute-start.16 = (f32[32,256]{1,0:T(8,128)}, f32[32,256]{1,0:T(8,128)S(1)}, u32[]{:S(2)}, u32[]{:S(2)}) collective-permute-start(f32[32,256]{1,0:T(8,128)} %shard_map.78), channel_id=1, source_target_pairs={{0,8},{1,9},{2,10},{3,11},{4,12},{5,13},{6,14},{7,15},{8,0},{9,1},... | collective-permute-start | bytes 98312 | tf_op jit(solution)/shard_map/ppermute | solution.py:117
  90.0 22.7 %collective-permute-start.9 = (f32[256,256]{1,0:T(8,128)S(1)}, f32[256,256]{1,0:T(8,128)S(1)}, u32[]{:S(2)}, u32[]{:S(2)}) collective-permute-start(f32[256,256]{1,0:T(8,128)S(1)} %maximum_select_fusion.9), channel_id=1, source_target_pairs={{0,1},{1,0},{2,3},{3,2},{4,5},{5,4},{6,7},{7,6},{8,9},{9,8},{10,11... | collective-permute-start | bytes 786440 | tf_op jit(solution)/shard_map/ppermute | solution.py:117
  91.5 5.8 %copy-start.1 = (f32[32,256]{1,0:T(8,128)S(1)}, f32[32,256]{1,0:T(8,128)}, u32[]{:S(2)}) copy-start(f32[32,256]{1,0:T(8,128)} %shard_map.78) | copy-start | bytes 98308
  96.4 5.1 %collective-permute-start.11 = (f32[32,256]{1,0:T(8,128)}, f32[32,256]{1,0:T(8,128)S(1)}, u32[]{:S(2)}, u32[]{:S(2)}) collective-permute-start(f32[32,256]{1,0:T(8,128)} %shard_map.77), channel_id=1, source_target_pairs={{0,8},{1,9},{2,10},{3,11},{4,12},{5,13},{6,14},{7,15},{8,0},{9,1},... | collective-permute-start | bytes 98312 | tf_op jit(solution)/shard_map/ppermute | solution.py:117
  97.4 7.4 %collective-permute-start.17 = (f32[64,256]{1,0:T(8,128)S(1)}, f32[64,256]{1,0:T(8,128)S(1)}, u32[]{:S(2)}, u32[]{:S(2)}) collective-permute-start(f32[64,256]{1,0:T(8,128)S(1)} %maximum_select_fusion.19), channel_id=1, source_target_pairs={{0,4},{1,5},{2,6},{3,7},{4,0},{5,1},{6,2},{7,3},{8,12},{9,13},{10,... | collective-permute-start | bytes 196616 | tf_op jit(solution)/shard_map/ppermute | solution.py:117
  102.4 4.6 %collective-permute-start.12 = (f32[64,256]{1,0:T(8,128)S(1)}, f32[64,256]{1,0:T(8,128)S(1)}, u32[]{:S(2)}, u32[]{:S(2)}) collective-permute-start(f32[64,256]{1,0:T(8,128)S(1)} %maximum_select_fusion.18), channel_id=1, source_target_pairs={{0,4},{1,5},{2,6},{3,7},{4,0},{5,1},{6,2},{7,3},{8,12},{9,13},{10,... | collective-permute-start | bytes 196616 | tf_op jit(solution)/shard_map/ppermute | solution.py:117
  104.8 5.0 %collective-permute-start.18 = (f32[128,256]{1,0:T(8,128)S(1)}, f32[128,256]{1,0:T(8,128)S(1)}, u32[]{:S(2)}, u32[]{:S(2)}) collective-permute-start(f32[128,256]{1,0:T(8,128)S(1)} %maximum_select_fusion.15), channel_id=1, source_target_pairs={{0,2},{1,3},{2,0},{3,1},{4,6},{5,7},{6,4},{7,5},{8,10},{9,11},{10,... | collective-permute-start | bytes 393224 | tf_op jit(solution)/shard_map/ppermute | solution.py:117
  107.1 5.0 %collective-permute-start.13 = (f32[128,256]{1,0:T(8,128)S(1)}, f32[128,256]{1,0:T(8,128)S(1)}, u32[]{:S(2)}, u32[]{:S(2)}) collective-permute-start(f32[128,256]{1,0:T(8,128)S(1)} %maximum_select_fusion.14), channel_id=1, source_target_pairs={{0,2},{1,3},{2,0},{3,1},{4,6},{5,7},{6,4},{7,5},{8,10},{9,11},{10,... | collective-permute-start | bytes 393224 | tf_op jit(solution)/shard_map/ppermute | solution.py:117
  108.7 15.9 %collective-permute-start.4 = (f32[256,256]{1,0:T(8,128)S(1)}, f32[256,256]{1,0:T(8,128)S(1)}, u32[]{:S(2)}, u32[]{:S(2)}) collective-permute-start(f32[256,256]{1,0:T(8,128)S(1)} %maximum_select_fusion.8), channel_id=1, source_target_pairs={{0,1},{1,0},{2,3},{3,2},{4,5},{5,4},{6,7},{7,6},{8,9},{9,8},{10,11... | collective-permute-start | bytes 786440 | tf_op jit(solution)/shard_map/ppermute | solution.py:117
  109.9 10.9 %collective-permute-start.19 = (f32[256,256]{1,0:T(8,128)S(1)}, f32[256,256]{1,0:T(8,128)S(1)}, u32[]{:S(2)}, u32[]{:S(2)}) collective-permute-start(f32[256,256]{1,0:T(8,128)S(1)} %maximum_select_fusion.11), channel_id=1, source_target_pairs={{0,1},{1,0},{2,3},{3,2},{4,5},{5,4},{6,7},{7,6},{8,9},{9,8},{10,11... | collective-permute-start | bytes 786440 | tf_op jit(solution)/shard_map/ppermute | solution.py:117
  112.1 11.4 %collective-permute-start.14 = (f32[256,256]{1,0:T(8,128)S(1)}, f32[256,256]{1,0:T(8,128)S(1)}, u32[]{:S(2)}, u32[]{:S(2)}) collective-permute-start(f32[256,256]{1,0:T(8,128)S(1)} %maximum_select_fusion.10), channel_id=1, source_target_pairs={{0,1},{1,0},{2,3},{3,2},{4,5},{5,4},{6,7},{7,6},{8,9},{9,8},{10,11... | collective-permute-start | bytes 786440 | tf_op jit(solution)/shard_map/ppermute | solution.py:117

commit v3 on v2

--- a/solution.py
+++ b/solution.py
@@ -165,11 +165,14 @@
     for c in range(chunks):
         if peaks[c] is None:
             peaks[c] = peaks_of(mines[c], receiveds[c])
-    pieces = [gather_rows(p, owners) for p in peaks]
-    ids = [
-        (np.asarray(order)[:, None] * gauges_here + c * per_chunk + np.arange(per_chunk)[None, :]).reshape(-1)
-        for c in range(chunks)
-    ]
+    split = (chunks + 1) // 2
+    bundles = [list(range(split)), list(range(split, chunks))] if chunks > 1 else [[0]]
+    pieces, ids = [], []
+    for bundle in bundles:
+        joined = jnp.concatenate([peaks[c] for c in bundle], 0) if len(bundle) > 1 else peaks[bundle[0]]
+        pieces.append(gather_rows(joined, owners))
+        local = np.concatenate([c * per_chunk + np.arange(per_chunk) for c in bundle])
+        ids.append((np.asarray(order)[:, None] * gauges_here + local[None, :]).reshape(-1))
     gauge_ids = jnp.asarray(np.concatenate(ids).astype(np.int32))
 
     tile_total = coast_gauges.shape[0]
@@ -182,16 +185,18 @@
     mine_weights = lax.dynamic_slice_in_dim(weights, first_tile, tiles_here, 0)
     matches = mine_gauges[:, :, None] == gauge_ids[None, None, :]
     tile_table = jnp.sum(jnp.where(matches, mine_weights[:, :, None], 0.0), axis=1)
-    span = owners * per_chunk
     onshore = None
-    for c in range(chunks):
+    start = 0
+    for piece in pieces:
+        span = piece.shape[0]
         term = lax.dot_general(
-            pieces[c],
-            tile_table[:, c * span:(c + 1) * span],
+            piece,
+            tile_table[:, start:start + span],
             (((0,), (1,)), ((), ())),
             precision=lax.Precision.HIGHEST,
             preferred_element_type=jnp.float32,
         )
+        start += span
         onshore = term if onshore is None else onshore + term
     return onshore
 

time: 127 us -> 126 us (level)
  starting transfers between devices: 24.6 us -> 13.8 us
  waiting for transfers between devices: 17 us -> 27.4 us
    ppermute x16 -> x8, starting transfers between devices: 23.6 us -> 12.8 us  [gather_rows(): got = lax.ppermute(held, 'rows', pairs)]
    ppermute x16 -> x8, waiting for transfers between devices: 17 us -> 25.2 us  [gather_rows(): got = lax.ppermute(held, 'rows', pairs)]
    ppermute x4, waiting for transfers between devices: 0.01 us -> 2.26 us  [body(): receiveds.append(lax.ppermute(other, 'src', pairs))]
    dot_general x4 -> x2, matrix products: 4.66 us -> 4.28 us  [body(): lax.dot_general(piece, tile_table[:, start:start + span], (((0,), (1,)),...]
  transfers between devices with their start and end apart: 20 -> 12, of which waited for: 8 -> 8; matrix products, arithmetic and copies ran while one was open for 7% -> 6% of each run, Pallas kernels for 43% -> 39%
where the time goes in v3:
time: 126 us
  Pallas kernels  67.2 us (53%)
  waiting for transfers between devices  27.4 us (22%)
  starting transfers between devices  13.8 us (11%)
  other arithmetic  9.05 us (7%)
  matrix products  4.28 us (3%)
  local copies, waits for them, and re-layouts  3.63 us (3%)
    pallas_call x2, Pallas kernels, fused_of(): pl.pallas_call(fused_kernel, grid=(steps,), in_specs=[pl.BlockSpec((sourc...  30.8 us
    pallas_call x2, Pallas kernels, partials_of(): pl.pallas_call(matmul_kernel, grid=(steps,), in_specs=[pl.BlockSpec((sour...  26.8 us
    ppermute x8, waiting for transfers between devices, gather_rows(): got = lax.ppermute(held, 'rows', pairs)  25.2 us
    ppermute x8, starting transfers between devices, gather_rows(): got = lax.ppermute(held, 'rows', pairs)  12.8 us
    pallas_call x2, Pallas kernels, peaks_of(): pl.pallas_call(peak_kernel, grid=(blocks,), in_specs=[pl.BlockSpec((SEG,...  9.66 us
    dot_general x2, matrix products, body(): lax.dot_general(piece, tile_table[:, start:start + span], (((0,), (1,)),...  4.28 us
    reduce_sum x1, other arithmetic, body(): jnp.sum(jnp.where(matches, mine_weights[:, :, None], 0.0), axis=1)  2.84 us
    convert_element_type x1, other arithmetic, body(): slip_t = (units_t * scale_rows).astype(jnp.bfloat16)  2.72 us
  transfers between devices with their start and end apart: 12, of which 8 were waited for; matrix products, arithmetic and copies ran while one was open for 6% of the time, Pallas kernels for 39%

profile of v3, /device:TPU:0, one launch (start us, length us, event | category | flops | bytes accessed | tf_op | source)
XLA Modules:
  0.0 125.6 jit_solution(5831904496273346436)
XLA Ops:
  1.0 1.6 %reshape.7 = f32[1000,512]{1,0:T(8,128)} reshape(f32[8,125,512]{2,1,0:T(8,128)S(1)} %broadcast_in_dim.23) | data formatting | bytes 4096000 | tf_op jit(solution)/shard_map/reshape | solution.py:135
  2.6 2.7 %fusion = bf16[1000,512]{1,0:T(8,128)(2,1)S(1)} fusion(f32[1000,512]{1,0:T(8,128)} %reshape.7, s32[512,1000]{0,1:T(8,128)} %param.7), kind=kLoop, calls=%fused_computation.2 | loop fusion | flops 1536000 | bytes 5120000 | tf_op jit(solution)/shard_map/convert_element_type | solution.py:136
  6.4 13.4 %shard_map.75 = (bf16[7680,256]{1,0:T(8,128)(2,1)}, bf16[7680,256]{1,0:T(8,128)(2,1)}) custom-call(bf16[1000,512]{1,0:T(8,128)(2,1)} %pad_maximum_fusion.slip_ref, bf16[1000,30720]{1,0:T(8,128)(2,1)} %green_ref.7), custom_call_target="tpu_custom_call" | custom-call | flops 7864320000 | bytes 23224320 | tf_op jit(solution)/shard_map/pallas_call | solution.py:27
  20.3 13.4 %shard_map.73 = (bf16[7680,256]{1,0:T(8,128)(2,1)}, bf16[7680,256]{1,0:T(8,128)(2,1)}) custom-call(bf16[1000,512]{1,0:T(8,128)(2,1)} %pad_maximum_fusion.slip_ref, bf16[1000,30720]{1,0:T(8,128)(2,1)} %green_ref.7), custom_call_target="tpu_custom_call" | custom-call | flops 7864320000 | bytes 23224320 | tf_op jit(solution)/shard_map/pallas_call | solution.py:27
  33.7 15.4 %shard_map.76 = (bf16[7680,256]{1,0:T(8,128)(2,1)}, bf16[7680,256]{1,0:T(8,128)(2,1)}, f32[32,256]{1,0:T(8,128)}) custom-call(bf16[1000,512]{1,0:T(8,128)(2,1)} %pad_maximum_fusion.slip_ref, bf16[1000,30720]{1,0:T(8,128)(2,1)} %green_ref.7, bf16[7680,256]{1,0:T(8,128)(2,1)} %get-tuple-element.18.mine_prev_ref, ...), custom_call_target="tpu_custom_call" | custom-call | flops 7864320000 | bytes 31088640 | tf_op jit(solution)/shard_map/pallas_call | solution.py:60
  49.5 15.4 %shard_map.74 = (bf16[7680,256]{1,0:T(8,128)(2,1)}, bf16[7680,256]{1,0:T(8,128)(2,1)}, f32[32,256]{1,0:T(8,128)}) custom-call(bf16[1000,512]{1,0:T(8,128)(2,1)} %pad_maximum_fusion.slip_ref, bf16[1000,30720]{1,0:T(8,128)(2,1)} %green_ref.7, bf16[7680,256]{1,0:T(8,128)(2,1)} %get-tuple-element.15.mine_prev_ref, ...), custom_call_target="tpu_custom_call" | custom-call | flops 7864320000 | bytes 31088640 | tf_op jit(solution)/shard_map/pallas_call | solution.py:60
  65.0 4.8 %shard_map.78 = f32[32,256]{1,0:T(8,128)} custom-call(bf16[7680,256]{1,0:T(8,128)(2,1)} %get-tuple-element.23.mine_ref, bf16[7680,256]{1,0:T(8,128)(2,1)} %collective-permute-done.7.recv_ref), custom_call_target="tpu_custom_call" | custom-call | flops 5898240 | bytes 7864320 | tf_op jit(solution)/shard_map/pallas_call | solution.py:91
  69.8 2.2 %collective-permute-done.6.recv_ref = bf16[7680,256]{1,0:T(8,128)(2,1)} collective-permute-done((bf16[7680,256]{1,0:T(8,128)(2,1)}, bf16[7680,256]{1,0:T(8,128)(2,1)}, u32[]{:S(2)}, u32[]{:S(2)}) %collective-permute-start.6) | collective-permute-done | bytes 3932192 | tf_op jit(solution)/shard_map/ppermute | solution.py:164
  72.1 4.8 %shard_map.77 = f32[32,256]{1,0:T(8,128)} custom-call(bf16[7680,256]{1,0:T(8,128)(2,1)} %get-tuple-element.21.mine_ref, bf16[7680,256]{1,0:T(8,128)(2,1)} %collective-permute-done.6.recv_ref), custom_call_target="tpu_custom_call" | custom-call | flops 5898240 | bytes 7864320 | tf_op jit(solution)/shard_map/pallas_call | solution.py:91
  77.7 3.7 %collective-permute-start.8 = (f32[64,256]{1,0:T(8,128)S(1)}, f32[64,256]{1,0:T(8,128)S(1)}, u32[]{:S(2)}, u32[]{:S(2)}) collective-permute-start(f32[64,256]{1,0:T(8,128)S(1)} %pad_maximum_fusion.2), channel_id=1, source_target_pairs={{0,8},{1,9},{2,10},{3,11},{4,12},{5,13},{6,14},{7,15},{8,0},{9,1},... | collective-permute-start | bytes 196616 | tf_op jit(solution)/shard_map/ppermute | solution.py:117
  81.6 4.1 %collective-permute-done.8 = f32[64,256]{1,0:T(8,128)S(1)} collective-permute-done((f32[64,256]{1,0:T(8,128)S(1)}, f32[64,256]{1,0:T(8,128)S(1)}, u32[]{:S(2)}, u32[]{:S(2)}) %collective-permute-start.8) | collective-permute-done | bytes 65568 | tf_op jit(solution)/shard_map/ppermute | solution.py:117
  86.5 2.1 %collective-permute-start.9 = (f32[128,256]{1,0:T(8,128)S(1)}, f32[128,256]{1,0:T(8,128)S(1)}, u32[]{:S(2)}, u32[]{:S(2)}) collective-permute-start(f32[128,256]{1,0:T(8,128)S(1)} %maximum_select_fusion.9), channel_id=1, source_target_pairs={{0,4},{1,5},{2,6},{3,7},{4,0},{5,1},{6,2},{7,3},{8,12},{9,13},{10,... | collective-permute-start | bytes 393224 | tf_op jit(solution)/shard_map/ppermute | solution.py:117
  89.9 3.0 %collective-permute-done.9 = f32[128,256]{1,0:T(8,128)S(1)} collective-permute-done((f32[128,256]{1,0:T(8,128)S(1)}, f32[128,256]{1,0:T(8,128)S(1)}, u32[]{:S(2)}, u32[]{:S(2)}) %collective-permute-start.9) | collective-permute-done | bytes 131104 | tf_op jit(solution)/shard_map/ppermute | solution.py:117
  92.9 1.7 %collective-permute-start.10 = (f32[256,256]{1,0:T(8,128)S(1)}, f32[256,256]{1,0:T(8,128)S(1)}, u32[]{:S(2)}, u32[]{:S(2)}) collective-permute-start(f32[256,256]{1,0:T(8,128)S(1)} %maximum_select_fusion.7), channel_id=1, source_target_pairs={{0,2},{1,3},{2,0},{3,1},{4,6},{5,7},{6,4},{7,5},{8,10},{9,11},{10,... | collective-permute-start | bytes 786440 | tf_op jit(solution)/shard_map/ppermute | solution.py:117
  95.1 1.6 %collective-permute-start.4 = (f32[256,256]{1,0:T(8,128)S(1)}, f32[256,256]{1,0:T(8,128)S(1)}, u32[]{:S(2)}, u32[]{:S(2)}) collective-permute-start(f32[256,256]{1,0:T(8,128)S(1)} %maximum_select_fusion.6), channel_id=1, source_target_pairs={{0,2},{1,3},{2,0},{3,1},{4,6},{5,7},{6,4},{7,5},{8,10},{9,11},{10,... | collective-permute-start | bytes 786440 | tf_op jit(solution)/shard_map/ppermute | solution.py:117
  97.5 4.8 %collective-permute-done.10 = f32[256,256]{1,0:T(8,128)S(1)} collective-permute-done((f32[256,256]{1,0:T(8,128)S(1)}, f32[256,256]{1,0:T(8,128)S(1)}, u32[]{:S(2)}, u32[]{:S(2)}) %collective-permute-start.10) | collective-permute-done | bytes 262176 | tf_op jit(solution)/shard_map/ppermute | solution.py:117
  102.3 1.7 %collective-permute-start.11 = (f32[512,256]{1,0:T(8,128)S(1)}, f32[512,256]{1,0:T(8,128)S(1)}, u32[]{:S(2)}, u32[]{:S(2)}) collective-permute-start(f32[512,256]{1,0:T(8,128)S(1)} %maximum_select_fusion.5), channel_id=1, source_target_pairs={{0,1},{1,0},{2,3},{3,2},{4,5},{5,4},{6,7},{7,6},{8,9},{9,8},{10,11... | collective-permute-start | bytes 1572872 | tf_op jit(solution)/shard_map/ppermute | solution.py:117
  104.1 1.6 %collective-permute-done.4 = f32[256,256]{1,0:T(8,128)S(1)} collective-permute-done((f32[256,256]{1,0:T(8,128)S(1)}, f32[256,256]{1,0:T(8,128)S(1)}, u32[]{:S(2)}, u32[]{:S(2)}) %collective-permute-start.4) | collective-permute-done | bytes 262176 | tf_op jit(solution)/shard_map/ppermute | solution.py:117
  105.7 1.4 %collective-permute-start.5 = (f32[512,256]{1,0:T(8,128)S(1)}, f32[512,256]{1,0:T(8,128)S(1)}, u32[]{:S(2)}, u32[]{:S(2)}) collective-permute-start(f32[512,256]{1,0:T(8,128)S(1)} %maximum_select_fusion.4), channel_id=1, source_target_pairs={{0,1},{1,0},{2,3},{3,2},{4,5},{5,4},{6,7},{7,6},{8,9},{9,8},{10,11... | collective-permute-start | bytes 1572872 | tf_op jit(solution)/shard_map/ppermute | solution.py:117
  107.1 2.8 %select_reduce_fusion = f32[128,2048]{1,0:T(8,128)S(1)} fusion(f32[128,8]{1,0:T(8,128)S(1)} %copy.13, s32[2048]{0:T(1024)S(1)} %copy-done.4, s32[128,8]{1,0:T(8,128)S(1)} %copy.12), kind=kLoop, calls=%fused_computation | loop fusion | flops 6029312 | bytes 1064960 | tf_op jit(solution)/shard_map/reduce_sum | solution.py:187
  109.9 7.3 %collective-permute-done.11 = f32[512,256]{1,0:T(8,128)S(1)} collective-permute-done((f32[512,256]{1,0:T(8,128)S(1)}, f32[512,256]{1,0:T(8,128)S(1)}, u32[]{:S(2)}, u32[]{:S(2)}) %collective-permute-start.11) | collective-permute-done | bytes 524320 | tf_op jit(solution)/shard_map/ppermute | solution.py:117
  117.2 1.8 %fusion.6 = f32[256,128]{1,0:T(8,128)S(1)} fusion(f32[512,256]{1,0:T(8,128)S(1)} %maximum_select_fusion.5, f32[512,256]{1,0:T(8,128)S(1)} %collective-permute-done.11, f32[128,2048]{1,0:T(8,128)S(1)} %select_reduce_fusion, pred[]{:T(512)S(6)} %ne.16), kind=kOutput, calls=%fused_computation.11 | convolution fusion | flops 403439616 | bytes 1703937 | tf_op jit(solution)/shard_map/dot_general | solution.py:192
  119.0 4.1 %collective-permute-done.5 = f32[512,256]{1,0:T(8,128)S(1)} collective-permute-done((f32[512,256]{1,0:T(8,128)S(1)}, f32[512,256]{1,0:T(8,128)S(1)}, u32[]{:S(2)}, u32[]{:S(2)}) %collective-permute-start.5) | collective-permute-done | bytes 524320 | tf_op jit(solution)/shard_map/ppermute | solution.py:117
  123.1 2.5 %convolution_add_fusion = f32[256,128]{1,0:T(8,128)} fusion(f32[256,128]{1,0:T(8,128)S(1)} %fusion.6, f32[512,256]{1,0:T(8,128)S(1)} %maximum_select_fusion.4, f32[512,256]{1,0:T(8,128)S(1)} %collective-permute-done.5, f32[128,2048]{1,0:T(8,128)S(1)} %select_reduce_fusion, pred[]{:T(512)S(6)} %ne.16), kind=kOutput, calls=%fused_computation.3 | convolution fusion | flops 403472384 | bytes 1835009 | tf_op jit(solution)/shard_map/dot_general | solution.py:192
  (37 shorter events, 7.6 us)
Async XLA Ops:
  0.0 104.0 %copy-start = (s32[2048,8]{0,1:T(8,128)S(1)}, s32[2048,8]{0,1:T(8,128)}, u32[]{:S(2)}) copy-start(s32[2048,8]{0,1:T(8,128)} %param.10) | copy-start | bytes 196612
  19.8 13.9 %collective-permute-start.1 = (bf16[7680,256]{1,0:T(8,128)(2,1)}, bf16[7680,256]{1,0:T(8,128)(2,1)}, u32[]{:S(2)}, u32[]{:S(2)}) collective-permute-start(bf16[7680,256]{1,0:T(8,128)(2,1)} %get-tuple-element.19), channel_id=1, source_target_pairs={{0,16},{16,0},{1,17},{17,1},{2,18},{18,2},{3,19},{19,3},{4,20},{20... | collective-permute-start | bytes 11796488 | tf_op jit(solution)/shard_map/ppermute | solution.py:164
  33.7 15.9 %collective-permute-start = (bf16[7680,256]{1,0:T(8,128)(2,1)}, bf16[7680,256]{1,0:T(8,128)(2,1)}, u32[]{:S(2)}, u32[]{:S(2)}) collective-permute-start(bf16[7680,256]{1,0:T(8,128)(2,1)} %get-tuple-element.16), channel_id=1, source_target_pairs={{0,16},{16,0},{1,17},{17,1},{2,18},{18,2},{3,19},{19,3},{4,20},{20... | collective-permute-start | bytes 11796488 | tf_op jit(solution)/shard_map/ppermute | solution.py:164
  49.1 15.9 %collective-permute-start.7 = (bf16[7680,256]{1,0:T(8,128)(2,1)}, bf16[7680,256]{1,0:T(8,128)(2,1)}, u32[]{:S(2)}, u32[]{:S(2)}) collective-permute-start(bf16[7680,256]{1,0:T(8,128)(2,1)} %get-tuple-element.24), channel_id=1, source_target_pairs={{0,16},{16,0},{1,17},{17,1},{2,18},{18,2},{3,19},{19,3},{4,20},{20... | collective-permute-start | bytes 11796488 | tf_op jit(solution)/shard_map/ppermute | solution.py:164
  65.0 7.1 %collective-permute-start.6 = (bf16[7680,256]{1,0:T(8,128)(2,1)}, bf16[7680,256]{1,0:T(8,128)(2,1)}, u32[]{:S(2)}, u32[]{:S(2)}) collective-permute-start(bf16[7680,256]{1,0:T(8,128)(2,1)} %get-tuple-element.22), channel_id=1, source_target_pairs={{0,16},{16,0},{1,17},{17,1},{2,18},{18,2},{3,19},{19,3},{4,20},{20... | collective-permute-start | bytes 11796488 | tf_op jit(solution)/shard_map/ppermute | solution.py:164
  72.1 4.9 %copy-start.1 = (f32[32,256]{1,0:T(8,128)S(1)}, f32[32,256]{1,0:T(8,128)}, u32[]{:S(2)}) copy-start(f32[32,256]{1,0:T(8,128)} %shard_map.78) | copy-start | bytes 98308
  72.1 9.4 %copy-start.2 = (f32[32,256]{1,0:T(8,128)S(1)}, f32[32,256]{1,0:T(8,128)}, u32[]{:S(2)}) copy-start(f32[32,256]{1,0:T(8,128)} %get-tuple-element.20) | copy-start | bytes 98308
  72.1 9.4 %copy-start.3 = (f32[32,256]{1,0:T(8,128)S(1)}, f32[32,256]{1,0:T(8,128)}, u32[]{:S(2)}) copy-start(f32[32,256]{1,0:T(8,128)} %get-tuple-element.17) | copy-start | bytes 98308
  76.9 30.1 %copy-start.4 = (s32[2048]{0:T(1024)S(1)}, s32[2048]{0:T(1024)}, u32[]{:S(2)}) copy-start(s32[2048]{0:T(1024)} %constant.32.clone) | copy-start | bytes 24580
  77.7 7.9 %collective-permute-start.8 = (f32[64,256]{1,0:T(8,128)S(1)}, f32[64,256]{1,0:T(8,128)S(1)}, u32[]{:S(2)}, u32[]{:S(2)}) collective-permute-start(f32[64,256]{1,0:T(8,128)S(1)} %pad_maximum_fusion.2), channel_id=1, source_target_pairs={{0,8},{1,9},{2,10},{3,11},{4,12},{5,13},{6,14},{7,15},{8,0},{9,1},... | collective-permute-start | bytes 196616 | tf_op jit(solution)/shard_map/ppermute | solution.py:117
  81.5 7.1 %collective-permute-start.2 = (f32[64,256]{1,0:T(8,128)S(1)}, f32[64,256]{1,0:T(8,128)S(1)}, u32[]{:S(2)}, u32[]{:S(2)}) collective-permute-start(f32[64,256]{1,0:T(8,128)S(1)} %pad_maximum_fusion.1), channel_id=1, source_target_pairs={{0,8},{1,9},{2,10},{3,11},{4,12},{5,13},{6,14},{7,15},{8,0},{9,1},... | collective-permute-start | bytes 196616 | tf_op jit(solution)/shard_map/ppermute | solution.py:117
  86.5 6.4 %collective-permute-start.9 = (f32[128,256]{1,0:T(8,128)S(1)}, f32[128,256]{1,0:T(8,128)S(1)}, u32[]{:S(2)}, u32[]{:S(2)}) collective-permute-start(f32[128,256]{1,0:T(8,128)S(1)} %maximum_select_fusion.9), channel_id=1, source_target_pairs={{0,4},{1,5},{2,6},{3,7},{4,0},{5,1},{6,2},{7,3},{8,12},{9,13},{10,... | collective-permute-start | bytes 393224 | tf_op jit(solution)/shard_map/ppermute | solution.py:117
  88.6 6.5 %collective-permute-start.3 = (f32[128,256]{1,0:T(8,128)S(1)}, f32[128,256]{1,0:T(8,128)S(1)}, u32[]{:S(2)}, u32[]{:S(2)}) collective-permute-start(f32[128,256]{1,0:T(8,128)S(1)} %maximum_select_fusion.8), channel_id=1, source_target_pairs={{0,4},{1,5},{2,6},{3,7},{4,0},{5,1},{6,2},{7,3},{8,12},{9,13},{10,... | collective-permute-start | bytes 393224 | tf_op jit(solution)/shard_map/ppermute | solution.py:117
  92.9 9.3 %collective-permute-start.10 = (f32[256,256]{1,0:T(8,128)S(1)}, f32[256,256]{1,0:T(8,128)S(1)}, u32[]{:S(2)}, u32[]{:S(2)}) collective-permute-start(f32[256,256]{1,0:T(8,128)S(1)} %maximum_select_fusion.7), channel_id=1, source_target_pairs={{0,2},{1,3},{2,0},{3,1},{4,6},{5,7},{6,4},{7,5},{8,10},{9,11},{10,... | collective-permute-start | bytes 786440 | tf_op jit(solution)/shard_map/ppermute | solution.py:117
  95.1 10.5 %collective-permute-start.4 = (f32[256,256]{1,0:T(8,128)S(1)}, f32[256,256]{1,0:T(8,128)S(1)}, u32[]{:S(2)}, u32[]{:S(2)}) collective-permute-start(f32[256,256]{1,0:T(8,128)S(1)} %maximum_select_fusion.6), channel_id=1, source_target_pairs={{0,2},{1,3},{2,0},{3,1},{4,6},{5,7},{6,4},{7,5},{8,10},{9,11},{10,... | collective-permute-start | bytes 786440 | tf_op jit(solution)/shard_map/ppermute | solution.py:117
  102.3 14.9 %collective-permute-start.11 = (f32[512,256]{1,0:T(8,128)S(1)}, f32[512,256]{1,0:T(8,128)S(1)}, u32[]{:S(2)}, u32[]{:S(2)}) collective-permute-start(f32[512,256]{1,0:T(8,128)S(1)} %maximum_select_fusion.5), channel_id=1, source_target_pairs={{0,1},{1,0},{2,3},{3,2},{4,5},{5,4},{6,7},{7,6},{8,9},{9,8},{10,11... | collective-permute-start | bytes 1572872 | tf_op jit(solution)/shard_map/ppermute | solution.py:117
  105.7 17.4 %collective-permute-start.5 = (f32[512,256]{1,0:T(8,128)S(1)}, f32[512,256]{1,0:T(8,128)S(1)}, u32[]{:S(2)}, u32[]{:S(2)}) collective-permute-start(f32[512,256]{1,0:T(8,128)S(1)} %maximum_select_fusion.4), channel_id=1, source_target_pairs={{0,1},{1,0},{2,3},{3,2},{4,5},{5,4},{6,7},{7,6},{8,9},{9,8},{10,11... | collective-permute-start | bytes 1572872 | tf_op jit(solution)/shard_map/ppermute | solution.py:117

commit v4 on v3

--- a/solution.py
+++ b/solution.py
@@ -1,3 +1,5 @@
+import functools
+
 import numpy as np
 import jax
 import jax.numpy as jnp
@@ -20,16 +22,17 @@
     mine_ref[...] = product[:, half:].astype(jnp.bfloat16)
 
 
-def partials_of(slip_ordered, green, chunk, width, tile):
+def partials_of(slip_ordered, green, first, steps):
     sources, scenarios = slip_ordered.shape
     half = scenarios // 2
-    steps = width // tile
+    tile = SEG
+    width = steps * tile
     return pl.pallas_call(
         matmul_kernel,
         grid=(steps,),
         in_specs=[
             pl.BlockSpec((sources, scenarios), lambda j: (0, 0)),
-            pl.BlockSpec((sources, tile), lambda j: (0, chunk * steps + j)),
+            pl.BlockSpec((sources, tile), lambda j: (0, first + j)),
         ],
         out_specs=[pl.BlockSpec((tile, half), lambda j: (j, 0))] * 2,
         out_shape=[jax.ShapeDtypeStruct((width, half), jnp.bfloat16)] * 2,
@@ -47,39 +50,43 @@
     out_ref[...] = jnp.max(jnp.abs(wave).reshape(gauges, NT, wave.shape[1]), axis=1)
 
 
-def fused_kernel(slip_ref, green_ref, mine_prev_ref, recv_prev_ref, other_ref, mine_ref, peaks_ref):
+def fused_kernel(slip_ref, green_ref, mine_prev_ref, recv_prev_ref, other_ref, mine_ref, peaks_ref, *, trail):
     matmul_kernel(slip_ref, green_ref, other_ref, mine_ref)
-    peak_kernel(mine_prev_ref, recv_prev_ref, peaks_ref)
-
-
-def fused_of(slip_ordered, green, chunk, width, mine_prev, recv_prev):
+
+    @pl.when(pl.program_id(0) < trail)
+    def _():
+        peak_kernel(mine_prev_ref, recv_prev_ref, peaks_ref)
+
+
+def fused_of(slip_ordered, green, first, steps, mine_prev, recv_prev):
     sources, scenarios = slip_ordered.shape
     half = scenarios // 2
-    steps = width // SEG
+    trail = mine_prev.shape[0] // SEG
     gauges = SEG // NT
+    back = lambda j: (jnp.minimum(j, trail - 1), 0)
     return pl.pallas_call(
-        fused_kernel,
+        functools.partial(fused_kernel, trail=trail),
         grid=(steps,),
         in_specs=[
             pl.BlockSpec((sources, scenarios), lambda j: (0, 0)),
-            pl.BlockSpec((sources, SEG), lambda j: (0, chunk * steps + j)),
-            pl.BlockSpec((SEG, half), lambda j: (j, 0)),
-            pl.BlockSpec((SEG, half), lambda j: (j, 0)),
+            pl.BlockSpec((sources, SEG), lambda j: (0, first + j)),
+            pl.BlockSpec((SEG, half), back),
+            pl.BlockSpec((SEG, half), back),
         ],
         out_specs=[
             pl.BlockSpec((SEG, half), lambda j: (j, 0)),
             pl.BlockSpec((SEG, half), lambda j: (j, 0)),
-            pl.BlockSpec((gauges, half), lambda j: (j, 0)),
+            pl.BlockSpec((gauges, half), back),
         ],
         out_shape=[
-            jax.ShapeDtypeStruct((width, half), jnp.bfloat16),
-            jax.ShapeDtypeStruct((width, half), jnp.bfloat16),
-            jax.ShapeDtypeStruct((steps * gauges, half), jnp.float32),
+            jax.ShapeDtypeStruct((steps * SEG, half), jnp.bfloat16),
+            jax.ShapeDtypeStruct((steps * SEG, half), jnp.bfloat16),
+            jax.ShapeDtypeStruct((trail * gauges, half), jnp.float32),
         ],
         cost_estimate=pl.CostEstimate(
-            flops=2 * scenarios * sources * width,
+            flops=2 * scenarios * sources * steps * SEG,
             transcendentals=0,
-            bytes_accessed=2 * (sources * width + 2 * scenarios * width),
+            bytes_accessed=2 * (sources * steps * SEG + scenarios * (steps + trail) * SEG),
         ),
     )(slip_ordered, green, mine_prev, recv_prev)
 
@@ -122,6 +129,14 @@
     return held
 
 
+def chunk_plan(segments):
+    if segments >= 8:
+        rest = segments - 2
+        size, extra = divmod(rest, 4)
+        return [size] * (4 - extra) + [size + 1] * extra + [1, 1]
+    return [1] * segments
+
+
 def arrival_order(owners):
     order = [0]
     for m in doubling_masks(owners):
@@ -146,32 +161,32 @@
     columns = green.shape[1]
     gauges_here = columns // NT
     segments = columns // SEG
-    chunks = max(c for c in (1, 2, 4) if segments % c == 0)
-    width = columns // chunks
-    tile = SEG
-    per_chunk = gauges_here // chunks
+    sizes = chunk_plan(segments)
+    chunks = len(sizes)
+    firsts = [sum(sizes[:c]) for c in range(chunks)]
+    gauges_per_seg = SEG // NT
     order = arrival_order(owners)
-    lag = 2 if chunks > 2 else 0
     mines, receiveds, peaks = [], [], [None] * chunks
     for c in range(chunks):
-        if lag and c >= lag:
-            other, mine, peaks[c - lag] = fused_of(
-                slip_ordered, green, c, width, mines[c - lag], receiveds[c - lag]
+        if c >= 2 and sizes[c - 2] <= sizes[c]:
+            other, mine, peaks[c - 2] = fused_of(
+                slip_ordered, green, firsts[c], sizes[c], mines[c - 2], receiveds[c - 2]
             )
         else:
-            other, mine = partials_of(slip_ordered, green, c, width, tile)
+            other, mine = partials_of(slip_ordered, green, firsts[c], sizes[c])
         mines.append(mine)
         receiveds.append(lax.ppermute(other, "src", pairs))
     for c in range(chunks):
         if peaks[c] is None:
             peaks[c] = peaks_of(mines[c], receiveds[c])
-    split = (chunks + 1) // 2
-    bundles = [list(range(split)), list(range(split, chunks))] if chunks > 1 else [[0]]
+    bundles = [list(range(chunks - 2)), [chunks - 2, chunks - 1]] if chunks > 2 else [list(range(chunks))]
     pieces, ids = [], []
     for bundle in bundles:
         joined = jnp.concatenate([peaks[c] for c in bundle], 0) if len(bundle) > 1 else peaks[bundle[0]]
         pieces.append(gather_rows(joined, owners))
-        local = np.concatenate([c * per_chunk + np.arange(per_chunk) for c in bundle])
+        local = np.concatenate(
+            [firsts[c] * gauges_per_seg + np.arange(sizes[c] * gauges_per_seg) for c in bundle]
+        )
         ids.append((np.asarray(order)[:, None] * gauges_here + local[None, :]).reshape(-1))
     gauge_ids = jnp.asarray(np.concatenate(ids).astype(np.int32))
 

time: 126 us -> 148 us (1.17)
  Pallas kernels: 67.2 us -> 78.7 us
  local copies, waits for them, and re-layouts: 3.63 us -> 8.76 us
  starting transfers between devices: 13.8 us -> 16 us
  matrix products: 4.28 us -> 5.81 us
    pallas_call x2 -> x4, Pallas kernels: 26.8 us -> 33.8 us  [partials_of(): pl.pallas_call(matmul_kernel, grid=(steps,), in_specs=[pl.BlockSpec((sour...]
    unnamed x10 -> x23, local copies, waits for them, and re-layouts: 0.02 us -> 5.12 us
    pallas_call x2 -> x4, Pallas kernels: 9.66 us -> 14.3 us  [peaks_of(): pl.pallas_call(peak_kernel, grid=(blocks,), in_specs=[pl.BlockSpec((SEG,...]
    ppermute x8, waiting for transfers between devices: 25.2 us -> 28.1 us  [gather_rows(): got = lax.ppermute(held, 'rows', pairs)]
    ppermute x4 -> x6, waiting for transfers between devices: 2.26 us -> 0.02 us  [body(): receiveds.append(lax.ppermute(other, 'src', pairs))]
    ppermute x8, starting transfers between devices: 12.8 us -> 14.5 us  [gather_rows(): got = lax.ppermute(held, 'rows', pairs)]
    dot_general x2, matrix products: 4.28 us -> 5.81 us  [body(): lax.dot_general(piece, tile_table[:, start:start + span], (((0,), (1,)),...]
  transfers between devices with their start and end apart: 12 -> 14, of which waited for: 8 -> 5; matrix products, arithmetic and copies ran while one was open for 6% -> 6% of each run, Pallas kernels for 39% -> 46%
where the time goes in v4:
time: 148 us; the launch traced here: 147 us
  Pallas kernels  78.7 us (53%)
  waiting for transfers between devices  28.1 us (19%)
  starting transfers between devices  16 us (11%)
  other arithmetic  9.54 us (6%)
  local copies, waits for them, and re-layouts  8.76 us (6%)
  matrix products  5.81 us (4%)
    pallas_call x4, Pallas kernels, partials_of(): pl.pallas_call(matmul_kernel, grid=(steps,), in_specs=[pl.BlockSpec((sour...  33.8 us
    pallas_call x2, Pallas kernels, fused_of(): pl.pallas_call(functools.partial(fused_kernel, trail=trail), grid=(steps,...  30.5 us
    ppermute x8, waiting for transfers between devices, gather_rows(): got = lax.ppermute(held, 'rows', pairs)  28.1 us
    ppermute x8, starting transfers between devices, gather_rows(): got = lax.ppermute(held, 'rows', pairs)  14.5 us
    pallas_call x4, Pallas kernels, peaks_of(): pl.pallas_call(peak_kernel, grid=(blocks,), in_specs=[pl.BlockSpec((SEG,...  14.3 us
    dot_general x2, matrix products, body(): lax.dot_general(piece, tile_table[:, start:start + span], (((0,), (1,)),...  5.81 us
    unnamed x23, local copies, waits for them, and re-layouts  5.12 us
  transfers between devices with their start and end apart: 14, of which 5 were waited for; matrix products, arithmetic and copies ran while one was open for 6% of the time, Pallas kernels for 46%

profile of v4, /device:TPU:0, one launch (start us, length us, event | category | flops | bytes accessed | tf_op | source)
XLA Modules:
  0.0 147.1 jit_solution(17033825187583833346)
XLA Ops:
  1.0 1.6 %reshape.7 = f32[1000,512]{1,0:T(8,128)} reshape(f32[8,125,512]{2,1,0:T(8,128)S(1)} %broadcast_in_dim.23) | data formatting | bytes 4096000 | tf_op jit(solution)/shard_map/reshape | solution.py:150
  2.6 2.7 %fusion = bf16[1000,512]{1,0:T(8,128)(2,1)S(1)} fusion(f32[1000,512]{1,0:T(8,128)} %reshape.7, s32[512,1000]{0,1:T(8,128)} %param.7), kind=kLoop, calls=%fused_computation.2 | loop fusion | flops 1536000 | bytes 5120000 | tf_op jit(solution)/shard_map/convert_element_type | solution.py:151
  6.4 11.0 %shard_map.75 = (bf16[5760,256]{1,0:T(8,128)(2,1)}, bf16[5760,256]{1,0:T(8,128)(2,1)}) custom-call(bf16[1000,512]{1,0:T(8,128)(2,1)} %pad_maximum_fusion.slip_ref, bf16[1000,30720]{1,0:T(8,128)(2,1)} %green_ref.11), custom_call_target="tpu_custom_call" | custom-call | flops 5898240000 | bytes 17418240 | tf_op jit(solution)/shard_map/pallas_call | solution.py:30
  17.9 11.0 %shard_map.73 = (bf16[5760,256]{1,0:T(8,128)(2,1)}, bf16[5760,256]{1,0:T(8,128)(2,1)}) custom-call(bf16[1000,512]{1,0:T(8,128)(2,1)} %pad_maximum_fusion.slip_ref, bf16[1000,30720]{1,0:T(8,128)(2,1)} %green_ref.11), custom_call_target="tpu_custom_call" | custom-call | flops 5898240000 | bytes 17418240 | tf_op jit(solution)/shard_map/pallas_call | solution.py:30
  28.9 15.2 %shard_map.76 = (bf16[7680,256]{1,0:T(8,128)(2,1)}, bf16[7680,256]{1,0:T(8,128)(2,1)}, f32[24,256]{1,0:T(8,128)}) custom-call(bf16[1000,512]{1,0:T(8,128)(2,1)} %pad_maximum_fusion.slip_ref, bf16[1000,30720]{1,0:T(8,128)(2,1)} %green_ref.11, bf16[5760,256]{1,0:T(8,128)(2,1)} %get-tuple-element.22.mine_prev_ref, ...), custom_call_target="tpu_custom_call" | custom-call | flops 7864320000 | bytes 29122560 | tf_op jit(solution)/shard_map/pallas_call | solution.py:67
  44.6 1.6 %copy-done.1 = bf16[5760,256]{1,0:T(8,128)(2,1)} copy-done((bf16[5760,256]{1,0:T(8,128)(2,1)}, bf16[5760,256]{1,0:T(8,128)(2,1)S(1)}, u32[]{:S(2)}) %copy-start.1) | copy-done | bytes 2949144
  46.2 15.3 %shard_map.74 = (bf16[7680,256]{1,0:T(8,128)(2,1)}, bf16[7680,256]{1,0:T(8,128)(2,1)}, f32[24,256]{1,0:T(8,128)}) custom-call(bf16[1000,512]{1,0:T(8,128)(2,1)} %pad_maximum_fusion.slip_ref, bf16[1000,30720]{1,0:T(8,128)(2,1)} %green_ref.11, bf16[5760,256]{1,0:T(8,128)(2,1)} %get-tuple-element.19.mine_prev_ref, bf16[5760,256]{1,0:T(8,128)(2,1)} %copy-done.1), custom_call_target="tpu_custom_call" | custom-call | flops 7864320000 | bytes 29122560 | tf_op jit(solution)/shard_map/pallas_call | solution.py:67
  61.6 5.9 %shard_map.79 = (bf16[1920,256]{1,0:T(8,128)(2,1)}, bf16[1920,256]{1,0:T(8,128)(2,1)}) custom-call(bf16[1000,512]{1,0:T(8,128)(2,1)} %pad_maximum_fusion.slip_ref, bf16[1000,30720]{1,0:T(8,128)(2,1)} %green_ref.11), custom_call_target="tpu_custom_call" | custom-call | flops 1966080000 | bytes 5806080 | tf_op jit(solution)/shard_map/pallas_call | solution.py:30
  68.0 6.0 %shard_map.81 = (bf16[1920,256]{1,0:T(8,128)(2,1)}, bf16[1920,256]{1,0:T(8,128)(2,1)}) custom-call(bf16[1000,512]{1,0:T(8,128)(2,1)} %pad_maximum_fusion.slip_ref, bf16[1000,30720]{1,0:T(8,128)(2,1)} %green_ref.11), custom_call_target="tpu_custom_call" | custom-call | flops 1966080000 | bytes 5806080 | tf_op jit(solution)/shard_map/pallas_call | solution.py:30
  74.0 4.8 %shard_map.78 = f32[32,256]{1,0:T(8,128)} custom-call(bf16[7680,256]{1,0:T(8,128)(2,1)} %get-tuple-element.27.mine_ref, bf16[7680,256]{1,0:T(8,128)(2,1)} %collective-permute-done.3.recv_ref), custom_call_target="tpu_custom_call" | custom-call | flops 5898240 | bytes 7864320 | tf_op jit(solution)/shard_map/pallas_call | solution.py:98
  78.8 4.8 %shard_map.77 = f32[32,256]{1,0:T(8,128)} custom-call(bf16[7680,256]{1,0:T(8,128)(2,1)} %get-tuple-element.25.mine_ref, bf16[7680,256]{1,0:T(8,128)(2,1)} %collective-permute-done.2.recv_ref), custom_call_target="tpu_custom_call" | custom-call | flops 5898240 | bytes 7864320 | tf_op jit(solution)/shard_map/pallas_call | solution.py:98
  84.4 4.1 %collective-permute-start.4 = (f32[112,256]{1,0:T(8,128)S(1)}, f32[112,256]{1,0:T(8,128)S(1)}, u32[]{:S(2)}, u32[]{:S(2)}) collective-permute-start(f32[112,256]{1,0:T(8,128)S(1)} %pad_maximum_fusion.1), channel_id=1, source_target_pairs={{0,8},{1,9},{2,10},{3,11},{4,12},{5,13},{6,14},{7,15},{8,0},{9,1},... | collective-permute-start | bytes 344072 | tf_op jit(solution)/shard_map/ppermute | solution.py:124
  89.3 5.0 %collective-permute-done.4 = f32[112,256]{1,0:T(8,128)S(1)} collective-permute-done((f32[112,256]{1,0:T(8,128)S(1)}, f32[112,256]{1,0:T(8,128)S(1)}, u32[]{:S(2)}, u32[]{:S(2)}) %collective-permute-start.4) | collective-permute-done | bytes 114720 | tf_op jit(solution)/shard_map/ppermute | solution.py:124
  96.0 6.3 %collective-permute-done.5 = f32[224,256]{1,0:T(8,128)S(1)} collective-permute-done((f32[224,256]{1,0:T(8,128)S(1)}, f32[224,256]{1,0:T(8,128)S(1)}, u32[]{:S(2)}, u32[]{:S(2)}) %collective-permute-start.5) | collective-permute-done | bytes 229408 | tf_op jit(solution)/shard_map/ppermute | solution.py:124
  102.3 1.3 collective-permute-start.6
  104.6 2.3 %shard_map.80 = f32[8,256]{1,0:T(8,128)} custom-call(bf16[1920,256]{1,0:T(8,128)(2,1)} %get-tuple-element.29.mine_ref, bf16[1920,256]{1,0:T(8,128)(2,1)} %copy-done.2), custom_call_target="tpu_custom_call" | custom-call | flops 1474560 | bytes 1966080 | tf_op jit(solution)/shard_map/pallas_call | solution.py:98
  107.9 2.4 %shard_map.82 = f32[8,256]{1,0:T(8,128)} custom-call(bf16[1920,256]{1,0:T(8,128)(2,1)} %get-tuple-element.31.mine_ref, bf16[1920,256]{1,0:T(8,128)(2,1)} %copy-done.3), custom_call_target="tpu_custom_call" | custom-call | flops 1474560 | bytes 1966080 | tf_op jit(solution)/shard_map/pallas_call | solution.py:98
  110.9 3.2 %collective-permute-start.10 = (f32[16,256]{1,0:T(8,128)S(1)}, f32[16,256]{1,0:T(8,128)S(1)}, u32[]{:S(2)}, u32[]{:S(2)}) collective-permute-start(f32[16,256]{1,0:T(8,128)S(1)} %pad_maximum_fusion.2), channel_id=1, source_target_pairs={{0,8},{1,9},{2,10},{3,11},{4,12},{5,13},{6,14},{7,15},{8,0},{9,1},... | collective-permute-start | bytes 49160 | tf_op jit(solution)/shard_map/ppermute | solution.py:124
  116.6 1.7 %collective-permute-start.11 = (f32[32,256]{1,0:T(8,128)S(1)}, f32[32,256]{1,0:T(8,128)S(1)}, u32[]{:S(2)}, u32[]{:S(2)}) collective-permute-start(f32[32,256]{1,0:T(8,128)S(1)} %maximum_select_fusion.10), channel_id=1, source_target_pairs={{0,4},{1,5},{2,6},{3,7},{4,0},{5,1},{6,2},{7,3},{8,12},{9,13},{10,... | collective-permute-start | bytes 98312 | tf_op jit(solution)/shard_map/ppermute | solution.py:124
  118.4 1.6 %collective-permute-start.7 = (f32[896,256]{1,0:T(8,128)S(1)}, f32[896,256]{1,0:T(8,128)}, u32[]{:S(2)}, u32[]{:S(2)}) collective-permute-start(f32[896,256]{1,0:T(8,128)S(1)} %maximum_select_fusion.4), channel_id=1, source_target_pairs={{0,1},{1,0},{2,3},{3,2},{4,5},{5,4},{6,7},{7,6},{8,9},{9,8},{10,11... | collective-permute-start | bytes 2752520 | tf_op jit(solution)/shard_map/ppermute | solution.py:124
  121.5 3.6 %collective-permute-done.12 = f32[64,256]{1,0:T(8,128)S(1)} collective-permute-done((f32[64,256]{1,0:T(8,128)S(1)}, f32[64,256]{1,0:T(8,128)S(1)}, u32[]{:S(2)}, u32[]{:S(2)}) %collective-permute-start.12) | collective-permute-done | bytes 65568 | tf_op jit(solution)/shard_map/ppermute | solution.py:124
  126.4 2.7 %select_reduce_fusion = f32[128,2048]{1,0:T(8,128)S(1)} fusion(f32[128,8]{1,0:T(8,128)S(1)} %copy.13, s32[2048]{0:T(1024)S(1)} %copy-done.7, s32[128,8]{1,0:T(8,128)S(1)} %copy.12), kind=kLoop, calls=%fused_computation | loop fusion | flops 6029312 | bytes 1064960 | tf_op jit(solution)/shard_map/reduce_sum | solution.py:202
  129.1 12.2 %collective-permute-done.13 = f32[128,256]{1,0:T(8,128)S(1)} collective-permute-done((f32[128,256]{1,0:T(8,128)S(1)}, f32[128,256]{1,0:T(8,128)S(1)}, u32[]{:S(2)}, u32[]{:S(2)}) %collective-permute-start.13) | collective-permute-done | bytes 131104 | tf_op jit(solution)/shard_map/ppermute | solution.py:124
  141.9 5.2 %fusion.7 = f32[256,128]{1,0:T(8,128)} fusion(f32[256,128]{1,0:T(8,128)S(1)} %fusion.10, f32[896,256]{1,0:T(8,128)S(1)} %maximum_select_fusion.4, f32[896,256]{1,0:T(8,128)} %collective-permute-done.7, f32[128,2048]{1,0:T(8,128)S(1)} %select_reduce_fusion, pred[]{:T(512)S(6)} %ne.16), kind=kOutput, calls=%fused_computation.10 | convolution fusion | flops 706052096 | bytes 3014657 | tf_op jit(solution)/shard_map/dot_general | solution.py:207
  (60 shorter events, 15.4 us)
Async XLA Ops:
  0.0 121.4 %copy-start = (s32[2048,8]{0,1:T(8,128)S(1)}, s32[2048,8]{0,1:T(8,128)}, u32[]{:S(2)}) copy-start(s32[2048,8]{0,1:T(8,128)} %param.10) | copy-start | bytes 196612
  17.4 11.5 %collective-permute-start.1 = (bf16[5760,256]{1,0:T(8,128)(2,1)}, bf16[5760,256]{1,0:T(8,128)(2,1)}, u32[]{:S(2)}, u32[]{:S(2)}) collective-permute-start(bf16[5760,256]{1,0:T(8,128)(2,1)} %get-tuple-element.23), channel_id=1, source_target_pairs={{0,16},{16,0},{1,17},{17,1},{2,18},{18,2},{3,19},{19,3},{4,20},{20... | collective-permute-start | bytes 8847368 | tf_op jit(solution)/shard_map/ppermute | solution.py:178
  28.9 15.7 %collective-permute-start = (bf16[5760,256]{1,0:T(8,128)(2,1)}, bf16[5760,256]{1,0:T(8,128)(2,1)S(1)}, u32[]{:S(2)}, u32[]{:S(2)}) collective-permute-start(bf16[5760,256]{1,0:T(8,128)(2,1)} %get-tuple-element.20), channel_id=1, source_target_pairs={{0,16},{16,0},{1,17},{17,1},{2,18},{18,2},{3,19},{19,3},{4,20},{20... | collective-permute-start | bytes 8847368 | tf_op jit(solution)/shard_map/ppermute | solution.py:178
  44.1 29.9 %collective-permute-start.3 = (bf16[7680,256]{1,0:T(8,128)(2,1)}, bf16[7680,256]{1,0:T(8,128)(2,1)}, u32[]{:S(2)}, u32[]{:S(2)}) collective-permute-start(bf16[7680,256]{1,0:T(8,128)(2,1)} %get-tuple-element.28), channel_id=1, source_target_pairs={{0,16},{16,0},{1,17},{17,1},{2,18},{18,2},{3,19},{19,3},{4,20},{20... | collective-permute-start | bytes 11796488 | tf_op jit(solution)/shard_map/ppermute | solution.py:178
  44.6 1.6 %copy-start.1 = (bf16[5760,256]{1,0:T(8,128)(2,1)}, bf16[5760,256]{1,0:T(8,128)(2,1)S(1)}, u32[]{:S(2)}) copy-start(bf16[5760,256]{1,0:T(8,128)(2,1)S(1)} %collective-permute-done.recv_prev_ref) | copy-start | bytes 8847364
  61.5 17.3 %collective-permute-start.2 = (bf16[7680,256]{1,0:T(8,128)(2,1)}, bf16[7680,256]{1,0:T(8,128)(2,1)}, u32[]{:S(2)}, u32[]{:S(2)}) collective-permute-start(bf16[7680,256]{1,0:T(8,128)(2,1)} %get-tuple-element.26), channel_id=1, source_target_pairs={{0,16},{16,0},{1,17},{17,1},{2,18},{18,2},{3,19},{19,3},{4,20},{20... | collective-permute-start | bytes 11796488 | tf_op jit(solution)/shard_map/ppermute | solution.py:178
  67.5 6.5 %copy-start.6 = (f32[24,256]{1,0:T(8,128)S(1)}, f32[24,256]{1,0:T(8,128)}, u32[]{:S(2)}) copy-start(f32[24,256]{1,0:T(8,128)} %get-tuple-element.21) | copy-start | bytes 73732
  67.5 6.5 %copy-start.5 = (f32[24,256]{1,0:T(8,128)S(1)}, f32[24,256]{1,0:T(8,128)}, u32[]{:S(2)}) copy-start(f32[24,256]{1,0:T(8,128)} %get-tuple-element.24) | copy-start | bytes 73732
  67.5 36.1 %collective-permute-start.8 = (bf16[1920,256]{1,0:T(8,128)(2,1)}, bf16[1920,256]{1,0:T(8,128)(2,1)S(1)}, u32[]{:S(2)}, u32[]{:S(2)}) collective-permute-start(bf16[1920,256]{1,0:T(8,128)(2,1)} %get-tuple-element.30), channel_id=1, source_target_pairs={{0,16},{16,0},{1,17},{17,1},{2,18},{18,2},{3,19},{19,3},{4,20},{20... | collective-permute-start | bytes 2949128 | tf_op jit(solution)/shard_map/ppermute | solution.py:178
  73.9 33.0 %collective-permute-start.9 = (bf16[1920,256]{1,0:T(8,128)(2,1)}, bf16[1920,256]{1,0:T(8,128)(2,1)S(1)}, u32[]{:S(2)}, u32[]{:S(2)}) collective-permute-start(bf16[1920,256]{1,0:T(8,128)(2,1)} %get-tuple-element.32), channel_id=1, source_target_pairs={{0,16},{16,0},{1,17},{17,1},{2,18},{18,2},{3,19},{19,3},{4,20},{20... | collective-permute-start | bytes 2949128 | tf_op jit(solution)/shard_map/ppermute | solution.py:178
  78.8 4.8 %copy-start.4 = (f32[32,256]{1,0:T(8,128)S(1)}, f32[32,256]{1,0:T(8,128)}, u32[]{:S(2)}) copy-start(f32[32,256]{1,0:T(8,128)} %shard_map.78) | copy-start | bytes 98308
  84.4 9.9 %collective-permute-start.4 = (f32[112,256]{1,0:T(8,128)S(1)}, f32[112,256]{1,0:T(8,128)S(1)}, u32[]{:S(2)}, u32[]{:S(2)}) collective-permute-start(f32[112,256]{1,0:T(8,128)S(1)} %pad_maximum_fusion.1), channel_id=1, source_target_pairs={{0,8},{1,9},{2,10},{3,11},{4,12},{5,13},{6,14},{7,15},{8,0},{9,1},... | collective-permute-start | bytes 344072 | tf_op jit(solution)/shard_map/ppermute | solution.py:124
  95.2 7.1 %collective-permute-start.5 = (f32[224,256]{1,0:T(8,128)S(1)}, f32[224,256]{1,0:T(8,128)S(1)}, u32[]{:S(2)}, u32[]{:S(2)}) collective-permute-start(f32[224,256]{1,0:T(8,128)S(1)} %broadcast_select_fusion), channel_id=1, source_target_pairs={{0,4},{1,5},{2,6},{3,7},{4,0},{5,1},{6,2},{7,3},{8,12},{9,13},{10,... | collective-permute-start | bytes 688136 | tf_op jit(solution)/shard_map/ppermute | solution.py:124
  102.3 16.0 %collective-permute-start.6 = (f32[448,256]{1,0:T(8,128)S(1)}, f32[448,256]{1,0:T(8,128)S(1)}, u32[]{:S(2)}, u32[]{:S(2)}) collective-permute-start(f32[448,256]{1,0:T(8,128)S(1)} %maximum_select_fusion.5), channel_id=1, source_target_pairs={{0,2},{1,3},{2,0},{3,1},{4,6},{5,7},{6,4},{7,5},{8,10},{9,11},{10,... | collective-permute-start | bytes 1376264 | tf_op jit(solution)/shard_map/ppermute | solution.py:124
  103.6 0.9 copy-start.2
  106.9 1.0 copy-start.3
  107.9 18.6 %copy-start.7 = (s32[2048]{0:T(1024)S(1)}, s32[2048]{0:T(1024)}, u32[]{:S(2)}) copy-start(s32[2048]{0:T(1024)} %constant.32.clone) | copy-start | bytes 24580
  110.9 4.9 %collective-permute-start.10 = (f32[16,256]{1,0:T(8,128)S(1)}, f32[16,256]{1,0:T(8,128)S(1)}, u32[]{:S(2)}, u32[]{:S(2)}) collective-permute-start(f32[16,256]{1,0:T(8,128)S(1)} %pad_maximum_fusion.2), channel_id=1, source_target_pairs={{0,8},{1,9},{2,10},{3,11},{4,12},{5,13},{6,14},{7,15},{8,0},{9,1},... | collective-permute-start | bytes 49160 | tf_op jit(solution)/shard_map/ppermute | solution.py:124
  116.6 4.2 %collective-permute-start.11 = (f32[32,256]{1,0:T(8,128)S(1)}, f32[32,256]{1,0:T(8,128)S(1)}, u32[]{:S(2)}, u32[]{:S(2)}) collective-permute-start(f32[32,256]{1,0:T(8,128)S(1)} %maximum_select_fusion.10), channel_id=1, source_target_pairs={{0,4},{1,5},{2,6},{3,7},{4,0},{5,1},{6,2},{7,3},{8,12},{9,13},{10,... | collective-permute-start | bytes 98312 | tf_op jit(solution)/shard_map/ppermute | solution.py:124
  118.4 23.5 %collective-permute-start.7 = (f32[896,256]{1,0:T(8,128)S(1)}, f32[896,256]{1,0:T(8,128)}, u32[]{:S(2)}, u32[]{:S(2)}) collective-permute-start(f32[896,256]{1,0:T(8,128)S(1)} %maximum_select_fusion.4), channel_id=1, source_target_pairs={{0,1},{1,0},{2,3},{3,2},{4,5},{5,4},{6,7},{7,6},{8,9},{9,8},{10,11... | collective-permute-start | bytes 2752520 | tf_op jit(solution)/shard_map/ppermute | solution.py:124
  120.8 4.3 %collective-permute-start.12 = (f32[64,256]{1,0:T(8,128)S(1)}, f32[64,256]{1,0:T(8,128)S(1)}, u32[]{:S(2)}, u32[]{:S(2)}) collective-permute-start(f32[64,256]{1,0:T(8,128)S(1)} %maximum_select_fusion.9), channel_id=1, source_target_pairs={{0,2},{1,3},{2,0},{3,1},{4,6},{5,7},{6,4},{7,5},{8,10},{9,11},{10,... | collective-permute-start | bytes 196616 | tf_op jit(solution)/shard_map/ppermute | solution.py:124
  125.1 16.2 %collective-permute-start.13 = (f32[128,256]{1,0:T(8,128)S(1)}, f32[128,256]{1,0:T(8,128)S(1)}, u32[]{:S(2)}, u32[]{:S(2)}) collective-permute-start(f32[128,256]{1,0:T(8,128)S(1)} %maximum_select_fusion.8), channel_id=1, source_target_pairs={{0,1},{1,0},{2,3},{3,2},{4,5},{5,4},{6,7},{7,6},{8,9},{9,8},{10,11... | collective-permute-start | bytes 393224 | tf_op jit(solution)/shard_map/ppermute | solution.py:124

commit v5 on v3

--- a/solution.py
+++ b/solution.py
@@ -111,7 +111,7 @@
 
 def gather_rows(block, owners):
     me = lax.axis_index("rows")
-    held = block
+    held = block.astype(jnp.bfloat16)
     for m in doubling_masks(owners):
         pairs = [(i, i ^ m) for i in range(owners)]
         got = lax.ppermute(held, "rows", pairs)
@@ -119,7 +119,7 @@
         held = jnp.where(
             upper, jnp.concatenate([got, held], 0), jnp.concatenate([held, got], 0)
         )
-    return held
+    return held.astype(jnp.float32)
 
 
 def arrival_order(owners):

time: 126 us -> 108 us (0.86)
  waiting for transfers between devices: 27.4 us -> 9.88 us
  matrix products: 4.28 us -> 2.16 us
    ppermute x8, waiting for transfers between devices: 25.2 us -> 9.87 us  [gather_rows(): got = lax.ppermute(held, 'rows', pairs)]
    another operation x0 -> x4, other arithmetic: none -> 2.29 us
    ppermute x4, waiting for transfers between devices: 2.26 us -> 0.01 us  [body(): receiveds.append(lax.ppermute(other, 'src', pairs))]
    dot_general x2, matrix products: 4.28 us -> 2.16 us  [body(): lax.dot_general(piece, tile_table[:, start:start + span], (((0,), (1,)),...]
  transfers between devices with their start and end apart: 12 -> 12, of which waited for: 8 -> 5; matrix products, arithmetic and copies ran while one was open for 6% -> 7% of each run, Pallas kernels for 39% -> 50%
where the time goes in v5:
time: 108 us
  Pallas kernels  67.3 us (62%)
  starting transfers between devices  15 us (14%)
  waiting for transfers between devices  9.88 us (9%)
  other arithmetic  9.73 us (9%)
  local copies, waits for them, and re-layouts  3.63 us (3%)
  matrix products  2.16 us (2%)
    pallas_call x2, Pallas kernels, fused_of(): pl.pallas_call(fused_kernel, grid=(steps,), in_specs=[pl.BlockSpec((sourc...  30.8 us
    pallas_call x2, Pallas kernels, partials_of(): pl.pallas_call(matmul_kernel, grid=(steps,), in_specs=[pl.BlockSpec((sour...  26.8 us
    ppermute x8, starting transfers between devices, gather_rows(): got = lax.ppermute(held, 'rows', pairs)  14 us
    ppermute x8, waiting for transfers between devices, gather_rows(): got = lax.ppermute(held, 'rows', pairs)  9.87 us
    pallas_call x2, Pallas kernels, peaks_of(): pl.pallas_call(peak_kernel, grid=(blocks,), in_specs=[pl.BlockSpec((SEG,...  9.64 us
    convert_element_type x1, other arithmetic, body(): slip_t = (units_t * scale_rows).astype(jnp.bfloat16)  2.72 us
    reduce_sum x1, other arithmetic, body(): jnp.sum(jnp.where(matches, mine_weights[:, :, None], 0.0), axis=1)  2.66 us
    another operation x4, other arithmetic  2.29 us
  transfers between devices with their start and end apart: 12, of which 5 were waited for; matrix products, arithmetic and copies ran while one was open for 7% of the time, Pallas kernels for 50%

profile of v5, /device:TPU:0, one launch (start us, length us, event | category | flops | bytes accessed | tf_op | source)
XLA Modules:
  0.0 107.8 jit_solution(12843263346668268414)
XLA Ops:
  0.0 1.0 broadcast_in_dim.23
  1.0 1.6 %reshape.7 = f32[1000,512]{1,0:T(8,128)} reshape(f32[8,125,512]{2,1,0:T(8,128)S(1)} %broadcast_in_dim.23) | data formatting | bytes 4096000 | tf_op jit(solution)/shard_map/reshape | solution.py:135
  2.6 2.7 %fusion = bf16[1000,512]{1,0:T(8,128)(2,1)S(1)} fusion(f32[1000,512]{1,0:T(8,128)} %reshape.7, s32[512,1000]{0,1:T(8,128)} %param.7), kind=kLoop, calls=%fused_computation.2 | loop fusion | flops 1536000 | bytes 5120000 | tf_op jit(solution)/shard_map/convert_element_type | solution.py:136
  5.4 1.1 pad_maximum_fusion.slip_ref
  6.5 13.4 %shard_map.75 = (bf16[7680,256]{1,0:T(8,128)(2,1)}, bf16[7680,256]{1,0:T(8,128)(2,1)}) custom-call(bf16[1000,512]{1,0:T(8,128)(2,1)} %pad_maximum_fusion.slip_ref, bf16[1000,30720]{1,0:T(8,128)(2,1)} %green_ref.7), custom_call_target="tpu_custom_call" | custom-call | flops 7864320000 | bytes 23224320 | tf_op jit(solution)/shard_map/pallas_call | solution.py:27
  20.3 13.4 %shard_map.73 = (bf16[7680,256]{1,0:T(8,128)(2,1)}, bf16[7680,256]{1,0:T(8,128)(2,1)}) custom-call(bf16[1000,512]{1,0:T(8,128)(2,1)} %pad_maximum_fusion.slip_ref, bf16[1000,30720]{1,0:T(8,128)(2,1)} %green_ref.7), custom_call_target="tpu_custom_call" | custom-call | flops 7864320000 | bytes 23224320 | tf_op jit(solution)/shard_map/pallas_call | solution.py:27
  33.8 15.4 %shard_map.76 = (bf16[7680,256]{1,0:T(8,128)(2,1)}, bf16[7680,256]{1,0:T(8,128)(2,1)}, f32[32,256]{1,0:T(8,128)}) custom-call(bf16[1000,512]{1,0:T(8,128)(2,1)} %pad_maximum_fusion.slip_ref, bf16[1000,30720]{1,0:T(8,128)(2,1)} %green_ref.7, bf16[7680,256]{1,0:T(8,128)(2,1)} %get-tuple-element.18.mine_prev_ref, ...), custom_call_target="tpu_custom_call" | custom-call | flops 7864320000 | bytes 31088640 | tf_op jit(solution)/shard_map/pallas_call | solution.py:60
  49.6 15.4 %shard_map.74 = (bf16[7680,256]{1,0:T(8,128)(2,1)}, bf16[7680,256]{1,0:T(8,128)(2,1)}, f32[32,256]{1,0:T(8,128)}) custom-call(bf16[1000,512]{1,0:T(8,128)(2,1)} %pad_maximum_fusion.slip_ref, bf16[1000,30720]{1,0:T(8,128)(2,1)} %green_ref.7, bf16[7680,256]{1,0:T(8,128)(2,1)} %get-tuple-element.15.mine_prev_ref, ...), custom_call_target="tpu_custom_call" | custom-call | flops 7864320000 | bytes 31088640 | tf_op jit(solution)/shard_map/pallas_call | solution.py:60
  66.6 0.8 convert.12
  67.4 4.0 %collective-permute-start.2 = (bf16[64,256]{1,0:T(8,128)(2,1)S(1)}, bf16[64,256]{1,0:T(8,128)(2,1)S(1)}, u32[]{:S(2)}, u32[]{:S(2)}) collective-permute-start(bf16[64,256]{1,0:T(8,128)(2,1)S(1)} %pad_maximum_fusion.1), channel_id=1, source_target_pairs={{0,8},{1,9},{2,10},{3,11},{4,12},{5,13},{6,14},{7,15},{8,0},{9,1},... | collective-permute-start | bytes 98312 | tf_op jit(solution)/shard_map/ppermute | solution.py:117
  71.4 4.8 %shard_map.78 = f32[32,256]{1,0:T(8,128)} custom-call(bf16[7680,256]{1,0:T(8,128)(2,1)} %get-tuple-element.23.mine_ref, bf16[7680,256]{1,0:T(8,128)(2,1)} %collective-permute-done.7.recv_ref), custom_call_target="tpu_custom_call" | custom-call | flops 5898240 | bytes 7864320 | tf_op jit(solution)/shard_map/pallas_call | solution.py:91
  77.0 4.8 %shard_map.77 = f32[32,256]{1,0:T(8,128)} custom-call(bf16[7680,256]{1,0:T(8,128)(2,1)} %get-tuple-element.21.mine_ref, bf16[7680,256]{1,0:T(8,128)(2,1)} %collective-permute-done.6.recv_ref), custom_call_target="tpu_custom_call" | custom-call | flops 5898240 | bytes 7864320 | tf_op jit(solution)/shard_map/pallas_call | solution.py:91
  82.6 2.0 %collective-permute-start.3 = (bf16[128,256]{1,0:T(8,128)(2,1)S(1)}, bf16[128,256]{1,0:T(8,128)(2,1)S(1)}, u32[]{:S(2)}, u32[]{:S(2)}) collective-permute-start(bf16[128,256]{1,0:T(8,128)(2,1)S(1)} %maximum_select_fusion.8), channel_id=1, source_target_pairs={{0,4},{1,5},{2,6},{3,7},{4,0},{5,1},{6,2},{7,3},{8,12},{9,13},{10,... | collective-permute-start | bytes 196616 | tf_op jit(solution)/shard_map/ppermute | solution.py:117
  84.6 3.0 %collective-permute-done.8 = bf16[64,256]{1,0:T(8,128)(2,1)S(1)} collective-permute-done((bf16[64,256]{1,0:T(8,128)(2,1)S(1)}, bf16[64,256]{1,0:T(8,128)(2,1)S(1)}, u32[]{:S(2)}, u32[]{:S(2)}) %collective-permute-start.8) | collective-permute-done | bytes 32800 | tf_op jit(solution)/shard_map/ppermute | solution.py:117
  87.5 1.5 %collective-permute-start.9 = (bf16[128,256]{1,0:T(8,128)(2,1)S(1)}, bf16[128,256]{1,0:T(8,128)(2,1)S(1)}, u32[]{:S(2)}, u32[]{:S(2)}) collective-permute-start(bf16[128,256]{1,0:T(8,128)(2,1)S(1)} %maximum_select_fusion.9), channel_id=1, source_target_pairs={{0,4},{1,5},{2,6},{3,7},{4,0},{5,1},{6,2},{7,3},{8,12},{9,13},{10,... | collective-permute-start | bytes 196616 | tf_op jit(solution)/shard_map/ppermute | solution.py:117
  89.1 1.6 %collective-permute-start.4 = (bf16[256,256]{1,0:T(8,128)(2,1)S(1)}, bf16[256,256]{1,0:T(8,128)(2,1)S(1)}, u32[]{:S(2)}, u32[]{:S(2)}) collective-permute-start(bf16[256,256]{1,0:T(8,128)(2,1)S(1)} %maximum_select_fusion.6), channel_id=1, source_target_pairs={{0,2},{1,3},{2,0},{3,1},{4,6},{5,7},{6,4},{7,5},{8,10},{9,11},{10,... | collective-permute-start | bytes 393224 | tf_op jit(solution)/shard_map/ppermute | solution.py:117
  90.7 1.2 %collective-permute-done.9 = bf16[128,256]{1,0:T(8,128)(2,1)S(1)} collective-permute-done((bf16[128,256]{1,0:T(8,128)(2,1)S(1)}, bf16[128,256]{1,0:T(8,128)(2,1)S(1)}, u32[]{:S(2)}, u32[]{:S(2)}) %collective-permute-start.9) | collective-permute-done | bytes 65568 | tf_op jit(solution)/shard_map/ppermute | solution.py:117
  91.9 1.7 %collective-permute-start.10 = (bf16[256,256]{1,0:T(8,128)(2,1)S(1)}, bf16[256,256]{1,0:T(8,128)(2,1)S(1)}, u32[]{:S(2)}, u32[]{:S(2)}) collective-permute-start(bf16[256,256]{1,0:T(8,128)(2,1)S(1)} %maximum_select_fusion.7), channel_id=1, source_target_pairs={{0,2},{1,3},{2,0},{3,1},{4,6},{5,7},{6,4},{7,5},{8,10},{9,11},{10,... | collective-permute-start | bytes 393224 | tf_op jit(solution)/shard_map/ppermute | solution.py:117
  93.8 0.9 collective-permute-done.4
  94.8 1.6 %collective-permute-start.5 = (bf16[512,256]{1,0:T(8,128)(2,1)S(1)}, bf16[512,256]{1,0:T(8,128)(2,1)S(1)}, u32[]{:S(2)}, u32[]{:S(2)}) collective-permute-start(bf16[512,256]{1,0:T(8,128)(2,1)S(1)} %maximum_select_fusion.4), channel_id=1, source_target_pairs={{0,1},{1,0},{2,3},{3,2},{4,5},{5,4},{6,7},{7,6},{8,9},{9,8},{10,11... | collective-permute-start | bytes 786440 | tf_op jit(solution)/shard_map/ppermute | solution.py:117
  97.1 1.6 %collective-permute-start.11 = (bf16[512,256]{1,0:T(8,128)(2,1)S(1)}, bf16[512,256]{1,0:T(8,128)(2,1)S(1)}, u32[]{:S(2)}, u32[]{:S(2)}) collective-permute-start(bf16[512,256]{1,0:T(8,128)(2,1)S(1)} %maximum_select_fusion.5), channel_id=1, source_target_pairs={{0,1},{1,0},{2,3},{3,2},{4,5},{5,4},{6,7},{7,6},{8,9},{9,8},{10,11... | collective-permute-start | bytes 786440 | tf_op jit(solution)/shard_map/ppermute | solution.py:117
  98.7 2.7 %select_reduce_fusion = f32[128,2048]{1,0:T(8,128)S(1)} fusion(f32[128,8]{1,0:T(8,128)S(1)} %copy.13, s32[2048]{0:T(1024)S(1)} %copy-done.2, s32[128,8]{1,0:T(8,128)S(1)} %copy.12), kind=kLoop, calls=%fused_computation | loop fusion | flops 6029312 | bytes 1064960 | tf_op jit(solution)/shard_map/reduce_sum | solution.py:187
  101.4 4.2 %collective-permute-done.11 = bf16[512,256]{1,0:T(8,128)(2,1)S(1)} collective-permute-done((bf16[512,256]{1,0:T(8,128)(2,1)S(1)}, bf16[512,256]{1,0:T(8,128)(2,1)S(1)}, u32[]{:S(2)}, u32[]{:S(2)}) %collective-permute-start.11) | collective-permute-done | bytes 262176 | tf_op jit(solution)/shard_map/ppermute | solution.py:117
  106.4 1.4 %convolution_add_fusion = f32[256,128]{1,0:T(8,128)} fusion(f32[256,128]{1,0:T(8,128)S(1)} %fusion.1, f32[128,2048]{1,0:T(8,128)S(1)} %select_reduce_fusion, bf16[512,256]{1,0:T(8,128)(2,1)S(1)} %maximum_select_fusion.4, bf16[512,256]{1,0:T(8,128)(2,1)S(1)} %collective-permute-done.5, pred[]{:T(512)S(6)} %ne.16), kind=kOutput, calls=%fused_computation.3 | convolution fusion | flops 405045248 | bytes 1310721 | tf_op jit(solution)/shard_map/dot_general | solution.py:192
  (37 shorter events, 6.0 us)
Async XLA Ops:
  0.0 93.6 %copy-start = (s32[2048,8]{0,1:T(8,128)S(1)}, s32[2048,8]{0,1:T(8,128)}, u32[]{:S(2)}) copy-start(s32[2048,8]{0,1:T(8,128)} %param.10) | copy-start | bytes 196612
  19.8 13.9 %collective-permute-start.1 = (bf16[7680,256]{1,0:T(8,128)(2,1)}, bf16[7680,256]{1,0:T(8,128)(2,1)}, u32[]{:S(2)}, u32[]{:S(2)}) collective-permute-start(bf16[7680,256]{1,0:T(8,128)(2,1)} %get-tuple-element.19), channel_id=1, source_target_pairs={{0,16},{16,0},{1,17},{17,1},{2,18},{18,2},{3,19},{19,3},{4,20},{20... | collective-permute-start | bytes 11796488 | tf_op jit(solution)/shard_map/ppermute | solution.py:164
  33.7 15.9 %collective-permute-start = (bf16[7680,256]{1,0:T(8,128)(2,1)}, bf16[7680,256]{1,0:T(8,128)(2,1)}, u32[]{:S(2)}, u32[]{:S(2)}) collective-permute-start(bf16[7680,256]{1,0:T(8,128)(2,1)} %get-tuple-element.16), channel_id=1, source_target_pairs={{0,16},{16,0},{1,17},{17,1},{2,18},{18,2},{3,19},{19,3},{4,20},{20... | collective-permute-start | bytes 11796488 | tf_op jit(solution)/shard_map/ppermute | solution.py:164
  49.2 22.2 %collective-permute-start.7 = (bf16[7680,256]{1,0:T(8,128)(2,1)}, bf16[7680,256]{1,0:T(8,128)(2,1)}, u32[]{:S(2)}, u32[]{:S(2)}) collective-permute-start(bf16[7680,256]{1,0:T(8,128)(2,1)} %get-tuple-element.24), channel_id=1, source_target_pairs={{0,16},{16,0},{1,17},{17,1},{2,18},{18,2},{3,19},{19,3},{4,20},{20... | collective-permute-start | bytes 11796488 | tf_op jit(solution)/shard_map/ppermute | solution.py:164
  49.6 16.9 %copy-start.1 = (f32[32,256]{1,0:T(8,128)S(1)}, f32[32,256]{1,0:T(8,128)}, u32[]{:S(2)}) copy-start(f32[32,256]{1,0:T(8,128)} %get-tuple-element.20) | copy-start | bytes 98308
  65.1 11.9 %collective-permute-start.6 = (bf16[7680,256]{1,0:T(8,128)(2,1)}, bf16[7680,256]{1,0:T(8,128)(2,1)}, u32[]{:S(2)}, u32[]{:S(2)}) collective-permute-start(bf16[7680,256]{1,0:T(8,128)(2,1)} %get-tuple-element.22), channel_id=1, source_target_pairs={{0,16},{16,0},{1,17},{17,1},{2,18},{18,2},{3,19},{19,3},{4,20},{20... | collective-permute-start | bytes 11796488 | tf_op jit(solution)/shard_map/ppermute | solution.py:164
  67.4 15.2 %collective-permute-start.2 = (bf16[64,256]{1,0:T(8,128)(2,1)S(1)}, bf16[64,256]{1,0:T(8,128)(2,1)S(1)}, u32[]{:S(2)}, u32[]{:S(2)}) collective-permute-start(bf16[64,256]{1,0:T(8,128)(2,1)S(1)} %pad_maximum_fusion.1), channel_id=1, source_target_pairs={{0,8},{1,9},{2,10},{3,11},{4,12},{5,13},{6,14},{7,15},{8,0},{9,1},... | collective-permute-start | bytes 98312 | tf_op jit(solution)/shard_map/ppermute | solution.py:117
  77.0 21.7 %copy-start.2 = (s32[2048]{0:T(1024)S(1)}, s32[2048]{0:T(1024)}, u32[]{:S(2)}) copy-start(s32[2048]{0:T(1024)} %constant.32.clone) | copy-start | bytes 24580
  82.6 5.0 %collective-permute-start.8 = (bf16[64,256]{1,0:T(8,128)(2,1)S(1)}, bf16[64,256]{1,0:T(8,128)(2,1)S(1)}, u32[]{:S(2)}, u32[]{:S(2)}) collective-permute-start(bf16[64,256]{1,0:T(8,128)(2,1)S(1)} %pad_maximum_fusion.2), channel_id=1, source_target_pairs={{0,8},{1,9},{2,10},{3,11},{4,12},{5,13},{6,14},{7,15},{8,0},{9,1},... | collective-permute-start | bytes 98312 | tf_op jit(solution)/shard_map/ppermute | solution.py:117
  82.6 6.4 %collective-permute-start.3 = (bf16[128,256]{1,0:T(8,128)(2,1)S(1)}, bf16[128,256]{1,0:T(8,128)(2,1)S(1)}, u32[]{:S(2)}, u32[]{:S(2)}) collective-permute-start(bf16[128,256]{1,0:T(8,128)(2,1)S(1)} %maximum_select_fusion.8), channel_id=1, source_target_pairs={{0,4},{1,5},{2,6},{3,7},{4,0},{5,1},{6,2},{7,3},{8,12},{9,13},{10,... | collective-permute-start | bytes 196616 | tf_op jit(solution)/shard_map/ppermute | solution.py:117
  87.5 4.3 %collective-permute-start.9 = (bf16[128,256]{1,0:T(8,128)(2,1)S(1)}, bf16[128,256]{1,0:T(8,128)(2,1)S(1)}, u32[]{:S(2)}, u32[]{:S(2)}) collective-permute-start(bf16[128,256]{1,0:T(8,128)(2,1)S(1)} %maximum_select_fusion.9), channel_id=1, source_target_pairs={{0,4},{1,5},{2,6},{3,7},{4,0},{5,1},{6,2},{7,3},{8,12},{9,13},{10,... | collective-permute-start | bytes 196616 | tf_op jit(solution)/shard_map/ppermute | solution.py:117
  89.1 5.6 %collective-permute-start.4 = (bf16[256,256]{1,0:T(8,128)(2,1)S(1)}, bf16[256,256]{1,0:T(8,128)(2,1)S(1)}, u32[]{:S(2)}, u32[]{:S(2)}) collective-permute-start(bf16[256,256]{1,0:T(8,128)(2,1)S(1)} %maximum_select_fusion.6), channel_id=1, source_target_pairs={{0,2},{1,3},{2,0},{3,1},{4,6},{5,7},{6,4},{7,5},{8,10},{9,11},{10,... | collective-permute-start | bytes 393224 | tf_op jit(solution)/shard_map/ppermute | solution.py:117
  91.9 5.0 %collective-permute-start.10 = (bf16[256,256]{1,0:T(8,128)(2,1)S(1)}, bf16[256,256]{1,0:T(8,128)(2,1)S(1)}, u32[]{:S(2)}, u32[]{:S(2)}) collective-permute-start(bf16[256,256]{1,0:T(8,128)(2,1)S(1)} %maximum_select_fusion.7), channel_id=1, source_target_pairs={{0,2},{1,3},{2,0},{3,1},{4,6},{5,7},{6,4},{7,5},{8,10},{9,11},{10,... | collective-permute-start | bytes 393224 | tf_op jit(solution)/shard_map/ppermute | solution.py:117
  94.8 11.6 %collective-permute-start.5 = (bf16[512,256]{1,0:T(8,128)(2,1)S(1)}, bf16[512,256]{1,0:T(8,128)(2,1)S(1)}, u32[]{:S(2)}, u32[]{:S(2)}) collective-permute-start(bf16[512,256]{1,0:T(8,128)(2,1)S(1)} %maximum_select_fusion.4), channel_id=1, source_target_pairs={{0,1},{1,0},{2,3},{3,2},{4,5},{5,4},{6,7},{7,6},{8,9},{9,8},{10,11... | collective-permute-start | bytes 786440 | tf_op jit(solution)/shard_map/ppermute | solution.py:117
  97.1 8.5 %collective-permute-start.11 = (bf16[512,256]{1,0:T(8,128)(2,1)S(1)}, bf16[512,256]{1,0:T(8,128)(2,1)S(1)}, u32[]{:S(2)}, u32[]{:S(2)}) collective-permute-start(bf16[512,256]{1,0:T(8,128)(2,1)S(1)} %maximum_select_fusion.5), channel_id=1, source_target_pairs={{0,1},{1,0},{2,3},{3,2},{4,5},{5,4},{6,7},{7,6},{8,9},{9,8},{10,11... | collective-permute-start | bytes 786440 | tf_op jit(solution)/shard_map/ppermute | solution.py:117

commit v6 on v5

--- a/solution.py
+++ b/solution.py
@@ -11,34 +11,11 @@
 SEG = 1920
 
 
-def matmul_kernel(slip_ref, green_ref, other_ref, mine_ref):
-    half = other_ref.shape[1]
+def half_kernel(slip_ref, green_ref, out_ref):
     product = lax.dot_general(
         green_ref[...], slip_ref[...], (((0,), (0,)), ((), ())), preferred_element_type=jnp.float32
     )
-    other_ref[...] = product[:, :half].astype(jnp.bfloat16)
-    mine_ref[...] = product[:, half:].astype(jnp.bfloat16)
-
-
-def partials_of(slip_ordered, green, chunk, width, tile):
-    sources, scenarios = slip_ordered.shape
-    half = scenarios // 2
-    steps = width // tile
-    return pl.pallas_call(
-        matmul_kernel,
-        grid=(steps,),
-        in_specs=[
-            pl.BlockSpec((sources, scenarios), lambda j: (0, 0)),
-            pl.BlockSpec((sources, tile), lambda j: (0, chunk * steps + j)),
-        ],
-        out_specs=[pl.BlockSpec((tile, half), lambda j: (j, 0))] * 2,
-        out_shape=[jax.ShapeDtypeStruct((width, half), jnp.bfloat16)] * 2,
-        cost_estimate=pl.CostEstimate(
-            flops=2 * scenarios * sources * width,
-            transcendentals=0,
-            bytes_accessed=2 * (sources * width + scenarios * width),
-        ),
-    )(slip_ordered, green)
+    out_ref[...] = product.astype(jnp.bfloat16)
 
 
 def peak_kernel(mine_ref, recv_ref, out_ref):
@@ -47,41 +24,41 @@
     out_ref[...] = jnp.max(jnp.abs(wave).reshape(gauges, NT, wave.shape[1]), axis=1)
 
 
-def fused_kernel(slip_ref, green_ref, mine_prev_ref, recv_prev_ref, other_ref, mine_ref, peaks_ref):
-    matmul_kernel(slip_ref, green_ref, other_ref, mine_ref)
+def fused_kernel(slip_ref, green_ref, mine_prev_ref, recv_prev_ref, out_ref, peaks_ref):
+    half_kernel(slip_ref, green_ref, out_ref)
     peak_kernel(mine_prev_ref, recv_prev_ref, peaks_ref)
 
 
-def fused_of(slip_ordered, green, chunk, width, mine_prev, recv_prev):
-    sources, scenarios = slip_ordered.shape
-    half = scenarios // 2
-    steps = width // SEG
+def half_of(slip_half, green, first, steps, previous=None):
+    sources, half = slip_half.shape
     gauges = SEG // NT
-    return pl.pallas_call(
-        fused_kernel,
+    in_specs = [
+        pl.BlockSpec((sources, half), lambda j: (0, 0)),
+        pl.BlockSpec((sources, SEG), lambda j: (0, first + j)),
+    ]
+    out_specs = [pl.BlockSpec((SEG, half), lambda j: (j, 0))]
+    out_shape = [jax.ShapeDtypeStruct((steps * SEG, half), jnp.bfloat16)]
+    operands = [slip_half, green]
+    kernel = half_kernel
+    moved = 2 * (sources * steps * SEG + half * steps * SEG)
+    if previous is not None:
+        kernel = fused_kernel
+        in_specs += [pl.BlockSpec((SEG, half), lambda j: (j, 0))] * 2
+        out_specs.append(pl.BlockSpec((gauges, half), lambda j: (j, 0)))
+        out_shape.append(jax.ShapeDtypeStruct((steps * gauges, half), jnp.float32))
+        operands += list(previous)
+        moved += 4 * half * steps * SEG
+    result = pl.pallas_call(
+        kernel,
         grid=(steps,),
-        in_specs=[
-            pl.BlockSpec((sources, scenarios), lambda j: (0, 0)),
-            pl.BlockSpec((sources, SEG), lambda j: (0, chunk * steps + j)),
-            pl.BlockSpec((SEG, half), lambda j: (j, 0)),
-            pl.BlockSpec((SEG, half), lambda j: (j, 0)),
-        ],
-        out_specs=[
-            pl.BlockSpec((SEG, half), lambda j: (j, 0)),
-            pl.BlockSpec((SEG, half), lambda j: (j, 0)),
-            pl.BlockSpec((gauges, half), lambda j: (j, 0)),
-        ],
-        out_shape=[
-            jax.ShapeDtypeStruct((width, half), jnp.bfloat16),
-            jax.ShapeDtypeStruct((width, half), jnp.bfloat16),
-            jax.ShapeDtypeStruct((steps * gauges, half), jnp.float32),
-        ],
+        in_specs=in_specs,
+        out_specs=out_specs,
+        out_shape=out_shape,
         cost_estimate=pl.CostEstimate(
-            flops=2 * scenarios * sources * width,
-            transcendentals=0,
-            bytes_accessed=2 * (sources * width + 2 * scenarios * width),
+            flops=2 * half * sources * steps * SEG, transcendentals=0, bytes_accessed=moved
         ),
-    )(slip_ordered, green, mine_prev, recv_prev)
+    )(*operands)
+    return result if previous is not None else (result[0], None)
 
 
 def peaks_of(mine, recv):
@@ -139,7 +116,6 @@
     portion = scenarios // groups
     slip_mine = lax.dynamic_slice_in_dim(slip_t, me * portion, portion, 1)
     slip_other = lax.dynamic_slice_in_dim(slip_t, (1 - me) * portion, portion, 1)
-    slip_ordered = jnp.concatenate([slip_other, slip_mine], 1)
     pairs = [(0, 1), (1, 0)]
 
     owners = lax.axis_size("rows")
@@ -151,17 +127,25 @@
     tile = SEG
     per_chunk = gauges_here // chunks
     order = arrival_order(owners)
-    lag = 2 if chunks > 2 else 0
+    steps = width // SEG
     mines, receiveds, peaks = [], [], [None] * chunks
     for c in range(chunks):
-        if lag and c >= lag:
-            other, mine, peaks[c - lag] = fused_of(
-                slip_ordered, green, c, width, mines[c - lag], receiveds[c - lag]
+        prev_o = c - 2 if c >= 2 and c - 2 >= 0 and peaks[c - 2] is None else None
+        if prev_o is not None:
+            other, peaks[prev_o] = half_of(
+                slip_other, green, c * steps, steps, (mines[prev_o], receiveds[prev_o])
             )
         else:
-            other, mine = partials_of(slip_ordered, green, c, width, tile)
+            other, _ = half_of(slip_other, green, c * steps, steps)
+        receiveds.append(lax.ppermute(other, "src", pairs))
+        prev_m = c - 1 if c >= 2 and peaks[c - 1] is None and c - 1 != prev_o else None
+        if prev_m is not None:
+            mine, peaks[prev_m] = half_of(
+                slip_mine, green, c * steps, steps, (mines[prev_m], receiveds[prev_m])
+            )
+        else:
+            mine, _ = half_of(slip_mine, green, c * steps, steps)
         mines.append(mine)
-        receiveds.append(lax.ppermute(other, "src", pairs))
     for c in range(chunks):
         if peaks[c] is None:
             peaks[c] = peaks_of(mines[c], receiveds[c])

time: 108 us -> 130 us (1.20)
  Pallas kernels: 67.3 us -> 90 us
  other arithmetic: 9.73 us -> 7.9 us
    pallas_call x4 -> x8, Pallas kernels: 57.6 us -> 85.1 us  [half_of(): pl.pallas_call(kernel, grid=(steps,), in_specs=in_specs, out_specs=out_sp...]
    pallas_call x2 -> x1, Pallas kernels: 9.64 us -> 4.84 us  [peaks_of(): pl.pallas_call(peak_kernel, grid=(blocks,), in_specs=[pl.BlockSpec((SEG,...]
  transfers between devices with their start and end apart: 12 -> 12, of which waited for: 5 -> 5; matrix products, arithmetic and copies ran while one was open for 7% -> 5% of each run, Pallas kernels for 50% -> 62%
where the time goes in v6:
time: 130 us
  Pallas kernels  90 us (69%)
  starting transfers between devices  15.1 us (12%)
  waiting for transfers between devices  9.88 us (8%)
  other arithmetic  7.9 us (6%)
  local copies, waits for them, and re-layouts  4.64 us (4%)
  matrix products  2.16 us (2%)
    pallas_call x8, Pallas kernels, half_of(): pl.pallas_call(kernel, grid=(steps,), in_specs=in_specs, out_specs=out_sp...  85.1 us
    ppermute x8, starting transfers between devices, gather_rows(): got = lax.ppermute(held, 'rows', pairs)  14 us
    ppermute x8, waiting for transfers between devices, gather_rows(): got = lax.ppermute(held, 'rows', pairs)  9.87 us
    pallas_call x1, Pallas kernels, peaks_of(): pl.pallas_call(peak_kernel, grid=(blocks,), in_specs=[pl.BlockSpec((SEG,...  4.84 us
    convert_element_type x1, other arithmetic, body(): slip_t = (units_t * scale_rows).astype(jnp.bfloat16)  2.72 us
    reduce_sum x1, other arithmetic, body(): jnp.sum(jnp.where(matches, mine_weights[:, :, None], 0.0), axis=1)  2.66 us
  transfers between devices with their start and end apart: 12, of which 5 were waited for; matrix products, arithmetic and copies ran while one was open for 5% of the time, Pallas kernels for 62%

profile of v6, /device:TPU:0, one launch (start us, length us, event | category | flops | bytes accessed | tf_op | source)
XLA Modules:
  0.0 129.7 jit_solution(14810247758866793007)
XLA Ops:
  1.0 1.6 %reshape.7 = f32[1000,512]{1,0:T(8,128)} reshape(f32[8,125,512]{2,1,0:T(8,128)S(1)} %broadcast_in_dim.23) | data formatting | bytes 4096000 | tf_op jit(solution)/shard_map/reshape | solution.py:112
  2.6 2.7 %fusion = bf16[1000,512]{1,0:T(8,128)(2,1)S(1)} fusion(f32[1000,512]{1,0:T(8,128)} %reshape.7, s32[512,1000]{0,1:T(8,128)} %param.7), kind=kLoop, calls=%fused_computation.2 | loop fusion | flops 1536000 | bytes 5120000 | tf_op jit(solution)/shard_map/convert_element_type | solution.py:113
  5.3 1.1 constant_dynamic-slice_fusion.2
  6.4 9.8 %shard_map.74 = bf16[7680,256]{1,0:T(8,128)(2,1)} custom-call(bf16[1000,256]{1,0:T(8,128)(2,1)} %get-tuple-element.17.slip_ref, bf16[1000,30720]{1,0:T(8,128)(2,1)} %green_ref.15), custom_call_target="tpu_custom_call" | custom-call | flops 3932160000 | bytes 19292160 | tf_op jit(solution)/shard_map/pallas_call | solution.py:51
  16.6 9.8 %shard_map.77 = bf16[7680,256]{1,0:T(8,128)(2,1)} custom-call(bf16[1000,256]{1,0:T(8,128)(2,1)} %get-tuple-element.17.slip_ref, bf16[1000,30720]{1,0:T(8,128)(2,1)} %green_ref.15), custom_call_target="tpu_custom_call" | custom-call | flops 3932160000 | bytes 19292160 | tf_op jit(solution)/shard_map/pallas_call | solution.py:51
  26.5 9.8 %shard_map.73.mine_prev_ref = bf16[7680,256]{1,0:T(8,128)(2,1)} custom-call(bf16[1000,256]{1,0:T(8,128)(2,1)} %get-tuple-element.18.slip_ref, bf16[1000,30720]{1,0:T(8,128)(2,1)} %green_ref.15), custom_call_target="tpu_custom_call" | custom-call | flops 3932160000 | bytes 19292160 | tf_op jit(solution)/shard_map/pallas_call | solution.py:51
  36.3 12.0 %shard_map.75 = (bf16[7680,256]{1,0:T(8,128)(2,1)}, f32[32,256]{1,0:T(8,128)}) custom-call(bf16[1000,256]{1,0:T(8,128)(2,1)} %get-tuple-element.17.slip_ref, bf16[1000,30720]{1,0:T(8,128)(2,1)} %green_ref.15, bf16[7680,256]{1,0:T(8,128)(2,1)} %shard_map.73.mine_prev_ref, bf16[7680,256]{1,0:T(8,128)(2,1)} %collective-permute-done.recv_prev_ref), custom_call_target="tpu_custom_call" | custom-call | flops 3932160000 | bytes 27156480 | tf_op jit(solution)/shard_map/pallas_call | solution.py:51
  48.8 9.8 %shard_map.80 = bf16[7680,256]{1,0:T(8,128)(2,1)} custom-call(bf16[1000,256]{1,0:T(8,128)(2,1)} %get-tuple-element.17.slip_ref, bf16[1000,30720]{1,0:T(8,128)(2,1)} %green_ref.15), custom_call_target="tpu_custom_call" | custom-call | flops 3932160000 | bytes 19292160 | tf_op jit(solution)/shard_map/pallas_call | solution.py:51
  60.1 9.9 %shard_map.76.mine_prev_ref = bf16[7680,256]{1,0:T(8,128)(2,1)} custom-call(bf16[1000,256]{1,0:T(8,128)(2,1)} %get-tuple-element.18.slip_ref, bf16[1000,30720]{1,0:T(8,128)(2,1)} %green_ref.15), custom_call_target="tpu_custom_call" | custom-call | flops 3932160000 | bytes 19292160 | tf_op jit(solution)/shard_map/pallas_call | solution.py:51
  69.9 12.0 %shard_map.78 = (bf16[7680,256]{1,0:T(8,128)(2,1)}, f32[32,256]{1,0:T(8,128)}) custom-call(bf16[1000,256]{1,0:T(8,128)(2,1)} %get-tuple-element.18.slip_ref, bf16[1000,30720]{1,0:T(8,128)(2,1)} %green_ref.15, bf16[7680,256]{1,0:T(8,128)(2,1)} %shard_map.76.mine_prev_ref, bf16[7680,256]{1,0:T(8,128)(2,1)} %collective-permute-done.1.recv_prev_ref), custom_call_target="tpu_custom_call" | custom-call | flops 3932160000 | bytes 27156480 | tf_op jit(solution)/shard_map/pallas_call | solution.py:51
  82.8 4.0 %collective-permute-start.2 = (bf16[64,256]{1,0:T(8,128)(2,1)S(1)}, bf16[64,256]{1,0:T(8,128)(2,1)S(1)}, u32[]{:S(2)}, u32[]{:S(2)}) collective-permute-start(bf16[64,256]{1,0:T(8,128)(2,1)S(1)} %pad_maximum_fusion), channel_id=1, source_target_pairs={{0,8},{1,9},{2,10},{3,11},{4,12},{5,13},{6,14},{7,15},{8,0},{9,1},... | collective-permute-start | bytes 98312 | tf_op jit(solution)/shard_map/ppermute | solution.py:94
  86.8 12.0 %shard_map.79 = (bf16[7680,256]{1,0:T(8,128)(2,1)}, f32[32,256]{1,0:T(8,128)}) custom-call(bf16[1000,256]{1,0:T(8,128)(2,1)} %get-tuple-element.18.slip_ref, bf16[1000,30720]{1,0:T(8,128)(2,1)} %green_ref.15, bf16[7680,256]{1,0:T(8,128)(2,1)} %get-tuple-element.13.mine_prev_ref, bf16[7680,256]{1,0:T(8,128)(2,1)} %collective-permute-done.6.recv_prev_ref), custom_call_target="tpu_custom_call" | custom-call | flops 3932160000 | bytes 27156480 | tf_op jit(solution)/shard_map/pallas_call | solution.py:51
  98.8 4.8 %shard_map.81 = f32[32,256]{1,0:T(8,128)} custom-call(bf16[7680,256]{1,0:T(8,128)(2,1)} %get-tuple-element.16.mine_ref, bf16[7680,256]{1,0:T(8,128)(2,1)} %collective-permute-done.7.recv_ref), custom_call_target="tpu_custom_call" | custom-call | flops 5898240 | bytes 7864320 | tf_op jit(solution)/shard_map/pallas_call | solution.py:68
  104.6 2.0 %collective-permute-start.3 = (bf16[128,256]{1,0:T(8,128)(2,1)S(1)}, bf16[128,256]{1,0:T(8,128)(2,1)S(1)}, u32[]{:S(2)}, u32[]{:S(2)}) collective-permute-start(bf16[128,256]{1,0:T(8,128)(2,1)S(1)} %maximum_select_fusion.8), channel_id=1, source_target_pairs={{0,4},{1,5},{2,6},{3,7},{4,0},{5,1},{6,2},{7,3},{8,12},{9,13},{10,... | collective-permute-start | bytes 196616 | tf_op jit(solution)/shard_map/ppermute | solution.py:94
  106.5 3.0 %collective-permute-done.8 = bf16[64,256]{1,0:T(8,128)(2,1)S(1)} collective-permute-done((bf16[64,256]{1,0:T(8,128)(2,1)S(1)}, bf16[64,256]{1,0:T(8,128)(2,1)S(1)}, u32[]{:S(2)}, u32[]{:S(2)}) %collective-permute-start.8) | collective-permute-done | bytes 32800 | tf_op jit(solution)/shard_map/ppermute | solution.py:94
  109.5 1.5 %collective-permute-start.9 = (bf16[128,256]{1,0:T(8,128)(2,1)S(1)}, bf16[128,256]{1,0:T(8,128)(2,1)S(1)}, u32[]{:S(2)}, u32[]{:S(2)}) collective-permute-start(bf16[128,256]{1,0:T(8,128)(2,1)S(1)} %maximum_select_fusion.9), channel_id=1, source_target_pairs={{0,4},{1,5},{2,6},{3,7},{4,0},{5,1},{6,2},{7,3},{8,12},{9,13},{10,... | collective-permute-start | bytes 196616 | tf_op jit(solution)/shard_map/ppermute | solution.py:94
  111.0 1.6 %collective-permute-start.4 = (bf16[256,256]{1,0:T(8,128)(2,1)S(1)}, bf16[256,256]{1,0:T(8,128)(2,1)S(1)}, u32[]{:S(2)}, u32[]{:S(2)}) collective-permute-start(bf16[256,256]{1,0:T(8,128)(2,1)S(1)} %maximum_select_fusion.6), channel_id=1, source_target_pairs={{0,2},{1,3},{2,0},{3,1},{4,6},{5,7},{6,4},{7,5},{8,10},{9,11},{10,... | collective-permute-start | bytes 393224 | tf_op jit(solution)/shard_map/ppermute | solution.py:94
  112.6 1.2 collective-permute-done.9
  113.9 1.7 %collective-permute-start.10 = (bf16[256,256]{1,0:T(8,128)(2,1)S(1)}, bf16[256,256]{1,0:T(8,128)(2,1)S(1)}, u32[]{:S(2)}, u32[]{:S(2)}) collective-permute-start(bf16[256,256]{1,0:T(8,128)(2,1)S(1)} %maximum_select_fusion.7), channel_id=1, source_target_pairs={{0,2},{1,3},{2,0},{3,1},{4,6},{5,7},{6,4},{7,5},{8,10},{9,11},{10,... | collective-permute-start | bytes 393224 | tf_op jit(solution)/shard_map/ppermute | solution.py:94
  116.7 1.6 %collective-permute-start.5 = (bf16[512,256]{1,0:T(8,128)(2,1)S(1)}, bf16[512,256]{1,0:T(8,128)(2,1)S(1)}, u32[]{:S(2)}, u32[]{:S(2)}) collective-permute-start(bf16[512,256]{1,0:T(8,128)(2,1)S(1)} %maximum_select_fusion.4), channel_id=1, source_target_pairs={{0,1},{1,0},{2,3},{3,2},{4,5},{5,4},{6,7},{7,6},{8,9},{9,8},{10,11... | collective-permute-start | bytes 786440 | tf_op jit(solution)/shard_map/ppermute | solution.py:94
  119.0 1.6 %collective-permute-start.11 = (bf16[512,256]{1,0:T(8,128)(2,1)S(1)}, bf16[512,256]{1,0:T(8,128)(2,1)S(1)}, u32[]{:S(2)}, u32[]{:S(2)}) collective-permute-start(bf16[512,256]{1,0:T(8,128)(2,1)S(1)} %maximum_select_fusion.5), channel_id=1, source_target_pairs={{0,1},{1,0},{2,3},{3,2},{4,5},{5,4},{6,7},{7,6},{8,9},{9,8},{10,11... | collective-permute-start | bytes 786440 | tf_op jit(solution)/shard_map/ppermute | solution.py:94
  120.7 2.7 %select_reduce_fusion = f32[128,2048]{1,0:T(8,128)S(1)} fusion(f32[128,8]{1,0:T(8,128)S(1)} %copy.13, s32[2048]{0:T(1024)S(1)} %copy-done.3, s32[128,8]{1,0:T(8,128)S(1)} %copy.12), kind=kLoop, calls=%fused_computation | loop fusion | flops 6029312 | bytes 1064960 | tf_op jit(solution)/shard_map/reduce_sum | solution.py:171
  123.3 4.2 %collective-permute-done.11 = bf16[512,256]{1,0:T(8,128)(2,1)S(1)} collective-permute-done((bf16[512,256]{1,0:T(8,128)(2,1)S(1)}, bf16[512,256]{1,0:T(8,128)(2,1)S(1)}, u32[]{:S(2)}, u32[]{:S(2)}) %collective-permute-start.11) | collective-permute-done | bytes 262176 | tf_op jit(solution)/shard_map/ppermute | solution.py:94
  128.3 1.4 %convolution_add_fusion = f32[256,128]{1,0:T(8,128)} fusion(f32[256,128]{1,0:T(8,128)S(1)} %fusion.1, f32[128,2048]{1,0:T(8,128)S(1)} %select_reduce_fusion, bf16[512,256]{1,0:T(8,128)(2,1)S(1)} %maximum_select_fusion.4, bf16[512,256]{1,0:T(8,128)(2,1)S(1)} %collective-permute-done.5, pred[]{:T(512)S(6)} %ne.16), kind=kOutput, calls=%fused_computation.3 | convolution fusion | flops 405045248 | bytes 1310721 | tf_op jit(solution)/shard_map/dot_general | solution.py:176
  (41 shorter events, 7.9 us)
Async XLA Ops:
  0.0 115.5 %copy-start = (s32[2048,8]{0,1:T(8,128)S(1)}, s32[2048,8]{0,1:T(8,128)}, u32[]{:S(2)}) copy-start(s32[2048,8]{0,1:T(8,128)} %param.10) | copy-start | bytes 196612
  16.2 20.1 %collective-permute-start = (bf16[7680,256]{1,0:T(8,128)(2,1)}, bf16[7680,256]{1,0:T(8,128)(2,1)}, u32[]{:S(2)}, u32[]{:S(2)}) collective-permute-start(bf16[7680,256]{1,0:T(8,128)(2,1)} %shard_map.74), channel_id=1, source_target_pairs={{0,16},{16,0},{1,17},{17,1},{2,18},{18,2},{3,19},{19,3},{4,20},{20... | collective-permute-start | bytes 11796488 | tf_op jit(solution)/shard_map/ppermute | solution.py:140
  26.4 43.5 %collective-permute-start.1 = (bf16[7680,256]{1,0:T(8,128)(2,1)}, bf16[7680,256]{1,0:T(8,128)(2,1)}, u32[]{:S(2)}, u32[]{:S(2)}) collective-permute-start(bf16[7680,256]{1,0:T(8,128)(2,1)} %shard_map.77), channel_id=1, source_target_pairs={{0,16},{16,0},{1,17},{17,1},{2,18},{18,2},{3,19},{19,3},{4,20},{20... | collective-permute-start | bytes 11796488 | tf_op jit(solution)/shard_map/ppermute | solution.py:140
  48.3 38.5 %collective-permute-start.6 = (bf16[7680,256]{1,0:T(8,128)(2,1)}, bf16[7680,256]{1,0:T(8,128)(2,1)}, u32[]{:S(2)}, u32[]{:S(2)}) collective-permute-start(bf16[7680,256]{1,0:T(8,128)(2,1)} %get-tuple-element.14), channel_id=1, source_target_pairs={{0,16},{16,0},{1,17},{17,1},{2,18},{18,2},{3,19},{19,3},{4,20},{20... | collective-permute-start | bytes 11796488 | tf_op jit(solution)/shard_map/ppermute | solution.py:140
  58.6 40.3 %collective-permute-start.7 = (bf16[7680,256]{1,0:T(8,128)(2,1)}, bf16[7680,256]{1,0:T(8,128)(2,1)}, u32[]{:S(2)}, u32[]{:S(2)}) collective-permute-start(bf16[7680,256]{1,0:T(8,128)(2,1)} %shard_map.80), channel_id=1, source_target_pairs={{0,16},{16,0},{1,17},{17,1},{2,18},{18,2},{3,19},{19,3},{4,20},{20... | collective-permute-start | bytes 11796488 | tf_op jit(solution)/shard_map/ppermute | solution.py:140
  60.1 9.9 %copy-start.1 = (f32[32,256]{1,0:T(8,128)S(1)}, f32[32,256]{1,0:T(8,128)}, u32[]{:S(2)}) copy-start(f32[32,256]{1,0:T(8,128)} %get-tuple-element.11) | copy-start | bytes 98308
  82.8 21.8 %collective-permute-start.2 = (bf16[64,256]{1,0:T(8,128)(2,1)S(1)}, bf16[64,256]{1,0:T(8,128)(2,1)S(1)}, u32[]{:S(2)}, u32[]{:S(2)}) collective-permute-start(bf16[64,256]{1,0:T(8,128)(2,1)S(1)} %pad_maximum_fusion), channel_id=1, source_target_pairs={{0,8},{1,9},{2,10},{3,11},{4,12},{5,13},{6,14},{7,15},{8,0},{9,1},... | collective-permute-start | bytes 98312 | tf_op jit(solution)/shard_map/ppermute | solution.py:94
  98.8 5.6 %copy-start.2 = (f32[32,256]{1,0:T(8,128)S(1)}, f32[32,256]{1,0:T(8,128)}, u32[]{:S(2)}) copy-start(f32[32,256]{1,0:T(8,128)} %get-tuple-element.15) | copy-start | bytes 98308
  98.8 21.8 %copy-start.3 = (s32[2048]{0:T(1024)S(1)}, s32[2048]{0:T(1024)}, u32[]{:S(2)}) copy-start(s32[2048]{0:T(1024)} %constant.32.clone) | copy-start | bytes 24580
  104.5 5.0 %collective-permute-start.8 = (bf16[64,256]{1,0:T(8,128)(2,1)S(1)}, bf16[64,256]{1,0:T(8,128)(2,1)S(1)}, u32[]{:S(2)}, u32[]{:S(2)}) collective-permute-start(bf16[64,256]{1,0:T(8,128)(2,1)S(1)} %pad_maximum_fusion.1), channel_id=1, source_target_pairs={{0,8},{1,9},{2,10},{3,11},{4,12},{5,13},{6,14},{7,15},{8,0},{9,1},... | collective-permute-start | bytes 98312 | tf_op jit(solution)/shard_map/ppermute | solution.py:94
  104.6 6.4 %collective-permute-start.3 = (bf16[128,256]{1,0:T(8,128)(2,1)S(1)}, bf16[128,256]{1,0:T(8,128)(2,1)S(1)}, u32[]{:S(2)}, u32[]{:S(2)}) collective-permute-start(bf16[128,256]{1,0:T(8,128)(2,1)S(1)} %maximum_select_fusion.8), channel_id=1, source_target_pairs={{0,4},{1,5},{2,6},{3,7},{4,0},{5,1},{6,2},{7,3},{8,12},{9,13},{10,... | collective-permute-start | bytes 196616 | tf_op jit(solution)/shard_map/ppermute | solution.py:94
  109.5 4.3 %collective-permute-start.9 = (bf16[128,256]{1,0:T(8,128)(2,1)S(1)}, bf16[128,256]{1,0:T(8,128)(2,1)S(1)}, u32[]{:S(2)}, u32[]{:S(2)}) collective-permute-start(bf16[128,256]{1,0:T(8,128)(2,1)S(1)} %maximum_select_fusion.9), channel_id=1, source_target_pairs={{0,4},{1,5},{2,6},{3,7},{4,0},{5,1},{6,2},{7,3},{8,12},{9,13},{10,... | collective-permute-start | bytes 196616 | tf_op jit(solution)/shard_map/ppermute | solution.py:94
  111.0 5.6 %collective-permute-start.4 = (bf16[256,256]{1,0:T(8,128)(2,1)S(1)}, bf16[256,256]{1,0:T(8,128)(2,1)S(1)}, u32[]{:S(2)}, u32[]{:S(2)}) collective-permute-start(bf16[256,256]{1,0:T(8,128)(2,1)S(1)} %maximum_select_fusion.6), channel_id=1, source_target_pairs={{0,2},{1,3},{2,0},{3,1},{4,6},{5,7},{6,4},{7,5},{8,10},{9,11},{10,... | collective-permute-start | bytes 393224 | tf_op jit(solution)/shard_map/ppermute | solution.py:94
  113.9 5.0 %collective-permute-start.10 = (bf16[256,256]{1,0:T(8,128)(2,1)S(1)}, bf16[256,256]{1,0:T(8,128)(2,1)S(1)}, u32[]{:S(2)}, u32[]{:S(2)}) collective-permute-start(bf16[256,256]{1,0:T(8,128)(2,1)S(1)} %maximum_select_fusion.7), channel_id=1, source_target_pairs={{0,2},{1,3},{2,0},{3,1},{4,6},{5,7},{6,4},{7,5},{8,10},{9,11},{10,... | collective-permute-start | bytes 393224 | tf_op jit(solution)/shard_map/ppermute | solution.py:94
  116.7 11.6 %collective-permute-start.5 = (bf16[512,256]{1,0:T(8,128)(2,1)S(1)}, bf16[512,256]{1,0:T(8,128)(2,1)S(1)}, u32[]{:S(2)}, u32[]{:S(2)}) collective-permute-start(bf16[512,256]{1,0:T(8,128)(2,1)S(1)} %maximum_select_fusion.4), channel_id=1, source_target_pairs={{0,1},{1,0},{2,3},{3,2},{4,5},{5,4},{6,7},{7,6},{8,9},{9,8},{10,11... | collective-permute-start | bytes 786440 | tf_op jit(solution)/shard_map/ppermute | solution.py:94
  119.0 8.5 %collective-permute-start.11 = (bf16[512,256]{1,0:T(8,128)(2,1)S(1)}, bf16[512,256]{1,0:T(8,128)(2,1)S(1)}, u32[]{:S(2)}, u32[]{:S(2)}) collective-permute-start(bf16[512,256]{1,0:T(8,128)(2,1)S(1)} %maximum_select_fusion.5), channel_id=1, source_target_pairs={{0,1},{1,0},{2,3},{3,2},{4,5},{5,4},{6,7},{7,6},{8,9},{9,8},{10,11... | collective-permute-start | bytes 786440 | tf_op jit(solution)/shard_map/ppermute | solution.py:94

commit v7 on v4

--- a/solution.py
+++ b/solution.py
@@ -50,10 +50,14 @@
     out_ref[...] = jnp.max(jnp.abs(wave).reshape(gauges, NT, wave.shape[1]), axis=1)
 
 
-def fused_kernel(slip_ref, green_ref, mine_prev_ref, recv_prev_ref, other_ref, mine_ref, peaks_ref, *, trail):
-    matmul_kernel(slip_ref, green_ref, other_ref, mine_ref)
-
-    @pl.when(pl.program_id(0) < trail)
+def fused_kernel(slip_ref, green_ref, mine_prev_ref, recv_prev_ref, other_ref, mine_ref, peaks_ref, *, steps, trail):
+    j = pl.program_id(0)
+
+    @pl.when(j < steps)
+    def _():
+        matmul_kernel(slip_ref, green_ref, other_ref, mine_ref)
+
+    @pl.when(j < trail)
     def _():
         peak_kernel(mine_prev_ref, recv_prev_ref, peaks_ref)
 
@@ -63,19 +67,20 @@
     half = scenarios // 2
     trail = mine_prev.shape[0] // SEG
     gauges = SEG // NT
+    here = lambda j: (jnp.minimum(j, steps - 1), 0)
     back = lambda j: (jnp.minimum(j, trail - 1), 0)
     return pl.pallas_call(
-        functools.partial(fused_kernel, trail=trail),
-        grid=(steps,),
+        functools.partial(fused_kernel, steps=steps, trail=trail),
+        grid=(max(steps, trail),),
         in_specs=[
             pl.BlockSpec((sources, scenarios), lambda j: (0, 0)),
-            pl.BlockSpec((sources, SEG), lambda j: (0, first + j)),
+            pl.BlockSpec((sources, SEG), lambda j: (0, first + jnp.minimum(j, steps - 1))),
             pl.BlockSpec((SEG, half), back),
             pl.BlockSpec((SEG, half), back),
         ],
         out_specs=[
-            pl.BlockSpec((SEG, half), lambda j: (j, 0)),
-            pl.BlockSpec((SEG, half), lambda j: (j, 0)),
+            pl.BlockSpec((SEG, half), here),
+            pl.BlockSpec((SEG, half), here),
             pl.BlockSpec((gauges, half), back),
         ],
         out_shape=[
@@ -107,6 +112,13 @@
     )(mine, recv)
 
 
+def chunk_plan(segments):
+    if segments >= 8 and segments % 4 == 0:
+        size = segments // 4
+        return [size] * 3 + [size // 2, size - size // 2]
+    return [1] * segments
+
+
 def doubling_masks(owners):
     masks = []
     m = 1
@@ -118,7 +130,7 @@
 
 def gather_rows(block, owners):
     me = lax.axis_index("rows")
-    held = block
+    held = block.astype(jnp.bfloat16)
     for m in doubling_masks(owners):
         pairs = [(i, i ^ m) for i in range(owners)]
         got = lax.ppermute(held, "rows", pairs)
@@ -126,15 +138,7 @@
         held = jnp.where(
             upper, jnp.concatenate([got, held], 0), jnp.concatenate([held, got], 0)
         )
-    return held
-
-
-def chunk_plan(segments):
-    if segments >= 8:
-        rest = segments - 2
-        size, extra = divmod(rest, 4)
-        return [size] * (4 - extra) + [size + 1] * extra + [1, 1]
-    return [1] * segments
+    return held.astype(jnp.float32)
 
 
 def arrival_order(owners):
@@ -168,7 +172,7 @@
     order = arrival_order(owners)
     mines, receiveds, peaks = [], [], [None] * chunks
     for c in range(chunks):
-        if c >= 2 and sizes[c - 2] <= sizes[c]:
+        if c >= 2 and sizes[c] >= 2:
             other, mine, peaks[c - 2] = fused_of(
                 slip_ordered, green, firsts[c], sizes[c], mines[c - 2], receiveds[c - 2]
             )
@@ -179,7 +183,8 @@
     for c in range(chunks):
         if peaks[c] is None:
             peaks[c] = peaks_of(mines[c], receiveds[c])
-    bundles = [list(range(chunks - 2)), [chunks - 2, chunks - 1]] if chunks > 2 else [list(range(chunks))]
+    tail = 2 if chunks > 2 else chunks
+    bundles = [list(range(chunks - tail)), list(range(chunks - tail, chunks))] if chunks > tail else [list(range(chunks))]
     pieces, ids = [], []
     for bundle in bundles:
         joined = jnp.concatenate([peaks[c] for c in bundle], 0) if len(bundle) > 1 else peaks[bundle[0]]

time: 148 us -> 114 us (0.77)
  waiting for transfers between devices: 28.1 us -> 10.5 us
  Pallas kernels: 78.7 us -> 70.9 us
  local copies, waits for them, and re-layouts: 8.76 us -> 4.92 us
  matrix products: 5.81 us -> 2.17 us
    ppermute x8, waiting for transfers between devices: 28.1 us -> 10.5 us  [gather_rows(): got = lax.ppermute(held, 'rows', pairs)]
    pallas_call x4 -> x2, Pallas kernels: 14.3 us -> 5.89 us  [peaks_of(): pl.pallas_call(peak_kernel, grid=(blocks,), in_specs=[pl.BlockSpec((SEG,...]
    pallas_call x2 -> x3, Pallas kernels: 30.5 us -> 38.3 us  [fused_of(): pl.pallas_call(functools.partial(fused_kernel, steps=steps, trail=trail),...]
    pallas_call x4 -> x2, Pallas kernels: 33.8 us -> 26.7 us  [partials_of(): pl.pallas_call(matmul_kernel, grid=(steps,), in_specs=[pl.BlockSpec((sour...]
    unnamed x23 -> x10, local copies, waits for them, and re-layouts: 5.12 us -> 1.3 us
    dot_general x2, matrix products: 5.81 us -> 2.17 us  [body(): lax.dot_general(piece, tile_table[:, start:start + span], (((0,), (1,)),...]
    another operation x0 -> x5, other arithmetic: none -> 2.21 us
  transfers between devices with their start and end apart: 14 -> 13, of which waited for: 5 -> 4; matrix products, arithmetic and copies ran while one was open for 6% -> 6% of each run, Pallas kernels for 46% -> 51%
where the time goes in v7:
time: 114 us; the launch traced here: 113 us
  Pallas kernels  70.9 us (62%)
  starting transfers between devices  15.1 us (13%)
  waiting for transfers between devices  10.5 us (9%)
  other arithmetic  9.61 us (8%)
  local copies, waits for them, and re-layouts  4.92 us (4%)
  matrix products  2.17 us (2%)
    pallas_call x3, Pallas kernels, fused_of(): pl.pallas_call(functools.partial(fused_kernel, steps=steps, trail=trail),...  38.3 us
    pallas_call x2, Pallas kernels, partials_of(): pl.pallas_call(matmul_kernel, grid=(steps,), in_specs=[pl.BlockSpec((sour...  26.7 us
    ppermute x8, starting transfers between devices, gather_rows(): got = lax.ppermute(held, 'rows', pairs)  13.7 us
    ppermute x8, waiting for transfers between devices, gather_rows(): got = lax.ppermute(held, 'rows', pairs)  10.5 us
    pallas_call x2, Pallas kernels, peaks_of(): pl.pallas_call(peak_kernel, grid=(blocks,), in_specs=[pl.BlockSpec((SEG,...  5.89 us
    convert_element_type x1, other arithmetic, body(): slip_t = (units_t * scale_rows).astype(jnp.bfloat16)  2.72 us
    reduce_sum x1, other arithmetic, body(): jnp.sum(jnp.where(matches, mine_weights[:, :, None], 0.0), axis=1)  2.66 us
  transfers between devices with their start and end apart: 13, of which 4 were waited for; matrix products, arithmetic and copies ran while one was open for 6% of the time, Pallas kernels for 51%

profile of v7, /device:TPU:0, one launch (start us, length us, event | category | flops | bytes accessed | tf_op | source)
XLA Modules:
  0.0 113.3 jit_solution(10850960993708110571)
XLA Ops:
  1.0 1.6 %reshape.7 = f32[1000,512]{1,0:T(8,128)} reshape(f32[8,125,512]{2,1,0:T(8,128)S(1)} %broadcast_in_dim.23) | data formatting | bytes 4096000 | tf_op jit(solution)/shard_map/reshape | solution.py:154
  2.6 2.7 %fusion = bf16[1000,512]{1,0:T(8,128)(2,1)S(1)} fusion(f32[1000,512]{1,0:T(8,128)} %reshape.7, s32[512,1000]{0,1:T(8,128)} %param.7), kind=kLoop, calls=%fused_computation.2 | loop fusion | flops 1536000 | bytes 5120000 | tf_op jit(solution)/shard_map/convert_element_type | solution.py:155
  5.4 1.0 pad_maximum_fusion.slip_ref
  6.4 13.4 %shard_map.73 = (bf16[7680,256]{1,0:T(8,128)(2,1)}, bf16[7680,256]{1,0:T(8,128)(2,1)}) custom-call(bf16[1000,512]{1,0:T(8,128)(2,1)} %pad_maximum_fusion.slip_ref, bf16[1000,30720]{1,0:T(8,128)(2,1)} %green_ref.9), custom_call_target="tpu_custom_call" | custom-call | flops 7864320000 | bytes 23224320 | tf_op jit(solution)/shard_map/pallas_call | solution.py:30
  20.3 13.4 %shard_map.75 = (bf16[7680,256]{1,0:T(8,128)(2,1)}, bf16[7680,256]{1,0:T(8,128)(2,1)}) custom-call(bf16[1000,512]{1,0:T(8,128)(2,1)} %pad_maximum_fusion.slip_ref, bf16[1000,30720]{1,0:T(8,128)(2,1)} %green_ref.9), custom_call_target="tpu_custom_call" | custom-call | flops 7864320000 | bytes 23224320 | tf_op jit(solution)/shard_map/pallas_call | solution.py:30
  33.7 15.4 %shard_map.74 = (bf16[7680,256]{1,0:T(8,128)(2,1)}, bf16[7680,256]{1,0:T(8,128)(2,1)}, f32[32,256]{1,0:T(8,128)}) custom-call(bf16[1000,512]{1,0:T(8,128)(2,1)} %pad_maximum_fusion.slip_ref, bf16[1000,30720]{1,0:T(8,128)(2,1)} %green_ref.9, bf16[7680,256]{1,0:T(8,128)(2,1)} %get-tuple-element.18.mine_prev_ref, ...), custom_call_target="tpu_custom_call" | custom-call | flops 7864320000 | bytes 31088640 | tf_op jit(solution)/shard_map/pallas_call | solution.py:72
  49.5 11.4 %shard_map.76 = (bf16[3840,256]{1,0:T(8,128)(2,1)}, bf16[3840,256]{1,0:T(8,128)(2,1)}, f32[32,256]{1,0:T(8,128)}) custom-call(bf16[1000,512]{1,0:T(8,128)(2,1)} %pad_maximum_fusion.slip_ref, bf16[1000,30720]{1,0:T(8,128)(2,1)} %green_ref.9, bf16[7680,256]{1,0:T(8,128)(2,1)} %get-tuple-element.21.mine_prev_ref, ...), custom_call_target="tpu_custom_call" | custom-call | flops 3932160000 | bytes 19476480 | tf_op jit(solution)/shard_map/pallas_call | solution.py:72
  61.0 11.4 %shard_map.77 = (bf16[3840,256]{1,0:T(8,128)(2,1)}, bf16[3840,256]{1,0:T(8,128)(2,1)}, f32[32,256]{1,0:T(8,128)}) custom-call(bf16[1000,512]{1,0:T(8,128)(2,1)} %pad_maximum_fusion.slip_ref, bf16[1000,30720]{1,0:T(8,128)(2,1)} %green_ref.9, bf16[7680,256]{1,0:T(8,128)(2,1)} %get-tuple-element.24.mine_prev_ref, ...), custom_call_target="tpu_custom_call" | custom-call | flops 3932160000 | bytes 19476480 | tf_op jit(solution)/shard_map/pallas_call | solution.py:72
  74.5 3.7 %collective-permute-start.3 = (bf16[96,256]{1,0:T(8,128)(2,1)S(1)}, bf16[96,256]{1,0:T(8,128)(2,1)S(1)}, u32[]{:S(2)}, u32[]{:S(2)}) collective-permute-start(bf16[96,256]{1,0:T(8,128)(2,1)S(1)} %pad_maximum_fusion.1), channel_id=1, source_target_pairs={{0,8},{1,9},{2,10},{3,11},{4,12},{5,13},{6,14},{7,15},{8,0},{9,1},... | collective-permute-start | bytes 147464 | tf_op jit(solution)/shard_map/ppermute | solution.py:136
  78.8 2.9 %shard_map.78 = f32[16,256]{1,0:T(8,128)} custom-call(bf16[3840,256]{1,0:T(8,128)(2,1)} %get-tuple-element.27.mine_ref, bf16[3840,256]{1,0:T(8,128)(2,1)} %collective-permute-done.7.recv_ref), custom_call_target="tpu_custom_call" | custom-call | flops 2949120 | bytes 3932160 | tf_op jit(solution)/shard_map/pallas_call | solution.py:103
  82.5 1.6 %collective-permute-start.4 = (bf16[192,256]{1,0:T(8,128)(2,1)S(1)}, bf16[192,256]{1,0:T(8,128)(2,1)S(1)}, u32[]{:S(2)}, u32[]{:S(2)}) collective-permute-start(bf16[192,256]{1,0:T(8,128)(2,1)S(1)} %maximum_select_fusion.7), channel_id=1, source_target_pairs={{0,4},{1,5},{2,6},{3,7},{4,0},{5,1},{6,2},{7,3},{8,12},{9,13},{10,... | collective-permute-start | bytes 294920 | tf_op jit(solution)/shard_map/ppermute | solution.py:136
  84.2 1.3 %copy-done.1 = bf16[3840,256]{1,0:T(8,128)(2,1)} copy-done((bf16[3840,256]{1,0:T(8,128)(2,1)}, bf16[3840,256]{1,0:T(8,128)(2,1)S(1)}, u32[]{:S(2)}) %copy-start.1) | copy-done | bytes 1966104
  85.5 2.9 %shard_map.79 = f32[16,256]{1,0:T(8,128)} custom-call(bf16[3840,256]{1,0:T(8,128)(2,1)} %get-tuple-element.29.mine_ref, bf16[3840,256]{1,0:T(8,128)(2,1)} %copy-done.1), custom_call_target="tpu_custom_call" | custom-call | flops 2949120 | bytes 3932160 | tf_op jit(solution)/shard_map/pallas_call | solution.py:103
  89.1 1.6 %collective-permute-start.9 = (bf16[32,256]{1,0:T(8,128)(2,1)S(1)}, bf16[32,256]{1,0:T(8,128)(2,1)S(1)}, u32[]{:S(2)}, u32[]{:S(2)}) collective-permute-start(bf16[32,256]{1,0:T(8,128)(2,1)S(1)} %pad_maximum_fusion.2), channel_id=1, source_target_pairs={{0,8},{1,9},{2,10},{3,11},{4,12},{5,13},{6,14},{7,15},{8,0},{9,1},... | collective-permute-start | bytes 49160 | tf_op jit(solution)/shard_map/ppermute | solution.py:136
  90.8 1.6 %collective-permute-start.5 = (bf16[384,256]{1,0:T(8,128)(2,1)S(1)}, bf16[384,256]{1,0:T(8,128)(2,1)S(1)}, u32[]{:S(2)}, u32[]{:S(2)}) collective-permute-start(bf16[384,256]{1,0:T(8,128)(2,1)S(1)} %maximum_select_fusion.5), channel_id=1, source_target_pairs={{0,2},{1,3},{2,0},{3,1},{4,6},{5,7},{6,4},{7,5},{8,10},{9,11},{10,... | collective-permute-start | bytes 589832 | tf_op jit(solution)/shard_map/ppermute | solution.py:136
  92.4 1.4 %collective-permute-done.9 = bf16[32,256]{1,0:T(8,128)(2,1)S(1)} collective-permute-done((bf16[32,256]{1,0:T(8,128)(2,1)S(1)}, bf16[32,256]{1,0:T(8,128)(2,1)S(1)}, u32[]{:S(2)}, u32[]{:S(2)}) %collective-permute-start.9) | collective-permute-done | bytes 16416 | tf_op jit(solution)/shard_map/ppermute | solution.py:136
  94.5 3.3 %collective-permute-done.10 = bf16[64,256]{1,0:T(8,128)(2,1)S(1)} collective-permute-done((bf16[64,256]{1,0:T(8,128)(2,1)S(1)}, bf16[64,256]{1,0:T(8,128)(2,1)S(1)}, u32[]{:S(2)}, u32[]{:S(2)}) %collective-permute-start.10) | collective-permute-done | bytes 32800 | tf_op jit(solution)/shard_map/ppermute | solution.py:136
  97.8 1.6 %collective-permute-start.11 = (bf16[128,256]{1,0:T(8,128)(2,1)S(1)}, bf16[128,256]{1,0:T(8,128)(2,1)S(1)}, u32[]{:S(2)}, u32[]{:S(2)}) collective-permute-start(bf16[128,256]{1,0:T(8,128)(2,1)S(1)} %maximum_select_fusion.8), channel_id=1, source_target_pairs={{0,2},{1,3},{2,0},{3,1},{4,6},{5,7},{6,4},{7,5},{8,10},{9,11},{10,... | collective-permute-start | bytes 196616 | tf_op jit(solution)/shard_map/ppermute | solution.py:136
  99.6 1.6 %collective-permute-start.6 = (bf16[768,256]{1,0:T(8,128)(2,1)S(1)}, bf16[768,256]{1,0:T(8,128)(2,1)S(1)}, u32[]{:S(2)}, u32[]{:S(2)}) collective-permute-start(bf16[768,256]{1,0:T(8,128)(2,1)S(1)} %maximum_select_fusion.2), channel_id=1, source_target_pairs={{0,1},{1,0},{2,3},{3,2},{4,5},{5,4},{6,7},{7,6},{8,9},{9,8},{10,11... | collective-permute-start | bytes 1179656 | tf_op jit(solution)/shard_map/ppermute | solution.py:136
  101.1 1.0 collective-permute-done.11
  102.2 1.6 %collective-permute-start.12 = (bf16[256,256]{1,0:T(8,128)(2,1)S(1)}, bf16[256,256]{1,0:T(8,128)(2,1)S(1)}, u32[]{:S(2)}, u32[]{:S(2)}) collective-permute-start(bf16[256,256]{1,0:T(8,128)(2,1)S(1)} %maximum_select_fusion.6), channel_id=1, source_target_pairs={{0,1},{1,0},{2,3},{3,2},{4,5},{5,4},{6,7},{7,6},{8,9},{9,8},{10,11... | collective-permute-start | bytes 393224 | tf_op jit(solution)/shard_map/ppermute | solution.py:136
  103.8 2.7 %select_reduce_fusion = f32[128,2048]{1,0:T(8,128)S(1)} fusion(f32[128,8]{1,0:T(8,128)S(1)} %copy.13, s32[2048]{0:T(1024)S(1)} %copy-done.4, s32[128,8]{1,0:T(8,128)S(1)} %copy.12), kind=kLoop, calls=%fused_computation | loop fusion | flops 6029312 | bytes 1064960 | tf_op jit(solution)/shard_map/reduce_sum | solution.py:207
  106.4 4.7 %collective-permute-done.12 = bf16[256,256]{1,0:T(8,128)(2,1)S(1)} collective-permute-done((bf16[256,256]{1,0:T(8,128)(2,1)S(1)}, bf16[256,256]{1,0:T(8,128)(2,1)S(1)}, u32[]{:S(2)}, u32[]{:S(2)}) %collective-permute-start.12) | collective-permute-done | bytes 131104 | tf_op jit(solution)/shard_map/ppermute | solution.py:136
  111.6 1.7 %convolution_add_fusion = f32[256,128]{1,0:T(8,128)} fusion(f32[256,128]{1,0:T(8,128)S(1)} %fusion.8, f32[128,2048]{1,0:T(8,128)S(1)} %select_reduce_fusion, bf16[768,256]{1,0:T(8,128)(2,1)S(1)} %maximum_select_fusion.2, bf16[768,256]{1,0:T(8,128)(2,1)S(1)} %collective-permute-done.6, pred[]{:T(512)S(6)} %ne.16), kind=kOutput, calls=%fused_computation.3 | convolution fusion | flops 607551488 | bytes 1835009 | tf_op jit(solution)/shard_map/dot_general | solution.py:212
  (45 shorter events, 7.7 us)
Async XLA Ops:
  0.0 94.3 %copy-start = (s32[2048,8]{0,1:T(8,128)S(1)}, s32[2048,8]{0,1:T(8,128)}, u32[]{:S(2)}) copy-start(s32[2048,8]{0,1:T(8,128)} %param.10) | copy-start | bytes 196612
  19.8 13.9 %collective-permute-start = (bf16[7680,256]{1,0:T(8,128)(2,1)}, bf16[7680,256]{1,0:T(8,128)(2,1)}, u32[]{:S(2)}, u32[]{:S(2)}) collective-permute-start(bf16[7680,256]{1,0:T(8,128)(2,1)} %get-tuple-element.19), channel_id=1, source_target_pairs={{0,16},{16,0},{1,17},{17,1},{2,18},{18,2},{3,19},{19,3},{4,20},{20... | collective-permute-start | bytes 11796488 | tf_op jit(solution)/shard_map/ppermute | solution.py:182
  33.6 15.9 %collective-permute-start.1 = (bf16[7680,256]{1,0:T(8,128)(2,1)}, bf16[7680,256]{1,0:T(8,128)(2,1)}, u32[]{:S(2)}, u32[]{:S(2)}) collective-permute-start(bf16[7680,256]{1,0:T(8,128)(2,1)} %get-tuple-element.22), channel_id=1, source_target_pairs={{0,16},{16,0},{1,17},{17,1},{2,18},{18,2},{3,19},{19,3},{4,20},{20... | collective-permute-start | bytes 11796488 | tf_op jit(solution)/shard_map/ppermute | solution.py:182
  49.1 12.0 %collective-permute-start.2 = (bf16[7680,256]{1,0:T(8,128)(2,1)}, bf16[7680,256]{1,0:T(8,128)(2,1)}, u32[]{:S(2)}, u32[]{:S(2)}) collective-permute-start(bf16[7680,256]{1,0:T(8,128)(2,1)} %get-tuple-element.25), channel_id=1, source_target_pairs={{0,16},{16,0},{1,17},{17,1},{2,18},{18,2},{3,19},{19,3},{4,20},{20... | collective-permute-start | bytes 11796488 | tf_op jit(solution)/shard_map/ppermute | solution.py:182
  61.0 17.9 %collective-permute-start.7 = (bf16[3840,256]{1,0:T(8,128)(2,1)}, bf16[3840,256]{1,0:T(8,128)(2,1)}, u32[]{:S(2)}, u32[]{:S(2)}) collective-permute-start(bf16[3840,256]{1,0:T(8,128)(2,1)} %get-tuple-element.28), channel_id=1, source_target_pairs={{0,16},{16,0},{1,17},{17,1},{2,18},{18,2},{3,19},{19,3},{4,20},{20... | collective-permute-start | bytes 5898248 | tf_op jit(solution)/shard_map/ppermute | solution.py:182
  61.0 12.6 %copy-start.3 = (f32[32,256]{1,0:T(8,128)S(1)}, f32[32,256]{1,0:T(8,128)}, u32[]{:S(2)}) copy-start(f32[32,256]{1,0:T(8,128)} %get-tuple-element.23) | copy-start | bytes 98308
  61.0 12.6 %copy-start.2 = (f32[32,256]{1,0:T(8,128)S(1)}, f32[32,256]{1,0:T(8,128)}, u32[]{:S(2)}) copy-start(f32[32,256]{1,0:T(8,128)} %get-tuple-element.20) | copy-start | bytes 98308
  72.4 11.7 %collective-permute-start.8 = (bf16[3840,256]{1,0:T(8,128)(2,1)}, bf16[3840,256]{1,0:T(8,128)(2,1)S(1)}, u32[]{:S(2)}, u32[]{:S(2)}) collective-permute-start(bf16[3840,256]{1,0:T(8,128)(2,1)} %get-tuple-element.30), channel_id=1, source_target_pairs={{0,16},{16,0},{1,17},{17,1},{2,18},{18,2},{3,19},{19,3},{4,20},{20... | collective-permute-start | bytes 5898248 | tf_op jit(solution)/shard_map/ppermute | solution.py:182
  74.5 8.0 %collective-permute-start.3 = (bf16[96,256]{1,0:T(8,128)(2,1)S(1)}, bf16[96,256]{1,0:T(8,128)(2,1)S(1)}, u32[]{:S(2)}, u32[]{:S(2)}) collective-permute-start(bf16[96,256]{1,0:T(8,128)(2,1)S(1)} %pad_maximum_fusion.1), channel_id=1, source_target_pairs={{0,8},{1,9},{2,10},{3,11},{4,12},{5,13},{6,14},{7,15},{8,0},{9,1},... | collective-permute-start | bytes 147464 | tf_op jit(solution)/shard_map/ppermute | solution.py:136
  82.5 8.2 %collective-permute-start.4 = (bf16[192,256]{1,0:T(8,128)(2,1)S(1)}, bf16[192,256]{1,0:T(8,128)(2,1)S(1)}, u32[]{:S(2)}, u32[]{:S(2)}) collective-permute-start(bf16[192,256]{1,0:T(8,128)(2,1)S(1)} %maximum_select_fusion.7), channel_id=1, source_target_pairs={{0,4},{1,5},{2,6},{3,7},{4,0},{5,1},{6,2},{7,3},{8,12},{9,13},{10,... | collective-permute-start | bytes 294920 | tf_op jit(solution)/shard_map/ppermute | solution.py:136
  84.2 1.3 %copy-start.1 = (bf16[3840,256]{1,0:T(8,128)(2,1)}, bf16[3840,256]{1,0:T(8,128)(2,1)S(1)}, u32[]{:S(2)}) copy-start(bf16[3840,256]{1,0:T(8,128)(2,1)S(1)} %collective-permute-done.8.recv_ref) | copy-start | bytes 5898244
  85.5 18.3 %copy-start.4 = (s32[2048]{0:T(1024)S(1)}, s32[2048]{0:T(1024)}, u32[]{:S(2)}) copy-start(s32[2048]{0:T(1024)} %constant.32.clone) | copy-start | bytes 24580
  89.1 4.7 %collective-permute-start.9 = (bf16[32,256]{1,0:T(8,128)(2,1)S(1)}, bf16[32,256]{1,0:T(8,128)(2,1)S(1)}, u32[]{:S(2)}, u32[]{:S(2)}) collective-permute-start(bf16[32,256]{1,0:T(8,128)(2,1)S(1)} %pad_maximum_fusion.2), channel_id=1, source_target_pairs={{0,8},{1,9},{2,10},{3,11},{4,12},{5,13},{6,14},{7,15},{8,0},{9,1},... | collective-permute-start | bytes 49160 | tf_op jit(solution)/shard_map/ppermute | solution.py:136
  90.8 8.6 %collective-permute-start.5 = (bf16[384,256]{1,0:T(8,128)(2,1)S(1)}, bf16[384,256]{1,0:T(8,128)(2,1)S(1)}, u32[]{:S(2)}, u32[]{:S(2)}) collective-permute-start(bf16[384,256]{1,0:T(8,128)(2,1)S(1)} %maximum_select_fusion.5), channel_id=1, source_target_pairs={{0,2},{1,3},{2,0},{3,1},{4,6},{5,7},{6,4},{7,5},{8,10},{9,11},{10,... | collective-permute-start | bytes 589832 | tf_op jit(solution)/shard_map/ppermute | solution.py:136
  93.8 4.0 %collective-permute-start.10 = (bf16[64,256]{1,0:T(8,128)(2,1)S(1)}, bf16[64,256]{1,0:T(8,128)(2,1)S(1)}, u32[]{:S(2)}, u32[]{:S(2)}) collective-permute-start(bf16[64,256]{1,0:T(8,128)(2,1)S(1)} %maximum_select_fusion.9), channel_id=1, source_target_pairs={{0,4},{1,5},{2,6},{3,7},{4,0},{5,1},{6,2},{7,3},{8,12},{9,13},{10,... | collective-permute-start | bytes 98312 | tf_op jit(solution)/shard_map/ppermute | solution.py:136
  97.8 4.3 %collective-permute-start.11 = (bf16[128,256]{1,0:T(8,128)(2,1)S(1)}, bf16[128,256]{1,0:T(8,128)(2,1)S(1)}, u32[]{:S(2)}, u32[]{:S(2)}) collective-permute-start(bf16[128,256]{1,0:T(8,128)(2,1)S(1)} %maximum_select_fusion.8), channel_id=1, source_target_pairs={{0,2},{1,3},{2,0},{3,1},{4,6},{5,7},{6,4},{7,5},{8,10},{9,11},{10,... | collective-permute-start | bytes 196616 | tf_op jit(solution)/shard_map/ppermute | solution.py:136
  99.6 12.0 %collective-permute-start.6 = (bf16[768,256]{1,0:T(8,128)(2,1)S(1)}, bf16[768,256]{1,0:T(8,128)(2,1)S(1)}, u32[]{:S(2)}, u32[]{:S(2)}) collective-permute-start(bf16[768,256]{1,0:T(8,128)(2,1)S(1)} %maximum_select_fusion.2), channel_id=1, source_target_pairs={{0,1},{1,0},{2,3},{3,2},{4,5},{5,4},{6,7},{7,6},{8,9},{9,8},{10,11... | collective-permute-start | bytes 1179656 | tf_op jit(solution)/shard_map/ppermute | solution.py:136
  102.2 8.9 %collective-permute-start.12 = (bf16[256,256]{1,0:T(8,128)(2,1)S(1)}, bf16[256,256]{1,0:T(8,128)(2,1)S(1)}, u32[]{:S(2)}, u32[]{:S(2)}) collective-permute-start(bf16[256,256]{1,0:T(8,128)(2,1)S(1)} %maximum_select_fusion.6), channel_id=1, source_target_pairs={{0,1},{1,0},{2,3},{3,2},{4,5},{5,4},{6,7},{7,6},{8,9},{9,8},{10,11... | collective-permute-start | bytes 393224 | tf_op jit(solution)/shard_map/ppermute | solution.py:136

commit v8 on v5

--- a/solution.py
+++ b/solution.py
@@ -132,7 +132,9 @@
 def body(slip_units, slip_scales, green, coast_gauges, coast_amps, coast_counts):
     scenarios = slip_units.shape[0]
     units_t = slip_units.T.astype(jnp.float32)
-    scale_rows = jnp.repeat(slip_scales.T, UBLK, axis=0)
+    block_of = jnp.arange(slip_units.shape[1], dtype=jnp.int32) // UBLK
+    picks = (block_of[:, None] == jnp.arange(slip_scales.shape[1], dtype=jnp.int32)[None, :]).astype(jnp.float32)
+    scale_rows = jnp.dot(picks, slip_scales.T, precision=lax.Precision.HIGHEST, preferred_element_type=jnp.float32)
     slip_t = (units_t * scale_rows).astype(jnp.bfloat16)
     me = lax.axis_index("src")
     groups = lax.axis_size("src")

time: 108 us -> 106 us (0.981)
  other arithmetic: 9.73 us -> 7.02 us
  matrix products: 2.16 us -> 4.82 us
  local copies, waits for them, and re-layouts: 3.63 us -> 1.05 us
    convert_element_type x1 -> x0, other arithmetic: 2.72 us -> none  [body(): slip_t = (units_t * scale_rows).astype(jnp.bfloat16)]
    dot_general x0 -> x1, matrix products: none -> 2.66 us  [body(): jnp.dot(picks, slip_scales.T, precision=lax.Precision.HIGHEST, preferred_...]
    reshape x1 -> x0, local copies, waits for them, and re-layouts: 1.58 us -> none  [body(): scale_rows = jnp.repeat(slip_scales.T, UBLK, axis=0)]
  transfers between devices with their start and end apart: 12 -> 12, of which waited for: 5 -> 5; matrix products, arithmetic and copies ran while one was open for 7% -> 7% of each run, Pallas kernels for 50% -> 51%
where the time goes in v8:
time: 106 us; the launch traced here: 105 us
  Pallas kernels  67.3 us (63%)
  starting transfers between devices  15 us (14%)
  waiting for transfers between devices  9.9 us (9%)
  other arithmetic  7.02 us (7%)
  matrix products  4.82 us (5%)
    pallas_call x2, Pallas kernels, fused_of(): pl.pallas_call(fused_kernel, grid=(steps,), in_specs=[pl.BlockSpec((sourc...  30.8 us
    pallas_call x2, Pallas kernels, partials_of(): pl.pallas_call(matmul_kernel, grid=(steps,), in_specs=[pl.BlockSpec((sour...  26.8 us
    ppermute x8, starting transfers between devices, gather_rows(): got = lax.ppermute(held, 'rows', pairs)  14 us
    ppermute x8, waiting for transfers between devices, gather_rows(): got = lax.ppermute(held, 'rows', pairs)  9.89 us
    pallas_call x2, Pallas kernels, peaks_of(): pl.pallas_call(peak_kernel, grid=(blocks,), in_specs=[pl.BlockSpec((SEG,...  9.64 us
    reduce_sum x1, other arithmetic, body(): jnp.sum(jnp.where(matches, mine_weights[:, :, None], 0.0), axis=1)  2.66 us
    dot_general x1, matrix products, body(): jnp.dot(picks, slip_scales.T, precision=lax.Precision.HIGHEST, preferred_...  2.66 us
    another operation x4, other arithmetic  2.29 us
  transfers between devices with their start and end apart: 12, of which 5 were waited for; matrix products, arithmetic and copies ran while one was open for 7% of the time, Pallas kernels for 51%

profile of v8, /device:TPU:0, one launch (start us, length us, event | category | flops | bytes accessed | tf_op | source)
XLA Modules:
  0.0 105.1 jit_solution(8672822195124829154)
XLA Ops:
  0.0 2.7 %fusion = bf16[1000,512]{1,0:T(8,128)(2,1)S(1)} fusion(s32[512,1000]{0,1:T(8,128)} %param.7, f32[512,8]{0,1:T(8,128)} %param.8, s32[1000]{0:T(1024)S(1)} %add_select_fusion), kind=kOutput, calls=%fused_computation.2 | convolution fusion | flops 50696000 | bytes 3092384 | tf_op jit(solution)/shard_map/dot_general | solution.py:137
  2.8 1.1 %pad_maximum_fusion.slip_ref = bf16[1000,512]{1,0:T(8,128)(2,1)} fusion(bf16[1000,256]{1,0:T(8,128)(2,1)S(1)} %get-tuple-element.26, bf16[1000,256]{1,0:T(8,128)(2,1)S(1)} %get-tuple-element.25), kind=kLoop, calls=%fused_computation.4 | loop fusion | flops 2048000 | bytes 2048000 | tf_op jit(solution)/shard_map/concatenate | solution.py:144
  3.8 13.4 %shard_map.75 = (bf16[7680,256]{1,0:T(8,128)(2,1)}, bf16[7680,256]{1,0:T(8,128)(2,1)}) custom-call(bf16[1000,512]{1,0:T(8,128)(2,1)} %pad_maximum_fusion.slip_ref, bf16[1000,30720]{1,0:T(8,128)(2,1)} %green_ref.7), custom_call_target="tpu_custom_call" | custom-call | flops 7864320000 | bytes 23224320 | tf_op jit(solution)/shard_map/pallas_call | solution.py:27
  17.7 13.4 %shard_map.73 = (bf16[7680,256]{1,0:T(8,128)(2,1)}, bf16[7680,256]{1,0:T(8,128)(2,1)}) custom-call(bf16[1000,512]{1,0:T(8,128)(2,1)} %pad_maximum_fusion.slip_ref, bf16[1000,30720]{1,0:T(8,128)(2,1)} %green_ref.7), custom_call_target="tpu_custom_call" | custom-call | flops 7864320000 | bytes 23224320 | tf_op jit(solution)/shard_map/pallas_call | solution.py:27
  31.1 15.4 %shard_map.76 = (bf16[7680,256]{1,0:T(8,128)(2,1)}, bf16[7680,256]{1,0:T(8,128)(2,1)}, f32[32,256]{1,0:T(8,128)}) custom-call(bf16[1000,512]{1,0:T(8,128)(2,1)} %pad_maximum_fusion.slip_ref, bf16[1000,30720]{1,0:T(8,128)(2,1)} %green_ref.7, bf16[7680,256]{1,0:T(8,128)(2,1)} %get-tuple-element.18.mine_prev_ref, ...), custom_call_target="tpu_custom_call" | custom-call | flops 7864320000 | bytes 31088640 | tf_op jit(solution)/shard_map/pallas_call | solution.py:60
  47.0 15.4 %shard_map.74 = (bf16[7680,256]{1,0:T(8,128)(2,1)}, bf16[7680,256]{1,0:T(8,128)(2,1)}, f32[32,256]{1,0:T(8,128)}) custom-call(bf16[1000,512]{1,0:T(8,128)(2,1)} %pad_maximum_fusion.slip_ref, bf16[1000,30720]{1,0:T(8,128)(2,1)} %green_ref.7, bf16[7680,256]{1,0:T(8,128)(2,1)} %get-tuple-element.15.mine_prev_ref, ...), custom_call_target="tpu_custom_call" | custom-call | flops 7864320000 | bytes 31088640 | tf_op jit(solution)/shard_map/pallas_call | solution.py:60
  64.0 0.8 convert.12
  64.7 4.0 %collective-permute-start.2 = (bf16[64,256]{1,0:T(8,128)(2,1)S(1)}, bf16[64,256]{1,0:T(8,128)(2,1)S(1)}, u32[]{:S(2)}, u32[]{:S(2)}) collective-permute-start(bf16[64,256]{1,0:T(8,128)(2,1)S(1)} %pad_maximum_fusion.1), channel_id=1, source_target_pairs={{0,8},{1,9},{2,10},{3,11},{4,12},{5,13},{6,14},{7,15},{8,0},{9,1},... | collective-permute-start | bytes 98312 | tf_op jit(solution)/shard_map/ppermute | solution.py:117
  68.8 4.8 %shard_map.78 = f32[32,256]{1,0:T(8,128)} custom-call(bf16[7680,256]{1,0:T(8,128)(2,1)} %get-tuple-element.23.mine_ref, bf16[7680,256]{1,0:T(8,128)(2,1)} %collective-permute-done.7.recv_ref), custom_call_target="tpu_custom_call" | custom-call | flops 5898240 | bytes 7864320 | tf_op jit(solution)/shard_map/pallas_call | solution.py:91
  73.6 0.8 convert.15
  74.3 4.8 %shard_map.77 = f32[32,256]{1,0:T(8,128)} custom-call(bf16[7680,256]{1,0:T(8,128)(2,1)} %get-tuple-element.21.mine_ref, bf16[7680,256]{1,0:T(8,128)(2,1)} %collective-permute-done.6.recv_ref), custom_call_target="tpu_custom_call" | custom-call | flops 5898240 | bytes 7864320 | tf_op jit(solution)/shard_map/pallas_call | solution.py:91
  79.2 0.8 convert.14
  80.0 2.0 %collective-permute-start.3 = (bf16[128,256]{1,0:T(8,128)(2,1)S(1)}, bf16[128,256]{1,0:T(8,128)(2,1)S(1)}, u32[]{:S(2)}, u32[]{:S(2)}) collective-permute-start(bf16[128,256]{1,0:T(8,128)(2,1)S(1)} %maximum_select_fusion.8), channel_id=1, source_target_pairs={{0,4},{1,5},{2,6},{3,7},{4,0},{5,1},{6,2},{7,3},{8,12},{9,13},{10,... | collective-permute-start | bytes 196616 | tf_op jit(solution)/shard_map/ppermute | solution.py:117
  81.9 3.0 %collective-permute-done.8 = bf16[64,256]{1,0:T(8,128)(2,1)S(1)} collective-permute-done((bf16[64,256]{1,0:T(8,128)(2,1)S(1)}, bf16[64,256]{1,0:T(8,128)(2,1)S(1)}, u32[]{:S(2)}, u32[]{:S(2)}) %collective-permute-start.8) | collective-permute-done | bytes 32800 | tf_op jit(solution)/shard_map/ppermute | solution.py:117
  84.9 1.5 %collective-permute-start.9 = (bf16[128,256]{1,0:T(8,128)(2,1)S(1)}, bf16[128,256]{1,0:T(8,128)(2,1)S(1)}, u32[]{:S(2)}, u32[]{:S(2)}) collective-permute-start(bf16[128,256]{1,0:T(8,128)(2,1)S(1)} %maximum_select_fusion.9), channel_id=1, source_target_pairs={{0,4},{1,5},{2,6},{3,7},{4,0},{5,1},{6,2},{7,3},{8,12},{9,13},{10,... | collective-permute-start | bytes 196616 | tf_op jit(solution)/shard_map/ppermute | solution.py:117
  86.5 1.6 %collective-permute-start.4 = (bf16[256,256]{1,0:T(8,128)(2,1)S(1)}, bf16[256,256]{1,0:T(8,128)(2,1)S(1)}, u32[]{:S(2)}, u32[]{:S(2)}) collective-permute-start(bf16[256,256]{1,0:T(8,128)(2,1)S(1)} %maximum_select_fusion.6), channel_id=1, source_target_pairs={{0,2},{1,3},{2,0},{3,1},{4,6},{5,7},{6,4},{7,5},{8,10},{9,11},{10,... | collective-permute-start | bytes 393224 | tf_op jit(solution)/shard_map/ppermute | solution.py:117
  88.0 1.2 %collective-permute-done.9 = bf16[128,256]{1,0:T(8,128)(2,1)S(1)} collective-permute-done((bf16[128,256]{1,0:T(8,128)(2,1)S(1)}, bf16[128,256]{1,0:T(8,128)(2,1)S(1)}, u32[]{:S(2)}, u32[]{:S(2)}) %collective-permute-start.9) | collective-permute-done | bytes 65568 | tf_op jit(solution)/shard_map/ppermute | solution.py:117
  89.3 1.7 %collective-permute-start.10 = (bf16[256,256]{1,0:T(8,128)(2,1)S(1)}, bf16[256,256]{1,0:T(8,128)(2,1)S(1)}, u32[]{:S(2)}, u32[]{:S(2)}) collective-permute-start(bf16[256,256]{1,0:T(8,128)(2,1)S(1)} %maximum_select_fusion.7), channel_id=1, source_target_pairs={{0,2},{1,3},{2,0},{3,1},{4,6},{5,7},{6,4},{7,5},{8,10},{9,11},{10,... | collective-permute-start | bytes 393224 | tf_op jit(solution)/shard_map/ppermute | solution.py:117
  91.2 0.9 collective-permute-done.4
  92.2 1.6 %collective-permute-start.5 = (bf16[512,256]{1,0:T(8,128)(2,1)S(1)}, bf16[512,256]{1,0:T(8,128)(2,1)S(1)}, u32[]{:S(2)}, u32[]{:S(2)}) collective-permute-start(bf16[512,256]{1,0:T(8,128)(2,1)S(1)} %maximum_select_fusion.4), channel_id=1, source_target_pairs={{0,1},{1,0},{2,3},{3,2},{4,5},{5,4},{6,7},{7,6},{8,9},{9,8},{10,11... | collective-permute-start | bytes 786440 | tf_op jit(solution)/shard_map/ppermute | solution.py:117
  94.4 1.6 %collective-permute-start.11 = (bf16[512,256]{1,0:T(8,128)(2,1)S(1)}, bf16[512,256]{1,0:T(8,128)(2,1)S(1)}, u32[]{:S(2)}, u32[]{:S(2)}) collective-permute-start(bf16[512,256]{1,0:T(8,128)(2,1)S(1)} %maximum_select_fusion.5), channel_id=1, source_target_pairs={{0,1},{1,0},{2,3},{3,2},{4,5},{5,4},{6,7},{7,6},{8,9},{9,8},{10,11... | collective-permute-start | bytes 786440 | tf_op jit(solution)/shard_map/ppermute | solution.py:117
  96.1 2.7 %select_reduce_fusion = f32[128,2048]{1,0:T(8,128)S(1)} fusion(f32[128,8]{1,0:T(8,128)S(1)} %copy.11, s32[2048]{0:T(1024)S(1)} %copy-done.2, s32[128,8]{1,0:T(8,128)S(1)} %copy.10), kind=kLoop, calls=%fused_computation | loop fusion | flops 6029312 | bytes 1064960 | tf_op jit(solution)/shard_map/reduce_sum | solution.py:189
  98.7 4.2 %collective-permute-done.11 = bf16[512,256]{1,0:T(8,128)(2,1)S(1)} collective-permute-done((bf16[512,256]{1,0:T(8,128)(2,1)S(1)}, bf16[512,256]{1,0:T(8,128)(2,1)S(1)}, u32[]{:S(2)}, u32[]{:S(2)}) %collective-permute-start.11) | collective-permute-done | bytes 262176 | tf_op jit(solution)/shard_map/ppermute | solution.py:117
  103.7 1.4 %convolution_add_fusion = f32[256,128]{1,0:T(8,128)} fusion(f32[256,128]{1,0:T(8,128)S(1)} %fusion.1, f32[128,2048]{1,0:T(8,128)S(1)} %select_reduce_fusion, bf16[512,256]{1,0:T(8,128)(2,1)S(1)} %maximum_select_fusion.4, bf16[512,256]{1,0:T(8,128)(2,1)S(1)} %collective-permute-done.5, pred[]{:T(512)S(6)} %ne.40), kind=kOutput, calls=%fused_computation.3 | convolution fusion | flops 405045248 | bytes 1310721 | tf_op jit(solution)/shard_map/dot_general | solution.py:194
  (36 shorter events, 4.5 us)
Async XLA Ops:
  0.0 91.0 %copy-start = (s32[2048,8]{0,1:T(8,128)S(1)}, s32[2048,8]{0,1:T(8,128)}, u32[]{:S(2)}) copy-start(s32[2048,8]{0,1:T(8,128)} %param.10) | copy-start | bytes 196612
  17.2 13.9 %collective-permute-start.1 = (bf16[7680,256]{1,0:T(8,128)(2,1)}, bf16[7680,256]{1,0:T(8,128)(2,1)}, u32[]{:S(2)}, u32[]{:S(2)}) collective-permute-start(bf16[7680,256]{1,0:T(8,128)(2,1)} %get-tuple-element.19), channel_id=1, source_target_pairs={{0,16},{16,0},{1,17},{17,1},{2,18},{18,2},{3,19},{19,3},{4,20},{20... | collective-permute-start | bytes 11796488 | tf_op jit(solution)/shard_map/ppermute | solution.py:166
  31.1 15.9 %collective-permute-start = (bf16[7680,256]{1,0:T(8,128)(2,1)}, bf16[7680,256]{1,0:T(8,128)(2,1)}, u32[]{:S(2)}, u32[]{:S(2)}) collective-permute-start(bf16[7680,256]{1,0:T(8,128)(2,1)} %get-tuple-element.16), channel_id=1, source_target_pairs={{0,16},{16,0},{1,17},{17,1},{2,18},{18,2},{3,19},{19,3},{4,20},{20... | collective-permute-start | bytes 11796488 | tf_op jit(solution)/shard_map/ppermute | solution.py:166
  46.5 22.2 %collective-permute-start.7 = (bf16[7680,256]{1,0:T(8,128)(2,1)}, bf16[7680,256]{1,0:T(8,128)(2,1)}, u32[]{:S(2)}, u32[]{:S(2)}) collective-permute-start(bf16[7680,256]{1,0:T(8,128)(2,1)} %get-tuple-element.24), channel_id=1, source_target_pairs={{0,16},{16,0},{1,17},{17,1},{2,18},{18,2},{3,19},{19,3},{4,20},{20... | collective-permute-start | bytes 11796488 | tf_op jit(solution)/shard_map/ppermute | solution.py:166
  47.0 16.9 %copy-start.1 = (f32[32,256]{1,0:T(8,128)S(1)}, f32[32,256]{1,0:T(8,128)}, u32[]{:S(2)}) copy-start(f32[32,256]{1,0:T(8,128)} %get-tuple-element.20) | copy-start | bytes 98308
  62.4 11.9 %collective-permute-start.6 = (bf16[7680,256]{1,0:T(8,128)(2,1)}, bf16[7680,256]{1,0:T(8,128)(2,1)}, u32[]{:S(2)}, u32[]{:S(2)}) collective-permute-start(bf16[7680,256]{1,0:T(8,128)(2,1)} %get-tuple-element.22), channel_id=1, source_target_pairs={{0,16},{16,0},{1,17},{17,1},{2,18},{18,2},{3,19},{19,3},{4,20},{20... | collective-permute-start | bytes 11796488 | tf_op jit(solution)/shard_map/ppermute | solution.py:166
  64.7 15.2 %collective-permute-start.2 = (bf16[64,256]{1,0:T(8,128)(2,1)S(1)}, bf16[64,256]{1,0:T(8,128)(2,1)S(1)}, u32[]{:S(2)}, u32[]{:S(2)}) collective-permute-start(bf16[64,256]{1,0:T(8,128)(2,1)S(1)} %pad_maximum_fusion.1), channel_id=1, source_target_pairs={{0,8},{1,9},{2,10},{3,11},{4,12},{5,13},{6,14},{7,15},{8,0},{9,1},... | collective-permute-start | bytes 98312 | tf_op jit(solution)/shard_map/ppermute | solution.py:117
  74.3 21.7 %copy-start.2 = (s32[2048]{0:T(1024)S(1)}, s32[2048]{0:T(1024)}, u32[]{:S(2)}) copy-start(s32[2048]{0:T(1024)} %constant.41.clone) | copy-start | bytes 24580
  79.9 5.0 %collective-permute-start.8 = (bf16[64,256]{1,0:T(8,128)(2,1)S(1)}, bf16[64,256]{1,0:T(8,128)(2,1)S(1)}, u32[]{:S(2)}, u32[]{:S(2)}) collective-permute-start(bf16[64,256]{1,0:T(8,128)(2,1)S(1)} %pad_maximum_fusion.2), channel_id=1, source_target_pairs={{0,8},{1,9},{2,10},{3,11},{4,12},{5,13},{6,14},{7,15},{8,0},{9,1},... | collective-permute-start | bytes 98312 | tf_op jit(solution)/shard_map/ppermute | solution.py:117
  80.0 6.4 %collective-permute-start.3 = (bf16[128,256]{1,0:T(8,128)(2,1)S(1)}, bf16[128,256]{1,0:T(8,128)(2,1)S(1)}, u32[]{:S(2)}, u32[]{:S(2)}) collective-permute-start(bf16[128,256]{1,0:T(8,128)(2,1)S(1)} %maximum_select_fusion.8), channel_id=1, source_target_pairs={{0,4},{1,5},{2,6},{3,7},{4,0},{5,1},{6,2},{7,3},{8,12},{9,13},{10,... | collective-permute-start | bytes 196616 | tf_op jit(solution)/shard_map/ppermute | solution.py:117
  84.9 4.3 %collective-permute-start.9 = (bf16[128,256]{1,0:T(8,128)(2,1)S(1)}, bf16[128,256]{1,0:T(8,128)(2,1)S(1)}, u32[]{:S(2)}, u32[]{:S(2)}) collective-permute-start(bf16[128,256]{1,0:T(8,128)(2,1)S(1)} %maximum_select_fusion.9), channel_id=1, source_target_pairs={{0,4},{1,5},{2,6},{3,7},{4,0},{5,1},{6,2},{7,3},{8,12},{9,13},{10,... | collective-permute-start | bytes 196616 | tf_op jit(solution)/shard_map/ppermute | solution.py:117
  86.5 5.6 %collective-permute-start.4 = (bf16[256,256]{1,0:T(8,128)(2,1)S(1)}, bf16[256,256]{1,0:T(8,128)(2,1)S(1)}, u32[]{:S(2)}, u32[]{:S(2)}) collective-permute-start(bf16[256,256]{1,0:T(8,128)(2,1)S(1)} %maximum_select_fusion.6), channel_id=1, source_target_pairs={{0,2},{1,3},{2,0},{3,1},{4,6},{5,7},{6,4},{7,5},{8,10},{9,11},{10,... | collective-permute-start | bytes 393224 | tf_op jit(solution)/shard_map/ppermute | solution.py:117
  89.3 5.0 %collective-permute-start.10 = (bf16[256,256]{1,0:T(8,128)(2,1)S(1)}, bf16[256,256]{1,0:T(8,128)(2,1)S(1)}, u32[]{:S(2)}, u32[]{:S(2)}) collective-permute-start(bf16[256,256]{1,0:T(8,128)(2,1)S(1)} %maximum_select_fusion.7), channel_id=1, source_target_pairs={{0,2},{1,3},{2,0},{3,1},{4,6},{5,7},{6,4},{7,5},{8,10},{9,11},{10,... | collective-permute-start | bytes 393224 | tf_op jit(solution)/shard_map/ppermute | solution.py:117
  92.2 11.6 %collective-permute-start.5 = (bf16[512,256]{1,0:T(8,128)(2,1)S(1)}, bf16[512,256]{1,0:T(8,128)(2,1)S(1)}, u32[]{:S(2)}, u32[]{:S(2)}) collective-permute-start(bf16[512,256]{1,0:T(8,128)(2,1)S(1)} %maximum_select_fusion.4), channel_id=1, source_target_pairs={{0,1},{1,0},{2,3},{3,2},{4,5},{5,4},{6,7},{7,6},{8,9},{9,8},{10,11... | collective-permute-start | bytes 786440 | tf_op jit(solution)/shard_map/ppermute | solution.py:117
  94.4 8.5 %collective-permute-start.11 = (bf16[512,256]{1,0:T(8,128)(2,1)S(1)}, bf16[512,256]{1,0:T(8,128)(2,1)S(1)}, u32[]{:S(2)}, u32[]{:S(2)}) collective-permute-start(bf16[512,256]{1,0:T(8,128)(2,1)S(1)} %maximum_select_fusion.5), channel_id=1, source_target_pairs={{0,1},{1,0},{2,3},{3,2},{4,5},{5,4},{6,7},{7,6},{8,9},{9,8},{10,11... | collective-permute-start | bytes 786440 | tf_op jit(solution)/shard_map/ppermute | solution.py:117

commit v9 on v8

--- a/solution.py
+++ b/solution.py
@@ -109,17 +109,21 @@
     return masks[::-1]
 
 
-def gather_rows(block, owners):
+def gather_rows(block, owners, ties=()):
     me = lax.axis_index("rows")
     held = block.astype(jnp.bfloat16)
-    for m in doubling_masks(owners):
-        pairs = [(i, i ^ m) for i in range(owners)]
+    tied = []
+    for i, m in enumerate(doubling_masks(owners)):
+        if 1 <= i <= len(ties):
+            held, value = lax.optimization_barrier((held, ties[i - 1]))
+            tied.append(value)
+        pairs = [(k, k ^ m) for k in range(owners)]
         got = lax.ppermute(held, "rows", pairs)
         upper = (me & m) != 0
         held = jnp.where(
             upper, jnp.concatenate([got, held], 0), jnp.concatenate([held, got], 0)
         )
-    return held.astype(jnp.float32)
+    return held.astype(jnp.float32), tied + list(ties[len(tied):])
 
 
 def arrival_order(owners):
@@ -164,15 +168,19 @@
             other, mine = partials_of(slip_ordered, green, c, width, tile)
         mines.append(mine)
         receiveds.append(lax.ppermute(other, "src", pairs))
-    for c in range(chunks):
-        if peaks[c] is None:
-            peaks[c] = peaks_of(mines[c], receiveds[c])
+    waiting = [c for c in range(chunks) if peaks[c] is None]
+    for c in waiting:
+        peaks[c] = peaks_of(mines[c], receiveds[c])
     split = (chunks + 1) // 2
     bundles = [list(range(split)), list(range(split, chunks))] if chunks > 1 else [[0]]
     pieces, ids = [], []
-    for bundle in bundles:
+    for b, bundle in enumerate(bundles):
         joined = jnp.concatenate([peaks[c] for c in bundle], 0) if len(bundle) > 1 else peaks[bundle[0]]
-        pieces.append(gather_rows(joined, owners))
+        ties = [peaks[c] for c in waiting if c not in bundle] if b == 0 else []
+        piece, tied = gather_rows(joined, owners, ties)
+        for c, value in zip([c for c in waiting if c not in bundle] if b == 0 else [], tied):
+            peaks[c] = value
+        pieces.append(piece)
         local = np.concatenate([c * per_chunk + np.arange(per_chunk) for c in bundle])
         ids.append((np.asarray(order)[:, None] * gauges_here + local[None, :]).reshape(-1))
     gauge_ids = jnp.asarray(np.concatenate(ids).astype(np.int32))

time: 106 us -> 107 us (level)
  starting transfers between devices: 15 us -> 17.8 us
  waiting for transfers between devices: 9.9 us -> 7.84 us
    ppermute x8, starting transfers between devices: 14 us -> 16.8 us  [gather_rows(): got = lax.ppermute(held, 'rows', pairs)]
    ppermute x8, waiting for transfers between devices: 9.89 us -> 7.83 us  [gather_rows(): got = lax.ppermute(held, 'rows', pairs)]
  transfers between devices with their start and end apart: 12 -> 12, of which waited for: 5 -> 5; matrix products, arithmetic and copies ran while one was open for 7% -> 6% of each run, Pallas kernels for 51% -> 51%
where the time goes in v9:
time: 107 us; the launch traced here: 106 us
  Pallas kernels  67.2 us (63%)
  starting transfers between devices  17.8 us (17%)
  waiting for transfers between devices  7.84 us (7%)
  other arithmetic  7.02 us (7%)
  matrix products  4.81 us (4%)
    pallas_call x2, Pallas kernels, fused_of(): pl.pallas_call(fused_kernel, grid=(steps,), in_specs=[pl.BlockSpec((sourc...  30.8 us
    pallas_call x2, Pallas kernels, partials_of(): pl.pallas_call(matmul_kernel, grid=(steps,), in_specs=[pl.BlockSpec((sour...  26.8 us
    ppermute x8, starting transfers between devices, gather_rows(): got = lax.ppermute(held, 'rows', pairs)  16.8 us
    pallas_call x2, Pallas kernels, peaks_of(): pl.pallas_call(peak_kernel, grid=(blocks,), in_specs=[pl.BlockSpec((SEG,...  9.65 us
    ppermute x8, waiting for transfers between devices, gather_rows(): got = lax.ppermute(held, 'rows', pairs)  7.83 us
    reduce_sum x1, other arithmetic, body(): jnp.sum(jnp.where(matches, mine_weights[:, :, None], 0.0), axis=1)  2.66 us
    dot_general x1, matrix products, body(): jnp.dot(picks, slip_scales.T, precision=lax.Precision.HIGHEST, preferred_...  2.66 us
    another operation x4, other arithmetic  2.29 us
  transfers between devices with their start and end apart: 12, of which 5 were waited for; matrix products, arithmetic and copies ran while one was open for 6% of the time, Pallas kernels for 51%

profile of v9, /device:TPU:0, one launch (start us, length us, event | category | flops | bytes accessed | tf_op | source)
XLA Modules:
  0.0 105.8 jit_solution(16996053338950596766)
XLA Ops:
  0.0 2.7 %fusion = bf16[1000,512]{1,0:T(8,128)(2,1)S(1)} fusion(s32[512,1000]{0,1:T(8,128)} %param.7, f32[512,8]{0,1:T(8,128)} %param.8, s32[1000]{0:T(1024)S(1)} %add_select_fusion), kind=kOutput, calls=%fused_computation.2 | convolution fusion | flops 50696000 | bytes 3092384 | tf_op jit(solution)/shard_map/dot_general | solution.py:141
  2.8 1.1 %pad_maximum_fusion.slip_ref = bf16[1000,512]{1,0:T(8,128)(2,1)} fusion(bf16[1000,256]{1,0:T(8,128)(2,1)S(1)} %get-tuple-element.34, bf16[1000,256]{1,0:T(8,128)(2,1)S(1)} %get-tuple-element.33), kind=kLoop, calls=%fused_computation.4 | loop fusion | flops 2048000 | bytes 2048000 | tf_op jit(solution)/shard_map/concatenate | solution.py:148
  3.8 13.4 %shard_map.73 = (bf16[7680,256]{1,0:T(8,128)(2,1)}, bf16[7680,256]{1,0:T(8,128)(2,1)}) custom-call(bf16[1000,512]{1,0:T(8,128)(2,1)} %pad_maximum_fusion.slip_ref, bf16[1000,30720]{1,0:T(8,128)(2,1)} %green_ref.7), custom_call_target="tpu_custom_call" | custom-call | flops 7864320000 | bytes 23224320 | tf_op jit(solution)/shard_map/pallas_call | solution.py:27
  17.6 13.4 %shard_map.75 = (bf16[7680,256]{1,0:T(8,128)(2,1)}, bf16[7680,256]{1,0:T(8,128)(2,1)}) custom-call(bf16[1000,512]{1,0:T(8,128)(2,1)} %pad_maximum_fusion.slip_ref, bf16[1000,30720]{1,0:T(8,128)(2,1)} %green_ref.7), custom_call_target="tpu_custom_call" | custom-call | flops 7864320000 | bytes 23224320 | tf_op jit(solution)/shard_map/pallas_call | solution.py:27
  31.1 15.4 %shard_map.74 = (bf16[7680,256]{1,0:T(8,128)(2,1)}, bf16[7680,256]{1,0:T(8,128)(2,1)}, f32[32,256]{1,0:T(8,128)}) custom-call(bf16[1000,512]{1,0:T(8,128)(2,1)} %pad_maximum_fusion.slip_ref, bf16[1000,30720]{1,0:T(8,128)(2,1)} %green_ref.7, bf16[7680,256]{1,0:T(8,128)(2,1)} %get-tuple-element.19.mine_prev_ref, ...), custom_call_target="tpu_custom_call" | custom-call | flops 7864320000 | bytes 31088640 | tf_op jit(solution)/shard_map/pallas_call | solution.py:60
  47.0 15.4 %shard_map.76 = (bf16[7680,256]{1,0:T(8,128)(2,1)}, bf16[7680,256]{1,0:T(8,128)(2,1)}, f32[32,256]{1,0:T(8,128)}) custom-call(bf16[1000,512]{1,0:T(8,128)(2,1)} %pad_maximum_fusion.slip_ref, bf16[1000,30720]{1,0:T(8,128)(2,1)} %green_ref.7, bf16[7680,256]{1,0:T(8,128)(2,1)} %get-tuple-element.22.mine_prev_ref, ...), custom_call_target="tpu_custom_call" | custom-call | flops 7864320000 | bytes 31088640 | tf_op jit(solution)/shard_map/pallas_call | solution.py:60
  62.4 0.8 convert.13
  63.2 4.0 %collective-permute-start.2 = (bf16[64,256]{1,0:T(8,128)(2,1)S(1)}, bf16[64,256]{1,0:T(8,128)(2,1)S(1)}, u32[]{:S(2)}, u32[]{:S(2)}) collective-permute-start(bf16[64,256]{1,0:T(8,128)(2,1)S(1)} %pad_maximum_fusion.1), channel_id=1, source_target_pairs={{0,8},{1,9},{2,10},{3,11},{4,12},{5,13},{6,14},{7,15},{8,0},{9,1},... | collective-permute-start | bytes 98312 | tf_op jit(solution)/shard_map/ppermute | solution.py:121
  67.2 1.9 %collective-permute-done.2 = bf16[64,256]{1,0:T(8,128)(2,1)S(1)} collective-permute-done((bf16[64,256]{1,0:T(8,128)(2,1)S(1)}, bf16[64,256]{1,0:T(8,128)(2,1)S(1)}, u32[]{:S(2)}, u32[]{:S(2)}) %collective-permute-start.2) | collective-permute-done | bytes 32800 | tf_op jit(solution)/shard_map/ppermute | solution.py:121
  69.2 4.8 %shard_map.77 = f32[32,256]{1,0:T(8,128)} custom-call(bf16[7680,256]{1,0:T(8,128)(2,1)} %get-tuple-element.25.mine_ref, bf16[7680,256]{1,0:T(8,128)(2,1)} %collective-permute-done.3.recv_ref), custom_call_target="tpu_custom_call" | custom-call | flops 5898240 | bytes 7864320 | tf_op jit(solution)/shard_map/pallas_call | solution.py:91
  74.0 1.9 %collective-permute-start.4 = (bf16[128,256]{1,0:T(8,128)(2,1)S(1)}, bf16[128,256]{1,0:T(8,128)(2,1)S(1)}, u32[]{:S(2)}, u32[]{:S(2)}) collective-permute-start(bf16[128,256]{1,0:T(8,128)(2,1)S(1)} %maximum_select_fusion.8), channel_id=1, source_target_pairs={{0,4},{1,5},{2,6},{3,7},{4,0},{5,1},{6,2},{7,3},{8,12},{9,13},{10,... | collective-permute-start | bytes 196616 | tf_op jit(solution)/shard_map/ppermute | solution.py:121
  76.7 4.8 %shard_map.78 = f32[32,256]{1,0:T(8,128)} custom-call(bf16[7680,256]{1,0:T(8,128)(2,1)} %get-tuple-element.28.mine_ref, bf16[7680,256]{1,0:T(8,128)(2,1)} %collective-permute-done.5.recv_ref), custom_call_target="tpu_custom_call" | custom-call | flops 5898240 | bytes 7864320 | tf_op jit(solution)/shard_map/pallas_call | solution.py:91
  81.5 0.8 convert.15
  82.3 2.8 %collective-permute-start.8 = (bf16[64,256]{1,0:T(8,128)(2,1)S(1)}, bf16[64,256]{1,0:T(8,128)(2,1)S(1)}, u32[]{:S(2)}, u32[]{:S(2)}) collective-permute-start(bf16[64,256]{1,0:T(8,128)(2,1)S(1)} %pad_maximum_fusion.2), channel_id=1, source_target_pairs={{0,8},{1,9},{2,10},{3,11},{4,12},{5,13},{6,14},{7,15},{8,0},{9,1},... | collective-permute-start | bytes 98312 | tf_op jit(solution)/shard_map/ppermute | solution.py:121
  85.9 1.2 %collective-permute-done.8 = bf16[64,256]{1,0:T(8,128)(2,1)S(1)} collective-permute-done((bf16[64,256]{1,0:T(8,128)(2,1)S(1)}, bf16[64,256]{1,0:T(8,128)(2,1)S(1)}, u32[]{:S(2)}, u32[]{:S(2)}) %collective-permute-start.8) | collective-permute-done | bytes 32800 | tf_op jit(solution)/shard_map/ppermute | solution.py:121
  88.0 2.3 %collective-permute-start.6 = (bf16[256,256]{1,0:T(8,128)(2,1)S(1)}, bf16[256,256]{1,0:T(8,128)(2,1)S(1)}, u32[]{:S(2)}, u32[]{:S(2)}) collective-permute-start(bf16[256,256]{1,0:T(8,128)(2,1)S(1)} %maximum_select_fusion.6), channel_id=1, source_target_pairs={{0,2},{1,3},{2,0},{3,1},{4,6},{5,7},{6,4},{7,5},{8,10},{9,11},{10,... | collective-permute-start | bytes 393224 | tf_op jit(solution)/shard_map/ppermute | solution.py:121
  90.3 1.2 %collective-permute-done.9 = bf16[128,256]{1,0:T(8,128)(2,1)S(1)} collective-permute-done((bf16[128,256]{1,0:T(8,128)(2,1)S(1)}, bf16[128,256]{1,0:T(8,128)(2,1)S(1)}, u32[]{:S(2)}, u32[]{:S(2)}) %collective-permute-start.9) | collective-permute-done | bytes 65568 | tf_op jit(solution)/shard_map/ppermute | solution.py:121
  91.5 1.9 %collective-permute-start.10 = (bf16[256,256]{1,0:T(8,128)(2,1)S(1)}, bf16[256,256]{1,0:T(8,128)(2,1)S(1)}, u32[]{:S(2)}, u32[]{:S(2)}) collective-permute-start(bf16[256,256]{1,0:T(8,128)(2,1)S(1)} %maximum_select_fusion.7), channel_id=1, source_target_pairs={{0,2},{1,3},{2,0},{3,1},{4,6},{5,7},{6,4},{7,5},{8,10},{9,11},{10,... | collective-permute-start | bytes 393224 | tf_op jit(solution)/shard_map/ppermute | solution.py:121
  93.8 1.7 %collective-permute-start.7 = (bf16[512,256]{1,0:T(8,128)(2,1)S(1)}, bf16[512,256]{1,0:T(8,128)(2,1)S(1)}, u32[]{:S(2)}, u32[]{:S(2)}) collective-permute-start(bf16[512,256]{1,0:T(8,128)(2,1)S(1)} %maximum_select_fusion.4), channel_id=1, source_target_pairs={{0,1},{1,0},{2,3},{3,2},{4,5},{5,4},{6,7},{7,6},{8,9},{9,8},{10,11... | collective-permute-start | bytes 786440 | tf_op jit(solution)/shard_map/ppermute | solution.py:121
  95.4 1.1 %collective-permute-done.10 = bf16[256,256]{1,0:T(8,128)(2,1)S(1)} collective-permute-done((bf16[256,256]{1,0:T(8,128)(2,1)S(1)}, bf16[256,256]{1,0:T(8,128)(2,1)S(1)}, u32[]{:S(2)}, u32[]{:S(2)}) %collective-permute-start.10) | collective-permute-done | bytes 131104 | tf_op jit(solution)/shard_map/ppermute | solution.py:121
  96.6 1.9 %collective-permute-start.11 = (bf16[512,256]{1,0:T(8,128)(2,1)S(1)}, bf16[512,256]{1,0:T(8,128)(2,1)S(1)}, u32[]{:S(2)}, u32[]{:S(2)}) collective-permute-start(bf16[512,256]{1,0:T(8,128)(2,1)S(1)} %maximum_select_fusion.5), channel_id=1, source_target_pairs={{0,1},{1,0},{2,3},{3,2},{4,5},{5,4},{6,7},{7,6},{8,9},{9,8},{10,11... | collective-permute-start | bytes 786440 | tf_op jit(solution)/shard_map/ppermute | solution.py:121
  98.6 2.7 %select_reduce_fusion = f32[128,2048]{1,0:T(8,128)S(1)} fusion(f32[128,8]{1,0:T(8,128)S(1)} %copy.11, s32[2048]{0:T(1024)S(1)} %copy-done.2, s32[128,8]{1,0:T(8,128)S(1)} %copy.10), kind=kLoop, calls=%fused_computation | loop fusion | flops 6029312 | bytes 1064960 | tf_op jit(solution)/shard_map/reduce_sum | solution.py:197
  101.2 2.4 %collective-permute-done.11 = bf16[512,256]{1,0:T(8,128)(2,1)S(1)} collective-permute-done((bf16[512,256]{1,0:T(8,128)(2,1)S(1)}, bf16[512,256]{1,0:T(8,128)(2,1)S(1)}, u32[]{:S(2)}, u32[]{:S(2)}) %collective-permute-start.11) | collective-permute-done | bytes 262176 | tf_op jit(solution)/shard_map/ppermute | solution.py:121
  104.4 1.4 %convolution_add_fusion = f32[256,128]{1,0:T(8,128)} fusion(f32[256,128]{1,0:T(8,128)S(1)} %fusion.1, f32[128,2048]{1,0:T(8,128)S(1)} %select_reduce_fusion, bf16[512,256]{1,0:T(8,128)(2,1)S(1)} %maximum_select_fusion.4, bf16[512,256]{1,0:T(8,128)(2,1)S(1)} %collective-permute-done.7, pred[]{:T(512)S(6)} %ne.40), kind=kOutput, calls=%fused_computation.3 | convolution fusion | flops 405045248 | bytes 1310721 | tf_op jit(solution)/shard_map/dot_general | solution.py:202
  (36 shorter events, 4.8 us)
Async XLA Ops:
  0.0 93.4 %copy-start = (s32[2048,8]{0,1:T(8,128)S(1)}, s32[2048,8]{0,1:T(8,128)}, u32[]{:S(2)}) copy-start(s32[2048,8]{0,1:T(8,128)} %param.10) | copy-start | bytes 196612
  17.2 13.9 %collective-permute-start = (bf16[7680,256]{1,0:T(8,128)(2,1)}, bf16[7680,256]{1,0:T(8,128)(2,1)}, u32[]{:S(2)}, u32[]{:S(2)}) collective-permute-start(bf16[7680,256]{1,0:T(8,128)(2,1)} %get-tuple-element.20), channel_id=1, source_target_pairs={{0,16},{16,0},{1,17},{17,1},{2,18},{18,2},{3,19},{19,3},{4,20},{20... | collective-permute-start | bytes 11796488 | tf_op jit(solution)/shard_map/ppermute | solution.py:170
  31.1 15.9 %collective-permute-start.1 = (bf16[7680,256]{1,0:T(8,128)(2,1)}, bf16[7680,256]{1,0:T(8,128)(2,1)}, u32[]{:S(2)}, u32[]{:S(2)}) collective-permute-start(bf16[7680,256]{1,0:T(8,128)(2,1)} %get-tuple-element.23), channel_id=1, source_target_pairs={{0,16},{16,0},{1,17},{17,1},{2,18},{18,2},{3,19},{19,3},{4,20},{20... | collective-permute-start | bytes 11796488 | tf_op jit(solution)/shard_map/ppermute | solution.py:170
  46.5 22.7 %collective-permute-start.3 = (bf16[7680,256]{1,0:T(8,128)(2,1)}, bf16[7680,256]{1,0:T(8,128)(2,1)}, u32[]{:S(2)}, u32[]{:S(2)}) collective-permute-start(bf16[7680,256]{1,0:T(8,128)(2,1)} %get-tuple-element.26), channel_id=1, source_target_pairs={{0,16},{16,0},{1,17},{17,1},{2,18},{18,2},{3,19},{19,3},{4,20},{20... | collective-permute-start | bytes 11796488 | tf_op jit(solution)/shard_map/ppermute | solution.py:170
  46.9 15.5 %copy-start.1 = (f32[32,256]{1,0:T(8,128)S(1)}, f32[32,256]{1,0:T(8,128)}, u32[]{:S(2)}) copy-start(f32[32,256]{1,0:T(8,128)} %get-tuple-element.21) | copy-start | bytes 98308
  62.4 14.3 %collective-permute-start.5 = (bf16[7680,256]{1,0:T(8,128)(2,1)}, bf16[7680,256]{1,0:T(8,128)(2,1)}, u32[]{:S(2)}, u32[]{:S(2)}) collective-permute-start(bf16[7680,256]{1,0:T(8,128)(2,1)} %get-tuple-element.29), channel_id=1, source_target_pairs={{0,16},{16,0},{1,17},{17,1},{2,18},{18,2},{3,19},{19,3},{4,20},{20... | collective-permute-start | bytes 11796488 | tf_op jit(solution)/shard_map/ppermute | solution.py:170
  63.2 5.9 %collective-permute-start.2 = (bf16[64,256]{1,0:T(8,128)(2,1)S(1)}, bf16[64,256]{1,0:T(8,128)(2,1)S(1)}, u32[]{:S(2)}, u32[]{:S(2)}) collective-permute-start(bf16[64,256]{1,0:T(8,128)(2,1)S(1)} %pad_maximum_fusion.1), channel_id=1, source_target_pairs={{0,8},{1,9},{2,10},{3,11},{4,12},{5,13},{6,14},{7,15},{8,0},{9,1},... | collective-permute-start | bytes 98312 | tf_op jit(solution)/shard_map/ppermute | solution.py:121
  74.0 7.5 %collective-permute-start.4 = (bf16[128,256]{1,0:T(8,128)(2,1)S(1)}, bf16[128,256]{1,0:T(8,128)(2,1)S(1)}, u32[]{:S(2)}, u32[]{:S(2)}) collective-permute-start(bf16[128,256]{1,0:T(8,128)(2,1)S(1)} %maximum_select_fusion.8), channel_id=1, source_target_pairs={{0,4},{1,5},{2,6},{3,7},{4,0},{5,1},{6,2},{7,3},{8,12},{9,13},{10,... | collective-permute-start | bytes 196616 | tf_op jit(solution)/shard_map/ppermute | solution.py:121
  76.7 21.9 %copy-start.2 = (s32[2048]{0:T(1024)S(1)}, s32[2048]{0:T(1024)}, u32[]{:S(2)}) copy-start(s32[2048]{0:T(1024)} %constant.41.clone) | copy-start | bytes 24580
  82.3 4.8 %collective-permute-start.8 = (bf16[64,256]{1,0:T(8,128)(2,1)S(1)}, bf16[64,256]{1,0:T(8,128)(2,1)S(1)}, u32[]{:S(2)}, u32[]{:S(2)}) collective-permute-start(bf16[64,256]{1,0:T(8,128)(2,1)S(1)} %pad_maximum_fusion.2), channel_id=1, source_target_pairs={{0,8},{1,9},{2,10},{3,11},{4,12},{5,13},{6,14},{7,15},{8,0},{9,1},... | collective-permute-start | bytes 98312 | tf_op jit(solution)/shard_map/ppermute | solution.py:121
  87.1 4.3 %collective-permute-start.9 = (bf16[128,256]{1,0:T(8,128)(2,1)S(1)}, bf16[128,256]{1,0:T(8,128)(2,1)S(1)}, u32[]{:S(2)}, u32[]{:S(2)}) collective-permute-start(bf16[128,256]{1,0:T(8,128)(2,1)S(1)} %maximum_select_fusion.9), channel_id=1, source_target_pairs={{0,4},{1,5},{2,6},{3,7},{4,0},{5,1},{6,2},{7,3},{8,12},{9,13},{10,... | collective-permute-start | bytes 196616 | tf_op jit(solution)/shard_map/ppermute | solution.py:121
  88.0 5.6 %collective-permute-start.6 = (bf16[256,256]{1,0:T(8,128)(2,1)S(1)}, bf16[256,256]{1,0:T(8,128)(2,1)S(1)}, u32[]{:S(2)}, u32[]{:S(2)}) collective-permute-start(bf16[256,256]{1,0:T(8,128)(2,1)S(1)} %maximum_select_fusion.6), channel_id=1, source_target_pairs={{0,2},{1,3},{2,0},{3,1},{4,6},{5,7},{6,4},{7,5},{8,10},{9,11},{10,... | collective-permute-start | bytes 393224 | tf_op jit(solution)/shard_map/ppermute | solution.py:121
  91.5 5.0 %collective-permute-start.10 = (bf16[256,256]{1,0:T(8,128)(2,1)S(1)}, bf16[256,256]{1,0:T(8,128)(2,1)S(1)}, u32[]{:S(2)}, u32[]{:S(2)}) collective-permute-start(bf16[256,256]{1,0:T(8,128)(2,1)S(1)} %maximum_select_fusion.7), channel_id=1, source_target_pairs={{0,2},{1,3},{2,0},{3,1},{4,6},{5,7},{6,4},{7,5},{8,10},{9,11},{10,... | collective-permute-start | bytes 393224 | tf_op jit(solution)/shard_map/ppermute | solution.py:121
  93.8 10.7 %collective-permute-start.7 = (bf16[512,256]{1,0:T(8,128)(2,1)S(1)}, bf16[512,256]{1,0:T(8,128)(2,1)S(1)}, u32[]{:S(2)}, u32[]{:S(2)}) collective-permute-start(bf16[512,256]{1,0:T(8,128)(2,1)S(1)} %maximum_select_fusion.4), channel_id=1, source_target_pairs={{0,1},{1,0},{2,3},{3,2},{4,5},{5,4},{6,7},{7,6},{8,9},{9,8},{10,11... | collective-permute-start | bytes 786440 | tf_op jit(solution)/shard_map/ppermute | solution.py:121
  96.6 7.0 %collective-permute-start.11 = (bf16[512,256]{1,0:T(8,128)(2,1)S(1)}, bf16[512,256]{1,0:T(8,128)(2,1)S(1)}, u32[]{:S(2)}, u32[]{:S(2)}) collective-permute-start(bf16[512,256]{1,0:T(8,128)(2,1)S(1)} %maximum_select_fusion.5), channel_id=1, source_target_pairs={{0,1},{1,0},{2,3},{3,2},{4,5},{5,4},{6,7},{7,6},{8,9},{9,8},{10,11... | collective-permute-start | bytes 786440 | tf_op jit(solution)/shard_map/ppermute | solution.py:121

commit v10 on v8

--- a/solution.py
+++ b/solution.py
@@ -11,34 +11,42 @@
 SEG = 1920
 
 
-def matmul_kernel(slip_ref, green_ref, other_ref, mine_ref):
-    half = other_ref.shape[1]
-    product = lax.dot_general(
-        green_ref[...], slip_ref[...], (((0,), (0,)), ((), ())), preferred_element_type=jnp.float32
-    )
-    other_ref[...] = product[:, :half].astype(jnp.bfloat16)
-    mine_ref[...] = product[:, half:].astype(jnp.bfloat16)
-
-
-def partials_of(slip_ordered, green, chunk, width, tile):
-    sources, scenarios = slip_ordered.shape
+def matmul_kernel(side_ref, other_slip_ref, mine_slip_ref, green_ref, other_ref, mine_ref):
+    block = green_ref[...]
+    for slip_ref, out_ref in ((other_slip_ref, other_ref), (mine_slip_ref, mine_ref)):
+        product = lax.dot_general(
+            block, slip_ref[...], (((0,), (0,)), ((), ())), preferred_element_type=jnp.float32
+        )
+        out_ref[...] = product.astype(jnp.bfloat16)
+
+
+def slip_specs(sources, half):
+    return [
+        pl.BlockSpec((sources, half), lambda j, side: (0, 1 - side[0])),
+        pl.BlockSpec((sources, half), lambda j, side: (0, side[0])),
+    ]
+
+
+def partials_of(side, slip_t, green, chunk, width, tile):
+    sources, scenarios = slip_t.shape
     half = scenarios // 2
     steps = width // tile
     return pl.pallas_call(
         matmul_kernel,
-        grid=(steps,),
-        in_specs=[
-            pl.BlockSpec((sources, scenarios), lambda j: (0, 0)),
-            pl.BlockSpec((sources, tile), lambda j: (0, chunk * steps + j)),
-        ],
-        out_specs=[pl.BlockSpec((tile, half), lambda j: (j, 0))] * 2,
+        grid_spec=pltpu.PrefetchScalarGridSpec(
+            num_scalar_prefetch=1,
+            grid=(steps,),
+            in_specs=slip_specs(sources, half)
+            + [pl.BlockSpec((sources, tile), lambda j, side: (0, chunk * steps + j))],
+            out_specs=[pl.BlockSpec((tile, half), lambda j, side: (j, 0))] * 2,
+        ),
         out_shape=[jax.ShapeDtypeStruct((width, half), jnp.bfloat16)] * 2,
         cost_estimate=pl.CostEstimate(
             flops=2 * scenarios * sources * width,
             transcendentals=0,
             bytes_accessed=2 * (sources * width + scenarios * width),
         ),
-    )(slip_ordered, green)
+    )(side, slip_t, slip_t, green)
 
 
 def peak_kernel(mine_ref, recv_ref, out_ref):
@@ -47,30 +55,33 @@
     out_ref[...] = jnp.max(jnp.abs(wave).reshape(gauges, NT, wave.shape[1]), axis=1)
 
 
-def fused_kernel(slip_ref, green_ref, mine_prev_ref, recv_prev_ref, other_ref, mine_ref, peaks_ref):
-    matmul_kernel(slip_ref, green_ref, other_ref, mine_ref)
+def fused_kernel(side_ref, other_slip_ref, mine_slip_ref, green_ref, mine_prev_ref, recv_prev_ref, other_ref, mine_ref, peaks_ref):
+    matmul_kernel(side_ref, other_slip_ref, mine_slip_ref, green_ref, other_ref, mine_ref)
     peak_kernel(mine_prev_ref, recv_prev_ref, peaks_ref)
 
 
-def fused_of(slip_ordered, green, chunk, width, mine_prev, recv_prev):
-    sources, scenarios = slip_ordered.shape
+def fused_of(side, slip_t, green, chunk, width, mine_prev, recv_prev):
+    sources, scenarios = slip_t.shape
     half = scenarios // 2
     steps = width // SEG
     gauges = SEG // NT
     return pl.pallas_call(
         fused_kernel,
-        grid=(steps,),
-        in_specs=[
-            pl.BlockSpec((sources, scenarios), lambda j: (0, 0)),
-            pl.BlockSpec((sources, SEG), lambda j: (0, chunk * steps + j)),
-            pl.BlockSpec((SEG, half), lambda j: (j, 0)),
-            pl.BlockSpec((SEG, half), lambda j: (j, 0)),
-        ],
-        out_specs=[
-            pl.BlockSpec((SEG, half), lambda j: (j, 0)),
-            pl.BlockSpec((SEG, half), lambda j: (j, 0)),
-            pl.BlockSpec((gauges, half), lambda j: (j, 0)),
-        ],
+        grid_spec=pltpu.PrefetchScalarGridSpec(
+            num_scalar_prefetch=1,
+            grid=(steps,),
+            in_specs=slip_specs(sources, half)
+            + [
+                pl.BlockSpec((sources, SEG), lambda j, side: (0, chunk * steps + j)),
+                pl.BlockSpec((SEG, half), lambda j, side: (j, 0)),
+                pl.BlockSpec((SEG, half), lambda j, side: (j, 0)),
+            ],
+            out_specs=[
+                pl.BlockSpec((SEG, half), lambda j, side: (j, 0)),
+                pl.BlockSpec((SEG, half), lambda j, side: (j, 0)),
+                pl.BlockSpec((gauges, half), lambda j, side: (j, 0)),
+            ],
+        ),
         out_shape=[
             jax.ShapeDtypeStruct((width, half), jnp.bfloat16),
             jax.ShapeDtypeStruct((width, half), jnp.bfloat16),
@@ -81,7 +92,7 @@
             transcendentals=0,
             bytes_accessed=2 * (sources * width + 2 * scenarios * width),
         ),
-    )(slip_ordered, green, mine_prev, recv_prev)
+    )(side, slip_t, slip_t, green, mine_prev, recv_prev)
 
 
 def peaks_of(mine, recv):
@@ -139,9 +150,7 @@
     me = lax.axis_index("src")
     groups = lax.axis_size("src")
     portion = scenarios // groups
-    slip_mine = lax.dynamic_slice_in_dim(slip_t, me * portion, portion, 1)
-    slip_other = lax.dynamic_slice_in_dim(slip_t, (1 - me) * portion, portion, 1)
-    slip_ordered = jnp.concatenate([slip_other, slip_mine], 1)
+    side = jnp.reshape(me, (1,)).astype(jnp.int32)
     pairs = [(0, 1), (1, 0)]
 
     owners = lax.axis_size("rows")
@@ -158,10 +167,10 @@
     for c in range(chunks):
         if lag and c >= lag:
             other, mine, peaks[c - lag] = fused_of(
-                slip_ordered, green, c, width, mines[c - lag], receiveds[c - lag]
+                side, slip_t, green, c, width, mines[c - lag], receiveds[c - lag]
             )
         else:
-            other, mine = partials_of(slip_ordered, green, c, width, tile)
+            other, mine = partials_of(side, slip_t, green, c, width, tile)
         mines.append(mine)
         receiveds.append(lax.ppermute(other, "src", pairs))
     for c in range(chunks):

time: 106 us -> 106 us (level)
  other arithmetic: 7.02 us -> 5.95 us
    concatenate x1 -> x0, other arithmetic: 1.07 us -> none  [body(): slip_ordered = jnp.concatenate([slip_other, slip_mine], 1)]
where the time goes in v10:
time: 106 us; the launch traced here: 105 us
  Pallas kernels  67.3 us (63%)
  starting transfers between devices  15 us (14%)
  waiting for transfers between devices  9.91 us (9%)
  other arithmetic  5.95 us (6%)
  matrix products  5.8 us (5%)
    pallas_call x2, Pallas kernels, fused_of(): pl.pallas_call(fused_kernel, grid_spec=pltpu.PrefetchScalarGridSpec(num_s...  30.8 us
    pallas_call x2, Pallas kernels, partials_of(): pl.pallas_call(matmul_kernel, grid_spec=pltpu.PrefetchScalarGridSpec(num_...  26.8 us
    ppermute x8, starting transfers between devices, gather_rows(): got = lax.ppermute(held, 'rows', pairs)  14 us
    ppermute x8, waiting for transfers between devices, gather_rows(): got = lax.ppermute(held, 'rows', pairs)  9.9 us
    pallas_call x2, Pallas kernels, peaks_of(): pl.pallas_call(peak_kernel, grid=(blocks,), in_specs=[pl.BlockSpec((SEG,...  9.64 us
    dot_general x1, matrix products, body(): jnp.dot(picks, slip_scales.T, precision=lax.Precision.HIGHEST, preferred_...  3.64 us
    reduce_sum x1, other arithmetic, body(): jnp.sum(jnp.where(matches, mine_weights[:, :, None], 0.0), axis=1)  2.66 us
    another operation x4, other arithmetic  2.29 us
  transfers between devices with their start and end apart: 12, of which 5 were waited for; matrix products, arithmetic and copies ran while one was open for 7% of the time, Pallas kernels for 51%

profile of v10, /device:TPU:0, one launch (start us, length us, event | category | flops | bytes accessed | tf_op | source)
XLA Modules:
  0.0 105.0 jit_solution(5150911249565409931)
XLA Ops:
  0.0 3.6 %fusion.other_slip_ref.mine_slip_ref = bf16[1000,512]{1,0:T(8,128)(2,1)} fusion(s32[512,1000]{0,1:T(8,128)} %param.7, f32[512,8]{0,1:T(8,128)} %param.8, s32[1000]{0:T(1024)S(1)} %add_select_fusion), kind=kOutput, calls=%fused_computation.2 | convolution fusion | flops 50696000 | bytes 3092384 | tf_op jit(solution)/shard_map/dot_general | solution.py:148
  3.7 13.4 %shard_map.75 = (bf16[7680,256]{1,0:T(8,128)(2,1)}, bf16[7680,256]{1,0:T(8,128)(2,1)}) custom-call(s32[1]{0:T(128)} %bitcast.side_ref, bf16[1000,512]{1,0:T(8,128)(2,1)} %fusion.other_slip_ref.mine_slip_ref, bf16[1000,512]{1,0:T(8,128)(2,1)} %fusion.other_slip_ref.mine_slip_ref, bf16[1000,30720]{1,0:T(8,128)(2,1)} %green_ref.7), custom_call_target="tpu_custom_call" | custom-call | flops 7864320000 | bytes 23224320 | tf_op jit(solution)/shard_map/pallas_call | solution.py:34
  17.5 13.4 %shard_map.73 = (bf16[7680,256]{1,0:T(8,128)(2,1)}, bf16[7680,256]{1,0:T(8,128)(2,1)}) custom-call(s32[1]{0:T(128)} %bitcast.side_ref, bf16[1000,512]{1,0:T(8,128)(2,1)} %fusion.other_slip_ref.mine_slip_ref, bf16[1000,512]{1,0:T(8,128)(2,1)} %fusion.other_slip_ref.mine_slip_ref, bf16[1000,30720]{1,0:T(8,128)(2,1)} %green_ref.7), custom_call_target="tpu_custom_call" | custom-call | flops 7864320000 | bytes 23224320 | tf_op jit(solution)/shard_map/pallas_call | solution.py:34
  31.0 15.4 %shard_map.76 = (bf16[7680,256]{1,0:T(8,128)(2,1)}, bf16[7680,256]{1,0:T(8,128)(2,1)}, f32[32,256]{1,0:T(8,128)}) custom-call(s32[1]{0:T(128)} %bitcast.side_ref, bf16[1000,512]{1,0:T(8,128)(2,1)} %fusion.other_slip_ref.mine_slip_ref, bf16[1000,512]{1,0:T(8,128)(2,1)} %fusion.other_slip_ref.mine_slip_ref, bf16[1000,30720]{1,0:T(8,128)(2,1)} %green_ref.7, ...), custom_call_target="tpu_custom_call" | custom-call | flops 7864320000 | bytes 31088640 | tf_op jit(solution)/shard_map/pallas_call | solution.py:68
  46.9 15.4 %shard_map.74 = (bf16[7680,256]{1,0:T(8,128)(2,1)}, bf16[7680,256]{1,0:T(8,128)(2,1)}, f32[32,256]{1,0:T(8,128)}) custom-call(s32[1]{0:T(128)} %bitcast.side_ref, bf16[1000,512]{1,0:T(8,128)(2,1)} %fusion.other_slip_ref.mine_slip_ref, bf16[1000,512]{1,0:T(8,128)(2,1)} %fusion.other_slip_ref.mine_slip_ref, bf16[1000,30720]{1,0:T(8,128)(2,1)} %green_ref.7, ...), custom_call_target="tpu_custom_call" | custom-call | flops 7864320000 | bytes 31088640 | tf_op jit(solution)/shard_map/pallas_call | solution.py:68
  62.3 0.8 dynamic-slice
  63.8 0.8 convert.12
  64.6 4.0 %collective-permute-start.2 = (bf16[64,256]{1,0:T(8,128)(2,1)S(1)}, bf16[64,256]{1,0:T(8,128)(2,1)S(1)}, u32[]{:S(2)}, u32[]{:S(2)}) collective-permute-start(bf16[64,256]{1,0:T(8,128)(2,1)S(1)} %pad_maximum_fusion), channel_id=1, source_target_pairs={{0,8},{1,9},{2,10},{3,11},{4,12},{5,13},{6,14},{7,15},{8,0},{9,1},... | collective-permute-start | bytes 98312 | tf_op jit(solution)/shard_map/ppermute | solution.py:128
  68.6 4.8 %shard_map.78 = f32[32,256]{1,0:T(8,128)} custom-call(bf16[7680,256]{1,0:T(8,128)(2,1)} %get-tuple-element.23.mine_ref, bf16[7680,256]{1,0:T(8,128)(2,1)} %collective-permute-done.7.recv_ref), custom_call_target="tpu_custom_call" | custom-call | flops 5898240 | bytes 7864320 | tf_op jit(solution)/shard_map/pallas_call | solution.py:102
  73.4 0.8 convert.15
  74.2 4.8 %shard_map.77 = f32[32,256]{1,0:T(8,128)} custom-call(bf16[7680,256]{1,0:T(8,128)(2,1)} %get-tuple-element.21.mine_ref, bf16[7680,256]{1,0:T(8,128)(2,1)} %collective-permute-done.6.recv_ref), custom_call_target="tpu_custom_call" | custom-call | flops 5898240 | bytes 7864320 | tf_op jit(solution)/shard_map/pallas_call | solution.py:102
  79.0 0.8 convert.14
  79.8 2.0 %collective-permute-start.3 = (bf16[128,256]{1,0:T(8,128)(2,1)S(1)}, bf16[128,256]{1,0:T(8,128)(2,1)S(1)}, u32[]{:S(2)}, u32[]{:S(2)}) collective-permute-start(bf16[128,256]{1,0:T(8,128)(2,1)S(1)} %maximum_select_fusion.8), channel_id=1, source_target_pairs={{0,4},{1,5},{2,6},{3,7},{4,0},{5,1},{6,2},{7,3},{8,12},{9,13},{10,... | collective-permute-start | bytes 196616 | tf_op jit(solution)/shard_map/ppermute | solution.py:128
  81.8 3.0 %collective-permute-done.8 = bf16[64,256]{1,0:T(8,128)(2,1)S(1)} collective-permute-done((bf16[64,256]{1,0:T(8,128)(2,1)S(1)}, bf16[64,256]{1,0:T(8,128)(2,1)S(1)}, u32[]{:S(2)}, u32[]{:S(2)}) %collective-permute-start.8) | collective-permute-done | bytes 32800 | tf_op jit(solution)/shard_map/ppermute | solution.py:128
  84.7 1.5 %collective-permute-start.9 = (bf16[128,256]{1,0:T(8,128)(2,1)S(1)}, bf16[128,256]{1,0:T(8,128)(2,1)S(1)}, u32[]{:S(2)}, u32[]{:S(2)}) collective-permute-start(bf16[128,256]{1,0:T(8,128)(2,1)S(1)} %maximum_select_fusion.9), channel_id=1, source_target_pairs={{0,4},{1,5},{2,6},{3,7},{4,0},{5,1},{6,2},{7,3},{8,12},{9,13},{10,... | collective-permute-start | bytes 196616 | tf_op jit(solution)/shard_map/ppermute | solution.py:128
  86.3 1.6 %collective-permute-start.4 = (bf16[256,256]{1,0:T(8,128)(2,1)S(1)}, bf16[256,256]{1,0:T(8,128)(2,1)S(1)}, u32[]{:S(2)}, u32[]{:S(2)}) collective-permute-start(bf16[256,256]{1,0:T(8,128)(2,1)S(1)} %maximum_select_fusion.6), channel_id=1, source_target_pairs={{0,2},{1,3},{2,0},{3,1},{4,6},{5,7},{6,4},{7,5},{8,10},{9,11},{10,... | collective-permute-start | bytes 393224 | tf_op jit(solution)/shard_map/ppermute | solution.py:128
  87.9 1.2 %collective-permute-done.9 = bf16[128,256]{1,0:T(8,128)(2,1)S(1)} collective-permute-done((bf16[128,256]{1,0:T(8,128)(2,1)S(1)}, bf16[128,256]{1,0:T(8,128)(2,1)S(1)}, u32[]{:S(2)}, u32[]{:S(2)}) %collective-permute-start.9) | collective-permute-done | bytes 65568 | tf_op jit(solution)/shard_map/ppermute | solution.py:128
  89.1 1.7 %collective-permute-start.10 = (bf16[256,256]{1,0:T(8,128)(2,1)S(1)}, bf16[256,256]{1,0:T(8,128)(2,1)S(1)}, u32[]{:S(2)}, u32[]{:S(2)}) collective-permute-start(bf16[256,256]{1,0:T(8,128)(2,1)S(1)} %maximum_select_fusion.7), channel_id=1, source_target_pairs={{0,2},{1,3},{2,0},{3,1},{4,6},{5,7},{6,4},{7,5},{8,10},{9,11},{10,... | collective-permute-start | bytes 393224 | tf_op jit(solution)/shard_map/ppermute | solution.py:128
  91.0 0.9 collective-permute-done.4
  92.0 1.6 %collective-permute-start.5 = (bf16[512,256]{1,0:T(8,128)(2,1)S(1)}, bf16[512,256]{1,0:T(8,128)(2,1)S(1)}, u32[]{:S(2)}, u32[]{:S(2)}) collective-permute-start(bf16[512,256]{1,0:T(8,128)(2,1)S(1)} %maximum_select_fusion.4), channel_id=1, source_target_pairs={{0,1},{1,0},{2,3},{3,2},{4,5},{5,4},{6,7},{7,6},{8,9},{9,8},{10,11... | collective-permute-start | bytes 786440 | tf_op jit(solution)/shard_map/ppermute | solution.py:128
  94.3 1.6 %collective-permute-start.11 = (bf16[512,256]{1,0:T(8,128)(2,1)S(1)}, bf16[512,256]{1,0:T(8,128)(2,1)S(1)}, u32[]{:S(2)}, u32[]{:S(2)}) collective-permute-start(bf16[512,256]{1,0:T(8,128)(2,1)S(1)} %maximum_select_fusion.5), channel_id=1, source_target_pairs={{0,1},{1,0},{2,3},{3,2},{4,5},{5,4},{6,7},{7,6},{8,9},{9,8},{10,11... | collective-permute-start | bytes 786440 | tf_op jit(solution)/shard_map/ppermute | solution.py:128
  95.9 2.7 %select_reduce_fusion = f32[128,2048]{1,0:T(8,128)S(1)} fusion(f32[128,8]{1,0:T(8,128)S(1)} %copy.11, s32[2048]{0:T(1024)S(1)} %copy-done.2, s32[128,8]{1,0:T(8,128)S(1)} %copy.10), kind=kLoop, calls=%fused_computation | loop fusion | flops 6029312 | bytes 1064960 | tf_op jit(solution)/shard_map/reduce_sum | solution.py:198
  98.6 4.2 %collective-permute-done.11 = bf16[512,256]{1,0:T(8,128)(2,1)S(1)} collective-permute-done((bf16[512,256]{1,0:T(8,128)(2,1)S(1)}, bf16[512,256]{1,0:T(8,128)(2,1)S(1)}, u32[]{:S(2)}, u32[]{:S(2)}) %collective-permute-start.11) | collective-permute-done | bytes 262176 | tf_op jit(solution)/shard_map/ppermute | solution.py:128
  103.6 1.4 %convolution_add_fusion = f32[256,128]{1,0:T(8,128)} fusion(f32[256,128]{1,0:T(8,128)S(1)} %fusion.1, f32[128,2048]{1,0:T(8,128)S(1)} %select_reduce_fusion, bf16[512,256]{1,0:T(8,128)(2,1)S(1)} %maximum_select_fusion.4, bf16[512,256]{1,0:T(8,128)(2,1)S(1)} %collective-permute-done.5, pred[]{:T(512)S(6)} %ne.40), kind=kOutput, calls=%fused_computation.3 | convolution fusion | flops 405045248 | bytes 1310721 | tf_op jit(solution)/shard_map/dot_general | solution.py:203
  (34 shorter events, 3.6 us)
Async XLA Ops:
  0.0 90.8 %copy-start = (s32[2048,8]{0,1:T(8,128)S(1)}, s32[2048,8]{0,1:T(8,128)}, u32[]{:S(2)}) copy-start(s32[2048,8]{0,1:T(8,128)} %param.10) | copy-start | bytes 196612
  17.0 13.9 %collective-permute-start.1 = (bf16[7680,256]{1,0:T(8,128)(2,1)}, bf16[7680,256]{1,0:T(8,128)(2,1)}, u32[]{:S(2)}, u32[]{:S(2)}) collective-permute-start(bf16[7680,256]{1,0:T(8,128)(2,1)} %get-tuple-element.19), channel_id=1, source_target_pairs={{0,16},{16,0},{1,17},{17,1},{2,18},{18,2},{3,19},{19,3},{4,20},{20... | collective-permute-start | bytes 11796488 | tf_op jit(solution)/shard_map/ppermute | solution.py:175
  30.9 15.9 %collective-permute-start = (bf16[7680,256]{1,0:T(8,128)(2,1)}, bf16[7680,256]{1,0:T(8,128)(2,1)}, u32[]{:S(2)}, u32[]{:S(2)}) collective-permute-start(bf16[7680,256]{1,0:T(8,128)(2,1)} %get-tuple-element.16), channel_id=1, source_target_pairs={{0,16},{16,0},{1,17},{17,1},{2,18},{18,2},{3,19},{19,3},{4,20},{20... | collective-permute-start | bytes 11796488 | tf_op jit(solution)/shard_map/ppermute | solution.py:175
  46.4 22.2 %collective-permute-start.7 = (bf16[7680,256]{1,0:T(8,128)(2,1)}, bf16[7680,256]{1,0:T(8,128)(2,1)}, u32[]{:S(2)}, u32[]{:S(2)}) collective-permute-start(bf16[7680,256]{1,0:T(8,128)(2,1)} %get-tuple-element.24), channel_id=1, source_target_pairs={{0,16},{16,0},{1,17},{17,1},{2,18},{18,2},{3,19},{19,3},{4,20},{20... | collective-permute-start | bytes 11796488 | tf_op jit(solution)/shard_map/ppermute | solution.py:175
  46.9 16.9 %copy-start.1 = (f32[32,256]{1,0:T(8,128)S(1)}, f32[32,256]{1,0:T(8,128)}, u32[]{:S(2)}) copy-start(f32[32,256]{1,0:T(8,128)} %get-tuple-element.20) | copy-start | bytes 98308
  62.3 11.9 %collective-permute-start.6 = (bf16[7680,256]{1,0:T(8,128)(2,1)}, bf16[7680,256]{1,0:T(8,128)(2,1)}, u32[]{:S(2)}, u32[]{:S(2)}) collective-permute-start(bf16[7680,256]{1,0:T(8,128)(2,1)} %get-tuple-element.22), channel_id=1, source_target_pairs={{0,16},{16,0},{1,17},{17,1},{2,18},{18,2},{3,19},{19,3},{4,20},{20... | collective-permute-start | bytes 11796488 | tf_op jit(solution)/shard_map/ppermute | solution.py:175
  64.6 15.2 %collective-permute-start.2 = (bf16[64,256]{1,0:T(8,128)(2,1)S(1)}, bf16[64,256]{1,0:T(8,128)(2,1)S(1)}, u32[]{:S(2)}, u32[]{:S(2)}) collective-permute-start(bf16[64,256]{1,0:T(8,128)(2,1)S(1)} %pad_maximum_fusion), channel_id=1, source_target_pairs={{0,8},{1,9},{2,10},{3,11},{4,12},{5,13},{6,14},{7,15},{8,0},{9,1},... | collective-permute-start | bytes 98312 | tf_op jit(solution)/shard_map/ppermute | solution.py:128
  74.2 21.7 %copy-start.2 = (s32[2048]{0:T(1024)S(1)}, s32[2048]{0:T(1024)}, u32[]{:S(2)}) copy-start(s32[2048]{0:T(1024)} %constant.37.clone) | copy-start | bytes 24580
  79.8 5.0 %collective-permute-start.8 = (bf16[64,256]{1,0:T(8,128)(2,1)S(1)}, bf16[64,256]{1,0:T(8,128)(2,1)S(1)}, u32[]{:S(2)}, u32[]{:S(2)}) collective-permute-start(bf16[64,256]{1,0:T(8,128)(2,1)S(1)} %pad_maximum_fusion.1), channel_id=1, source_target_pairs={{0,8},{1,9},{2,10},{3,11},{4,12},{5,13},{6,14},{7,15},{8,0},{9,1},... | collective-permute-start | bytes 98312 | tf_op jit(solution)/shard_map/ppermute | solution.py:128
  79.8 6.4 %collective-permute-start.3 = (bf16[128,256]{1,0:T(8,128)(2,1)S(1)}, bf16[128,256]{1,0:T(8,128)(2,1)S(1)}, u32[]{:S(2)}, u32[]{:S(2)}) collective-permute-start(bf16[128,256]{1,0:T(8,128)(2,1)S(1)} %maximum_select_fusion.8), channel_id=1, source_target_pairs={{0,4},{1,5},{2,6},{3,7},{4,0},{5,1},{6,2},{7,3},{8,12},{9,13},{10,... | collective-permute-start | bytes 196616 | tf_op jit(solution)/shard_map/ppermute | solution.py:128
  84.7 4.3 %collective-permute-start.9 = (bf16[128,256]{1,0:T(8,128)(2,1)S(1)}, bf16[128,256]{1,0:T(8,128)(2,1)S(1)}, u32[]{:S(2)}, u32[]{:S(2)}) collective-permute-start(bf16[128,256]{1,0:T(8,128)(2,1)S(1)} %maximum_select_fusion.9), channel_id=1, source_target_pairs={{0,4},{1,5},{2,6},{3,7},{4,0},{5,1},{6,2},{7,3},{8,12},{9,13},{10,... | collective-permute-start | bytes 196616 | tf_op jit(solution)/shard_map/ppermute | solution.py:128
  86.3 5.6 %collective-permute-start.4 = (bf16[256,256]{1,0:T(8,128)(2,1)S(1)}, bf16[256,256]{1,0:T(8,128)(2,1)S(1)}, u32[]{:S(2)}, u32[]{:S(2)}) collective-permute-start(bf16[256,256]{1,0:T(8,128)(2,1)S(1)} %maximum_select_fusion.6), channel_id=1, source_target_pairs={{0,2},{1,3},{2,0},{3,1},{4,6},{5,7},{6,4},{7,5},{8,10},{9,11},{10,... | collective-permute-start | bytes 393224 | tf_op jit(solution)/shard_map/ppermute | solution.py:128
  89.1 5.0 %collective-permute-start.10 = (bf16[256,256]{1,0:T(8,128)(2,1)S(1)}, bf16[256,256]{1,0:T(8,128)(2,1)S(1)}, u32[]{:S(2)}, u32[]{:S(2)}) collective-permute-start(bf16[256,256]{1,0:T(8,128)(2,1)S(1)} %maximum_select_fusion.7), channel_id=1, source_target_pairs={{0,2},{1,3},{2,0},{3,1},{4,6},{5,7},{6,4},{7,5},{8,10},{9,11},{10,... | collective-permute-start | bytes 393224 | tf_op jit(solution)/shard_map/ppermute | solution.py:128
  92.0 11.6 %collective-permute-start.5 = (bf16[512,256]{1,0:T(8,128)(2,1)S(1)}, bf16[512,256]{1,0:T(8,128)(2,1)S(1)}, u32[]{:S(2)}, u32[]{:S(2)}) collective-permute-start(bf16[512,256]{1,0:T(8,128)(2,1)S(1)} %maximum_select_fusion.4), channel_id=1, source_target_pairs={{0,1},{1,0},{2,3},{3,2},{4,5},{5,4},{6,7},{7,6},{8,9},{9,8},{10,11... | collective-permute-start | bytes 786440 | tf_op jit(solution)/shard_map/ppermute | solution.py:128
  94.3 8.5 %collective-permute-start.11 = (bf16[512,256]{1,0:T(8,128)(2,1)S(1)}, bf16[512,256]{1,0:T(8,128)(2,1)S(1)}, u32[]{:S(2)}, u32[]{:S(2)}) collective-permute-start(bf16[512,256]{1,0:T(8,128)(2,1)S(1)} %maximum_select_fusion.5), channel_id=1, source_target_pairs={{0,1},{1,0},{2,3},{3,2},{4,5},{5,4},{6,7},{7,6},{8,9},{9,8},{10,11... | collective-permute-start | bytes 786440 | tf_op jit(solution)/shard_map/ppermute | solution.py:128

commit v11 on v10

--- a/solution.py
+++ b/solution.py
@@ -109,6 +109,22 @@
             flops=3 * rows * cols, transcendentals=0, bytes_accessed=4 * rows * cols
         ),
     )(mine, recv)
+
+
+def slip_kernel(units_ref, scales_ref, out_ref, acc_ref):
+    for b in range(scales_ref.shape[0]):
+        rows = pl.ds(b * UBLK, UBLK)
+        acc_ref[rows, :] = units_ref[rows, :].astype(jnp.float32) * scales_ref[b:b + 1, :]
+    out_ref[...] = acc_ref[...].astype(jnp.bfloat16)
+
+
+def slip_of(units_t, scales_t):
+    sources, scenarios = units_t.shape
+    return pl.pallas_call(
+        slip_kernel,
+        out_shape=jax.ShapeDtypeStruct((sources, scenarios), jnp.bfloat16),
+        scratch_shapes=[pltpu.VMEM((sources, scenarios), jnp.float32)],
+    )(units_t, scales_t)
 
 
 def doubling_masks(owners):
@@ -142,11 +158,7 @@
 
 def body(slip_units, slip_scales, green, coast_gauges, coast_amps, coast_counts):
     scenarios = slip_units.shape[0]
-    units_t = slip_units.T.astype(jnp.float32)
-    block_of = jnp.arange(slip_units.shape[1], dtype=jnp.int32) // UBLK
-    picks = (block_of[:, None] == jnp.arange(slip_scales.shape[1], dtype=jnp.int32)[None, :]).astype(jnp.float32)
-    scale_rows = jnp.dot(picks, slip_scales.T, precision=lax.Precision.HIGHEST, preferred_element_type=jnp.float32)
-    slip_t = (units_t * scale_rows).astype(jnp.bfloat16)
+    slip_t = slip_of(slip_units.T, slip_scales.T)
     me = lax.axis_index("src")
     groups = lax.axis_size("src")
     portion = scenarios // groups

time: 106 us -> 105 us (level)
  matrix products: 5.8 us -> 2.16 us
  Pallas kernels: 67.3 us -> 70.2 us
    dot_general x1 -> x0, matrix products: 3.64 us -> none  [body(): jnp.dot(picks, slip_scales.T, precision=lax.Precision.HIGHEST, preferred_...]
    pallas_call x0 -> x1, Pallas kernels: none -> 2.88 us  [slip_of(): pl.pallas_call(slip_kernel, out_shape=jax.ShapeDtypeStruct((sources, scen...]
  transfers between devices with their start and end apart: 12 -> 12, of which waited for: 5 -> 5; matrix products, arithmetic and copies ran while one was open for 7% -> 7% of each run, Pallas kernels for 51% -> 52%
where the time goes in v11:
time: 105 us; the launch traced here: 104 us
  Pallas kernels  70.2 us (67%)
  starting transfers between devices  15 us (14%)
  waiting for transfers between devices  9.93 us (9%)
  other arithmetic  5.94 us (6%)
  matrix products  2.16 us (2%)
    pallas_call x2, Pallas kernels, fused_of(): pl.pallas_call(fused_kernel, grid_spec=pltpu.PrefetchScalarGridSpec(num_s...  30.8 us
    pallas_call x2, Pallas kernels, partials_of(): pl.pallas_call(matmul_kernel, grid_spec=pltpu.PrefetchScalarGridSpec(num_...  26.8 us
    ppermute x8, starting transfers between devices, gather_rows(): got = lax.ppermute(held, 'rows', pairs)  13.9 us
    ppermute x8, waiting for transfers between devices, gather_rows(): got = lax.ppermute(held, 'rows', pairs)  9.92 us
    pallas_call x2, Pallas kernels, peaks_of(): pl.pallas_call(peak_kernel, grid=(blocks,), in_specs=[pl.BlockSpec((SEG,...  9.64 us
    pallas_call x1, Pallas kernels, slip_of(): pl.pallas_call(slip_kernel, out_shape=jax.ShapeDtypeStruct((sources, scen...  2.88 us
    reduce_sum x1, other arithmetic, body(): jnp.sum(jnp.where(matches, mine_weights[:, :, None], 0.0), axis=1)  2.66 us
    another operation x4, other arithmetic  2.29 us
  transfers between devices with their start and end apart: 12, of which 5 were waited for; matrix products, arithmetic and copies ran while one was open for 7% of the time, Pallas kernels for 52%

profile of v11, /device:TPU:0, one launch (start us, length us, event | category | flops | bytes accessed | tf_op | source)
XLA Modules:
  0.0 104.2 jit_solution(4448630502816743769)
XLA Ops:
  0.0 2.9 %shard_map.73.other_slip_ref.mine_slip_ref = bf16[1000,512]{1,0:T(8,128)(2,1)} custom-call(s32[1000,512]{1,0:T(8,128)} %bitcast.3, f32[8,512]{1,0:T(8,128)} %bitcast.4), custom_call_target="tpu_custom_call" | custom-call | tf_op jit(solution)/shard_map/pallas_call | solution.py:123
  2.9 13.4 %shard_map.76 = (bf16[7680,256]{1,0:T(8,128)(2,1)}, bf16[7680,256]{1,0:T(8,128)(2,1)}) custom-call(s32[1]{0:T(128)} %bitcast.side_ref, bf16[1000,512]{1,0:T(8,128)(2,1)} %shard_map.73.other_slip_ref.mine_slip_ref, bf16[1000,512]{1,0:T(8,128)(2,1)} %shard_map.73.other_slip_ref.mine_slip_ref, bf16[1000,30720]{1,0:T(8,128)(2,1)} %green_ref.7), custom_call_target="tpu_custom_call" | custom-call | flops 7864320000 | bytes 23224320 | tf_op jit(solution)/shard_map/pallas_call | solution.py:34
  16.7 13.4 %shard_map.74 = (bf16[7680,256]{1,0:T(8,128)(2,1)}, bf16[7680,256]{1,0:T(8,128)(2,1)}) custom-call(s32[1]{0:T(128)} %bitcast.side_ref, bf16[1000,512]{1,0:T(8,128)(2,1)} %shard_map.73.other_slip_ref.mine_slip_ref, bf16[1000,512]{1,0:T(8,128)(2,1)} %shard_map.73.other_slip_ref.mine_slip_ref, bf16[1000,30720]{1,0:T(8,128)(2,1)} %green_ref.7), custom_call_target="tpu_custom_call" | custom-call | flops 7864320000 | bytes 23224320 | tf_op jit(solution)/shard_map/pallas_call | solution.py:34
  30.2 15.4 %shard_map.77 = (bf16[7680,256]{1,0:T(8,128)(2,1)}, bf16[7680,256]{1,0:T(8,128)(2,1)}, f32[32,256]{1,0:T(8,128)}) custom-call(s32[1]{0:T(128)} %bitcast.side_ref, bf16[1000,512]{1,0:T(8,128)(2,1)} %shard_map.73.other_slip_ref.mine_slip_ref, bf16[1000,512]{1,0:T(8,128)(2,1)} %shard_map.73.other_slip_ref.mine_slip_ref, bf16[1000,30720]{1,0:T(8,128)(2,1)} %green_ref.7, ...), custom_call_target="tpu_custom_call" | custom-call | flops 7864320000 | bytes 31088640 | tf_op jit(solution)/shard_map/pallas_call | solution.py:68
  46.1 15.4 %shard_map.75 = (bf16[7680,256]{1,0:T(8,128)(2,1)}, bf16[7680,256]{1,0:T(8,128)(2,1)}, f32[32,256]{1,0:T(8,128)}) custom-call(s32[1]{0:T(128)} %bitcast.side_ref, bf16[1000,512]{1,0:T(8,128)(2,1)} %shard_map.73.other_slip_ref.mine_slip_ref, bf16[1000,512]{1,0:T(8,128)(2,1)} %shard_map.73.other_slip_ref.mine_slip_ref, bf16[1000,30720]{1,0:T(8,128)(2,1)} %green_ref.7, ...), custom_call_target="tpu_custom_call" | custom-call | flops 7864320000 | bytes 31088640 | tf_op jit(solution)/shard_map/pallas_call | solution.py:68
  61.5 0.8 dynamic-slice
  63.0 0.8 convert.12
  63.8 4.0 %collective-permute-start.2 = (bf16[64,256]{1,0:T(8,128)(2,1)S(1)}, bf16[64,256]{1,0:T(8,128)(2,1)S(1)}, u32[]{:S(2)}, u32[]{:S(2)}) collective-permute-start(bf16[64,256]{1,0:T(8,128)(2,1)S(1)} %pad_maximum_fusion), channel_id=1, source_target_pairs={{0,8},{1,9},{2,10},{3,11},{4,12},{5,13},{6,14},{7,15},{8,0},{9,1},... | collective-permute-start | bytes 98312 | tf_op jit(solution)/shard_map/ppermute | solution.py:144
  67.8 4.8 %shard_map.79 = f32[32,256]{1,0:T(8,128)} custom-call(bf16[7680,256]{1,0:T(8,128)(2,1)} %get-tuple-element.23.mine_ref, bf16[7680,256]{1,0:T(8,128)(2,1)} %collective-permute-done.7.recv_ref), custom_call_target="tpu_custom_call" | custom-call | flops 5898240 | bytes 7864320 | tf_op jit(solution)/shard_map/pallas_call | solution.py:102
  72.6 0.8 convert.15
  73.4 4.8 %shard_map.78 = f32[32,256]{1,0:T(8,128)} custom-call(bf16[7680,256]{1,0:T(8,128)(2,1)} %get-tuple-element.21.mine_ref, bf16[7680,256]{1,0:T(8,128)(2,1)} %collective-permute-done.6.recv_ref), custom_call_target="tpu_custom_call" | custom-call | flops 5898240 | bytes 7864320 | tf_op jit(solution)/shard_map/pallas_call | solution.py:102
  78.2 0.8 convert.14
  79.0 2.0 %collective-permute-start.3 = (bf16[128,256]{1,0:T(8,128)(2,1)S(1)}, bf16[128,256]{1,0:T(8,128)(2,1)S(1)}, u32[]{:S(2)}, u32[]{:S(2)}) collective-permute-start(bf16[128,256]{1,0:T(8,128)(2,1)S(1)} %maximum_select_fusion.8), channel_id=1, source_target_pairs={{0,4},{1,5},{2,6},{3,7},{4,0},{5,1},{6,2},{7,3},{8,12},{9,13},{10,... | collective-permute-start | bytes 196616 | tf_op jit(solution)/shard_map/ppermute | solution.py:144
  81.0 3.0 %collective-permute-done.8 = bf16[64,256]{1,0:T(8,128)(2,1)S(1)} collective-permute-done((bf16[64,256]{1,0:T(8,128)(2,1)S(1)}, bf16[64,256]{1,0:T(8,128)(2,1)S(1)}, u32[]{:S(2)}, u32[]{:S(2)}) %collective-permute-start.8) | collective-permute-done | bytes 32800 | tf_op jit(solution)/shard_map/ppermute | solution.py:144
  84.0 1.5 %collective-permute-start.9 = (bf16[128,256]{1,0:T(8,128)(2,1)S(1)}, bf16[128,256]{1,0:T(8,128)(2,1)S(1)}, u32[]{:S(2)}, u32[]{:S(2)}) collective-permute-start(bf16[128,256]{1,0:T(8,128)(2,1)S(1)} %maximum_select_fusion.9), channel_id=1, source_target_pairs={{0,4},{1,5},{2,6},{3,7},{4,0},{5,1},{6,2},{7,3},{8,12},{9,13},{10,... | collective-permute-start | bytes 196616 | tf_op jit(solution)/shard_map/ppermute | solution.py:144
  85.5 1.6 %collective-permute-start.4 = (bf16[256,256]{1,0:T(8,128)(2,1)S(1)}, bf16[256,256]{1,0:T(8,128)(2,1)S(1)}, u32[]{:S(2)}, u32[]{:S(2)}) collective-permute-start(bf16[256,256]{1,0:T(8,128)(2,1)S(1)} %maximum_select_fusion.6), channel_id=1, source_target_pairs={{0,2},{1,3},{2,0},{3,1},{4,6},{5,7},{6,4},{7,5},{8,10},{9,11},{10,... | collective-permute-start | bytes 393224 | tf_op jit(solution)/shard_map/ppermute | solution.py:144
  87.1 1.2 %collective-permute-done.9 = bf16[128,256]{1,0:T(8,128)(2,1)S(1)} collective-permute-done((bf16[128,256]{1,0:T(8,128)(2,1)S(1)}, bf16[128,256]{1,0:T(8,128)(2,1)S(1)}, u32[]{:S(2)}, u32[]{:S(2)}) %collective-permute-start.9) | collective-permute-done | bytes 65568 | tf_op jit(solution)/shard_map/ppermute | solution.py:144
  88.3 1.7 %collective-permute-start.10 = (bf16[256,256]{1,0:T(8,128)(2,1)S(1)}, bf16[256,256]{1,0:T(8,128)(2,1)S(1)}, u32[]{:S(2)}, u32[]{:S(2)}) collective-permute-start(bf16[256,256]{1,0:T(8,128)(2,1)S(1)} %maximum_select_fusion.7), channel_id=1, source_target_pairs={{0,2},{1,3},{2,0},{3,1},{4,6},{5,7},{6,4},{7,5},{8,10},{9,11},{10,... | collective-permute-start | bytes 393224 | tf_op jit(solution)/shard_map/ppermute | solution.py:144
  90.2 0.9 collective-permute-done.4
  91.2 1.6 %collective-permute-start.5 = (bf16[512,256]{1,0:T(8,128)(2,1)S(1)}, bf16[512,256]{1,0:T(8,128)(2,1)S(1)}, u32[]{:S(2)}, u32[]{:S(2)}) collective-permute-start(bf16[512,256]{1,0:T(8,128)(2,1)S(1)} %maximum_select_fusion.4), channel_id=1, source_target_pairs={{0,1},{1,0},{2,3},{3,2},{4,5},{5,4},{6,7},{7,6},{8,9},{9,8},{10,11... | collective-permute-start | bytes 786440 | tf_op jit(solution)/shard_map/ppermute | solution.py:144
  93.5 1.6 %collective-permute-start.11 = (bf16[512,256]{1,0:T(8,128)(2,1)S(1)}, bf16[512,256]{1,0:T(8,128)(2,1)S(1)}, u32[]{:S(2)}, u32[]{:S(2)}) collective-permute-start(bf16[512,256]{1,0:T(8,128)(2,1)S(1)} %maximum_select_fusion.5), channel_id=1, source_target_pairs={{0,1},{1,0},{2,3},{3,2},{4,5},{5,4},{6,7},{7,6},{8,9},{9,8},{10,11... | collective-permute-start | bytes 786440 | tf_op jit(solution)/shard_map/ppermute | solution.py:144
  95.1 2.7 %select_reduce_fusion = f32[128,2048]{1,0:T(8,128)S(1)} fusion(f32[128,8]{1,0:T(8,128)S(1)} %copy.11, s32[2048]{0:T(1024)S(1)} %copy-done.2, s32[128,8]{1,0:T(8,128)S(1)} %copy.10), kind=kLoop, calls=%fused_computation | loop fusion | flops 6029312 | bytes 1064960 | tf_op jit(solution)/shard_map/reduce_sum | solution.py:210
  97.8 4.2 %collective-permute-done.11 = bf16[512,256]{1,0:T(8,128)(2,1)S(1)} collective-permute-done((bf16[512,256]{1,0:T(8,128)(2,1)S(1)}, bf16[512,256]{1,0:T(8,128)(2,1)S(1)}, u32[]{:S(2)}, u32[]{:S(2)}) %collective-permute-start.11) | collective-permute-done | bytes 262176 | tf_op jit(solution)/shard_map/ppermute | solution.py:144
  102.8 1.4 %convolution_add_fusion = f32[256,128]{1,0:T(8,128)} fusion(f32[256,128]{1,0:T(8,128)S(1)} %fusion, f32[128,2048]{1,0:T(8,128)S(1)} %select_reduce_fusion, bf16[512,256]{1,0:T(8,128)(2,1)S(1)} %maximum_select_fusion.4, bf16[512,256]{1,0:T(8,128)(2,1)S(1)} %collective-permute-done.5, pred[]{:T(512)S(6)} %ne.16), kind=kOutput, calls=%fused_computation.1 | convolution fusion | flops 405045248 | bytes 1310721 | tf_op jit(solution)/shard_map/dot_general | solution.py:215
  (33 shorter events, 3.6 us)
Async XLA Ops:
  0.0 90.0 %copy-start = (s32[2048,8]{0,1:T(8,128)S(1)}, s32[2048,8]{0,1:T(8,128)}, u32[]{:S(2)}) copy-start(s32[2048,8]{0,1:T(8,128)} %param.10) | copy-start | bytes 196612
  16.3 13.9 %collective-permute-start.1 = (bf16[7680,256]{1,0:T(8,128)(2,1)}, bf16[7680,256]{1,0:T(8,128)(2,1)}, u32[]{:S(2)}, u32[]{:S(2)}) collective-permute-start(bf16[7680,256]{1,0:T(8,128)(2,1)} %get-tuple-element.19), channel_id=1, source_target_pairs={{0,16},{16,0},{1,17},{17,1},{2,18},{18,2},{3,19},{19,3},{4,20},{20... | collective-permute-start | bytes 11796488 | tf_op jit(solution)/shard_map/ppermute | solution.py:187
  30.1 15.9 %collective-permute-start = (bf16[7680,256]{1,0:T(8,128)(2,1)}, bf16[7680,256]{1,0:T(8,128)(2,1)}, u32[]{:S(2)}, u32[]{:S(2)}) collective-permute-start(bf16[7680,256]{1,0:T(8,128)(2,1)} %get-tuple-element.16), channel_id=1, source_target_pairs={{0,16},{16,0},{1,17},{17,1},{2,18},{18,2},{3,19},{19,3},{4,20},{20... | collective-permute-start | bytes 11796488 | tf_op jit(solution)/shard_map/ppermute | solution.py:187
  45.6 22.2 %collective-permute-start.7 = (bf16[7680,256]{1,0:T(8,128)(2,1)}, bf16[7680,256]{1,0:T(8,128)(2,1)}, u32[]{:S(2)}, u32[]{:S(2)}) collective-permute-start(bf16[7680,256]{1,0:T(8,128)(2,1)} %get-tuple-element.24), channel_id=1, source_target_pairs={{0,16},{16,0},{1,17},{17,1},{2,18},{18,2},{3,19},{19,3},{4,20},{20... | collective-permute-start | bytes 11796488 | tf_op jit(solution)/shard_map/ppermute | solution.py:187
  46.1 16.9 %copy-start.1 = (f32[32,256]{1,0:T(8,128)S(1)}, f32[32,256]{1,0:T(8,128)}, u32[]{:S(2)}) copy-start(f32[32,256]{1,0:T(8,128)} %get-tuple-element.20) | copy-start | bytes 98308
  61.5 11.9 %collective-permute-start.6 = (bf16[7680,256]{1,0:T(8,128)(2,1)}, bf16[7680,256]{1,0:T(8,128)(2,1)}, u32[]{:S(2)}, u32[]{:S(2)}) collective-permute-start(bf16[7680,256]{1,0:T(8,128)(2,1)} %get-tuple-element.22), channel_id=1, source_target_pairs={{0,16},{16,0},{1,17},{17,1},{2,18},{18,2},{3,19},{19,3},{4,20},{20... | collective-permute-start | bytes 11796488 | tf_op jit(solution)/shard_map/ppermute | solution.py:187
  63.8 15.2 %collective-permute-start.2 = (bf16[64,256]{1,0:T(8,128)(2,1)S(1)}, bf16[64,256]{1,0:T(8,128)(2,1)S(1)}, u32[]{:S(2)}, u32[]{:S(2)}) collective-permute-start(bf16[64,256]{1,0:T(8,128)(2,1)S(1)} %pad_maximum_fusion), channel_id=1, source_target_pairs={{0,8},{1,9},{2,10},{3,11},{4,12},{5,13},{6,14},{7,15},{8,0},{9,1},... | collective-permute-start | bytes 98312 | tf_op jit(solution)/shard_map/ppermute | solution.py:144
  73.4 21.7 %copy-start.2 = (s32[2048]{0:T(1024)S(1)}, s32[2048]{0:T(1024)}, u32[]{:S(2)}) copy-start(s32[2048]{0:T(1024)} %constant.28.clone) | copy-start | bytes 24580
  79.0 5.0 %collective-permute-start.8 = (bf16[64,256]{1,0:T(8,128)(2,1)S(1)}, bf16[64,256]{1,0:T(8,128)(2,1)S(1)}, u32[]{:S(2)}, u32[]{:S(2)}) collective-permute-start(bf16[64,256]{1,0:T(8,128)(2,1)S(1)} %pad_maximum_fusion.1), channel_id=1, source_target_pairs={{0,8},{1,9},{2,10},{3,11},{4,12},{5,13},{6,14},{7,15},{8,0},{9,1},... | collective-permute-start | bytes 98312 | tf_op jit(solution)/shard_map/ppermute | solution.py:144
  79.0 6.4 %collective-permute-start.3 = (bf16[128,256]{1,0:T(8,128)(2,1)S(1)}, bf16[128,256]{1,0:T(8,128)(2,1)S(1)}, u32[]{:S(2)}, u32[]{:S(2)}) collective-permute-start(bf16[128,256]{1,0:T(8,128)(2,1)S(1)} %maximum_select_fusion.8), channel_id=1, source_target_pairs={{0,4},{1,5},{2,6},{3,7},{4,0},{5,1},{6,2},{7,3},{8,12},{9,13},{10,... | collective-permute-start | bytes 196616 | tf_op jit(solution)/shard_map/ppermute | solution.py:144
  84.0 4.3 %collective-permute-start.9 = (bf16[128,256]{1,0:T(8,128)(2,1)S(1)}, bf16[128,256]{1,0:T(8,128)(2,1)S(1)}, u32[]{:S(2)}, u32[]{:S(2)}) collective-permute-start(bf16[128,256]{1,0:T(8,128)(2,1)S(1)} %maximum_select_fusion.9), channel_id=1, source_target_pairs={{0,4},{1,5},{2,6},{3,7},{4,0},{5,1},{6,2},{7,3},{8,12},{9,13},{10,... | collective-permute-start | bytes 196616 | tf_op jit(solution)/shard_map/ppermute | solution.py:144
  85.5 5.6 %collective-permute-start.4 = (bf16[256,256]{1,0:T(8,128)(2,1)S(1)}, bf16[256,256]{1,0:T(8,128)(2,1)S(1)}, u32[]{:S(2)}, u32[]{:S(2)}) collective-permute-start(bf16[256,256]{1,0:T(8,128)(2,1)S(1)} %maximum_select_fusion.6), channel_id=1, source_target_pairs={{0,2},{1,3},{2,0},{3,1},{4,6},{5,7},{6,4},{7,5},{8,10},{9,11},{10,... | collective-permute-start | bytes 393224 | tf_op jit(solution)/shard_map/ppermute | solution.py:144
  88.3 5.0 %collective-permute-start.10 = (bf16[256,256]{1,0:T(8,128)(2,1)S(1)}, bf16[256,256]{1,0:T(8,128)(2,1)S(1)}, u32[]{:S(2)}, u32[]{:S(2)}) collective-permute-start(bf16[256,256]{1,0:T(8,128)(2,1)S(1)} %maximum_select_fusion.7), channel_id=1, source_target_pairs={{0,2},{1,3},{2,0},{3,1},{4,6},{5,7},{6,4},{7,5},{8,10},{9,11},{10,... | collective-permute-start | bytes 393224 | tf_op jit(solution)/shard_map/ppermute | solution.py:144
  91.2 11.6 %collective-permute-start.5 = (bf16[512,256]{1,0:T(8,128)(2,1)S(1)}, bf16[512,256]{1,0:T(8,128)(2,1)S(1)}, u32[]{:S(2)}, u32[]{:S(2)}) collective-permute-start(bf16[512,256]{1,0:T(8,128)(2,1)S(1)} %maximum_select_fusion.4), channel_id=1, source_target_pairs={{0,1},{1,0},{2,3},{3,2},{4,5},{5,4},{6,7},{7,6},{8,9},{9,8},{10,11... | collective-permute-start | bytes 786440 | tf_op jit(solution)/shard_map/ppermute | solution.py:144
  93.5 8.5 %collective-permute-start.11 = (bf16[512,256]{1,0:T(8,128)(2,1)S(1)}, bf16[512,256]{1,0:T(8,128)(2,1)S(1)}, u32[]{:S(2)}, u32[]{:S(2)}) collective-permute-start(bf16[512,256]{1,0:T(8,128)(2,1)S(1)} %maximum_select_fusion.5), channel_id=1, source_target_pairs={{0,1},{1,0},{2,3},{3,2},{4,5},{5,4},{6,7},{7,6},{8,9},{9,8},{10,11... | collective-permute-start | bytes 786440 | tf_op jit(solution)/shard_map/ppermute | solution.py:144

commit v12 on v11

--- a/solution.py
+++ b/solution.py
@@ -120,10 +120,18 @@
 
 def slip_of(units_t, scales_t):
     sources, scenarios = units_t.shape
+    blocks = scales_t.shape[0]
+    lanes = 128 if scenarios % 128 == 0 else scenarios
     return pl.pallas_call(
         slip_kernel,
+        grid=(scenarios // lanes,),
+        in_specs=[
+            pl.BlockSpec((sources, lanes), lambda j: (0, j)),
+            pl.BlockSpec((blocks, lanes), lambda j: (0, j)),
+        ],
+        out_specs=pl.BlockSpec((sources, lanes), lambda j: (0, j)),
         out_shape=jax.ShapeDtypeStruct((sources, scenarios), jnp.bfloat16),
-        scratch_shapes=[pltpu.VMEM((sources, scenarios), jnp.float32)],
+        scratch_shapes=[pltpu.VMEM((sources, lanes), jnp.float32)],
     )(units_t, scales_t)
 
 

time: 105 us -> 106 us (level)
  transfers between devices with their start and end apart: 12 -> 12, of which waited for: 5 -> 5; matrix products, arithmetic and copies ran while one was open for 7% -> 7% of each run, Pallas kernels for 52% -> 51%
where the time goes in v12:
time: 106 us; the launch traced here: 105 us
  Pallas kernels  71 us (67%)
  starting transfers between devices  15 us (14%)
  waiting for transfers between devices  9.91 us (9%)
  other arithmetic  5.94 us (6%)
  matrix products  2.16 us (2%)
    pallas_call x2, Pallas kernels, fused_of(): pl.pallas_call(fused_kernel, grid_spec=pltpu.PrefetchScalarGridSpec(num_s...  30.8 us
    pallas_call x2, Pallas kernels, partials_of(): pl.pallas_call(matmul_kernel, grid_spec=pltpu.PrefetchScalarGridSpec(num_...  26.8 us
    ppermute x8, starting transfers between devices, gather_rows(): got = lax.ppermute(held, 'rows', pairs)  14 us
    ppermute x8, waiting for transfers between devices, gather_rows(): got = lax.ppermute(held, 'rows', pairs)  9.9 us
    pallas_call x2, Pallas kernels, peaks_of(): pl.pallas_call(peak_kernel, grid=(blocks,), in_specs=[pl.BlockSpec((SEG,...  9.64 us
    pallas_call x1, Pallas kernels, slip_of(): pl.pallas_call(slip_kernel, grid=(scenarios // lanes,), in_specs=[pl.Bloc...  3.74 us
    reduce_sum x1, other arithmetic, body(): jnp.sum(jnp.where(matches, mine_weights[:, :, None], 0.0), axis=1)  2.66 us
    another operation x4, other arithmetic  2.29 us
  transfers between devices with their start and end apart: 12, of which 5 were waited for; matrix products, arithmetic and copies ran while one was open for 7% of the time, Pallas kernels for 51%

profile of v12, /device:TPU:0, one launch (start us, length us, event | category | flops | bytes accessed | tf_op | source)
XLA Modules:
  0.0 105.1 jit_solution(5289528543013135685)
XLA Ops:
  0.0 3.7 %shard_map.73.other_slip_ref.mine_slip_ref = bf16[1000,512]{1,0:T(8,128)(2,1)} custom-call(s32[1000,512]{1,0:T(8,128)} %bitcast.3, f32[8,512]{1,0:T(8,128)} %bitcast.4), custom_call_target="tpu_custom_call" | custom-call | tf_op jit(solution)/shard_map/pallas_call | solution.py:125
  3.7 13.4 %shard_map.76 = (bf16[7680,256]{1,0:T(8,128)(2,1)}, bf16[7680,256]{1,0:T(8,128)(2,1)}) custom-call(s32[1]{0:T(128)} %bitcast.side_ref, bf16[1000,512]{1,0:T(8,128)(2,1)} %shard_map.73.other_slip_ref.mine_slip_ref, bf16[1000,512]{1,0:T(8,128)(2,1)} %shard_map.73.other_slip_ref.mine_slip_ref, bf16[1000,30720]{1,0:T(8,128)(2,1)} %green_ref.7), custom_call_target="tpu_custom_call" | custom-call | flops 7864320000 | bytes 23224320 | tf_op jit(solution)/shard_map/pallas_call | solution.py:34
  17.6 13.4 %shard_map.74 = (bf16[7680,256]{1,0:T(8,128)(2,1)}, bf16[7680,256]{1,0:T(8,128)(2,1)}) custom-call(s32[1]{0:T(128)} %bitcast.side_ref, bf16[1000,512]{1,0:T(8,128)(2,1)} %shard_map.73.other_slip_ref.mine_slip_ref, bf16[1000,512]{1,0:T(8,128)(2,1)} %shard_map.73.other_slip_ref.mine_slip_ref, bf16[1000,30720]{1,0:T(8,128)(2,1)} %green_ref.7), custom_call_target="tpu_custom_call" | custom-call | flops 7864320000 | bytes 23224320 | tf_op jit(solution)/shard_map/pallas_call | solution.py:34
  31.1 15.4 %shard_map.77 = (bf16[7680,256]{1,0:T(8,128)(2,1)}, bf16[7680,256]{1,0:T(8,128)(2,1)}, f32[32,256]{1,0:T(8,128)}) custom-call(s32[1]{0:T(128)} %bitcast.side_ref, bf16[1000,512]{1,0:T(8,128)(2,1)} %shard_map.73.other_slip_ref.mine_slip_ref, bf16[1000,512]{1,0:T(8,128)(2,1)} %shard_map.73.other_slip_ref.mine_slip_ref, bf16[1000,30720]{1,0:T(8,128)(2,1)} %green_ref.7, ...), custom_call_target="tpu_custom_call" | custom-call | flops 7864320000 | bytes 31088640 | tf_op jit(solution)/shard_map/pallas_call | solution.py:68
  47.0 15.4 %shard_map.75 = (bf16[7680,256]{1,0:T(8,128)(2,1)}, bf16[7680,256]{1,0:T(8,128)(2,1)}, f32[32,256]{1,0:T(8,128)}) custom-call(s32[1]{0:T(128)} %bitcast.side_ref, bf16[1000,512]{1,0:T(8,128)(2,1)} %shard_map.73.other_slip_ref.mine_slip_ref, bf16[1000,512]{1,0:T(8,128)(2,1)} %shard_map.73.other_slip_ref.mine_slip_ref, bf16[1000,30720]{1,0:T(8,128)(2,1)} %green_ref.7, ...), custom_call_target="tpu_custom_call" | custom-call | flops 7864320000 | bytes 31088640 | tf_op jit(solution)/shard_map/pallas_call | solution.py:68
  62.4 0.8 dynamic-slice
  63.9 0.8 convert.12
  64.6 4.0 %collective-permute-start.2 = (bf16[64,256]{1,0:T(8,128)(2,1)S(1)}, bf16[64,256]{1,0:T(8,128)(2,1)S(1)}, u32[]{:S(2)}, u32[]{:S(2)}) collective-permute-start(bf16[64,256]{1,0:T(8,128)(2,1)S(1)} %pad_maximum_fusion), channel_id=1, source_target_pairs={{0,8},{1,9},{2,10},{3,11},{4,12},{5,13},{6,14},{7,15},{8,0},{9,1},... | collective-permute-start | bytes 98312 | tf_op jit(solution)/shard_map/ppermute | solution.py:152
  68.7 4.8 %shard_map.79 = f32[32,256]{1,0:T(8,128)} custom-call(bf16[7680,256]{1,0:T(8,128)(2,1)} %get-tuple-element.23.mine_ref, bf16[7680,256]{1,0:T(8,128)(2,1)} %collective-permute-done.7.recv_ref), custom_call_target="tpu_custom_call" | custom-call | flops 5898240 | bytes 7864320 | tf_op jit(solution)/shard_map/pallas_call | solution.py:102
  73.5 0.8 convert.15
  74.3 4.8 %shard_map.78 = f32[32,256]{1,0:T(8,128)} custom-call(bf16[7680,256]{1,0:T(8,128)(2,1)} %get-tuple-element.21.mine_ref, bf16[7680,256]{1,0:T(8,128)(2,1)} %collective-permute-done.6.recv_ref), custom_call_target="tpu_custom_call" | custom-call | flops 5898240 | bytes 7864320 | tf_op jit(solution)/shard_map/pallas_call | solution.py:102
  79.1 0.8 convert.14
  79.9 2.0 %collective-permute-start.3 = (bf16[128,256]{1,0:T(8,128)(2,1)S(1)}, bf16[128,256]{1,0:T(8,128)(2,1)S(1)}, u32[]{:S(2)}, u32[]{:S(2)}) collective-permute-start(bf16[128,256]{1,0:T(8,128)(2,1)S(1)} %maximum_select_fusion.8), channel_id=1, source_target_pairs={{0,4},{1,5},{2,6},{3,7},{4,0},{5,1},{6,2},{7,3},{8,12},{9,13},{10,... | collective-permute-start | bytes 196616 | tf_op jit(solution)/shard_map/ppermute | solution.py:152
  81.9 3.0 %collective-permute-done.8 = bf16[64,256]{1,0:T(8,128)(2,1)S(1)} collective-permute-done((bf16[64,256]{1,0:T(8,128)(2,1)S(1)}, bf16[64,256]{1,0:T(8,128)(2,1)S(1)}, u32[]{:S(2)}, u32[]{:S(2)}) %collective-permute-start.8) | collective-permute-done | bytes 32800 | tf_op jit(solution)/shard_map/ppermute | solution.py:152
  84.8 1.5 %collective-permute-start.9 = (bf16[128,256]{1,0:T(8,128)(2,1)S(1)}, bf16[128,256]{1,0:T(8,128)(2,1)S(1)}, u32[]{:S(2)}, u32[]{:S(2)}) collective-permute-start(bf16[128,256]{1,0:T(8,128)(2,1)S(1)} %maximum_select_fusion.9), channel_id=1, source_target_pairs={{0,4},{1,5},{2,6},{3,7},{4,0},{5,1},{6,2},{7,3},{8,12},{9,13},{10,... | collective-permute-start | bytes 196616 | tf_op jit(solution)/shard_map/ppermute | solution.py:152
  86.4 1.6 %collective-permute-start.4 = (bf16[256,256]{1,0:T(8,128)(2,1)S(1)}, bf16[256,256]{1,0:T(8,128)(2,1)S(1)}, u32[]{:S(2)}, u32[]{:S(2)}) collective-permute-start(bf16[256,256]{1,0:T(8,128)(2,1)S(1)} %maximum_select_fusion.6), channel_id=1, source_target_pairs={{0,2},{1,3},{2,0},{3,1},{4,6},{5,7},{6,4},{7,5},{8,10},{9,11},{10,... | collective-permute-start | bytes 393224 | tf_op jit(solution)/shard_map/ppermute | solution.py:152
  88.0 1.2 %collective-permute-done.9 = bf16[128,256]{1,0:T(8,128)(2,1)S(1)} collective-permute-done((bf16[128,256]{1,0:T(8,128)(2,1)S(1)}, bf16[128,256]{1,0:T(8,128)(2,1)S(1)}, u32[]{:S(2)}, u32[]{:S(2)}) %collective-permute-start.9) | collective-permute-done | bytes 65568 | tf_op jit(solution)/shard_map/ppermute | solution.py:152
  89.2 1.7 %collective-permute-start.10 = (bf16[256,256]{1,0:T(8,128)(2,1)S(1)}, bf16[256,256]{1,0:T(8,128)(2,1)S(1)}, u32[]{:S(2)}, u32[]{:S(2)}) collective-permute-start(bf16[256,256]{1,0:T(8,128)(2,1)S(1)} %maximum_select_fusion.7), channel_id=1, source_target_pairs={{0,2},{1,3},{2,0},{3,1},{4,6},{5,7},{6,4},{7,5},{8,10},{9,11},{10,... | collective-permute-start | bytes 393224 | tf_op jit(solution)/shard_map/ppermute | solution.py:152
  91.1 0.9 collective-permute-done.4
  92.1 1.6 %collective-permute-start.5 = (bf16[512,256]{1,0:T(8,128)(2,1)S(1)}, bf16[512,256]{1,0:T(8,128)(2,1)S(1)}, u32[]{:S(2)}, u32[]{:S(2)}) collective-permute-start(bf16[512,256]{1,0:T(8,128)(2,1)S(1)} %maximum_select_fusion.4), channel_id=1, source_target_pairs={{0,1},{1,0},{2,3},{3,2},{4,5},{5,4},{6,7},{7,6},{8,9},{9,8},{10,11... | collective-permute-start | bytes 786440 | tf_op jit(solution)/shard_map/ppermute | solution.py:152
  94.3 1.6 %collective-permute-start.11 = (bf16[512,256]{1,0:T(8,128)(2,1)S(1)}, bf16[512,256]{1,0:T(8,128)(2,1)S(1)}, u32[]{:S(2)}, u32[]{:S(2)}) collective-permute-start(bf16[512,256]{1,0:T(8,128)(2,1)S(1)} %maximum_select_fusion.5), channel_id=1, source_target_pairs={{0,1},{1,0},{2,3},{3,2},{4,5},{5,4},{6,7},{7,6},{8,9},{9,8},{10,11... | collective-permute-start | bytes 786440 | tf_op jit(solution)/shard_map/ppermute | solution.py:152
  96.0 2.7 %select_reduce_fusion = f32[128,2048]{1,0:T(8,128)S(1)} fusion(f32[128,8]{1,0:T(8,128)S(1)} %copy.11, s32[2048]{0:T(1024)S(1)} %copy-done.2, s32[128,8]{1,0:T(8,128)S(1)} %copy.10), kind=kLoop, calls=%fused_computation | loop fusion | flops 6029312 | bytes 1064960 | tf_op jit(solution)/shard_map/reduce_sum | solution.py:218
  98.7 4.2 %collective-permute-done.11 = bf16[512,256]{1,0:T(8,128)(2,1)S(1)} collective-permute-done((bf16[512,256]{1,0:T(8,128)(2,1)S(1)}, bf16[512,256]{1,0:T(8,128)(2,1)S(1)}, u32[]{:S(2)}, u32[]{:S(2)}) %collective-permute-start.11) | collective-permute-done | bytes 262176 | tf_op jit(solution)/shard_map/ppermute | solution.py:152
  103.6 1.4 %convolution_add_fusion = f32[256,128]{1,0:T(8,128)} fusion(f32[256,128]{1,0:T(8,128)S(1)} %fusion, f32[128,2048]{1,0:T(8,128)S(1)} %select_reduce_fusion, bf16[512,256]{1,0:T(8,128)(2,1)S(1)} %maximum_select_fusion.4, bf16[512,256]{1,0:T(8,128)(2,1)S(1)} %collective-permute-done.5, pred[]{:T(512)S(6)} %ne.16), kind=kOutput, calls=%fused_computation.1 | convolution fusion | flops 405045248 | bytes 1310721 | tf_op jit(solution)/shard_map/dot_general | solution.py:223
  (33 shorter events, 3.6 us)
Async XLA Ops:
  0.0 90.9 %copy-start = (s32[2048,8]{0,1:T(8,128)S(1)}, s32[2048,8]{0,1:T(8,128)}, u32[]{:S(2)}) copy-start(s32[2048,8]{0,1:T(8,128)} %param.10) | copy-start | bytes 196612
  17.1 13.9 %collective-permute-start.1 = (bf16[7680,256]{1,0:T(8,128)(2,1)}, bf16[7680,256]{1,0:T(8,128)(2,1)}, u32[]{:S(2)}, u32[]{:S(2)}) collective-permute-start(bf16[7680,256]{1,0:T(8,128)(2,1)} %get-tuple-element.19), channel_id=1, source_target_pairs={{0,16},{16,0},{1,17},{17,1},{2,18},{18,2},{3,19},{19,3},{4,20},{20... | collective-permute-start | bytes 11796488 | tf_op jit(solution)/shard_map/ppermute | solution.py:195
  31.0 15.9 %collective-permute-start = (bf16[7680,256]{1,0:T(8,128)(2,1)}, bf16[7680,256]{1,0:T(8,128)(2,1)}, u32[]{:S(2)}, u32[]{:S(2)}) collective-permute-start(bf16[7680,256]{1,0:T(8,128)(2,1)} %get-tuple-element.16), channel_id=1, source_target_pairs={{0,16},{16,0},{1,17},{17,1},{2,18},{18,2},{3,19},{19,3},{4,20},{20... | collective-permute-start | bytes 11796488 | tf_op jit(solution)/shard_map/ppermute | solution.py:195
  46.5 22.2 %collective-permute-start.7 = (bf16[7680,256]{1,0:T(8,128)(2,1)}, bf16[7680,256]{1,0:T(8,128)(2,1)}, u32[]{:S(2)}, u32[]{:S(2)}) collective-permute-start(bf16[7680,256]{1,0:T(8,128)(2,1)} %get-tuple-element.24), channel_id=1, source_target_pairs={{0,16},{16,0},{1,17},{17,1},{2,18},{18,2},{3,19},{19,3},{4,20},{20... | collective-permute-start | bytes 11796488 | tf_op jit(solution)/shard_map/ppermute | solution.py:195
  47.0 16.9 %copy-start.1 = (f32[32,256]{1,0:T(8,128)S(1)}, f32[32,256]{1,0:T(8,128)}, u32[]{:S(2)}) copy-start(f32[32,256]{1,0:T(8,128)} %get-tuple-element.20) | copy-start | bytes 98308
  62.4 11.9 %collective-permute-start.6 = (bf16[7680,256]{1,0:T(8,128)(2,1)}, bf16[7680,256]{1,0:T(8,128)(2,1)}, u32[]{:S(2)}, u32[]{:S(2)}) collective-permute-start(bf16[7680,256]{1,0:T(8,128)(2,1)} %get-tuple-element.22), channel_id=1, source_target_pairs={{0,16},{16,0},{1,17},{17,1},{2,18},{18,2},{3,19},{19,3},{4,20},{20... | collective-permute-start | bytes 11796488 | tf_op jit(solution)/shard_map/ppermute | solution.py:195
  64.6 15.2 %collective-permute-start.2 = (bf16[64,256]{1,0:T(8,128)(2,1)S(1)}, bf16[64,256]{1,0:T(8,128)(2,1)S(1)}, u32[]{:S(2)}, u32[]{:S(2)}) collective-permute-start(bf16[64,256]{1,0:T(8,128)(2,1)S(1)} %pad_maximum_fusion), channel_id=1, source_target_pairs={{0,8},{1,9},{2,10},{3,11},{4,12},{5,13},{6,14},{7,15},{8,0},{9,1},... | collective-permute-start | bytes 98312 | tf_op jit(solution)/shard_map/ppermute | solution.py:152
  74.3 21.7 %copy-start.2 = (s32[2048]{0:T(1024)S(1)}, s32[2048]{0:T(1024)}, u32[]{:S(2)}) copy-start(s32[2048]{0:T(1024)} %constant.28.clone) | copy-start | bytes 24580
  79.9 5.0 %collective-permute-start.8 = (bf16[64,256]{1,0:T(8,128)(2,1)S(1)}, bf16[64,256]{1,0:T(8,128)(2,1)S(1)}, u32[]{:S(2)}, u32[]{:S(2)}) collective-permute-start(bf16[64,256]{1,0:T(8,128)(2,1)S(1)} %pad_maximum_fusion.1), channel_id=1, source_target_pairs={{0,8},{1,9},{2,10},{3,11},{4,12},{5,13},{6,14},{7,15},{8,0},{9,1},... | collective-permute-start | bytes 98312 | tf_op jit(solution)/shard_map/ppermute | solution.py:152
  79.9 6.4 %collective-permute-start.3 = (bf16[128,256]{1,0:T(8,128)(2,1)S(1)}, bf16[128,256]{1,0:T(8,128)(2,1)S(1)}, u32[]{:S(2)}, u32[]{:S(2)}) collective-permute-start(bf16[128,256]{1,0:T(8,128)(2,1)S(1)} %maximum_select_fusion.8), channel_id=1, source_target_pairs={{0,4},{1,5},{2,6},{3,7},{4,0},{5,1},{6,2},{7,3},{8,12},{9,13},{10,... | collective-permute-start | bytes 196616 | tf_op jit(solution)/shard_map/ppermute | solution.py:152
  84.8 4.3 %collective-permute-start.9 = (bf16[128,256]{1,0:T(8,128)(2,1)S(1)}, bf16[128,256]{1,0:T(8,128)(2,1)S(1)}, u32[]{:S(2)}, u32[]{:S(2)}) collective-permute-start(bf16[128,256]{1,0:T(8,128)(2,1)S(1)} %maximum_select_fusion.9), channel_id=1, source_target_pairs={{0,4},{1,5},{2,6},{3,7},{4,0},{5,1},{6,2},{7,3},{8,12},{9,13},{10,... | collective-permute-start | bytes 196616 | tf_op jit(solution)/shard_map/ppermute | solution.py:152
  86.4 5.6 %collective-permute-start.4 = (bf16[256,256]{1,0:T(8,128)(2,1)S(1)}, bf16[256,256]{1,0:T(8,128)(2,1)S(1)}, u32[]{:S(2)}, u32[]{:S(2)}) collective-permute-start(bf16[256,256]{1,0:T(8,128)(2,1)S(1)} %maximum_select_fusion.6), channel_id=1, source_target_pairs={{0,2},{1,3},{2,0},{3,1},{4,6},{5,7},{6,4},{7,5},{8,10},{9,11},{10,... | collective-permute-start | bytes 393224 | tf_op jit(solution)/shard_map/ppermute | solution.py:152
  89.2 5.0 %collective-permute-start.10 = (bf16[256,256]{1,0:T(8,128)(2,1)S(1)}, bf16[256,256]{1,0:T(8,128)(2,1)S(1)}, u32[]{:S(2)}, u32[]{:S(2)}) collective-permute-start(bf16[256,256]{1,0:T(8,128)(2,1)S(1)} %maximum_select_fusion.7), channel_id=1, source_target_pairs={{0,2},{1,3},{2,0},{3,1},{4,6},{5,7},{6,4},{7,5},{8,10},{9,11},{10,... | collective-permute-start | bytes 393224 | tf_op jit(solution)/shard_map/ppermute | solution.py:152
  92.1 11.6 %collective-permute-start.5 = (bf16[512,256]{1,0:T(8,128)(2,1)S(1)}, bf16[512,256]{1,0:T(8,128)(2,1)S(1)}, u32[]{:S(2)}, u32[]{:S(2)}) collective-permute-start(bf16[512,256]{1,0:T(8,128)(2,1)S(1)} %maximum_select_fusion.4), channel_id=1, source_target_pairs={{0,1},{1,0},{2,3},{3,2},{4,5},{5,4},{6,7},{7,6},{8,9},{9,8},{10,11... | collective-permute-start | bytes 786440 | tf_op jit(solution)/shard_map/ppermute | solution.py:152
  94.3 8.5 %collective-permute-start.11 = (bf16[512,256]{1,0:T(8,128)(2,1)S(1)}, bf16[512,256]{1,0:T(8,128)(2,1)S(1)}, u32[]{:S(2)}, u32[]{:S(2)}) collective-permute-start(bf16[512,256]{1,0:T(8,128)(2,1)S(1)} %maximum_select_fusion.5), channel_id=1, source_target_pairs={{0,1},{1,0},{2,3},{3,2},{4,5},{5,4},{6,7},{7,6},{8,9},{9,8},{10,11... | collective-permute-start | bytes 786440 | tf_op jit(solution)/shard_map/ppermute | solution.py:152

commit v13 on v11

--- a/solution.py
+++ b/solution.py
@@ -109,6 +109,27 @@
             flops=3 * rows * cols, transcendentals=0, bytes_accessed=4 * rows * cols
         ),
     )(mine, recv)
+
+
+def pair_kernel(mine_a, recv_a, mine_b, recv_b, out_a, out_b):
+    peak_kernel(mine_a, recv_a, out_a)
+    peak_kernel(mine_b, recv_b, out_b)
+
+
+def pair_peaks_of(mine_a, recv_a, mine_b, recv_b):
+    cols, rows = mine_a.shape
+    blocks = cols // SEG
+    gauges = SEG // NT
+    return pl.pallas_call(
+        pair_kernel,
+        grid=(blocks,),
+        in_specs=[pl.BlockSpec((SEG, rows), lambda j: (j, 0))] * 4,
+        out_specs=[pl.BlockSpec((gauges, rows), lambda j: (j, 0))] * 2,
+        out_shape=[jax.ShapeDtypeStruct((blocks * gauges, rows), jnp.float32)] * 2,
+        cost_estimate=pl.CostEstimate(
+            flops=6 * rows * cols, transcendentals=0, bytes_accessed=8 * rows * cols
+        ),
+    )(mine_a, recv_a, mine_b, recv_b)
 
 
 def slip_kernel(units_ref, scales_ref, out_ref, acc_ref):
@@ -185,8 +206,14 @@
             other, mine = partials_of(side, slip_t, green, c, width, tile)
         mines.append(mine)
         receiveds.append(lax.ppermute(other, "src", pairs))
-    for c in range(chunks):
-        if peaks[c] is None:
+    waiting = [c for c in range(chunks) if peaks[c] is None]
+    if len(waiting) == 2 and mines[waiting[0]].shape == mines[waiting[1]].shape:
+        first, second = waiting
+        peaks[first], peaks[second] = pair_peaks_of(
+            mines[first], receiveds[first], mines[second], receiveds[second]
+        )
+    else:
+        for c in waiting:
             peaks[c] = peaks_of(mines[c], receiveds[c])
     split = (chunks + 1) // 2
     bundles = [list(range(split)), list(range(split, chunks))] if chunks > 1 else [[0]]

time: 105 us -> 105 us (level)
  starting transfers between devices: 15 us -> 19.1 us
  Pallas kernels: 70.2 us -> 67.5 us
  waiting for transfers between devices: 9.93 us -> 8.72 us
    ppermute x8, starting transfers between devices: 13.9 us -> 18 us  [gather_rows(): got = lax.ppermute(held, 'rows', pairs)]
    pallas_call x2 -> x1, Pallas kernels: 9.64 us -> 7.13 us  [pair_peaks_of(): pl.pallas_call(pair_kernel, grid=(blocks,), in_specs=[pl.BlockSpec((SEG,...]
    ppermute x8, waiting for transfers between devices: 9.92 us -> 7.91 us  [gather_rows(): got = lax.ppermute(held, 'rows', pairs)]
  transfers between devices with their start and end apart: 12 -> 12, of which waited for: 5 -> 6; matrix products, arithmetic and copies ran while one was open for 7% -> 7% of each run, Pallas kernels for 52% -> 49%
where the time goes in v13:
time: 105 us; the launch traced here: 104 us
  Pallas kernels  67.5 us (64%)
  starting transfers between devices  19.1 us (18%)
  waiting for transfers between devices  8.72 us (8%)
  other arithmetic  5.94 us (6%)
  matrix products  2.16 us (2%)
    pallas_call x2, Pallas kernels, fused_of(): pl.pallas_call(fused_kernel, grid_spec=pltpu.PrefetchScalarGridSpec(num_s...  30.8 us
    pallas_call x2, Pallas kernels, partials_of(): pl.pallas_call(matmul_kernel, grid_spec=pltpu.PrefetchScalarGridSpec(num_...  26.7 us
    ppermute x8, starting transfers between devices, gather_rows(): got = lax.ppermute(held, 'rows', pairs)  18 us
    ppermute x8, waiting for transfers between devices, gather_rows(): got = lax.ppermute(held, 'rows', pairs)  7.91 us
    pallas_call x1, Pallas kernels, pair_peaks_of(): pl.pallas_call(pair_kernel, grid=(blocks,), in_specs=[pl.BlockSpec((SEG,...  7.13 us
    pallas_call x1, Pallas kernels, slip_of(): pl.pallas_call(slip_kernel, out_shape=jax.ShapeDtypeStruct((sources, scen...  2.89 us
    reduce_sum x1, other arithmetic, body(): jnp.sum(jnp.where(matches, mine_weights[:, :, None], 0.0), axis=1)  2.66 us
    another operation x4, other arithmetic  2.29 us
  transfers between devices with their start and end apart: 12, of which 6 were waited for; matrix products, arithmetic and copies ran while one was open for 7% of the time, Pallas kernels for 49%

profile of v13, /device:TPU:0, one launch (start us, length us, event | category | flops | bytes accessed | tf_op | source)
XLA Modules:
  0.0 104.5 jit_solution(14281112522303463836)
XLA Ops:
  0.0 2.9 %shard_map.73.other_slip_ref.mine_slip_ref = bf16[1000,512]{1,0:T(8,128)(2,1)} custom-call(s32[1000,512]{1,0:T(8,128)} %bitcast.3, f32[8,512]{1,0:T(8,128)} %bitcast.4), custom_call_target="tpu_custom_call" | custom-call | tf_op jit(solution)/shard_map/pallas_call | solution.py:144
  2.9 13.4 %shard_map.76 = (bf16[7680,256]{1,0:T(8,128)(2,1)}, bf16[7680,256]{1,0:T(8,128)(2,1)}) custom-call(s32[1]{0:T(128)} %bitcast.side_ref, bf16[1000,512]{1,0:T(8,128)(2,1)} %shard_map.73.other_slip_ref.mine_slip_ref, bf16[1000,512]{1,0:T(8,128)(2,1)} %shard_map.73.other_slip_ref.mine_slip_ref, bf16[1000,30720]{1,0:T(8,128)(2,1)} %green_ref.7), custom_call_target="tpu_custom_call" | custom-call | flops 7864320000 | bytes 23224320 | tf_op jit(solution)/shard_map/pallas_call | solution.py:34
  16.7 13.3 %shard_map.74 = (bf16[7680,256]{1,0:T(8,128)(2,1)}, bf16[7680,256]{1,0:T(8,128)(2,1)}) custom-call(s32[1]{0:T(128)} %bitcast.side_ref, bf16[1000,512]{1,0:T(8,128)(2,1)} %shard_map.73.other_slip_ref.mine_slip_ref, bf16[1000,512]{1,0:T(8,128)(2,1)} %shard_map.73.other_slip_ref.mine_slip_ref, bf16[1000,30720]{1,0:T(8,128)(2,1)} %green_ref.7), custom_call_target="tpu_custom_call" | custom-call | flops 7864320000 | bytes 23224320 | tf_op jit(solution)/shard_map/pallas_call | solution.py:34
  30.1 15.4 %shard_map.77 = (bf16[7680,256]{1,0:T(8,128)(2,1)}, bf16[7680,256]{1,0:T(8,128)(2,1)}, f32[32,256]{1,0:T(8,128)}) custom-call(s32[1]{0:T(128)} %bitcast.side_ref, bf16[1000,512]{1,0:T(8,128)(2,1)} %shard_map.73.other_slip_ref.mine_slip_ref, bf16[1000,512]{1,0:T(8,128)(2,1)} %shard_map.73.other_slip_ref.mine_slip_ref, bf16[1000,30720]{1,0:T(8,128)(2,1)} %green_ref.7, ...), custom_call_target="tpu_custom_call" | custom-call | flops 7864320000 | bytes 31088640 | tf_op jit(solution)/shard_map/pallas_call | solution.py:68
  46.0 15.4 %shard_map.75 = (bf16[7680,256]{1,0:T(8,128)(2,1)}, bf16[7680,256]{1,0:T(8,128)(2,1)}, f32[32,256]{1,0:T(8,128)}) custom-call(s32[1]{0:T(128)} %bitcast.side_ref, bf16[1000,512]{1,0:T(8,128)(2,1)} %shard_map.73.other_slip_ref.mine_slip_ref, bf16[1000,512]{1,0:T(8,128)(2,1)} %shard_map.73.other_slip_ref.mine_slip_ref, bf16[1000,30720]{1,0:T(8,128)(2,1)} %green_ref.7, ...), custom_call_target="tpu_custom_call" | custom-call | flops 7864320000 | bytes 31088640 | tf_op jit(solution)/shard_map/pallas_call | solution.py:68
  61.4 0.8 dynamic-slice
  62.9 0.8 convert.12
  63.7 4.0 %collective-permute-start.2 = (bf16[64,256]{1,0:T(8,128)(2,1)S(1)}, bf16[64,256]{1,0:T(8,128)(2,1)S(1)}, u32[]{:S(2)}, u32[]{:S(2)}) collective-permute-start(bf16[64,256]{1,0:T(8,128)(2,1)S(1)} %pad_maximum_fusion), channel_id=1, source_target_pairs={{0,8},{1,9},{2,10},{3,11},{4,12},{5,13},{6,14},{7,15},{8,0},{9,1},... | collective-permute-start | bytes 98312 | tf_op jit(solution)/shard_map/ppermute | solution.py:165
  67.7 0.8 collective-permute-done.6.recv_a
  68.5 7.1 %shard_map.78 = (f32[32,256]{1,0:T(8,128)}, f32[32,256]{1,0:T(8,128)}) custom-call(bf16[7680,256]{1,0:T(8,128)(2,1)} %get-tuple-element.23.mine_a, bf16[7680,256]{1,0:T(8,128)(2,1)} %collective-permute-done.6.recv_a, bf16[7680,256]{1,0:T(8,128)(2,1)} %get-tuple-element.25.mine_b, bf16[7680,256]{1,0:T(8,128)(2,1)} %collective-permute-done.7.recv_b), custom_call_target="tpu_custom_call" | custom-call | flops 11796480 | bytes 15728640 | tf_op jit(solution)/shard_map/pallas_call | solution.py:123
  75.6 0.8 convert.14
  76.4 0.8 convert.15
  77.2 3.7 %collective-permute-start.8 = (bf16[64,256]{1,0:T(8,128)(2,1)S(1)}, bf16[64,256]{1,0:T(8,128)(2,1)S(1)}, u32[]{:S(2)}, u32[]{:S(2)}) collective-permute-start(bf16[64,256]{1,0:T(8,128)(2,1)S(1)} %pad_maximum_fusion.1), channel_id=1, source_target_pairs={{0,8},{1,9},{2,10},{3,11},{4,12},{5,13},{6,14},{7,15},{8,0},{9,1},... | collective-permute-start | bytes 98312 | tf_op jit(solution)/shard_map/ppermute | solution.py:165
  80.9 1.6 %collective-permute-start.3 = (bf16[128,256]{1,0:T(8,128)(2,1)S(1)}, bf16[128,256]{1,0:T(8,128)(2,1)S(1)}, u32[]{:S(2)}, u32[]{:S(2)}) collective-permute-start(bf16[128,256]{1,0:T(8,128)(2,1)S(1)} %maximum_select_fusion.8), channel_id=1, source_target_pairs={{0,4},{1,5},{2,6},{3,7},{4,0},{5,1},{6,2},{7,3},{8,12},{9,13},{10,... | collective-permute-start | bytes 196616 | tf_op jit(solution)/shard_map/ppermute | solution.py:165
  82.8 2.2 %collective-permute-start.9 = (bf16[128,256]{1,0:T(8,128)(2,1)S(1)}, bf16[128,256]{1,0:T(8,128)(2,1)S(1)}, u32[]{:S(2)}, u32[]{:S(2)}) collective-permute-start(bf16[128,256]{1,0:T(8,128)(2,1)S(1)} %maximum_select_fusion.9), channel_id=1, source_target_pairs={{0,4},{1,5},{2,6},{3,7},{4,0},{5,1},{6,2},{7,3},{8,12},{9,13},{10,... | collective-permute-start | bytes 196616 | tf_op jit(solution)/shard_map/ppermute | solution.py:165
  85.3 1.8 %collective-permute-start.4 = (bf16[256,256]{1,0:T(8,128)(2,1)S(1)}, bf16[256,256]{1,0:T(8,128)(2,1)S(1)}, u32[]{:S(2)}, u32[]{:S(2)}) collective-permute-start(bf16[256,256]{1,0:T(8,128)(2,1)S(1)} %maximum_select_fusion.6), channel_id=1, source_target_pairs={{0,2},{1,3},{2,0},{3,1},{4,6},{5,7},{6,4},{7,5},{8,10},{9,11},{10,... | collective-permute-start | bytes 393224 | tf_op jit(solution)/shard_map/ppermute | solution.py:165
  87.3 1.7 %collective-permute-start.10 = (bf16[256,256]{1,0:T(8,128)(2,1)S(1)}, bf16[256,256]{1,0:T(8,128)(2,1)S(1)}, u32[]{:S(2)}, u32[]{:S(2)}) collective-permute-start(bf16[256,256]{1,0:T(8,128)(2,1)S(1)} %maximum_select_fusion.7), channel_id=1, source_target_pairs={{0,2},{1,3},{2,0},{3,1},{4,6},{5,7},{6,4},{7,5},{8,10},{9,11},{10,... | collective-permute-start | bytes 393224 | tf_op jit(solution)/shard_map/ppermute | solution.py:165
  89.3 2.0 %collective-permute-done.4 = bf16[256,256]{1,0:T(8,128)(2,1)S(1)} collective-permute-done((bf16[256,256]{1,0:T(8,128)(2,1)S(1)}, bf16[256,256]{1,0:T(8,128)(2,1)S(1)}, u32[]{:S(2)}, u32[]{:S(2)}) %collective-permute-start.4) | collective-permute-done | bytes 131104 | tf_op jit(solution)/shard_map/ppermute | solution.py:165
  91.4 1.5 %collective-permute-start.5 = (bf16[512,256]{1,0:T(8,128)(2,1)S(1)}, bf16[512,256]{1,0:T(8,128)(2,1)S(1)}, u32[]{:S(2)}, u32[]{:S(2)}) collective-permute-start(bf16[512,256]{1,0:T(8,128)(2,1)S(1)} %maximum_select_fusion.4), channel_id=1, source_target_pairs={{0,1},{1,0},{2,3},{3,2},{4,5},{5,4},{6,7},{7,6},{8,9},{9,8},{10,11... | collective-permute-start | bytes 786440 | tf_op jit(solution)/shard_map/ppermute | solution.py:165
  93.1 1.3 %collective-permute-start.11 = (bf16[512,256]{1,0:T(8,128)(2,1)S(1)}, bf16[512,256]{1,0:T(8,128)(2,1)S(1)}, u32[]{:S(2)}, u32[]{:S(2)}) collective-permute-start(bf16[512,256]{1,0:T(8,128)(2,1)S(1)} %maximum_select_fusion.5), channel_id=1, source_target_pairs={{0,1},{1,0},{2,3},{3,2},{4,5},{5,4},{6,7},{7,6},{8,9},{9,8},{10,11... | collective-permute-start | bytes 786440 | tf_op jit(solution)/shard_map/ppermute | solution.py:165
  94.3 2.7 %select_reduce_fusion = f32[128,2048]{1,0:T(8,128)S(1)} fusion(f32[128,8]{1,0:T(8,128)S(1)} %copy.11, s32[2048]{0:T(1024)S(1)} %copy-done.2, s32[128,8]{1,0:T(8,128)S(1)} %copy.10), kind=kLoop, calls=%fused_computation | loop fusion | flops 6029312 | bytes 1064960 | tf_op jit(solution)/shard_map/reduce_sum | solution.py:237
  97.0 5.3 %collective-permute-done.11 = bf16[512,256]{1,0:T(8,128)(2,1)S(1)} collective-permute-done((bf16[512,256]{1,0:T(8,128)(2,1)S(1)}, bf16[512,256]{1,0:T(8,128)(2,1)S(1)}, u32[]{:S(2)}, u32[]{:S(2)}) %collective-permute-start.11) | collective-permute-done | bytes 262176 | tf_op jit(solution)/shard_map/ppermute | solution.py:165
  102.3 0.7 fusion
  103.0 1.4 %convolution_add_fusion = f32[256,128]{1,0:T(8,128)} fusion(f32[256,128]{1,0:T(8,128)S(1)} %fusion, f32[128,2048]{1,0:T(8,128)S(1)} %select_reduce_fusion, bf16[512,256]{1,0:T(8,128)(2,1)S(1)} %maximum_select_fusion.4, bf16[512,256]{1,0:T(8,128)(2,1)S(1)} %collective-permute-done.5, pred[]{:T(512)S(6)} %ne.16), kind=kOutput, calls=%fused_computation.1 | convolution fusion | flops 405045248 | bytes 1310721 | tf_op jit(solution)/shard_map/dot_general | solution.py:242
  (32 shorter events, 2.9 us)
Async XLA Ops:
  0.0 89.1 %copy-start = (s32[2048,8]{0,1:T(8,128)S(1)}, s32[2048,8]{0,1:T(8,128)}, u32[]{:S(2)}) copy-start(s32[2048,8]{0,1:T(8,128)} %param.10) | copy-start | bytes 196612
  16.3 13.8 %collective-permute-start.1 = (bf16[7680,256]{1,0:T(8,128)(2,1)}, bf16[7680,256]{1,0:T(8,128)(2,1)}, u32[]{:S(2)}, u32[]{:S(2)}) collective-permute-start(bf16[7680,256]{1,0:T(8,128)(2,1)} %get-tuple-element.21), channel_id=1, source_target_pairs={{0,16},{16,0},{1,17},{17,1},{2,18},{18,2},{3,19},{19,3},{4,20},{20... | collective-permute-start | bytes 11796488 | tf_op jit(solution)/shard_map/ppermute | solution.py:208
  30.1 15.9 %collective-permute-start = (bf16[7680,256]{1,0:T(8,128)(2,1)}, bf16[7680,256]{1,0:T(8,128)(2,1)}, u32[]{:S(2)}, u32[]{:S(2)}) collective-permute-start(bf16[7680,256]{1,0:T(8,128)(2,1)} %get-tuple-element.18), channel_id=1, source_target_pairs={{0,16},{16,0},{1,17},{17,1},{2,18},{18,2},{3,19},{19,3},{4,20},{20... | collective-permute-start | bytes 11796488 | tf_op jit(solution)/shard_map/ppermute | solution.py:208
  45.5 22.2 %collective-permute-start.7 = (bf16[7680,256]{1,0:T(8,128)(2,1)}, bf16[7680,256]{1,0:T(8,128)(2,1)}, u32[]{:S(2)}, u32[]{:S(2)}) collective-permute-start(bf16[7680,256]{1,0:T(8,128)(2,1)} %get-tuple-element.26), channel_id=1, source_target_pairs={{0,16},{16,0},{1,17},{17,1},{2,18},{18,2},{3,19},{19,3},{4,20},{20... | collective-permute-start | bytes 11796488 | tf_op jit(solution)/shard_map/ppermute | solution.py:208
  46.0 16.9 %copy-start.1 = (f32[32,256]{1,0:T(8,128)S(1)}, f32[32,256]{1,0:T(8,128)}, u32[]{:S(2)}) copy-start(f32[32,256]{1,0:T(8,128)} %get-tuple-element.22) | copy-start | bytes 98308
  61.4 7.1 %collective-permute-start.6 = (bf16[7680,256]{1,0:T(8,128)(2,1)}, bf16[7680,256]{1,0:T(8,128)(2,1)}, u32[]{:S(2)}, u32[]{:S(2)}) collective-permute-start(bf16[7680,256]{1,0:T(8,128)(2,1)} %get-tuple-element.24), channel_id=1, source_target_pairs={{0,16},{16,0},{1,17},{17,1},{2,18},{18,2},{3,19},{19,3},{4,20},{20... | collective-permute-start | bytes 11796488 | tf_op jit(solution)/shard_map/ppermute | solution.py:208
  63.7 17.2 %collective-permute-start.2 = (bf16[64,256]{1,0:T(8,128)(2,1)S(1)}, bf16[64,256]{1,0:T(8,128)(2,1)S(1)}, u32[]{:S(2)}, u32[]{:S(2)}) collective-permute-start(bf16[64,256]{1,0:T(8,128)(2,1)S(1)} %pad_maximum_fusion), channel_id=1, source_target_pairs={{0,8},{1,9},{2,10},{3,11},{4,12},{5,13},{6,14},{7,15},{8,0},{9,1},... | collective-permute-start | bytes 98312 | tf_op jit(solution)/shard_map/ppermute | solution.py:165
  68.5 25.8 %copy-start.2 = (s32[2048]{0:T(1024)S(1)}, s32[2048]{0:T(1024)}, u32[]{:S(2)}) copy-start(s32[2048]{0:T(1024)} %constant.28.clone) | copy-start | bytes 24580
  77.2 5.6 %collective-permute-start.8 = (bf16[64,256]{1,0:T(8,128)(2,1)S(1)}, bf16[64,256]{1,0:T(8,128)(2,1)S(1)}, u32[]{:S(2)}, u32[]{:S(2)}) collective-permute-start(bf16[64,256]{1,0:T(8,128)(2,1)S(1)} %pad_maximum_fusion.1), channel_id=1, source_target_pairs={{0,8},{1,9},{2,10},{3,11},{4,12},{5,13},{6,14},{7,15},{8,0},{9,1},... | collective-permute-start | bytes 98312 | tf_op jit(solution)/shard_map/ppermute | solution.py:165
  80.9 4.3 %collective-permute-start.3 = (bf16[128,256]{1,0:T(8,128)(2,1)S(1)}, bf16[128,256]{1,0:T(8,128)(2,1)S(1)}, u32[]{:S(2)}, u32[]{:S(2)}) collective-permute-start(bf16[128,256]{1,0:T(8,128)(2,1)S(1)} %maximum_select_fusion.8), channel_id=1, source_target_pairs={{0,4},{1,5},{2,6},{3,7},{4,0},{5,1},{6,2},{7,3},{8,12},{9,13},{10,... | collective-permute-start | bytes 196616 | tf_op jit(solution)/shard_map/ppermute | solution.py:165
  82.8 4.5 %collective-permute-start.9 = (bf16[128,256]{1,0:T(8,128)(2,1)S(1)}, bf16[128,256]{1,0:T(8,128)(2,1)S(1)}, u32[]{:S(2)}, u32[]{:S(2)}) collective-permute-start(bf16[128,256]{1,0:T(8,128)(2,1)S(1)} %maximum_select_fusion.9), channel_id=1, source_target_pairs={{0,4},{1,5},{2,6},{3,7},{4,0},{5,1},{6,2},{7,3},{8,12},{9,13},{10,... | collective-permute-start | bytes 196616 | tf_op jit(solution)/shard_map/ppermute | solution.py:165
  85.3 6.0 %collective-permute-start.4 = (bf16[256,256]{1,0:T(8,128)(2,1)S(1)}, bf16[256,256]{1,0:T(8,128)(2,1)S(1)}, u32[]{:S(2)}, u32[]{:S(2)}) collective-permute-start(bf16[256,256]{1,0:T(8,128)(2,1)S(1)} %maximum_select_fusion.6), channel_id=1, source_target_pairs={{0,2},{1,3},{2,0},{3,1},{4,6},{5,7},{6,4},{7,5},{8,10},{9,11},{10,... | collective-permute-start | bytes 393224 | tf_op jit(solution)/shard_map/ppermute | solution.py:165
  87.3 5.6 %collective-permute-start.10 = (bf16[256,256]{1,0:T(8,128)(2,1)S(1)}, bf16[256,256]{1,0:T(8,128)(2,1)S(1)}, u32[]{:S(2)}, u32[]{:S(2)}) collective-permute-start(bf16[256,256]{1,0:T(8,128)(2,1)S(1)} %maximum_select_fusion.7), channel_id=1, source_target_pairs={{0,2},{1,3},{2,0},{3,1},{4,6},{5,7},{6,4},{7,5},{8,10},{9,11},{10,... | collective-permute-start | bytes 393224 | tf_op jit(solution)/shard_map/ppermute | solution.py:165
  91.4 11.6 %collective-permute-start.5 = (bf16[512,256]{1,0:T(8,128)(2,1)S(1)}, bf16[512,256]{1,0:T(8,128)(2,1)S(1)}, u32[]{:S(2)}, u32[]{:S(2)}) collective-permute-start(bf16[512,256]{1,0:T(8,128)(2,1)S(1)} %maximum_select_fusion.4), channel_id=1, source_target_pairs={{0,1},{1,0},{2,3},{3,2},{4,5},{5,4},{6,7},{7,6},{8,9},{9,8},{10,11... | collective-permute-start | bytes 786440 | tf_op jit(solution)/shard_map/ppermute | solution.py:165
  93.1 9.2 %collective-permute-start.11 = (bf16[512,256]{1,0:T(8,128)(2,1)S(1)}, bf16[512,256]{1,0:T(8,128)(2,1)S(1)}, u32[]{:S(2)}, u32[]{:S(2)}) collective-permute-start(bf16[512,256]{1,0:T(8,128)(2,1)S(1)} %maximum_select_fusion.5), channel_id=1, source_target_pairs={{0,1},{1,0},{2,3},{3,2},{4,5},{5,4},{6,7},{7,6},{8,9},{9,8},{10,11... | collective-permute-start | bytes 786440 | tf_op jit(solution)/shard_map/ppermute | solution.py:165

commit v14 on v11

--- a/solution.py
+++ b/solution.py
@@ -147,6 +147,29 @@
             upper, jnp.concatenate([got, held], 0), jnp.concatenate([held, got], 0)
         )
     return held.astype(jnp.float32)
+
+
+def fan_levels(owners):
+    levels, span = [], 1
+    while span < owners:
+        levels.append([d * span for d in range(1, 4) if d * span < owners])
+        span *= 4
+    return levels
+
+
+def gather_fan(block, owners):
+    held = block.astype(jnp.bfloat16)
+    for masks in fan_levels(owners):
+        got = [lax.ppermute(held, "rows", [(k, k ^ m) for k in range(owners)]) for m in masks]
+        held = jnp.concatenate([held] + got, 0)
+    return held.astype(jnp.float32)
+
+
+def fan_offsets(owners):
+    offsets = [0]
+    for masks in fan_levels(owners):
+        offsets = offsets + [x ^ m for m in masks for x in offsets]
+    return offsets
 
 
 def arrival_order(owners):
@@ -191,12 +214,18 @@
     split = (chunks + 1) // 2
     bundles = [list(range(split)), list(range(split, chunks))] if chunks > 1 else [[0]]
     pieces, ids = [], []
-    for bundle in bundles:
+    row_me = lax.axis_index("rows")
+    for b, bundle in enumerate(bundles):
         joined = jnp.concatenate([peaks[c] for c in bundle], 0) if len(bundle) > 1 else peaks[bundle[0]]
-        pieces.append(gather_rows(joined, owners))
         local = np.concatenate([c * per_chunk + np.arange(per_chunk) for c in bundle])
-        ids.append((np.asarray(order)[:, None] * gauges_here + local[None, :]).reshape(-1))
-    gauge_ids = jnp.asarray(np.concatenate(ids).astype(np.int32))
+        if b == len(bundles) - 1 and len(bundles) > 1:
+            pieces.append(gather_fan(joined, owners))
+            sources_at = jnp.bitwise_xor(row_me, jnp.asarray(np.asarray(fan_offsets(owners), np.int32)))
+            ids.append((sources_at[:, None] * gauges_here + jnp.asarray(local.astype(np.int32))[None, :]).reshape(-1))
+        else:
+            pieces.append(gather_rows(joined, owners))
+            ids.append(jnp.asarray((np.asarray(order)[:, None] * gauges_here + local[None, :]).reshape(-1).astype(np.int32)))
+    gauge_ids = jnp.concatenate(ids)
 
     tile_total = coast_gauges.shape[0]
     slot_count = coast_gauges.shape[1]

time: 105 us -> 111 us (1.057)
  waiting for transfers between devices: 9.93 us -> 14 us
  starting transfers between devices: 15 us -> 17.6 us
    ppermute x0 -> x6, waiting for transfers between devices: none -> 10 us  [gather_fan(): lax.ppermute(held, 'rows', [(k, k ^ m) for k in range(owners)])]
    ppermute x0 -> x6, starting transfers between devices: none -> 7.6 us  [gather_fan(): lax.ppermute(held, 'rows', [(k, k ^ m) for k in range(owners)])]
    ppermute x8 -> x4, waiting for transfers between devices: 9.92 us -> 3.98 us  [gather_rows(): got = lax.ppermute(held, 'rows', pairs)]
    ppermute x8 -> x4, starting transfers between devices: 13.9 us -> 8.94 us  [gather_rows(): got = lax.ppermute(held, 'rows', pairs)]
    unnamed x0 -> x2, other arithmetic: none -> 1.52 us
    another operation x4 -> x2, other arithmetic: 2.29 us -> 0.77 us
  transfers between devices with their start and end apart: 12 -> 14, of which waited for: 5 -> 7; matrix products, arithmetic and copies ran while one was open for 7% -> 7% of each run, Pallas kernels for 52% -> 49%
where the time goes in v14:
time: 111 us
  Pallas kernels  70 us (63%)
  starting transfers between devices  17.6 us (16%)
  waiting for transfers between devices  14 us (13%)
  other arithmetic  5.87 us (5%)
  matrix products  2.11 us (2%)
    pallas_call x2, Pallas kernels, fused_of(): pl.pallas_call(fused_kernel, grid_spec=pltpu.PrefetchScalarGridSpec(num_s...  30.7 us
    pallas_call x2, Pallas kernels, partials_of(): pl.pallas_call(matmul_kernel, grid_spec=pltpu.PrefetchScalarGridSpec(num_...  26.8 us
    ppermute x6, waiting for transfers between devices, gather_fan(): lax.ppermute(held, 'rows', [(k, k ^ m) for k in range(owners)])  10 us
    pallas_call x2, Pallas kernels, peaks_of(): pl.pallas_call(peak_kernel, grid=(blocks,), in_specs=[pl.BlockSpec((SEG,...  9.64 us
    ppermute x4, starting transfers between devices, gather_rows(): got = lax.ppermute(held, 'rows', pairs)  8.94 us
    ppermute x6, starting transfers between devices, gather_fan(): lax.ppermute(held, 'rows', [(k, k ^ m) for k in range(owners)])  7.6 us
    ppermute x4, waiting for transfers between devices, gather_rows(): got = lax.ppermute(held, 'rows', pairs)  3.98 us
    pallas_call x1, Pallas kernels, slip_of(): pl.pallas_call(slip_kernel, out_shape=jax.ShapeDtypeStruct((sources, scen...  2.86 us
  transfers between devices with their start and end apart: 14, of which 7 were waited for; matrix products, arithmetic and copies ran while one was open for 7% of the time, Pallas kernels for 49%

profile of v14, /device:TPU:0, one launch (start us, length us, event | category | flops | bytes accessed | tf_op | source)
XLA Modules:
  0.0 110.8 jit_solution(8207177342927023931)
XLA Ops:
  0.0 2.9 %shard_map.91.other_slip_ref.mine_slip_ref = bf16[1000,512]{1,0:T(8,128)(2,1)} custom-call(s32[1000,512]{1,0:T(8,128)} %bitcast.4, f32[8,512]{1,0:T(8,128)} %bitcast.5), custom_call_target="tpu_custom_call" | custom-call | tf_op jit(solution)/shard_map/pallas_call | solution.py:123
  2.9 13.4 %shard_map.92 = (bf16[7680,256]{1,0:T(8,128)(2,1)}, bf16[7680,256]{1,0:T(8,128)(2,1)}) custom-call(s32[1]{0:T(128)} %bitcast.side_ref, bf16[1000,512]{1,0:T(8,128)(2,1)} %shard_map.91.other_slip_ref.mine_slip_ref, bf16[1000,512]{1,0:T(8,128)(2,1)} %shard_map.91.other_slip_ref.mine_slip_ref, bf16[1000,30720]{1,0:T(8,128)(2,1)} %green_ref.7), custom_call_target="tpu_custom_call" | custom-call | flops 7864320000 | bytes 23224320 | tf_op jit(solution)/shard_map/pallas_call | solution.py:34
  16.7 13.4 %shard_map.94 = (bf16[7680,256]{1,0:T(8,128)(2,1)}, bf16[7680,256]{1,0:T(8,128)(2,1)}) custom-call(s32[1]{0:T(128)} %bitcast.side_ref, bf16[1000,512]{1,0:T(8,128)(2,1)} %shard_map.91.other_slip_ref.mine_slip_ref, bf16[1000,512]{1,0:T(8,128)(2,1)} %shard_map.91.other_slip_ref.mine_slip_ref, bf16[1000,30720]{1,0:T(8,128)(2,1)} %green_ref.7), custom_call_target="tpu_custom_call" | custom-call | flops 7864320000 | bytes 23224320 | tf_op jit(solution)/shard_map/pallas_call | solution.py:34
  30.1 15.3 %shard_map.93 = (bf16[7680,256]{1,0:T(8,128)(2,1)}, bf16[7680,256]{1,0:T(8,128)(2,1)}, f32[32,256]{1,0:T(8,128)}) custom-call(s32[1]{0:T(128)} %bitcast.side_ref, bf16[1000,512]{1,0:T(8,128)(2,1)} %shard_map.91.other_slip_ref.mine_slip_ref, bf16[1000,512]{1,0:T(8,128)(2,1)} %shard_map.91.other_slip_ref.mine_slip_ref, bf16[1000,30720]{1,0:T(8,128)(2,1)} %green_ref.7, ...), custom_call_target="tpu_custom_call" | custom-call | flops 7864320000 | bytes 31088640 | tf_op jit(solution)/shard_map/pallas_call | solution.py:68
  45.9 15.4 %shard_map.95 = (bf16[7680,256]{1,0:T(8,128)(2,1)}, bf16[7680,256]{1,0:T(8,128)(2,1)}, f32[32,256]{1,0:T(8,128)}) custom-call(s32[1]{0:T(128)} %bitcast.side_ref, bf16[1000,512]{1,0:T(8,128)(2,1)} %shard_map.91.other_slip_ref.mine_slip_ref, bf16[1000,512]{1,0:T(8,128)(2,1)} %shard_map.91.other_slip_ref.mine_slip_ref, bf16[1000,30720]{1,0:T(8,128)(2,1)} %green_ref.7, ...), custom_call_target="tpu_custom_call" | custom-call | flops 7864320000 | bytes 31088640 | tf_op jit(solution)/shard_map/pallas_call | solution.py:68
  62.9 0.8 convert.13
  63.7 4.1 %collective-permute-start.2 = (bf16[64,256]{1,0:T(8,128)(2,1)S(1)}, bf16[64,256]{1,0:T(8,128)(2,1)S(1)}, u32[]{:S(2)}, u32[]{:S(2)}) collective-permute-start(bf16[64,256]{1,0:T(8,128)(2,1)S(1)} %pad_maximum_fusion), channel_id=1, source_target_pairs={{0,8},{1,9},{2,10},{3,11},{4,12},{5,13},{6,14},{7,15},{8,0},{9,1},... | collective-permute-start | bytes 98312 | tf_op jit(solution)/shard_map/ppermute | solution.py:144
  68.1 1.6 %collective-permute-done.2 = bf16[64,256]{1,0:T(8,128)(2,1)S(1)} collective-permute-done((bf16[64,256]{1,0:T(8,128)(2,1)S(1)}, bf16[64,256]{1,0:T(8,128)(2,1)S(1)}, u32[]{:S(2)}, u32[]{:S(2)}) %collective-permute-start.2) | collective-permute-done | bytes 32800 | tf_op jit(solution)/shard_map/ppermute | solution.py:144
  69.7 2.0 %collective-permute-start.3 = (bf16[128,256]{1,0:T(8,128)(2,1)S(1)}, bf16[128,256]{1,0:T(8,128)(2,1)S(1)}, u32[]{:S(2)}, u32[]{:S(2)}) collective-permute-start(bf16[128,256]{1,0:T(8,128)(2,1)S(1)} %maximum_select_fusion.4), channel_id=1, source_target_pairs={{0,4},{1,5},{2,6},{3,7},{4,0},{5,1},{6,2},{7,3},{8,12},{9,13},{10,... | collective-permute-start | bytes 196616 | tf_op jit(solution)/shard_map/ppermute | solution.py:144
  71.7 2.4 %collective-permute-done.3 = bf16[128,256]{1,0:T(8,128)(2,1)S(1)} collective-permute-done((bf16[128,256]{1,0:T(8,128)(2,1)S(1)}, bf16[128,256]{1,0:T(8,128)(2,1)S(1)}, u32[]{:S(2)}, u32[]{:S(2)}) %collective-permute-start.3) | collective-permute-done | bytes 65568 | tf_op jit(solution)/shard_map/ppermute | solution.py:144
  74.1 2.3 %collective-permute-start.4 = (bf16[256,256]{1,0:T(8,128)(2,1)S(1)}, bf16[256,256]{1,0:T(8,128)(2,1)S(1)}, u32[]{:S(2)}, u32[]{:S(2)}) collective-permute-start(bf16[256,256]{1,0:T(8,128)(2,1)S(1)} %maximum_select_fusion.3), channel_id=1, source_target_pairs={{0,2},{1,3},{2,0},{3,1},{4,6},{5,7},{6,4},{7,5},{8,10},{9,11},{10,... | collective-permute-start | bytes 393224 | tf_op jit(solution)/shard_map/ppermute | solution.py:144
  76.3 4.8 %shard_map.96 = f32[32,256]{1,0:T(8,128)} custom-call(bf16[7680,256]{1,0:T(8,128)(2,1)} %get-tuple-element.21.mine_ref, bf16[7680,256]{1,0:T(8,128)(2,1)} %collective-permute-done.6.recv_ref), custom_call_target="tpu_custom_call" | custom-call | flops 5898240 | bytes 7864320 | tf_op jit(solution)/shard_map/pallas_call | solution.py:102
  81.2 0.8 constant_dynamic-update-slice_fusion.4
  81.9 4.8 %shard_map.97 = f32[32,256]{1,0:T(8,128)} custom-call(bf16[7680,256]{1,0:T(8,128)(2,1)} %get-tuple-element.23.mine_ref, bf16[7680,256]{1,0:T(8,128)(2,1)} %collective-permute-done.7.recv_ref), custom_call_target="tpu_custom_call" | custom-call | flops 5898240 | bytes 7864320 | tf_op jit(solution)/shard_map/pallas_call | solution.py:102
  87.5 1.5 %collective-permute-start.8 = (bf16[64,256]{1,0:T(8,128)(2,1)S(1)}, bf16[64,256]{1,0:T(8,128)(2,1)S(1)}, u32[]{:S(2)}, u32[]{:S(2)}) collective-permute-start(bf16[64,256]{1,0:T(8,128)(2,1)S(1)} %pad_maximum_fusion.1), channel_id=1, source_target_pairs={{0,1},{1,0},{2,3},{3,2},{4,5},{5,4},{6,7},{7,6},{8,9},{9,8},{10,11... | collective-permute-start | bytes 98312 | tf_op jit(solution)/shard_map/ppermute | solution.py:163
  89.5 1.5 %collective-permute-start.10 = (bf16[64,256]{1,0:T(8,128)(2,1)S(1)}, bf16[64,256]{1,0:T(8,128)(2,1)S(1)}, u32[]{:S(2)}, u32[]{:S(2)}) collective-permute-start(bf16[64,256]{1,0:T(8,128)(2,1)S(1)} %pad_maximum_fusion.1), channel_id=1, source_target_pairs={{0,3},{1,2},{2,1},{3,0},{4,7},{5,6},{6,5},{7,4},{8,11},{9,10},{10,... | collective-permute-start | bytes 98312 | tf_op jit(solution)/shard_map/ppermute | solution.py:163
  91.4 1.5 %collective-permute-done.9 = bf16[64,256]{1,0:T(8,128)(2,1)S(1)} collective-permute-done((bf16[64,256]{1,0:T(8,128)(2,1)S(1)}, bf16[64,256]{1,0:T(8,128)(2,1)S(1)}, u32[]{:S(2)}, u32[]{:S(2)}) %collective-permute-start.9) | collective-permute-done | bytes 32800 | tf_op jit(solution)/shard_map/ppermute | solution.py:163
  92.9 1.4 %collective-permute-done.10 = bf16[64,256]{1,0:T(8,128)(2,1)S(1)} collective-permute-done((bf16[64,256]{1,0:T(8,128)(2,1)S(1)}, bf16[64,256]{1,0:T(8,128)(2,1)S(1)}, u32[]{:S(2)}, u32[]{:S(2)}) %collective-permute-start.10) | collective-permute-done | bytes 32800 | tf_op jit(solution)/shard_map/ppermute | solution.py:163
  94.3 1.2 %collective-permute-start.11 = (bf16[256,256]{1,0:T(8,128)(2,1)S(1)}, bf16[256,256]{1,0:T(8,128)(2,1)S(1)}, u32[]{:S(2)}, u32[]{:S(2)}) collective-permute-start(bf16[256,256]{1,0:T(8,128)(2,1)S(1)} %get-tuple-element.29), channel_id=1, source_target_pairs={{0,4},{1,5},{2,6},{3,7},{4,0},{5,1},{6,2},{7,3},{8,12},{9,13},{10,... | collective-permute-start | bytes 393224 | tf_op jit(solution)/shard_map/ppermute | solution.py:163
  95.6 2.7 %select_reduce_fusion = f32[128,2048]{1,0:T(8,128)S(1)} fusion(f32[128,8]{1,0:T(8,128)S(1)} %copy.13, s32[2048]{0:T(1024)S(1)} %pad_add_fusion, s32[128,8]{1,0:T(8,128)S(1)} %copy.12), kind=kLoop, calls=%fused_computation | loop fusion | flops 6029312 | bytes 1064960 | tf_op jit(solution)/shard_map/reduce_sum | solution.py:239
  98.2 2.9 %collective-permute-start.12 = (bf16[256,256]{1,0:T(8,128)(2,1)S(1)}, bf16[256,256]{1,0:T(8,128)(2,1)S(1)}, u32[]{:S(2)}, u32[]{:S(2)}) collective-permute-start(bf16[256,256]{1,0:T(8,128)(2,1)S(1)} %get-tuple-element.29), channel_id=1, source_target_pairs={{0,8},{1,9},{2,10},{3,11},{4,12},{5,13},{6,14},{7,15},{8,0},{9,1},... | collective-permute-start | bytes 393224 | tf_op jit(solution)/shard_map/ppermute | solution.py:163
  101.9 3.8 %collective-permute-done.12 = bf16[256,256]{1,0:T(8,128)(2,1)S(1)} collective-permute-done((bf16[256,256]{1,0:T(8,128)(2,1)S(1)}, bf16[256,256]{1,0:T(8,128)(2,1)S(1)}, u32[]{:S(2)}, u32[]{:S(2)}) %collective-permute-start.12) | collective-permute-done | bytes 131104 | tf_op jit(solution)/shard_map/ppermute | solution.py:163
  105.7 2.9 %collective-permute-done.13 = bf16[256,256]{1,0:T(8,128)(2,1)S(1)} collective-permute-done((bf16[256,256]{1,0:T(8,128)(2,1)S(1)}, bf16[256,256]{1,0:T(8,128)(2,1)S(1)}, u32[]{:S(2)}, u32[]{:S(2)}) %collective-permute-start.13) | collective-permute-done | bytes 131104 | tf_op jit(solution)/shard_map/ppermute | solution.py:163
  109.3 1.4 %convolution_add_fusion = f32[256,128]{1,0:T(8,128)} fusion(f32[256,128]{1,0:T(8,128)S(1)} %fusion, f32[128,2048]{1,0:T(8,128)S(1)} %select_reduce_fusion, bf16[512,256]{1,0:T(8,128)(2,1)S(1)} %maximum_select_fusion.2, bf16[512,256]{1,0:T(8,128)(2,1)S(1)} %collective-permute-done.5, pred[]{:T(512)S(6)} %ne.12), kind=kOutput, calls=%fused_computation.1 | convolution fusion | flops 405045248 | bytes 1310721 | tf_op jit(solution)/shard_map/dot_general | solution.py:244
  (48 shorter events, 6.0 us)
Async XLA Ops:
  0.0 67.8 %copy-start = (s32[2048,8]{0,1:T(8,128)S(1)}, s32[2048,8]{0,1:T(8,128)}, u32[]{:S(2)}) copy-start(s32[2048,8]{0,1:T(8,128)} %param.12) | copy-start | bytes 196612
  16.2 13.9 %collective-permute-start = (bf16[7680,256]{1,0:T(8,128)(2,1)}, bf16[7680,256]{1,0:T(8,128)(2,1)}, u32[]{:S(2)}, u32[]{:S(2)}) collective-permute-start(bf16[7680,256]{1,0:T(8,128)(2,1)} %get-tuple-element.16), channel_id=1, source_target_pairs={{0,16},{16,0},{1,17},{17,1},{2,18},{18,2},{3,19},{19,3},{4,20},{20... | collective-permute-start | bytes 11796488 | tf_op jit(solution)/shard_map/ppermute | solution.py:210
  30.1 15.9 %collective-permute-start.1 = (bf16[7680,256]{1,0:T(8,128)(2,1)}, bf16[7680,256]{1,0:T(8,128)(2,1)}, u32[]{:S(2)}, u32[]{:S(2)}) collective-permute-start(bf16[7680,256]{1,0:T(8,128)(2,1)} %get-tuple-element.19), channel_id=1, source_target_pairs={{0,16},{16,0},{1,17},{17,1},{2,18},{18,2},{3,19},{19,3},{4,20},{20... | collective-permute-start | bytes 11796488 | tf_op jit(solution)/shard_map/ppermute | solution.py:210
  45.5 30.9 %collective-permute-start.6 = (bf16[7680,256]{1,0:T(8,128)(2,1)}, bf16[7680,256]{1,0:T(8,128)(2,1)}, u32[]{:S(2)}, u32[]{:S(2)}) collective-permute-start(bf16[7680,256]{1,0:T(8,128)(2,1)} %get-tuple-element.22), channel_id=1, source_target_pairs={{0,16},{16,0},{1,17},{17,1},{2,18},{18,2},{3,19},{19,3},{4,20},{20... | collective-permute-start | bytes 11796488 | tf_op jit(solution)/shard_map/ppermute | solution.py:210
  45.9 16.9 %copy-start.3 = (s32[64]{0:T(128)S(1)}, s32[64]{0:T(128)}, u32[]{:S(2)}) copy-start(s32[64]{0:T(128)} %constant.34.clone) | copy-start | bytes 772
  45.9 17.8 %copy-start.1 = (f32[32,256]{1,0:T(8,128)S(1)}, f32[32,256]{1,0:T(8,128)}, u32[]{:S(2)}) copy-start(f32[32,256]{1,0:T(8,128)} %get-tuple-element.17) | copy-start | bytes 98308
  45.9 25.8 %copy-start.2 = (s32[1024]{0:T(1024)S(1)}, s32[1024]{0:T(1024)}, u32[]{:S(2)}) copy-start(s32[1024]{0:T(1024)} %constant.33.clone) | copy-start | bytes 12292
  61.3 20.6 %collective-permute-start.7 = (bf16[7680,256]{1,0:T(8,128)(2,1)}, bf16[7680,256]{1,0:T(8,128)(2,1)}, u32[]{:S(2)}, u32[]{:S(2)}) collective-permute-start(bf16[7680,256]{1,0:T(8,128)(2,1)} %get-tuple-element.24), channel_id=1, source_target_pairs={{0,16},{16,0},{1,17},{17,1},{2,18},{18,2},{3,19},{19,3},{4,20},{20... | collective-permute-start | bytes 11796488 | tf_op jit(solution)/shard_map/ppermute | solution.py:210
  63.7 6.0 %collective-permute-start.2 = (bf16[64,256]{1,0:T(8,128)(2,1)S(1)}, bf16[64,256]{1,0:T(8,128)(2,1)S(1)}, u32[]{:S(2)}, u32[]{:S(2)}) collective-permute-start(bf16[64,256]{1,0:T(8,128)(2,1)S(1)} %pad_maximum_fusion), channel_id=1, source_target_pairs={{0,8},{1,9},{2,10},{3,11},{4,12},{5,13},{6,14},{7,15},{8,0},{9,1},... | collective-permute-start | bytes 98312 | tf_op jit(solution)/shard_map/ppermute | solution.py:144
  69.7 4.3 %collective-permute-start.3 = (bf16[128,256]{1,0:T(8,128)(2,1)S(1)}, bf16[128,256]{1,0:T(8,128)(2,1)S(1)}, u32[]{:S(2)}, u32[]{:S(2)}) collective-permute-start(bf16[128,256]{1,0:T(8,128)(2,1)S(1)} %maximum_select_fusion.4), channel_id=1, source_target_pairs={{0,4},{1,5},{2,6},{3,7},{4,0},{5,1},{6,2},{7,3},{8,12},{9,13},{10,... | collective-permute-start | bytes 196616 | tf_op jit(solution)/shard_map/ppermute | solution.py:144
  74.1 27.1 %collective-permute-start.4 = (bf16[256,256]{1,0:T(8,128)(2,1)S(1)}, bf16[256,256]{1,0:T(8,128)(2,1)S(1)}, u32[]{:S(2)}, u32[]{:S(2)}) collective-permute-start(bf16[256,256]{1,0:T(8,128)(2,1)S(1)} %maximum_select_fusion.3), channel_id=1, source_target_pairs={{0,2},{1,3},{2,0},{3,1},{4,6},{5,7},{6,4},{7,5},{8,10},{9,11},{10,... | collective-permute-start | bytes 393224 | tf_op jit(solution)/shard_map/ppermute | solution.py:144
  87.5 3.9 %collective-permute-start.8 = (bf16[64,256]{1,0:T(8,128)(2,1)S(1)}, bf16[64,256]{1,0:T(8,128)(2,1)S(1)}, u32[]{:S(2)}, u32[]{:S(2)}) collective-permute-start(bf16[64,256]{1,0:T(8,128)(2,1)S(1)} %pad_maximum_fusion.1), channel_id=1, source_target_pairs={{0,1},{1,0},{2,3},{3,2},{4,5},{5,4},{6,7},{7,6},{8,9},{9,8},{10,11... | collective-permute-start | bytes 98312 | tf_op jit(solution)/shard_map/ppermute | solution.py:163
  89.0 3.9 %collective-permute-start.9 = (bf16[64,256]{1,0:T(8,128)(2,1)S(1)}, bf16[64,256]{1,0:T(8,128)(2,1)S(1)}, u32[]{:S(2)}, u32[]{:S(2)}) collective-permute-start(bf16[64,256]{1,0:T(8,128)(2,1)S(1)} %pad_maximum_fusion.1), channel_id=1, source_target_pairs={{0,2},{1,3},{2,0},{3,1},{4,6},{5,7},{6,4},{7,5},{8,10},{9,11},{10,... | collective-permute-start | bytes 98312 | tf_op jit(solution)/shard_map/ppermute | solution.py:163
  89.5 4.8 %collective-permute-start.10 = (bf16[64,256]{1,0:T(8,128)(2,1)S(1)}, bf16[64,256]{1,0:T(8,128)(2,1)S(1)}, u32[]{:S(2)}, u32[]{:S(2)}) collective-permute-start(bf16[64,256]{1,0:T(8,128)(2,1)S(1)} %pad_maximum_fusion.1), channel_id=1, source_target_pairs={{0,3},{1,2},{2,1},{3,0},{4,7},{5,6},{6,5},{7,4},{8,11},{9,10},{10,... | collective-permute-start | bytes 98312 | tf_op jit(solution)/shard_map/ppermute | solution.py:163
  94.3 7.5 %collective-permute-start.11 = (bf16[256,256]{1,0:T(8,128)(2,1)S(1)}, bf16[256,256]{1,0:T(8,128)(2,1)S(1)}, u32[]{:S(2)}, u32[]{:S(2)}) collective-permute-start(bf16[256,256]{1,0:T(8,128)(2,1)S(1)} %get-tuple-element.29), channel_id=1, source_target_pairs={{0,4},{1,5},{2,6},{3,7},{4,0},{5,1},{6,2},{7,3},{8,12},{9,13},{10,... | collective-permute-start | bytes 393224 | tf_op jit(solution)/shard_map/ppermute | solution.py:163
  98.2 7.4 %collective-permute-start.12 = (bf16[256,256]{1,0:T(8,128)(2,1)S(1)}, bf16[256,256]{1,0:T(8,128)(2,1)S(1)}, u32[]{:S(2)}, u32[]{:S(2)}) collective-permute-start(bf16[256,256]{1,0:T(8,128)(2,1)S(1)} %get-tuple-element.29), channel_id=1, source_target_pairs={{0,8},{1,9},{2,10},{3,11},{4,12},{5,13},{6,14},{7,15},{8,0},{9,1},... | collective-permute-start | bytes 393224 | tf_op jit(solution)/shard_map/ppermute | solution.py:163
  101.2 8.1 %collective-permute-start.5 = (bf16[512,256]{1,0:T(8,128)(2,1)S(1)}, bf16[512,256]{1,0:T(8,128)(2,1)S(1)}, u32[]{:S(2)}, u32[]{:S(2)}) collective-permute-start(bf16[512,256]{1,0:T(8,128)(2,1)S(1)} %maximum_select_fusion.2), channel_id=1, source_target_pairs={{0,1},{1,0},{2,3},{3,2},{4,5},{5,4},{6,7},{7,6},{8,9},{9,8},{10,11... | collective-permute-start | bytes 786440 | tf_op jit(solution)/shard_map/ppermute | solution.py:144
  101.8 6.8 %collective-permute-start.13 = (bf16[256,256]{1,0:T(8,128)(2,1)S(1)}, bf16[256,256]{1,0:T(8,128)(2,1)S(1)}, u32[]{:S(2)}, u32[]{:S(2)}) collective-permute-start(bf16[256,256]{1,0:T(8,128)(2,1)S(1)} %get-tuple-element.29), channel_id=1, source_target_pairs={{0,12},{1,13},{2,14},{3,15},{4,8},{5,9},{6,10},{7,11},{8,4},{9,5},... | collective-permute-start | bytes 393224 | tf_op jit(solution)/shard_map/ppermute | solution.py:163

commit v15 on v11

--- a/solution.py
+++ b/solution.py
@@ -136,10 +136,10 @@
     return masks[::-1]
 
 
-def gather_rows(block, owners):
+def gather_rows(block, owners, masks):
     me = lax.axis_index("rows")
     held = block.astype(jnp.bfloat16)
-    for m in doubling_masks(owners):
+    for m in masks:
         pairs = [(i, i ^ m) for i in range(owners)]
         got = lax.ppermute(held, "rows", pairs)
         upper = (me & m) != 0
@@ -149,9 +149,9 @@
     return held.astype(jnp.float32)
 
 
-def arrival_order(owners):
+def arrival_order(masks):
     order = [0]
-    for m in doubling_masks(owners):
+    for m in masks:
         order = order + [d ^ m for d in order]
     return order
 
@@ -173,7 +173,6 @@
     width = columns // chunks
     tile = SEG
     per_chunk = gauges_here // chunks
-    order = arrival_order(owners)
     lag = 2 if chunks > 2 else 0
     mines, receiveds, peaks = [], [], [None] * chunks
     for c in range(chunks):
@@ -191,11 +190,12 @@
     split = (chunks + 1) // 2
     bundles = [list(range(split)), list(range(split, chunks))] if chunks > 1 else [[0]]
     pieces, ids = [], []
-    for bundle in bundles:
+    for b, bundle in enumerate(bundles):
+        masks = doubling_masks(owners)[:: (-1 if b % 2 else 1)]
         joined = jnp.concatenate([peaks[c] for c in bundle], 0) if len(bundle) > 1 else peaks[bundle[0]]
-        pieces.append(gather_rows(joined, owners))
+        pieces.append(gather_rows(joined, owners, masks))
         local = np.concatenate([c * per_chunk + np.arange(per_chunk) for c in bundle])
-        ids.append((np.asarray(order)[:, None] * gauges_here + local[None, :]).reshape(-1))
+        ids.append((np.asarray(arrival_order(masks))[:, None] * gauges_here + local[None, :]).reshape(-1))
     gauge_ids = jnp.asarray(np.concatenate(ids).astype(np.int32))
 
     tile_total = coast_gauges.shape[0]

time: 105 us -> 107 us (1.019)
  waiting for transfers between devices: 9.93 us -> 12.8 us
    ppermute x8, waiting for transfers between devices: 9.92 us -> 12.8 us  [gather_rows(): got = lax.ppermute(held, 'rows', pairs)]
  transfers between devices with their start and end apart: 12 -> 12, of which waited for: 5 -> 6; matrix products, arithmetic and copies ran while one was open for 7% -> 7% of each run, Pallas kernels for 52% -> 51%
where the time goes in v15:
time: 107 us; the launch traced here: 106 us
  Pallas kernels  70.2 us (66%)
  starting transfers between devices  14.3 us (13%)
  waiting for transfers between devices  12.8 us (12%)
  other arithmetic  5.95 us (6%)
  matrix products  2.16 us (2%)
    pallas_call x2, Pallas kernels, fused_of(): pl.pallas_call(fused_kernel, grid_spec=pltpu.PrefetchScalarGridSpec(num_s...  30.8 us
    pallas_call x2, Pallas kernels, partials_of(): pl.pallas_call(matmul_kernel, grid_spec=pltpu.PrefetchScalarGridSpec(num_...  26.8 us
    ppermute x8, starting transfers between devices, gather_rows(): got = lax.ppermute(held, 'rows', pairs)  13.3 us
    ppermute x8, waiting for transfers between devices, gather_rows(): got = lax.ppermute(held, 'rows', pairs)  12.8 us
    pallas_call x2, Pallas kernels, peaks_of(): pl.pallas_call(peak_kernel, grid=(blocks,), in_specs=[pl.BlockSpec((SEG,...  9.64 us
    pallas_call x1, Pallas kernels, slip_of(): pl.pallas_call(slip_kernel, out_shape=jax.ShapeDtypeStruct((sources, scen...  2.88 us
    reduce_sum x1, other arithmetic, body(): jnp.sum(jnp.where(matches, mine_weights[:, :, None], 0.0), axis=1)  2.67 us
    another operation x4, other arithmetic  2.29 us
  transfers between devices with their start and end apart: 12, of which 6 were waited for; matrix products, arithmetic and copies ran while one was open for 7% of the time, Pallas kernels for 51%

profile of v15, /device:TPU:0, one launch (start us, length us, event | category | flops | bytes accessed | tf_op | source)
XLA Modules:
  0.0 106.5 jit_solution(15750700317375558377)
XLA Ops:
  0.0 2.9 %shard_map.73.other_slip_ref.mine_slip_ref = bf16[1000,512]{1,0:T(8,128)(2,1)} custom-call(s32[1000,512]{1,0:T(8,128)} %bitcast.3, f32[8,512]{1,0:T(8,128)} %bitcast.4), custom_call_target="tpu_custom_call" | custom-call | tf_op jit(solution)/shard_map/pallas_call | solution.py:123
  2.9 13.4 %shard_map.76 = (bf16[7680,256]{1,0:T(8,128)(2,1)}, bf16[7680,256]{1,0:T(8,128)(2,1)}) custom-call(s32[1]{0:T(128)} %bitcast.side_ref, bf16[1000,512]{1,0:T(8,128)(2,1)} %shard_map.73.other_slip_ref.mine_slip_ref, bf16[1000,512]{1,0:T(8,128)(2,1)} %shard_map.73.other_slip_ref.mine_slip_ref, bf16[1000,30720]{1,0:T(8,128)(2,1)} %green_ref.7), custom_call_target="tpu_custom_call" | custom-call | flops 7864320000 | bytes 23224320 | tf_op jit(solution)/shard_map/pallas_call | solution.py:34
  16.7 13.4 %shard_map.74 = (bf16[7680,256]{1,0:T(8,128)(2,1)}, bf16[7680,256]{1,0:T(8,128)(2,1)}) custom-call(s32[1]{0:T(128)} %bitcast.side_ref, bf16[1000,512]{1,0:T(8,128)(2,1)} %shard_map.73.other_slip_ref.mine_slip_ref, bf16[1000,512]{1,0:T(8,128)(2,1)} %shard_map.73.other_slip_ref.mine_slip_ref, bf16[1000,30720]{1,0:T(8,128)(2,1)} %green_ref.7), custom_call_target="tpu_custom_call" | custom-call | flops 7864320000 | bytes 23224320 | tf_op jit(solution)/shard_map/pallas_call | solution.py:34
  30.2 15.4 %shard_map.77 = (bf16[7680,256]{1,0:T(8,128)(2,1)}, bf16[7680,256]{1,0:T(8,128)(2,1)}, f32[32,256]{1,0:T(8,128)}) custom-call(s32[1]{0:T(128)} %bitcast.side_ref, bf16[1000,512]{1,0:T(8,128)(2,1)} %shard_map.73.other_slip_ref.mine_slip_ref, bf16[1000,512]{1,0:T(8,128)(2,1)} %shard_map.73.other_slip_ref.mine_slip_ref, bf16[1000,30720]{1,0:T(8,128)(2,1)} %green_ref.7, ...), custom_call_target="tpu_custom_call" | custom-call | flops 7864320000 | bytes 31088640 | tf_op jit(solution)/shard_map/pallas_call | solution.py:68
  46.1 15.4 %shard_map.75 = (bf16[7680,256]{1,0:T(8,128)(2,1)}, bf16[7680,256]{1,0:T(8,128)(2,1)}, f32[32,256]{1,0:T(8,128)}) custom-call(s32[1]{0:T(128)} %bitcast.side_ref, bf16[1000,512]{1,0:T(8,128)(2,1)} %shard_map.73.other_slip_ref.mine_slip_ref, bf16[1000,512]{1,0:T(8,128)(2,1)} %shard_map.73.other_slip_ref.mine_slip_ref, bf16[1000,30720]{1,0:T(8,128)(2,1)} %green_ref.7, ...), custom_call_target="tpu_custom_call" | custom-call | flops 7864320000 | bytes 31088640 | tf_op jit(solution)/shard_map/pallas_call | solution.py:68
  61.5 0.8 dynamic-slice
  63.0 0.8 convert.12
  63.8 4.0 %collective-permute-start.2 = (bf16[64,256]{1,0:T(8,128)(2,1)S(1)}, bf16[64,256]{1,0:T(8,128)(2,1)S(1)}, u32[]{:S(2)}, u32[]{:S(2)}) collective-permute-start(bf16[64,256]{1,0:T(8,128)(2,1)S(1)} %pad_maximum_fusion), channel_id=1, source_target_pairs={{0,8},{1,9},{2,10},{3,11},{4,12},{5,13},{6,14},{7,15},{8,0},{9,1},... | collective-permute-start | bytes 98312 | tf_op jit(solution)/shard_map/ppermute | solution.py:144
  67.8 4.8 %shard_map.79 = f32[32,256]{1,0:T(8,128)} custom-call(bf16[7680,256]{1,0:T(8,128)(2,1)} %get-tuple-element.23.mine_ref, bf16[7680,256]{1,0:T(8,128)(2,1)} %collective-permute-done.7.recv_ref), custom_call_target="tpu_custom_call" | custom-call | flops 5898240 | bytes 7864320 | tf_op jit(solution)/shard_map/pallas_call | solution.py:102
  72.6 0.8 convert.15
  73.4 4.8 %shard_map.78 = f32[32,256]{1,0:T(8,128)} custom-call(bf16[7680,256]{1,0:T(8,128)(2,1)} %get-tuple-element.21.mine_ref, bf16[7680,256]{1,0:T(8,128)(2,1)} %collective-permute-done.6.recv_ref), custom_call_target="tpu_custom_call" | custom-call | flops 5898240 | bytes 7864320 | tf_op jit(solution)/shard_map/pallas_call | solution.py:102
  78.2 0.8 convert.14
  79.0 1.5 %collective-permute-start.8 = (bf16[64,256]{1,0:T(8,128)(2,1)S(1)}, bf16[64,256]{1,0:T(8,128)(2,1)S(1)}, u32[]{:S(2)}, u32[]{:S(2)}) collective-permute-start(bf16[64,256]{1,0:T(8,128)(2,1)S(1)} %pad_maximum_fusion.1), channel_id=1, source_target_pairs={{0,1},{1,0},{2,3},{3,2},{4,5},{5,4},{6,7},{7,6},{8,9},{9,8},{10,11... | collective-permute-start | bytes 98312 | tf_op jit(solution)/shard_map/ppermute | solution.py:144
  80.5 1.6 %collective-permute-start.3 = (bf16[128,256]{1,0:T(8,128)(2,1)S(1)}, bf16[128,256]{1,0:T(8,128)(2,1)S(1)}, u32[]{:S(2)}, u32[]{:S(2)}) collective-permute-start(bf16[128,256]{1,0:T(8,128)(2,1)S(1)} %maximum_select_fusion.8), channel_id=1, source_target_pairs={{0,4},{1,5},{2,6},{3,7},{4,0},{5,1},{6,2},{7,3},{8,12},{9,13},{10,... | collective-permute-start | bytes 196616 | tf_op jit(solution)/shard_map/ppermute | solution.py:144
  82.2 0.8 collective-permute-done.8
  82.9 1.6 %collective-permute-start.9 = (bf16[128,256]{1,0:T(8,128)(2,1)S(1)}, bf16[128,256]{1,0:T(8,128)(2,1)S(1)}, u32[]{:S(2)}, u32[]{:S(2)}) collective-permute-start(bf16[128,256]{1,0:T(8,128)(2,1)S(1)} %maximum_select_fusion.9), channel_id=1, source_target_pairs={{0,2},{1,3},{2,0},{3,1},{4,6},{5,7},{6,4},{7,5},{8,10},{9,11},{10,... | collective-permute-start | bytes 196616 | tf_op jit(solution)/shard_map/ppermute | solution.py:144
  84.9 1.6 %collective-permute-start.4 = (bf16[256,256]{1,0:T(8,128)(2,1)S(1)}, bf16[256,256]{1,0:T(8,128)(2,1)S(1)}, u32[]{:S(2)}, u32[]{:S(2)}) collective-permute-start(bf16[256,256]{1,0:T(8,128)(2,1)S(1)} %maximum_select_fusion.6), channel_id=1, source_target_pairs={{0,2},{1,3},{2,0},{3,1},{4,6},{5,7},{6,4},{7,5},{8,10},{9,11},{10,... | collective-permute-start | bytes 393224 | tf_op jit(solution)/shard_map/ppermute | solution.py:144
  86.5 1.5 %collective-permute-done.9 = bf16[128,256]{1,0:T(8,128)(2,1)S(1)} collective-permute-done((bf16[128,256]{1,0:T(8,128)(2,1)S(1)}, bf16[128,256]{1,0:T(8,128)(2,1)S(1)}, u32[]{:S(2)}, u32[]{:S(2)}) %collective-permute-start.9) | collective-permute-done | bytes 65568 | tf_op jit(solution)/shard_map/ppermute | solution.py:144
  87.9 1.6 %collective-permute-start.10 = (bf16[256,256]{1,0:T(8,128)(2,1)S(1)}, bf16[256,256]{1,0:T(8,128)(2,1)S(1)}, u32[]{:S(2)}, u32[]{:S(2)}) collective-permute-start(bf16[256,256]{1,0:T(8,128)(2,1)S(1)} %maximum_select_fusion.7), channel_id=1, source_target_pairs={{0,4},{1,5},{2,6},{3,7},{4,0},{5,1},{6,2},{7,3},{8,12},{9,13},{10,... | collective-permute-start | bytes 393224 | tf_op jit(solution)/shard_map/ppermute | solution.py:144
  90.0 1.2 %collective-permute-start.5 = (bf16[512,256]{1,0:T(8,128)(2,1)S(1)}, bf16[512,256]{1,0:T(8,128)(2,1)S(1)}, u32[]{:S(2)}, u32[]{:S(2)}) collective-permute-start(bf16[512,256]{1,0:T(8,128)(2,1)S(1)} %maximum_select_fusion.4), channel_id=1, source_target_pairs={{0,1},{1,0},{2,3},{3,2},{4,5},{5,4},{6,7},{7,6},{8,9},{9,8},{10,11... | collective-permute-start | bytes 786440 | tf_op jit(solution)/shard_map/ppermute | solution.py:144
  91.2 2.8 %collective-permute-done.10 = bf16[256,256]{1,0:T(8,128)(2,1)S(1)} collective-permute-done((bf16[256,256]{1,0:T(8,128)(2,1)S(1)}, bf16[256,256]{1,0:T(8,128)(2,1)S(1)}, u32[]{:S(2)}, u32[]{:S(2)}) %collective-permute-start.10) | collective-permute-done | bytes 131104 | tf_op jit(solution)/shard_map/ppermute | solution.py:144
  94.2 2.7 %select_reduce_fusion = f32[128,2048]{1,0:T(8,128)S(1)} fusion(f32[128,8]{1,0:T(8,128)S(1)} %copy.11, s32[2048]{0:T(1024)S(1)} %copy-done.2, s32[128,8]{1,0:T(8,128)S(1)} %copy.10), kind=kLoop, calls=%fused_computation | loop fusion | flops 6029312 | bytes 1064960 | tf_op jit(solution)/shard_map/reduce_sum | solution.py:210
  96.9 7.4 %collective-permute-done.11 = bf16[512,256]{1,0:T(8,128)(2,1)S(1)} collective-permute-done((bf16[512,256]{1,0:T(8,128)(2,1)S(1)}, bf16[512,256]{1,0:T(8,128)(2,1)S(1)}, u32[]{:S(2)}, u32[]{:S(2)}) %collective-permute-start.11) | collective-permute-done | bytes 262176 | tf_op jit(solution)/shard_map/ppermute | solution.py:144
  105.1 1.4 %convolution_add_fusion = f32[256,128]{1,0:T(8,128)} fusion(f32[256,128]{1,0:T(8,128)S(1)} %fusion, f32[128,2048]{1,0:T(8,128)S(1)} %select_reduce_fusion, bf16[512,256]{1,0:T(8,128)(2,1)S(1)} %maximum_select_fusion.4, bf16[512,256]{1,0:T(8,128)(2,1)S(1)} %collective-permute-done.5, pred[]{:T(512)S(6)} %ne.16), kind=kOutput, calls=%fused_computation.1 | convolution fusion | flops 405045248 | bytes 1310721 | tf_op jit(solution)/shard_map/dot_general | solution.py:215
  (33 shorter events, 3.5 us)
Async XLA Ops:
  0.0 89.6 %copy-start = (s32[2048,8]{0,1:T(8,128)S(1)}, s32[2048,8]{0,1:T(8,128)}, u32[]{:S(2)}) copy-start(s32[2048,8]{0,1:T(8,128)} %param.10) | copy-start | bytes 196612
  16.3 13.9 %collective-permute-start.1 = (bf16[7680,256]{1,0:T(8,128)(2,1)}, bf16[7680,256]{1,0:T(8,128)(2,1)}, u32[]{:S(2)}, u32[]{:S(2)}) collective-permute-start(bf16[7680,256]{1,0:T(8,128)(2,1)} %get-tuple-element.19), channel_id=1, source_target_pairs={{0,16},{16,0},{1,17},{17,1},{2,18},{18,2},{3,19},{19,3},{4,20},{20... | collective-permute-start | bytes 11796488 | tf_op jit(solution)/shard_map/ppermute | solution.py:186
  30.1 15.9 %collective-permute-start = (bf16[7680,256]{1,0:T(8,128)(2,1)}, bf16[7680,256]{1,0:T(8,128)(2,1)}, u32[]{:S(2)}, u32[]{:S(2)}) collective-permute-start(bf16[7680,256]{1,0:T(8,128)(2,1)} %get-tuple-element.16), channel_id=1, source_target_pairs={{0,16},{16,0},{1,17},{17,1},{2,18},{18,2},{3,19},{19,3},{4,20},{20... | collective-permute-start | bytes 11796488 | tf_op jit(solution)/shard_map/ppermute | solution.py:186
  45.6 22.2 %collective-permute-start.7 = (bf16[7680,256]{1,0:T(8,128)(2,1)}, bf16[7680,256]{1,0:T(8,128)(2,1)}, u32[]{:S(2)}, u32[]{:S(2)}) collective-permute-start(bf16[7680,256]{1,0:T(8,128)(2,1)} %get-tuple-element.24), channel_id=1, source_target_pairs={{0,16},{16,0},{1,17},{17,1},{2,18},{18,2},{3,19},{19,3},{4,20},{20... | collective-permute-start | bytes 11796488 | tf_op jit(solution)/shard_map/ppermute | solution.py:186
  46.1 16.9 %copy-start.1 = (f32[32,256]{1,0:T(8,128)S(1)}, f32[32,256]{1,0:T(8,128)}, u32[]{:S(2)}) copy-start(f32[32,256]{1,0:T(8,128)} %get-tuple-element.20) | copy-start | bytes 98308
  61.5 11.9 %collective-permute-start.6 = (bf16[7680,256]{1,0:T(8,128)(2,1)}, bf16[7680,256]{1,0:T(8,128)(2,1)}, u32[]{:S(2)}, u32[]{:S(2)}) collective-permute-start(bf16[7680,256]{1,0:T(8,128)(2,1)} %get-tuple-element.22), channel_id=1, source_target_pairs={{0,16},{16,0},{1,17},{17,1},{2,18},{18,2},{3,19},{19,3},{4,20},{20... | collective-permute-start | bytes 11796488 | tf_op jit(solution)/shard_map/ppermute | solution.py:186
  63.8 16.7 %collective-permute-start.2 = (bf16[64,256]{1,0:T(8,128)(2,1)S(1)}, bf16[64,256]{1,0:T(8,128)(2,1)S(1)}, u32[]{:S(2)}, u32[]{:S(2)}) collective-permute-start(bf16[64,256]{1,0:T(8,128)(2,1)S(1)} %pad_maximum_fusion), channel_id=1, source_target_pairs={{0,8},{1,9},{2,10},{3,11},{4,12},{5,13},{6,14},{7,15},{8,0},{9,1},... | collective-permute-start | bytes 98312 | tf_op jit(solution)/shard_map/ppermute | solution.py:144
  73.4 20.8 %copy-start.2 = (s32[2048]{0:T(1024)S(1)}, s32[2048]{0:T(1024)}, u32[]{:S(2)}) copy-start(s32[2048]{0:T(1024)} %constant.28.clone) | copy-start | bytes 24580
  79.0 3.9 %collective-permute-start.8 = (bf16[64,256]{1,0:T(8,128)(2,1)S(1)}, bf16[64,256]{1,0:T(8,128)(2,1)S(1)}, u32[]{:S(2)}, u32[]{:S(2)}) collective-permute-start(bf16[64,256]{1,0:T(8,128)(2,1)S(1)} %pad_maximum_fusion.1), channel_id=1, source_target_pairs={{0,1},{1,0},{2,3},{3,2},{4,5},{5,4},{6,7},{7,6},{8,9},{9,8},{10,11... | collective-permute-start | bytes 98312 | tf_op jit(solution)/shard_map/ppermute | solution.py:144
  80.5 4.3 %collective-permute-start.3 = (bf16[128,256]{1,0:T(8,128)(2,1)S(1)}, bf16[128,256]{1,0:T(8,128)(2,1)S(1)}, u32[]{:S(2)}, u32[]{:S(2)}) collective-permute-start(bf16[128,256]{1,0:T(8,128)(2,1)S(1)} %maximum_select_fusion.8), channel_id=1, source_target_pairs={{0,4},{1,5},{2,6},{3,7},{4,0},{5,1},{6,2},{7,3},{8,12},{9,13},{10,... | collective-permute-start | bytes 196616 | tf_op jit(solution)/shard_map/ppermute | solution.py:144
  82.9 5.0 %collective-permute-start.9 = (bf16[128,256]{1,0:T(8,128)(2,1)S(1)}, bf16[128,256]{1,0:T(8,128)(2,1)S(1)}, u32[]{:S(2)}, u32[]{:S(2)}) collective-permute-start(bf16[128,256]{1,0:T(8,128)(2,1)S(1)} %maximum_select_fusion.9), channel_id=1, source_target_pairs={{0,2},{1,3},{2,0},{3,1},{4,6},{5,7},{6,4},{7,5},{8,10},{9,11},{10,... | collective-permute-start | bytes 196616 | tf_op jit(solution)/shard_map/ppermute | solution.py:144
  84.9 5.0 %collective-permute-start.4 = (bf16[256,256]{1,0:T(8,128)(2,1)S(1)}, bf16[256,256]{1,0:T(8,128)(2,1)S(1)}, u32[]{:S(2)}, u32[]{:S(2)}) collective-permute-start(bf16[256,256]{1,0:T(8,128)(2,1)S(1)} %maximum_select_fusion.6), channel_id=1, source_target_pairs={{0,2},{1,3},{2,0},{3,1},{4,6},{5,7},{6,4},{7,5},{8,10},{9,11},{10,... | collective-permute-start | bytes 393224 | tf_op jit(solution)/shard_map/ppermute | solution.py:144
  87.9 6.1 %collective-permute-start.10 = (bf16[256,256]{1,0:T(8,128)(2,1)S(1)}, bf16[256,256]{1,0:T(8,128)(2,1)S(1)}, u32[]{:S(2)}, u32[]{:S(2)}) collective-permute-start(bf16[256,256]{1,0:T(8,128)(2,1)S(1)} %maximum_select_fusion.7), channel_id=1, source_target_pairs={{0,4},{1,5},{2,6},{3,7},{4,0},{5,1},{6,2},{7,3},{8,12},{9,13},{10,... | collective-permute-start | bytes 393224 | tf_op jit(solution)/shard_map/ppermute | solution.py:144
  90.0 15.0 %collective-permute-start.5 = (bf16[512,256]{1,0:T(8,128)(2,1)S(1)}, bf16[512,256]{1,0:T(8,128)(2,1)S(1)}, u32[]{:S(2)}, u32[]{:S(2)}) collective-permute-start(bf16[512,256]{1,0:T(8,128)(2,1)S(1)} %maximum_select_fusion.4), channel_id=1, source_target_pairs={{0,1},{1,0},{2,3},{3,2},{4,5},{5,4},{6,7},{7,6},{8,9},{9,8},{10,11... | collective-permute-start | bytes 786440 | tf_op jit(solution)/shard_map/ppermute | solution.py:144
  94.2 10.1 %collective-permute-start.11 = (bf16[512,256]{1,0:T(8,128)(2,1)S(1)}, bf16[512,256]{1,0:T(8,128)(2,1)S(1)}, u32[]{:S(2)}, u32[]{:S(2)}) collective-permute-start(bf16[512,256]{1,0:T(8,128)(2,1)S(1)} %maximum_select_fusion.5), channel_id=1, source_target_pairs={{0,8},{1,9},{2,10},{3,11},{4,12},{5,13},{6,14},{7,15},{8,0},{9,1},... | collective-permute-start | bytes 786440 | tf_op jit(solution)/shard_map/ppermute | solution.py:144

commit v16 on v11

--- a/solution.py
+++ b/solution.py
@@ -216,7 +216,7 @@
             piece,
             tile_table[:, start:start + span],
             (((0,), (1,)), ((), ())),
-            precision=lax.Precision.HIGHEST,
+            precision=lax.Precision.HIGH,
             preferred_element_type=jnp.float32,
         )
         start += span

time: 105 us -> 105 us (level)
  no operation moved by 1% of the time
where the time goes in v16:
time: 105 us; the launch traced here: 104 us
  Pallas kernels  70.2 us (67%)
  starting transfers between devices  15 us (14%)
  waiting for transfers between devices  9.93 us (9%)
  other arithmetic  5.94 us (6%)
  matrix products  1.79 us (2%)
    pallas_call x2, Pallas kernels, fused_of(): pl.pallas_call(fused_kernel, grid_spec=pltpu.PrefetchScalarGridSpec(num_s...  30.8 us
    pallas_call x2, Pallas kernels, partials_of(): pl.pallas_call(matmul_kernel, grid_spec=pltpu.PrefetchScalarGridSpec(num_...  26.8 us
    ppermute x8, starting transfers between devices, gather_rows(): got = lax.ppermute(held, 'rows', pairs)  13.9 us
    ppermute x8, waiting for transfers between devices, gather_rows(): got = lax.ppermute(held, 'rows', pairs)  9.92 us
    pallas_call x2, Pallas kernels, peaks_of(): pl.pallas_call(peak_kernel, grid=(blocks,), in_specs=[pl.BlockSpec((SEG,...  9.64 us
    pallas_call x1, Pallas kernels, slip_of(): pl.pallas_call(slip_kernel, out_shape=jax.ShapeDtypeStruct((sources, scen...  2.88 us
    reduce_sum x1, other arithmetic, body(): jnp.sum(jnp.where(matches, mine_weights[:, :, None], 0.0), axis=1)  2.66 us
    another operation x4, other arithmetic  2.29 us
  transfers between devices with their start and end apart: 12, of which 5 were waited for; matrix products, arithmetic and copies ran while one was open for 7% of the time, Pallas kernels for 52%

profile of v16, /device:TPU:0, one launch (start us, length us, event | category | flops | bytes accessed | tf_op | source)
XLA Modules:
  0.0 103.8 jit_solution(2375584337360062051)
XLA Ops:
  0.0 2.9 %shard_map.73.other_slip_ref.mine_slip_ref = bf16[1000,512]{1,0:T(8,128)(2,1)} custom-call(s32[1000,512]{1,0:T(8,128)} %bitcast.3, f32[8,512]{1,0:T(8,128)} %bitcast.4), custom_call_target="tpu_custom_call" | custom-call | tf_op jit(solution)/shard_map/pallas_call | solution.py:123
  2.9 13.4 %shard_map.76 = (bf16[7680,256]{1,0:T(8,128)(2,1)}, bf16[7680,256]{1,0:T(8,128)(2,1)}) custom-call(s32[1]{0:T(128)} %bitcast.side_ref, bf16[1000,512]{1,0:T(8,128)(2,1)} %shard_map.73.other_slip_ref.mine_slip_ref, bf16[1000,512]{1,0:T(8,128)(2,1)} %shard_map.73.other_slip_ref.mine_slip_ref, bf16[1000,30720]{1,0:T(8,128)(2,1)} %green_ref.7), custom_call_target="tpu_custom_call" | custom-call | flops 7864320000 | bytes 23224320 | tf_op jit(solution)/shard_map/pallas_call | solution.py:34
  16.7 13.4 %shard_map.74 = (bf16[7680,256]{1,0:T(8,128)(2,1)}, bf16[7680,256]{1,0:T(8,128)(2,1)}) custom-call(s32[1]{0:T(128)} %bitcast.side_ref, bf16[1000,512]{1,0:T(8,128)(2,1)} %shard_map.73.other_slip_ref.mine_slip_ref, bf16[1000,512]{1,0:T(8,128)(2,1)} %shard_map.73.other_slip_ref.mine_slip_ref, bf16[1000,30720]{1,0:T(8,128)(2,1)} %green_ref.7), custom_call_target="tpu_custom_call" | custom-call | flops 7864320000 | bytes 23224320 | tf_op jit(solution)/shard_map/pallas_call | solution.py:34
  30.2 15.4 %shard_map.77 = (bf16[7680,256]{1,0:T(8,128)(2,1)}, bf16[7680,256]{1,0:T(8,128)(2,1)}, f32[32,256]{1,0:T(8,128)}) custom-call(s32[1]{0:T(128)} %bitcast.side_ref, bf16[1000,512]{1,0:T(8,128)(2,1)} %shard_map.73.other_slip_ref.mine_slip_ref, bf16[1000,512]{1,0:T(8,128)(2,1)} %shard_map.73.other_slip_ref.mine_slip_ref, bf16[1000,30720]{1,0:T(8,128)(2,1)} %green_ref.7, ...), custom_call_target="tpu_custom_call" | custom-call | flops 7864320000 | bytes 31088640 | tf_op jit(solution)/shard_map/pallas_call | solution.py:68
  46.1 15.4 %shard_map.75 = (bf16[7680,256]{1,0:T(8,128)(2,1)}, bf16[7680,256]{1,0:T(8,128)(2,1)}, f32[32,256]{1,0:T(8,128)}) custom-call(s32[1]{0:T(128)} %bitcast.side_ref, bf16[1000,512]{1,0:T(8,128)(2,1)} %shard_map.73.other_slip_ref.mine_slip_ref, bf16[1000,512]{1,0:T(8,128)(2,1)} %shard_map.73.other_slip_ref.mine_slip_ref, bf16[1000,30720]{1,0:T(8,128)(2,1)} %green_ref.7, ...), custom_call_target="tpu_custom_call" | custom-call | flops 7864320000 | bytes 31088640 | tf_op jit(solution)/shard_map/pallas_call | solution.py:68
  61.5 0.8 dynamic-slice
  63.0 0.8 convert.12
  63.8 4.0 %collective-permute-start.2 = (bf16[64,256]{1,0:T(8,128)(2,1)S(1)}, bf16[64,256]{1,0:T(8,128)(2,1)S(1)}, u32[]{:S(2)}, u32[]{:S(2)}) collective-permute-start(bf16[64,256]{1,0:T(8,128)(2,1)S(1)} %pad_maximum_fusion), channel_id=1, source_target_pairs={{0,8},{1,9},{2,10},{3,11},{4,12},{5,13},{6,14},{7,15},{8,0},{9,1},... | collective-permute-start | bytes 98312 | tf_op jit(solution)/shard_map/ppermute | solution.py:144
  67.8 4.8 %shard_map.79 = f32[32,256]{1,0:T(8,128)} custom-call(bf16[7680,256]{1,0:T(8,128)(2,1)} %get-tuple-element.23.mine_ref, bf16[7680,256]{1,0:T(8,128)(2,1)} %collective-permute-done.7.recv_ref), custom_call_target="tpu_custom_call" | custom-call | flops 5898240 | bytes 7864320 | tf_op jit(solution)/shard_map/pallas_call | solution.py:102
  72.6 0.8 convert.15
  73.4 4.8 %shard_map.78 = f32[32,256]{1,0:T(8,128)} custom-call(bf16[7680,256]{1,0:T(8,128)(2,1)} %get-tuple-element.21.mine_ref, bf16[7680,256]{1,0:T(8,128)(2,1)} %collective-permute-done.6.recv_ref), custom_call_target="tpu_custom_call" | custom-call | flops 5898240 | bytes 7864320 | tf_op jit(solution)/shard_map/pallas_call | solution.py:102
  78.2 0.8 convert.14
  79.0 2.0 %collective-permute-start.3 = (bf16[128,256]{1,0:T(8,128)(2,1)S(1)}, bf16[128,256]{1,0:T(8,128)(2,1)S(1)}, u32[]{:S(2)}, u32[]{:S(2)}) collective-permute-start(bf16[128,256]{1,0:T(8,128)(2,1)S(1)} %maximum_select_fusion.8), channel_id=1, source_target_pairs={{0,4},{1,5},{2,6},{3,7},{4,0},{5,1},{6,2},{7,3},{8,12},{9,13},{10,... | collective-permute-start | bytes 196616 | tf_op jit(solution)/shard_map/ppermute | solution.py:144
  81.0 3.0 %collective-permute-done.8 = bf16[64,256]{1,0:T(8,128)(2,1)S(1)} collective-permute-done((bf16[64,256]{1,0:T(8,128)(2,1)S(1)}, bf16[64,256]{1,0:T(8,128)(2,1)S(1)}, u32[]{:S(2)}, u32[]{:S(2)}) %collective-permute-start.8) | collective-permute-done | bytes 32800 | tf_op jit(solution)/shard_map/ppermute | solution.py:144
  84.0 1.5 %collective-permute-start.9 = (bf16[128,256]{1,0:T(8,128)(2,1)S(1)}, bf16[128,256]{1,0:T(8,128)(2,1)S(1)}, u32[]{:S(2)}, u32[]{:S(2)}) collective-permute-start(bf16[128,256]{1,0:T(8,128)(2,1)S(1)} %maximum_select_fusion.9), channel_id=1, source_target_pairs={{0,4},{1,5},{2,6},{3,7},{4,0},{5,1},{6,2},{7,3},{8,12},{9,13},{10,... | collective-permute-start | bytes 196616 | tf_op jit(solution)/shard_map/ppermute | solution.py:144
  85.5 1.6 %collective-permute-start.4 = (bf16[256,256]{1,0:T(8,128)(2,1)S(1)}, bf16[256,256]{1,0:T(8,128)(2,1)S(1)}, u32[]{:S(2)}, u32[]{:S(2)}) collective-permute-start(bf16[256,256]{1,0:T(8,128)(2,1)S(1)} %maximum_select_fusion.6), channel_id=1, source_target_pairs={{0,2},{1,3},{2,0},{3,1},{4,6},{5,7},{6,4},{7,5},{8,10},{9,11},{10,... | collective-permute-start | bytes 393224 | tf_op jit(solution)/shard_map/ppermute | solution.py:144
  87.1 1.2 %collective-permute-done.9 = bf16[128,256]{1,0:T(8,128)(2,1)S(1)} collective-permute-done((bf16[128,256]{1,0:T(8,128)(2,1)S(1)}, bf16[128,256]{1,0:T(8,128)(2,1)S(1)}, u32[]{:S(2)}, u32[]{:S(2)}) %collective-permute-start.9) | collective-permute-done | bytes 65568 | tf_op jit(solution)/shard_map/ppermute | solution.py:144
  88.3 1.7 %collective-permute-start.10 = (bf16[256,256]{1,0:T(8,128)(2,1)S(1)}, bf16[256,256]{1,0:T(8,128)(2,1)S(1)}, u32[]{:S(2)}, u32[]{:S(2)}) collective-permute-start(bf16[256,256]{1,0:T(8,128)(2,1)S(1)} %maximum_select_fusion.7), channel_id=1, source_target_pairs={{0,2},{1,3},{2,0},{3,1},{4,6},{5,7},{6,4},{7,5},{8,10},{9,11},{10,... | collective-permute-start | bytes 393224 | tf_op jit(solution)/shard_map/ppermute | solution.py:144
  90.2 0.9 collective-permute-done.4
  91.2 1.6 %collective-permute-start.5 = (bf16[512,256]{1,0:T(8,128)(2,1)S(1)}, bf16[512,256]{1,0:T(8,128)(2,1)S(1)}, u32[]{:S(2)}, u32[]{:S(2)}) collective-permute-start(bf16[512,256]{1,0:T(8,128)(2,1)S(1)} %maximum_select_fusion.4), channel_id=1, source_target_pairs={{0,1},{1,0},{2,3},{3,2},{4,5},{5,4},{6,7},{7,6},{8,9},{9,8},{10,11... | collective-permute-start | bytes 786440 | tf_op jit(solution)/shard_map/ppermute | solution.py:144
  93.5 1.6 %collective-permute-start.11 = (bf16[512,256]{1,0:T(8,128)(2,1)S(1)}, bf16[512,256]{1,0:T(8,128)(2,1)S(1)}, u32[]{:S(2)}, u32[]{:S(2)}) collective-permute-start(bf16[512,256]{1,0:T(8,128)(2,1)S(1)} %maximum_select_fusion.5), channel_id=1, source_target_pairs={{0,1},{1,0},{2,3},{3,2},{4,5},{5,4},{6,7},{7,6},{8,9},{9,8},{10,11... | collective-permute-start | bytes 786440 | tf_op jit(solution)/shard_map/ppermute | solution.py:144
  95.1 2.7 %select_reduce_fusion = f32[128,2048]{1,0:T(8,128)S(1)} fusion(f32[128,8]{1,0:T(8,128)S(1)} %copy.11, s32[2048]{0:T(1024)S(1)} %copy-done.2, s32[128,8]{1,0:T(8,128)S(1)} %copy.10), kind=kLoop, calls=%fused_computation | loop fusion | flops 6029312 | bytes 1064960 | tf_op jit(solution)/shard_map/reduce_sum | solution.py:210
  97.8 4.2 %collective-permute-done.11 = bf16[512,256]{1,0:T(8,128)(2,1)S(1)} collective-permute-done((bf16[512,256]{1,0:T(8,128)(2,1)S(1)}, bf16[512,256]{1,0:T(8,128)(2,1)S(1)}, u32[]{:S(2)}, u32[]{:S(2)}) %collective-permute-start.11) | collective-permute-done | bytes 262176 | tf_op jit(solution)/shard_map/ppermute | solution.py:144
  102.6 1.2 %convolution_add_fusion = f32[256,128]{1,0:T(8,128)} fusion(f32[256,128]{1,0:T(8,128)S(1)} %fusion, f32[128,2048]{1,0:T(8,128)S(1)} %select_reduce_fusion, bf16[512,256]{1,0:T(8,128)(2,1)S(1)} %maximum_select_fusion.4, bf16[512,256]{1,0:T(8,128)(2,1)S(1)} %collective-permute-done.5, pred[]{:T(512)S(6)} %ne.16), kind=kOutput, calls=%fused_computation.1 | convolution fusion | flops 203718656 | bytes 1310721 | tf_op jit(solution)/shard_map/dot_general | solution.py:215
  (33 shorter events, 3.4 us)
Async XLA Ops:
  0.0 90.0 %copy-start = (s32[2048,8]{0,1:T(8,128)S(1)}, s32[2048,8]{0,1:T(8,128)}, u32[]{:S(2)}) copy-start(s32[2048,8]{0,1:T(8,128)} %param.10) | copy-start | bytes 196612
  16.3 13.9 %collective-permute-start.1 = (bf16[7680,256]{1,0:T(8,128)(2,1)}, bf16[7680,256]{1,0:T(8,128)(2,1)}, u32[]{:S(2)}, u32[]{:S(2)}) collective-permute-start(bf16[7680,256]{1,0:T(8,128)(2,1)} %get-tuple-element.19), channel_id=1, source_target_pairs={{0,16},{16,0},{1,17},{17,1},{2,18},{18,2},{3,19},{19,3},{4,20},{20... | collective-permute-start | bytes 11796488 | tf_op jit(solution)/shard_map/ppermute | solution.py:187
  30.1 15.9 %collective-permute-start = (bf16[7680,256]{1,0:T(8,128)(2,1)}, bf16[7680,256]{1,0:T(8,128)(2,1)}, u32[]{:S(2)}, u32[]{:S(2)}) collective-permute-start(bf16[7680,256]{1,0:T(8,128)(2,1)} %get-tuple-element.16), channel_id=1, source_target_pairs={{0,16},{16,0},{1,17},{17,1},{2,18},{18,2},{3,19},{19,3},{4,20},{20... | collective-permute-start | bytes 11796488 | tf_op jit(solution)/shard_map/ppermute | solution.py:187
  45.6 22.2 %collective-permute-start.7 = (bf16[7680,256]{1,0:T(8,128)(2,1)}, bf16[7680,256]{1,0:T(8,128)(2,1)}, u32[]{:S(2)}, u32[]{:S(2)}) collective-permute-start(bf16[7680,256]{1,0:T(8,128)(2,1)} %get-tuple-element.24), channel_id=1, source_target_pairs={{0,16},{16,0},{1,17},{17,1},{2,18},{18,2},{3,19},{19,3},{4,20},{20... | collective-permute-start | bytes 11796488 | tf_op jit(solution)/shard_map/ppermute | solution.py:187
  46.1 16.9 %copy-start.1 = (f32[32,256]{1,0:T(8,128)S(1)}, f32[32,256]{1,0:T(8,128)}, u32[]{:S(2)}) copy-start(f32[32,256]{1,0:T(8,128)} %get-tuple-element.20) | copy-start | bytes 98308
  61.5 11.9 %collective-permute-start.6 = (bf16[7680,256]{1,0:T(8,128)(2,1)}, bf16[7680,256]{1,0:T(8,128)(2,1)}, u32[]{:S(2)}, u32[]{:S(2)}) collective-permute-start(bf16[7680,256]{1,0:T(8,128)(2,1)} %get-tuple-element.22), channel_id=1, source_target_pairs={{0,16},{16,0},{1,17},{17,1},{2,18},{18,2},{3,19},{19,3},{4,20},{20... | collective-permute-start | bytes 11796488 | tf_op jit(solution)/shard_map/ppermute | solution.py:187
  63.8 15.2 %collective-permute-start.2 = (bf16[64,256]{1,0:T(8,128)(2,1)S(1)}, bf16[64,256]{1,0:T(8,128)(2,1)S(1)}, u32[]{:S(2)}, u32[]{:S(2)}) collective-permute-start(bf16[64,256]{1,0:T(8,128)(2,1)S(1)} %pad_maximum_fusion), channel_id=1, source_target_pairs={{0,8},{1,9},{2,10},{3,11},{4,12},{5,13},{6,14},{7,15},{8,0},{9,1},... | collective-permute-start | bytes 98312 | tf_op jit(solution)/shard_map/ppermute | solution.py:144
  73.4 21.7 %copy-start.2 = (s32[2048]{0:T(1024)S(1)}, s32[2048]{0:T(1024)}, u32[]{:S(2)}) copy-start(s32[2048]{0:T(1024)} %constant.28.clone) | copy-start | bytes 24580
  79.0 5.0 %collective-permute-start.8 = (bf16[64,256]{1,0:T(8,128)(2,1)S(1)}, bf16[64,256]{1,0:T(8,128)(2,1)S(1)}, u32[]{:S(2)}, u32[]{:S(2)}) collective-permute-start(bf16[64,256]{1,0:T(8,128)(2,1)S(1)} %pad_maximum_fusion.1), channel_id=1, source_target_pairs={{0,8},{1,9},{2,10},{3,11},{4,12},{5,13},{6,14},{7,15},{8,0},{9,1},... | collective-permute-start | bytes 98312 | tf_op jit(solution)/shard_map/ppermute | solution.py:144
  79.0 6.4 %collective-permute-start.3 = (bf16[128,256]{1,0:T(8,128)(2,1)S(1)}, bf16[128,256]{1,0:T(8,128)(2,1)S(1)}, u32[]{:S(2)}, u32[]{:S(2)}) collective-permute-start(bf16[128,256]{1,0:T(8,128)(2,1)S(1)} %maximum_select_fusion.8), channel_id=1, source_target_pairs={{0,4},{1,5},{2,6},{3,7},{4,0},{5,1},{6,2},{7,3},{8,12},{9,13},{10,... | collective-permute-start | bytes 196616 | tf_op jit(solution)/shard_map/ppermute | solution.py:144
  84.0 4.3 %collective-permute-start.9 = (bf16[128,256]{1,0:T(8,128)(2,1)S(1)}, bf16[128,256]{1,0:T(8,128)(2,1)S(1)}, u32[]{:S(2)}, u32[]{:S(2)}) collective-permute-start(bf16[128,256]{1,0:T(8,128)(2,1)S(1)} %maximum_select_fusion.9), channel_id=1, source_target_pairs={{0,4},{1,5},{2,6},{3,7},{4,0},{5,1},{6,2},{7,3},{8,12},{9,13},{10,... | collective-permute-start | bytes 196616 | tf_op jit(solution)/shard_map/ppermute | solution.py:144
  85.5 5.6 %collective-permute-start.4 = (bf16[256,256]{1,0:T(8,128)(2,1)S(1)}, bf16[256,256]{1,0:T(8,128)(2,1)S(1)}, u32[]{:S(2)}, u32[]{:S(2)}) collective-permute-start(bf16[256,256]{1,0:T(8,128)(2,1)S(1)} %maximum_select_fusion.6), channel_id=1, source_target_pairs={{0,2},{1,3},{2,0},{3,1},{4,6},{5,7},{6,4},{7,5},{8,10},{9,11},{10,... | collective-permute-start | bytes 393224 | tf_op jit(solution)/shard_map/ppermute | solution.py:144
  88.3 5.0 %collective-permute-start.10 = (bf16[256,256]{1,0:T(8,128)(2,1)S(1)}, bf16[256,256]{1,0:T(8,128)(2,1)S(1)}, u32[]{:S(2)}, u32[]{:S(2)}) collective-permute-start(bf16[256,256]{1,0:T(8,128)(2,1)S(1)} %maximum_select_fusion.7), channel_id=1, source_target_pairs={{0,2},{1,3},{2,0},{3,1},{4,6},{5,7},{6,4},{7,5},{8,10},{9,11},{10,... | collective-permute-start | bytes 393224 | tf_op jit(solution)/shard_map/ppermute | solution.py:144
  91.2 11.4 %collective-permute-start.5 = (bf16[512,256]{1,0:T(8,128)(2,1)S(1)}, bf16[512,256]{1,0:T(8,128)(2,1)S(1)}, u32[]{:S(2)}, u32[]{:S(2)}) collective-permute-start(bf16[512,256]{1,0:T(8,128)(2,1)S(1)} %maximum_select_fusion.4), channel_id=1, source_target_pairs={{0,1},{1,0},{2,3},{3,2},{4,5},{5,4},{6,7},{7,6},{8,9},{9,8},{10,11... | collective-permute-start | bytes 786440 | tf_op jit(solution)/shard_map/ppermute | solution.py:144
  93.5 8.5 %collective-permute-start.11 = (bf16[512,256]{1,0:T(8,128)(2,1)S(1)}, bf16[512,256]{1,0:T(8,128)(2,1)S(1)}, u32[]{:S(2)}, u32[]{:S(2)}) collective-permute-start(bf16[512,256]{1,0:T(8,128)(2,1)S(1)} %maximum_select_fusion.5), channel_id=1, source_target_pairs={{0,1},{1,0},{2,3},{3,2},{4,5},{5,4},{6,7},{7,6},{8,9},{9,8},{10,11... | collective-permute-start | bytes 786440 | tf_op jit(solution)/shard_map/ppermute | solution.py:144
